TPU v7x, 32 devices: a whole 2x2x4 slice. The times are simulated.
32 devices in a mesh: rep: 4 (over x, core), frame: 4 (over z), row: 2 (over y).
Axes of the slice: x: 2, y: 2, z: 4, core: 2. Of those that a mesh axis runs over, the one named last changes fastest.
Arguments:
- activations: bfloat16 [4, 4, 16, 32, 1280], P('rep', 'frame', 'row'), may hold values from -70 to 70, as said below
- spatial_weight: bfloat16 [9, 1280, 1280], P(None, None, ('rep', 'frame')), may hold values from -0.0546875 to 0.0546875
- temporal_weight: bfloat16 [3, 1280, 1280], P(None, None, ('rep', 'frame')), may hold values from -0.09375 to 0.09375
- first_gain: float32 [1280], replicated, may hold values from 0.25 to 1.75
- first_shift: float32 [1280], replicated, may hold values from -1.5 to 1.5
- spatial_bias: float32 [1280], replicated, may hold values from -2.5 to 2.5
- second_gain: float32 [1280], replicated, may hold values from 0.25 to 1.75
- second_shift: float32 [1280], replicated, may hold values from -1.5 to 1.5
- temporal_bias: float32 [1280], replicated, may hold values from -1.5 to 1.5
Outputs:
- block_out: float32 [4, 4, 16, 32, 1280], P('rep', 'frame', 'row')
Inputs may be any that keep to these rules, and one draw needn't show every extreme that they name: `activations`: finite values.
All inputs are finite; a program needn't handle non-finite values.
Results may differ from a plain program's by a relative error of at most 0.0009.
Values may be sent and summed in bfloat16 or wider, within the bound.
No kernel may reach another device: no remote copies, remote signals or barrier semaphores. Data moves between devices by JAX's collectives and lax.ppermute only.
A program may use at most 128 MiB of HBM per device.

v0:
```python
import jax
import jax.numpy as jnp
from jax import lax
from jax.sharding import PartitionSpec as P

GROUPS = 32


EPS = 1e-05


def padded_2(block, sides, width):
    for axis, dim in sides:
        count = lax.axis_size(axis)
        forward = [(i, i + 1) for i in range(count - 1)]
        backward = [(target, source) for source, target in forward]
        low = lax.ppermute(
            lax.slice_in_dim(block, block.shape[dim] - width, None, axis=dim), axis, forward
        )
        high = lax.ppermute(lax.slice_in_dim(block, 0, width, axis=dim), axis, backward)
        block = jnp.concatenate([low, block, high], axis=dim)
    return block


def norm_silu(field, gain, shift):
    samples = field.shape[0]
    width = field.shape[-1] // GROUPS
    grouped = field.reshape(samples, -1, GROUPS, width)
    sums = jnp.sum(grouped, axis=(1, 3))
    squares = jnp.sum(grouped * grouped, axis=(1, 3))
    sums, squares = lax.psum((sums, squares), ("frame", "row"))
    count = grouped.shape[1] * width * lax.axis_size("frame") * lax.axis_size("row")
    mean = sums / count
    variance = squares / count - mean * mean
    inverse = lax.rsqrt(variance + EPS)
    mean_full = jnp.repeat(mean, width, axis=1)[:, None, None, None, :]
    inverse_full = jnp.repeat(inverse, width, axis=1)[:, None, None, None, :]
    normed = (field - mean_full) * inverse_full * gain + shift
    return jax.nn.silu(normed).astype(jnp.bfloat16)


def conv_taps(padded, weights, rows, cols):
    leading = padded.shape[0] * padded.shape[1]
    channels = padded.shape[-1]
    summed = jnp.zeros((leading * rows * cols, weights.shape[-1]), jnp.float32)
    for row_tap in range(3):
        for col_tap in range(3):
            section = padded[:, :, row_tap : row_tap + rows, col_tap : col_tap + cols, :].reshape(
                -1, channels
            )
            summed = summed + jnp.dot(
                section, weights[3 * row_tap + col_tap], preferred_element_type=jnp.float32
            )
    return summed.reshape(padded.shape[0], padded.shape[1], rows, cols, -1)


def time_taps(window, weights, frames_dev):
    channels = window.shape[-1]
    samples, rows, cols = (window.shape[0], window.shape[2], window.shape[3])
    summed = jnp.zeros((samples * frames_dev * rows * cols, weights.shape[-1]), jnp.float32)
    for tap in range(3):
        section = window[:, tap : tap + frames_dev].reshape(-1, channels)
        summed = summed + jnp.dot(section, weights[tap], preferred_element_type=jnp.float32)
    return summed.reshape(samples, frames_dev, rows, cols, -1)


def shards(
    activations,
    spatial_weight,
    temporal_weight,
    first_gain,
    first_shift,
    spatial_bias,
    second_gain,
    second_shift,
    temporal_bias,
):
    frames_dev = activations.shape[1]
    rows_dev = activations.shape[2]
    cols = activations.shape[3]
    inputs = activations.astype(jnp.float32)
    first = norm_silu(inputs, first_gain, first_shift)
    with_rims = padded_2(first, (("row", 2),), 1)
    gathered = lax.all_gather(with_rims, "rep", axis=0, tiled=True)
    padded = jnp.pad(gathered, ((0, 0), (0, 0), (0, 0), (1, 1), (0, 0)))
    quarter = conv_taps(
        padded, lax.all_gather(spatial_weight, "frame", axis=2, tiled=True), rows_dev, cols
    )
    spatial = lax.all_to_all(
        quarter.astype(jnp.bfloat16), "rep", split_axis=0, concat_axis=4, tiled=True
    ).astype(quarter.dtype)
    spatial = spatial + spatial_bias
    second = norm_silu(spatial, second_gain, second_shift)
    window = padded_2(second, (("frame", 1),), 1)
    window_all = lax.all_gather(window, "rep", axis=0, tiled=True)
    quarter_time = time_taps(
        window_all, lax.all_gather(temporal_weight, "frame", axis=2, tiled=True), frames_dev
    )
    temporal = lax.all_to_all(
        quarter_time.astype(jnp.bfloat16), "rep", split_axis=0, concat_axis=4, tiled=True
    ).astype(quarter_time.dtype)
    return inputs + temporal + temporal_bias


def solution(mesh):
    placed = (
        P("rep", "frame", "row", None, None),
        P(None, None, ("rep", "frame")),
        P(None, None, ("rep", "frame")),
        P(),
        P(),
        P(),
        P(),
        P(),
        P(),
    )
    return jax.shard_map(
        shards,
        mesh=mesh,
        in_specs=placed,
        out_specs=P("rep", "frame", "row", None, None),
        check_vma=False,
    )
```

profile of v0, /device:TPU:0, one launch (start us, length us, event | category | flops | bytes accessed | tf_op | source)
XLA Modules:
  0.0 412.9 jit_solution(1252224786105186306)
XLA Ops:
  6.5 1.3 convert_reduce_fusion
  8.2 23.2 %all-reduce.2 = (f32[1,32]{1,0:T(1,128)S(1)}, f32[1,32]{1,0:T(1,128)S(1)}) all-reduce(f32[1,32]{1,0:T(1,128)S(1)} %bitcast.114, f32[1,32]{1,0:T(1,128)S(1)} %bitcast.112), channel_id=1, replica_groups=mesh['rep'=4,'frame'=4,'row'=2] {'frame','row'}, use_global_device_ids=true, to_apply=%region_5.6 | all-reduce | flops 64 | bytes 512 | tf_op jit(solution)/shard_map/psum | solution.py:31
  31.7 1.6 fusion.14
  33.3 1.3 collective-permute-start
  34.6 1.3 collective-permute-start.1
  36.6 4.3 %collective-permute-done.1 = bf16[1,1,1,32,1280]{4,3,2,1,0:T(8,128)(2,1)S(1)} collective-permute-done((bf16[1,1,1,32,1280]{4,3,2,1,0:T(8,128)(2,1)S(1)}, bf16[1,1,1,32,1280]{4,3,2,1,0:T(8,128)(2,1)S(1)}, u32[]{:S(2)}, u32[]{:S(2)}) %collective-permute-start.1) | collective-permute-done | bytes 81952 | tf_op jit(solution)/shard_map/ppermute | solution.py:20
  42.7 26.3 %all-gather.5.cloned.1.call-done = bf16[4,1,10,32,1280]{4,3,2,1,0:T(8,128)(2,1)} async-done(((bf16[1,1,10,32,1280]{4,3,2,1,0:T(8,128)(2,1)}), bf16[4,1,10,32,1280]{4,3,2,1,0:T(8,128)(2,1)}) %all-gather.5.cloned.1.call-update) | async-done | bytes 3276816 | tf_op jit(solution)/shard_map/all_gather | solution.py:84
  69.0 19.4 %pad_slice_fusion = (bf16[4,1,8,32,1280]{4,3,2,1,0:T(8,128)(2,1)S(1)}, bf16[4,1,8,32,1280]{4,3,2,1,0:T(8,128)(2,1)}, bf16[4,1,8,32,1280]{4,3,2,1,0:T(8,128)(2,1)...) fusion(bf16[4,1,10,32,1280]{4,3,2,1,0:T(8,128)(2,1)} %all-gathe, ...), kind=kLoop, calls=%fused_computation | loop fusion | bytes 34734080 | tf_op jit(solution)/shard_map/slice | solution.py:48
  88.3 115.2 %all-gather.7.cloned.1.call-done = bf16[9,1280,320]{1,2,0:T(8,128)(2,1)} async-done(((bf16[9,1280,80]{1,2,0:T(8,128)(2,1)}), bf16[9,1280,320]{1,2,0:T(8,128)(2,1)}) %all-gather.7.cloned.1.call-update) | async-done | bytes 7372816 | tf_op jit(solution)/shard_map/all_gather | solution.py:87
  203.6 3.1 fusion.18
  206.7 3.0 convolution_add_fusion.9
  211.5 1.0 convolution_add_fusion.7
  215.0 1.0 convolution_add_fusion.5
  216.7 1.0 convolution_add_fusion.4
  219.5 1.1 fusion.4
  220.6 1.2 copy.24
  221.7 3.5 all-to-all-start
  225.4 11.5 %all-to-all-done = bf16[4,1,8,32,320]{4,3,2,1,0:T(8,128)(2,1)S(1)} async-done(((bf16[4,1,8,32,320]{4,3,2,1,0:T(8,128)(2,1)}), bf16[4,1,8,32,320]{4,3,2,1,0:T(8,128)(2,1)S(1)}, u32[]{:S(2)}, u32[]{:S(2)}) %all-to-all-start) | async-done | bytes 655392 | tf_op jit(solution)/shard_map/all_to_all | solution.py:89
  237.5 18.8 %all-reduce.1 = (f32[1,32]{1,0:T(1,128)S(1)}, f32[1,32]{1,0:T(1,128)S(1)}) all-reduce(f32[1,32]{1,0:T(1,128)S(1)} %bitcast.113, f32[1,32]{1,0:T(1,128)S(1)} %bitcast.111), channel_id=1, replica_groups=mesh['rep'=4,'frame'=4,'row'=2] {'frame','row'}, use_global_device_ids=true, to_apply=%region_11.12 | all-reduce | flops 64 | bytes 512 | tf_op jit(solution)/shard_map/psum | solution.py:31
  259.3 1.3 collective-permute-start.2
  260.6 1.3 collective-permute-start.3
  261.9 8.9 %collective-permute-done.2 = bf16[1,1,8,32,1280]{4,3,2,1,0:T(8,128)(2,1)S(1)} collective-permute-done((bf16[1,1,8,32,1280]{4,3,2,1,0:T(8,128)(2,1)S(1)}, bf16[1,1,8,32,1280]{4,3,2,1,0:T(8,128)(2,1)S(1)}, u32[]{:S(2)}, u32[]{:S(2)}) %collective-permute-start.2) | collective-permute-done | bytes 655392 | tf_op jit(solution)/shard_map/ppermute | solution.py:17
  270.8 4.2 %collective-permute-done.3 = bf16[1,1,8,32,1280]{4,3,2,1,0:T(8,128)(2,1)S(1)} collective-permute-done((bf16[1,1,8,32,1280]{4,3,2,1,0:T(8,128)(2,1)S(1)}, bf16[1,1,8,32,1280]{4,3,2,1,0:T(8,128)(2,1)S(1)}, u32[]{:S(2)}, u32[]{:S(2)}) %collective-permute-start.3) | collective-permute-done | bytes 655392 | tf_op jit(solution)/shard_map/ppermute | solution.py:20
  274.9 1.6 pad_maximum_fusion
  277.1 52.2 %all-gather.9.cloned.1.call-done = bf16[4,3,8,32,1280]{4,3,2,1,0:T(8,128)(2,1)} async-done(((bf16[1,3,8,32,1280]{4,3,2,1,0:T(8,128)(2,1)}), bf16[4,3,8,32,1280]{4,3,2,1,0:T(8,128)(2,1)}) %all-gather.9.cloned.1.call-update) | async-done | bytes 7864336 | tf_op jit(solution)/shard_map/all_gather | solution.py:95
  329.3 5.2 %fusion.19 = (bf16[4,1,8,32,1280]{4,3,2,1,0:T(8,128)(2,1)S(1)}, bf16[4,1,8,32,1280]{4,3,2,1,0:T(8,128)(2,1)}, bf16[4,1,8,32,1280]{4,3,2,1,0:T(8,128)(2,1)}) fusion(bf16[4,3,8,32,1280]{4,3,2,1,0:T(8,128)(2,1)} %all-gather.9.cloned.1.call-done), kind=kLoop, calls=%fused_computation.61 | loop fusion | bytes 15728640 | tf_op jit(solution)/shard_map/slice | solution.py:62
  334.5 48.2 %all-gather.11.cloned.1.call-done = bf16[3,1280,320]{1,2,0:T(8,128)(2,1)} async-done(((bf16[3,1280,80]{1,2,0:T(8,128)(2,1)}), bf16[3,1280,320]{1,2,0:T(8,128)(2,1)}) %all-gather.11.cloned.1.call-update) | async-done | bytes 2457616 | tf_op jit(solution)/shard_map/all_gather | solution.py:97
  382.7 3.1 fusion.17
  386.2 1.0 convolution_add_fusion.1
  387.3 1.0 fusion.5
  388.7 14.2 %all_to_all.8 = bf16[4,1,8,32,320]{4,3,2,1,0:T(8,128)(2,1)S(1)} all-to-all(bf16[4,1,8,32,320]{4,3,2,1,0:T(8,128)(2,1)S(1)} %bitcast.98), channel_id=1, replica_groups=mesh['rep'=4,'frame'=4,'row'=2] {'rep'}, dimensions={0} | all-to-all | bytes 1310720 | tf_op jit(solution)/shard_map/all_to_all | solution.py:99
  405.1 1.2 fusion.16
  (72 shorter events, 17.2 us)
Async XLA Ops:
  6.5 62.4 %all-gather.5.cloned.1.call-start = ((), (), s32[]{:S(2)}) async-start(), calls=%async_computation.2 | async-start | bytes 4096000 | tf_op jit(solution)/shard_map/all_gather | solution.py:84
  33.3 3.3 collective-permute-start
  34.6 6.3 %collective-permute-start.1 = (bf16[1,1,1,32,1280]{4,3,2,1,0:T(8,128)(2,1)S(1)}, bf16[1,1,1,32,1280]{4,3,2,1,0:T(8,128)(2,1)S(1)}, u32[]{:S(2)}, u32[]{:S(2)}) collective-permute-start(bf16[1,1,1,32,1280]{4,3,2,1,0:T(8,128)(2,1)S(1)} %get-tuple-element.26), channel_id=1, source_target_pairs={{1,0},{3,2},{5,4},{7,6},{9,8},{11,10},{13,12},{15,14},{17,16},{19,... | collective-permute-start | bytes 245768 | tf_op jit(solution)/shard_map/ppermute | solution.py:20
  42.0 161.6 %all-gather.7.cloned.1.call-start = ((), (), s32[]{:S(2)}) async-start(), calls=%async_computation.3 | async-start | bytes 9216000 | tf_op jit(solution)/shard_map/all_gather | solution.py:87
  203.6 3.1 copy-start.7
  203.6 6.1 %copy-start.13 = (bf16[9,1280,320]{1,2,0:T(8,128)(2,1)S(1)}, bf16[9,1280,320]{1,2,0:T(8,128)(2,1)}, u32[]{:S(2)}) copy-start(bf16[9,1280,320]{1,2,0:T(8,128)(2,1)} %all-gather.7.cloned.1.call-done) | copy-start | bytes 22118404
  206.7 3.0 copy-start.6
  209.7 1.7 copy-start.5
  211.5 1.7 copy-start.4
  213.2 1.7 copy-start.3
  215.0 1.7 copy-start.2
  216.7 1.7 copy-start.1
  220.6 4.7 %copy-start.9 = (f32[1280]{0:T(1024)S(1)}, f32[1280]{0:T(1024)}, u32[]{:S(2)}) copy-start(f32[1280]{0:T(1024)} %param.14) | copy-start | bytes 15364
  221.7 15.1 %all-to-all-start = ((bf16[4,1,8,32,320]{4,3,2,1,0:T(8,128)(2,1)}), bf16[4,1,8,32,320]{4,3,2,1,0:T(8,128)(2,1)S(1)}, u32[]{:S(2)}, u32[]{:S(2)}) async-start(bf16[4,1,8,32,320]{4,3,2,1,0:T(8,128)(2,1)} %bitcast.23), calls=%async_computation | async-start | bytes 1572864 | tf_op jit(solution)/shard_map/all_to_all | solution.py:89
  225.2 104.1 %all-gather.9.cloned.1.call-start = ((), (), s32[]{:S(2)}) async-start(), calls=%async_computation.4 | async-start | bytes 9830400 | tf_op jit(solution)/shard_map/all_gather | solution.py:95
  257.9 0.9 copy-start.10
  257.9 0.9 copy-start.11
  259.3 11.5 %collective-permute-start.2 = (bf16[1,1,8,32,1280]{4,3,2,1,0:T(8,128)(2,1)S(1)}, bf16[1,1,8,32,1280]{4,3,2,1,0:T(8,128)(2,1)S(1)}, u32[]{:S(2)}, u32[]{:S(2)}) collective-permute-start(bf16[1,1,8,32,1280]{4,3,2,1,0:T(8,128)(2,1)S(1)} %multiply_convert_fusion), channel_id=1, source_target_pairs={{0,2},{2,4},{4,6},{1,3},{3,5},{5,7},{8,10},{10,12},{12,14},{9,11},... | collective-permute-start | bytes 1966088 | tf_op jit(solution)/shard_map/ppermute | solution.py:17
  260.6 14.3 %collective-permute-start.3 = (bf16[1,1,8,32,1280]{4,3,2,1,0:T(8,128)(2,1)S(1)}, bf16[1,1,8,32,1280]{4,3,2,1,0:T(8,128)(2,1)S(1)}, u32[]{:S(2)}, u32[]{:S(2)}) collective-permute-start(bf16[1,1,8,32,1280]{4,3,2,1,0:T(8,128)(2,1)S(1)} %multiply_convert_fusion), channel_id=1, source_target_pairs={{2,0},{4,2},{6,4},{3,1},{5,3},{7,5},{10,8},{12,10},{14,12},{11,9},... | collective-permute-start | bytes 1966088 | tf_op jit(solution)/shard_map/ppermute | solution.py:20
  276.5 106.2 %all-gather.11.cloned.1.call-start = ((), (), s32[]{:S(2)}) async-start(), calls=%async_computation.5 | async-start | bytes 3072000 | tf_op jit(solution)/shard_map/all_gather | solution.py:97
  382.7 3.1 copy-start.8
  382.7 3.5 copy-start.14
  404.1 1.1 copy-start
  404.1 1.1 copy-start.12
Sparse Core Ops, SparseCore 0:
  42.1 26.8 all-gather.4
  70.5 132.9 all-gather.6
  276.7 52.6 all-gather.8
  330.8 51.8 all-gather.10
where the time goes:
time: 413 us
  waiting for transfers between devices  273 us (66%)
  blocking collectives  56.1 us (14%)
  local copies, waits for them, and re-layouts  35 us (8%)
  matrix products  18.6 us (5%)
  between operations  13.5 us (3%)
  starting transfers between devices  8.83 us (2%)
  other arithmetic  8.25 us (2%)
    all_gather x1, waiting for transfers between devices, shards(): lax.all_gather(spatial_weight, 'frame', axis=2, tiled=True)  115 us
    all_gather x1, waiting for transfers between devices, shards(): window_all = lax.all_gather(window, 'rep', axis=0, tiled=True)  52.2 us
    all_gather x1, waiting for transfers between devices, shards(): lax.all_gather(temporal_weight, 'frame', axis=2, tiled=True)  48.2 us
    psum x2, blocking collectives, norm_silu(): sums, squares = lax.psum((sums, squares), ('frame', 'row'))  41.9 us
    all_gather x1, waiting for transfers between devices, shards(): gathered = lax.all_gather(with_rims, 'rep', axis=0, tiled=True)  26.3 us
    slice x1, local copies, waits for them, and re-layouts, conv_taps(): padded[:, :, row_tap:row_tap + rows, col_tap:col_tap + cols, :]  19.4 us
    all_to_all x1, blocking collectives, shards(): lax.all_to_all(quarter_time.astype(jnp.bfloat16), 'rep', split_axis=0, co...  14.2 us
    dot_general x9, matrix products, conv_taps(): jnp.dot(section, weights[3 * row_tap + col_tap], preferred_element_type=j...  13.4 us
  transfers between devices with their start and end apart: 9, of which 9 were waited for; matrix products, arithmetic and copies ran while one was open for 6% of the time, Pallas kernels for 0%

commit v1 on v0

v1 whole, which is shorter than its diff:
```python
import numpy as np

import jax
import jax.numpy as jnp
from jax import lax
from jax.sharding import PartitionSpec as P

GROUPS = 32


EPS = 1e-05


def pair_sum(value, axis):
    if lax.axis_size(axis) == 2:
        return jax.tree.map(
            lambda v: v + lax.ppermute(v, axis, [(0, 1), (1, 0)]), value
        )
    return lax.psum(value, axis)


def gather_rep(w):
    size = lax.axis_size("rep")
    if size & (size - 1) != 0:
        return lax.all_gather(w, "rep", axis=w.ndim - 1, tiled=True), list(range(size))
    index = lax.axis_index("rep")
    blocks = w[None]
    order = [0]
    step = size // 2
    while step >= 1:
        recv = lax.ppermute(blocks, "rep", [(k, k ^ step) for k in range(size)])
        upper = (index & step) != 0
        low = jnp.where(upper, recv, blocks)
        high = jnp.where(upper, blocks, recv)
        blocks = jnp.concatenate([low, high], axis=0)
        order = order + [o + step for o in order]
        step //= 2
    out = jnp.moveaxis(blocks, 0, -2)
    return out.reshape(out.shape[:-2] + (-1,)), order


def local_vector(vec, order, frame_index, rep_size, frame_size):
    width = vec.shape[0] // (rep_size * frame_size)
    table = vec.reshape(rep_size, frame_size, width)[np.array(order)]
    return lax.dynamic_index_in_dim(table, frame_index, axis=1, keepdims=False).reshape(-1)


def silu_bf16(normed):
    return jax.nn.silu(normed).astype(jnp.bfloat16)


def shards(
    activations,
    spatial_weight,
    temporal_weight,
    first_gain,
    first_shift,
    spatial_bias,
    second_gain,
    second_shift,
    temporal_bias,
):
    rep_size = lax.axis_size("rep")
    frame_size = lax.axis_size("frame")
    row_size = lax.axis_size("row")
    frame_index = lax.axis_index("frame")
    row_index = lax.axis_index("row")
    channels = activations.shape[-1]
    rows = activations.shape[2]
    cols = activations.shape[3]
    width = channels // GROUPS
    shard_width = spatial_weight.shape[-1]

    spatial_w, order = gather_rep(spatial_weight)
    temporal_w, _ = gather_rep(temporal_weight)
    local = spatial_w.shape[-1]

    raw = lax.all_gather(activations, "frame", axis=1, tiled=True)
    frames = raw.shape[1]

    if row_size > 1:
        down = [(i, i + 1) for i in range(row_size - 1)]
        up = [(i + 1, i) for i in range(row_size - 1)]
        above = lax.ppermute(raw[:, :, rows - 1 :], "row", down)
        below = lax.ppermute(raw[:, :, :1], "row", up)
    else:
        above = jnp.zeros_like(raw[:, :, :1])
        below = jnp.zeros_like(raw[:, :, :1])

    inputs = raw.astype(jnp.float32)
    grouped = inputs.reshape(1, -1, GROUPS, width)
    sums = jnp.sum(grouped, axis=(1, 3))
    squares = jnp.sum(grouped * grouped, axis=(1, 3))
    sums, squares = pair_sum((sums, squares), "row")
    count = grouped.shape[1] * width * row_size
    mean = sums / count
    variance = squares / count - mean * mean
    inverse = lax.rsqrt(variance + EPS)
    mean_full = jnp.repeat(mean, width, axis=1)[:, None, None, None, :]
    inverse_full = jnp.repeat(inverse, width, axis=1)[:, None, None, None, :]

    def first_norm(x):
        normed = (x.astype(jnp.float32) - mean_full) * inverse_full * first_gain + first_shift
        return silu_bf16(normed)

    first_mid = first_norm(raw)
    first_above = jnp.where(row_index > 0, first_norm(above), jnp.zeros((), jnp.bfloat16))
    first_below = jnp.where(
        row_index < row_size - 1, first_norm(below), jnp.zeros((), jnp.bfloat16)
    )
    padded = jnp.concatenate([first_above, first_mid, first_below], axis=2)

    lhs = padded.reshape(frames, rows + 2, cols, channels)
    kernel = spatial_w.reshape(3, 3, channels, local)
    spatial = lax.conv_general_dilated(
        lhs,
        kernel,
        window_strides=(1, 1),
        padding=((0, 0), (1, 1)),
        dimension_numbers=("NHWC", "HWIO", "NHWC"),
        preferred_element_type=jnp.float32,
    )
    spatial = spatial + local_vector(spatial_bias, order, frame_index, rep_size, frame_size)

    g2 = local_vector(second_gain, order, frame_index, rep_size, frame_size)
    s2 = local_vector(second_shift, order, frame_index, rep_size, frame_size)
    if shard_width % width == 0:
        grouped2 = spatial.reshape(-1, local // width, width)
        sums2 = jnp.sum(grouped2, axis=(0, 2))
        squares2 = jnp.sum(grouped2 * grouped2, axis=(0, 2))
        sums2, squares2 = pair_sum((sums2, squares2), "row")
        count2 = grouped2.shape[0] * width * row_size
        mean2 = sums2 / count2
        variance2 = squares2 / count2 - mean2 * mean2
        inverse2 = lax.rsqrt(variance2 + EPS)
        mean2_full = jnp.repeat(mean2, width)
        inverse2_full = jnp.repeat(inverse2, width)
    else:
        flat = spatial.reshape(-1, local)
        csum = jnp.sum(flat, axis=0)
        csq = jnp.sum(flat * flat, axis=0)
        csum, csq = pair_sum((csum, csq), "row")
        both = lax.all_gather(jnp.stack([csum, csq]), "frame", axis=0)
        both = both.reshape(frame_size, 2, rep_size, shard_width)
        inv_order = np.argsort(np.array(order))
        both = both[:, :, inv_order]
        both = jnp.transpose(both, (1, 2, 0, 3)).reshape(2, GROUPS, -1)
        gsum = jnp.sum(both, axis=2)
        count2 = flat.shape[0] * row_size * width
        gmean = gsum[0] / count2
        gvar = gsum[1] / count2 - gmean * gmean
        ginv = lax.rsqrt(gvar + EPS)
        mean2_full = local_vector(jnp.repeat(gmean, width), order, frame_index, rep_size, frame_size)
        inverse2_full = local_vector(jnp.repeat(ginv, width), order, frame_index, rep_size, frame_size)
    second = silu_bf16((spatial - mean2_full) * inverse2_full * g2 + s2)

    second_all = lax.all_gather(second, "frame", axis=3, tiled=True)
    rows_order = np.arange(channels).reshape(rep_size, frame_size, shard_width)
    rows_order = rows_order[np.array(order)].transpose(1, 0, 2).reshape(-1)
    temporal_w = temporal_w[:, rows_order, :]
    lhs_t = second_all.reshape(frames, rows * cols, frame_size * local)[None]
    kernel_t = temporal_w.reshape(3, 1, frame_size * local, local)
    temporal = lax.conv_general_dilated(
        lhs_t,
        kernel_t,
        window_strides=(1, 1),
        padding=((1, 1), (0, 0)),
        dimension_numbers=("NHWC", "HWIO", "NHWC"),
        preferred_element_type=jnp.float32,
    )
    temporal = temporal.reshape(1, frames, rows, cols, local).astype(jnp.bfloat16)
    back = lax.all_to_all(temporal, "frame", split_axis=1, concat_axis=4, tiled=True)
    per_frame = frames // frame_size
    back = back.reshape(1, per_frame, rows, cols, frame_size, rep_size, shard_width)
    back = back[:, :, :, :, :, np.argsort(np.array(order))]
    back = jnp.swapaxes(back, 4, 5).reshape(1, per_frame, rows, cols, channels)
    return activations.astype(jnp.float32) + back.astype(jnp.float32) + temporal_bias


def solution(mesh):
    placed = (
        P("rep", "frame", "row", None, None),
        P(None, None, ("rep", "frame")),
        P(None, None, ("rep", "frame")),
        P(),
        P(),
        P(),
        P(),
        P(),
        P(),
    )
    return jax.shard_map(
        shards,
        mesh=mesh,
        in_specs=placed,
        out_specs=P("rep", "frame", "row", None, None),
        check_vma=False,
    )
```

time: 413 us -> 382 us (0.925)
  waiting for transfers between devices: 273 us -> 217 us
  blocking collectives: 56.1 us -> 23 us
  other arithmetic: 8.25 us -> 32.9 us
  local copies, waits for them, and re-layouts: 35 us -> 57.4 us
  matrix products: 18.6 us -> 24 us
  starting transfers between devices: 8.83 us -> 13.6 us
    all_gather x4 -> x2, waiting for transfers between devices: 242 us -> 160 us  [the longest x1 149 us: shards(): second_all = lax.all_gather(second, 'frame', axis=3, tiled=True)]
    psum x2 -> x0, blocking collectives: 41.9 us -> none  [norm_silu(): sums, squares = lax.psum((sums, squares), ('frame', 'row'))]
    ppermute x4 -> x10, waiting for transfers between devices: 18 us -> 56.2 us  [the longest x4 49.5 us: gather_rep(): recv = lax.ppermute(blocks, 'rep', [(k, k ^ step) for k in range(size)])]
    conv_general_dilated x0 -> x2, matrix products: none -> 24 us  [the longest x1 17.7 us: shards(): lax.conv_general_dilated(lhs, kernel, window_strides=(1, 1), padding=((0,...]
    slice x3 -> x1, local copies, waits for them, and re-layouts: 24.6 us -> 1.12 us  [shards(): above = lax.ppermute(raw[:, :, rows - 1:], 'row', down)]
    dot_general x12 -> x0, matrix products: 18.6 us -> none  [the longest x9 13.4 us: conv_taps(): jnp.dot(section, weights[3 * row_tap + col_tap], preferred_element_type=j...]
    gather x0 -> x5, local copies, waits for them, and re-layouts: none -> 14.5 us  [the longest x1 12 us: shards(): temporal_w = temporal_w[:, rows_order, :]]
    all_gather x0 -> x1, local copies, waits for them, and re-layouts: none -> 12.8 us  [shards(): second_all = lax.all_gather(second, 'frame', axis=3, tiled=True)]
  transfers between devices with their start and end apart: 9 -> 12, of which waited for: 9 -> 9; matrix products, arithmetic and copies ran while one was open for 6% -> 12% of each run, Pallas kernels for 0% -> 0%
where the time goes in v1:
time: 382 us; the launch traced here: 381 us
  waiting for transfers between devices  217 us (57%)
  local copies, waits for them, and re-layouts  57.4 us (15%)
  other arithmetic  32.9 us (9%)
  matrix products  24 us (6%)
  blocking collectives  23 us (6%)
  between operations  13.7 us (4%)
  starting transfers between devices  13.6 us (4%)
    all_gather x1, waiting for transfers between devices, shards(): second_all = lax.all_gather(second, 'frame', axis=3, tiled=True)  149 us
    ppermute x4, waiting for transfers between devices, gather_rep(): recv = lax.ppermute(blocks, 'rep', [(k, k ^ step) for k in range(size)])  49.5 us
    all_to_all x1, blocking collectives, shards(): lax.all_to_all(temporal, 'frame', split_axis=1, concat_axis=4, tiled=True)  23 us
    conv_general_dilated x1, matrix products, shards(): lax.conv_general_dilated(lhs, kernel, window_strides=(1, 1), padding=((0,...  17.7 us
    all_gather x1, local copies, waits for them, and re-layouts, shards(): second_all = lax.all_gather(second, 'frame', axis=3, tiled=True)  12.8 us
    gather x1, local copies, waits for them, and re-layouts, shards(): temporal_w = temporal_w[:, rows_order, :]  12 us
    all_gather x1, waiting for transfers between devices, shards(): raw = lax.all_gather(activations, 'frame', axis=1, tiled=True)  10.8 us
  transfers between devices with their start and end apart: 12, of which 9 were waited for; matrix products, arithmetic and copies ran while one was open for 12% of the time, Pallas kernels for 0%

profile of v1, /device:TPU:0, one launch (start us, length us, event | category | flops | bytes accessed | tf_op | source)
XLA Modules:
  0.0 381.3 jit_solution(2174034292066160613)
XLA Ops:
  7.3 3.0 collective-permute-start.4
  15.4 35.5 %collective-permute-done.4 = bf16[1,9,1280,80]{2,3,1,0:T(8,128)(2,1)} collective-permute-done((bf16[1,9,1280,80]{2,3,1,0:T(8,128)(2,1)}, bf16[1,9,1280,80]{2,3,1,0:T(8,128)(2,1)}, u32[]{:S(2)}, u32[]{:S(2)}) %collective-permute-start.4) | collective-permute-done | bytes 1843232 | tf_op jit(solution)/shard_map/ppermute | solution.py:31
  50.8 2.3 broadcast_select_fusion.3
  53.2 2.4 pad_maximum_fusion
  55.6 10.8 %all-gather.3.cloned.1.call-done = bf16[1,4,8,32,1280]{4,3,2,0,1:T(8,128)(2,1)} async-done(((bf16[1,1,8,32,1280]{4,3,2,0,1:T(8,128)(2,1)}), bf16[1,4,8,32,1280]{4,3,2,0,1:T(8,128)(2,1)}) %all-gather.3.cloned.1.call-update) | async-done | bytes 2621456 | tf_op jit(solution)/shard_map/all_gather | solution.py:78
  67.5 3.4 collective-permute-start
  70.9 2.5 convert_reduce_fusion
  73.9 2.1 collective-permute-start.2
  78.1 3.5 fusion.14
  81.7 4.6 %collective-permute-done.3 = bf16[1,4,1,32,1280]{4,3,2,0,1:T(8,128)(2,1)S(1)} collective-permute-done((bf16[1,4,1,32,1280]{4,3,2,0,1:T(8,128)(2,1)S(1)}, bf16[1,4,1,32,1280]{4,3,2,0,1:T(8,128)(2,1)S(1)}, u32[]{:S(2)}, u32[]{:S(2)}) %collective-permute-start.3) | collective-permute-done | bytes 327712 | tf_op jit(solution)/shard_map/ppermute | solution.py:85
  87.2 2.5 copy.78
  89.7 1.6 pad.clone
  91.9 4.8 %fusion.1 = bf16[10,4,8,7,1280]{4,1,3,2,0:T(4,128)(2,1)} fusion(bf16[10,4,7,2,1280]{4,1,3,2,0:T(4,128)(2,1)S(1)} %slice.23, bf16[10,4,8,5,1280]{4,1,3,2,0:T(4,128)(2,1)S(1)} %bitcast.63), kind=kLoop, calls=%fused_computation.11 | loop fusion | flops 17203200 | bytes 11264000 | tf_op jit(solution)/shard_map/conv_general_dilated | solution.py:115
  96.7 4.7 %broadcast_select_fusion.1 = (bf16[2,9,1280,80]{2,3,1,0:T(8,128)(2,1)}, bf16[2,9,1280,80]{2,3,1,0:T(8,128)(2,1)}) fusion(bf16[2,9,1280,80]{2,3,1,0:T(8,128)(2,1)} %collective-permute-done.5, pred[]{:T(512)S(6)} %ne.8, bf16[1,9,1280,80]{2,3,1,0:T(8,128)(2,1)S(1)} %copy-done.1, bf16[1,9,1280,80]{2,3,1,0:T(8,128)(2,1)S(1)} %get-tuple-element.13), kind=kLoop, calls=%fused_computation.27 | loop fusion | flops 5529600 | bytes 14745601 | tf_op jit(solution)/shard_map/jit(_where)/select_n | solution.py:33
  101.5 6.8 %maximum_bitcast_fusion = bf16[9,1280,4,80]{1,3,0,2:T(8,128)(2,1)} fusion(bf16[2,9,1280,80]{2,3,1,0:T(8,128)(2,1)} %get-tuple-element.12, bf16[2,9,1280,80]{2,3,1,0:T(8,128)(2,1)} %get-tuple-element.11), kind=kLoop, calls=%fused_computation.10 | loop fusion | flops 3686400 | bytes 14745600 | tf_op jit(solution)/shard_map/transpose | solution.py:38
  108.2 3.8 copy.66
  112.0 17.7 %select_reduce_fusion = (f32[320]{0:T(512)S(1)}, f32[320]{0:T(512)S(1)}, f32[8,32,5,320]{3,1,2,0:T(8,128)S(1)}) fusion(pred[32,5]{0,1:T(8,128)(4,1)S(1)} %copy-done.7, f32[320]{0:T(512)S(1)} %add.127, bf16[3,3,1280,320]{2,3,1,0:T(8,128)(2,1)S(1)} %bitcast.65, bf16[10,4,8,7,1280]{4,1,3,2,0:T(4,128)(2,1)} %fusion.1), kind=kOutput, calls=%fused_computation.34 | convolution fusion | flops 9440051200 | bytes 14749600 | tf_op jit(solution)/shard_map/conv_general_dilated | solution.py:115
  130.2 2.1 collective-permute-start.6
  132.3 1.3 collective-permute-done.7
  135.2 5.4 %copy.68 = bf16[4,8,32,320]{2,1,0,3:T(8,128)(2,1)} copy(bf16[4,8,32,320]{3,1,2,0:T(8,128)(2,1)S(1)} %slice_bitcast_fusion) | data formatting | bytes 1310720 | tf_op jit(solution)/shard_map/convert_element_type | solution.py:49
  140.7 1.5 collective-permute-start.8
  142.3 11.1 %collective-permute-done.8 = bf16[1,3,1280,80]{2,3,0,1:T(8,128)(2,1)S(1)} collective-permute-done((bf16[1,3,1280,80]{2,3,0,1:T(8,128)(2,1)S(1)}, bf16[1,3,1280,80]{2,3,0,1:T(8,128)(2,1)S(1)}, u32[]{:S(2)}, u32[]{:S(2)}) %collective-permute-start.8) | collective-permute-done | bytes 614432 | tf_op jit(solution)/shard_map/ppermute | solution.py:31
  153.7 2.9 collective-permute-done.9
  157.0 6.3 %copy.69 = bf16[3,1280,320]{2,0,1:T(4,128)(2,1)} copy(bf16[3,1280,320]{1,2,0:T(8,128)(2,1)S(1)} %bitcast.64) | data formatting | bytes 4915200 | tf_op jit(solution)/shard_map/reshape | solution.py:39
  163.3 12.0 %gather_fusion.3 = bf16[1280,3,320]{2,1,0:T(4,128)(2,1)} fusion(bf16[3,1280,320]{2,0,1:T(4,128)(2,1)} %copy.69, s32[2048]{0:T(1024)S(1)} %pad_clamp_fusion), kind=kCustom, calls=%fused_computation.3 | custom fusion | bytes 4920320 | tf_op jit(solution)/shard_map/gather | solution.py:160
  175.4 148.9 %all-gather.5.cloned.1.call-done = bf16[4,8,32,1280]{2,1,0,3:T(8,128)(2,1)} async-done(((bf16[4,8,32,320]{2,1,0,3:T(8,128)(2,1)}), bf16[4,8,32,1280]{2,1,0,3:T(8,128)(2,1)}) %all-gather.5.cloned.1.call-update) | async-done | bytes 2621456 | tf_op jit(solution)/shard_map/all_gather | solution.py:157
  324.3 12.8 %copy.70 = bf16[4,8,32,1280]{3,1,2,0:T(8,128)(2,1)S(1)} copy(bf16[4,8,32,1280]{2,1,0,3:T(8,128)(2,1)} %all-gather.5.cloned.1.call-done) | data formatting | bytes 5242880 | tf_op jit(solution)/shard_map/all_gather | solution.py:157
  337.1 6.3 %fusion.22 = bf16[1,4,8,32,320]{4,2,3,0,1:T(8,128)(2,1)S(1)} fusion(bf16[4,8,32,1280]{3,1,2,0:T(8,128)(2,1)S(1)} %copy.70, bf16[3,1,1280,320]{3,0,2,1:T(4,128)(2,1)} %bitcast.69), kind=kOutput, calls=%fused_computation.41 | convolution fusion | flops 2097479680 | bytes 5734400 | tf_op jit(solution)/shard_map/conv_general_dilated | solution.py:163
  343.5 23.0 %all_to_all.15 = bf16[1,4,8,32,320]{4,2,3,0,1:T(8,128)(2,1)S(1)} all-to-all(bf16[1,4,8,32,320]{4,2,3,0,1:T(8,128)(2,1)S(1)} %fusion.22), channel_id=1, replica_groups=mesh['rep'=4,'frame'=4,'row'=2] {'frame'}, dimensions={1} | all-to-all | bytes 1310720 | tf_op jit(solution)/shard_map/all_to_all | solution.py:172
  368.5 1.4 copy.75
  369.9 2.2 reshape.124
  372.2 2.3 add_add_fusion
  (76 shorter events, 15.8 us)
Async XLA Ops:
  6.5 59.9 %all-gather.3.cloned.1.call-start = ((), (), s32[]{:S(2)}) async-start(), calls=%async_computation.1 | async-start | bytes 3276800 | tf_op jit(solution)/shard_map/all_gather | solution.py:78
  7.3 317.0 %all-gather.5.cloned.1.call-start = ((), (), s32[]{:S(2)}) async-start(), calls=%async_computation.2 | async-start | bytes 13107200 | tf_op jit(solution)/shard_map/all_gather | solution.py:157
  7.3 43.5 %collective-permute-start.4 = (bf16[1,9,1280,80]{2,3,1,0:T(8,128)(2,1)}, bf16[1,9,1280,80]{2,3,1,0:T(8,128)(2,1)}, u32[]{:S(2)}, u32[]{:S(2)}) collective-permute-start(bf16[1,9,1280,80]{2,3,1,0:T(8,128)(2,1)} %bitcast.70), channel_id=1, source_target_pairs={{0,16},{8,24},{16,0},{24,8},{1,17},{9,25},{17,1},{25,9},{2,18},{10... | collective-permute-start | bytes 5529608 | tf_op jit(solution)/shard_map/ppermute | solution.py:31
  53.1 2.4 copy-start
  55.6 22.5 %copy-start.3 = (f32[1280]{0:T(1024)S(1)}, f32[1280]{0:T(1024)}, u32[]{:S(2)}) copy-start(f32[1280]{0:T(1024)} %param.23) | copy-start | bytes 15364
  55.6 22.5 %copy-start.4 = (f32[1280]{0:T(1024)S(1)}, f32[1280]{0:T(1024)}, u32[]{:S(2)}) copy-start(f32[1280]{0:T(1024)} %param.22) | copy-start | bytes 15364
  55.6 41.2 %collective-permute-start.5 = (bf16[2,9,1280,80]{2,3,1,0:T(8,128)(2,1)}, bf16[2,9,1280,80]{2,3,1,0:T(8,128)(2,1)}, u32[]{:S(2)}, u32[]{:S(2)}) collective-permute-start(bf16[2,9,1280,80]{2,3,1,0:T(8,128)(2,1)} %pad_maximum_fusion), channel_id=1, source_target_pairs={{0,8},{8,0},{16,24},{24,16},{1,9},{9,1},{17,25},{25,17},{2,10},{10... | collective-permute-start | bytes 11059208 | tf_op jit(solution)/shard_map/ppermute | solution.py:31
  67.5 14.1 %collective-permute-start = (bf16[1,4,1,32,1280]{4,3,2,0,1:T(8,128)(2,1)S(1)}, bf16[1,4,1,32,1280]{4,3,2,0,1:T(8,128)(2,1)S(1)}, u32[]{:S(2)}, u32[]{:S(2)}) collective-permute-start(bf16[1,4,1,32,1280]{4,3,2,0,1:T(8,128)(2,1)S(1)} %get-tuple-element.15), channel_id=1, source_target_pairs={{0,1},{2,3},{4,5},{6,7},{8,9},{10,11},{12,13},{14,15},{16,17},{18,... | collective-permute-start | bytes 983048 | tf_op jit(solution)/shard_map/ppermute | solution.py:84
  73.6 4.1 %collective-permute-start.1 = (f32[1,32]{1,0:T(1,128)S(1)}, f32[1,32]{1,0:T(1,128)S(1)}, u32[]{:S(2)}, u32[]{:S(2)}) collective-permute-start(f32[1,32]{1,0:T(1,128)S(1)} %bitcast.72), channel_id=1, source_target_pairs={{0,1},{1,0},{2,3},{3,2},{4,5},{5,4},{6,7},{7,6},{8,9},{9,8},{10,11... | collective-permute-start | bytes 392 | tf_op jit(solution)/shard_map/ppermute | solution.py:17
  73.9 3.9 %collective-permute-start.2 = (f32[1,32]{1,0:T(1,128)S(1)}, f32[1,32]{1,0:T(1,128)S(1)}, u32[]{:S(2)}, u32[]{:S(2)}) collective-permute-start(f32[1,32]{1,0:T(1,128)S(1)} %bitcast.73), channel_id=1, source_target_pairs={{0,1},{1,0},{2,3},{3,2},{4,5},{5,4},{6,7},{7,6},{8,9},{9,8},{10,11... | collective-permute-start | bytes 392 | tf_op jit(solution)/shard_map/ppermute | solution.py:17
  76.0 10.3 %collective-permute-start.3 = (bf16[1,4,1,32,1280]{4,3,2,0,1:T(8,128)(2,1)S(1)}, bf16[1,4,1,32,1280]{4,3,2,0,1:T(8,128)(2,1)S(1)}, u32[]{:S(2)}, u32[]{:S(2)}) collective-permute-start(bf16[1,4,1,32,1280]{4,3,2,0,1:T(8,128)(2,1)S(1)} %get-tuple-element.16), channel_id=1, source_target_pairs={{1,0},{3,2},{5,4},{7,6},{9,8},{11,10},{13,12},{15,14},{17,16},{19,... | collective-permute-start | bytes 983048 | tf_op jit(solution)/shard_map/ppermute | solution.py:85
  91.9 4.8 %copy-start.1 = (bf16[1,9,1280,80]{2,3,1,0:T(8,128)(2,1)S(1)}, bf16[1,9,1280,80]{2,3,1,0:T(8,128)(2,1)}, u32[]{:S(2)}) copy-start(bf16[1,9,1280,80]{2,3,1,0:T(8,128)(2,1)} %copy-done) | copy-start | bytes 5529604
  108.2 3.8 copy-start.7
  129.9 3.6 collective-permute-start.7
  130.2 3.6 collective-permute-start.6
  135.2 5.5 %copy-start.2 = (bf16[3,1280,80]{1,2,0:T(8,128)(2,1)S(1)}, bf16[3,1280,80]{1,2,0:T(8,128)(2,1)}, u32[]{:S(2)}) copy-start(bf16[3,1280,80]{1,2,0:T(8,128)(2,1)} %param.21) | copy-start | bytes 1843204
  140.7 13.0 %copy-start.6 = (s32[1280]{0:T(1024)S(1)}, s32[1280]{0:T(1024)}, u32[]{:S(2)}) copy-start(s32[1280]{0:T(1024)} %constant.82) | copy-start | bytes 15364
  140.7 12.6 %collective-permute-start.8 = (bf16[1,3,1280,80]{2,3,0,1:T(8,128)(2,1)S(1)}, bf16[1,3,1280,80]{2,3,0,1:T(8,128)(2,1)S(1)}, u32[]{:S(2)}, u32[]{:S(2)}) collective-permute-start(bf16[1,3,1280,80]{2,3,0,1:T(8,128)(2,1)S(1)} %bitcast.71), channel_id=1, source_target_pairs={{0,16},{8,24},{16,0},{24,8},{1,17},{9,25},{17,1},{25,9},{2,18},{10... | collective-permute-start | bytes 1843208 | tf_op jit(solution)/shard_map/ppermute | solution.py:31
  153.6 3.0 collective-permute-start.9
  369.9 2.3 copy-start.5
Sparse Core Ops, SparseCore 0:
  8.9 57.4 all-gather.2
  140.8 183.4 all-gather.4

commit v2 on v1

v2 whole, which is shorter than its diff:
```python
import numpy as np

import jax
import jax.numpy as jnp
from jax import lax
from jax.sharding import PartitionSpec as P

GROUPS = 32


EPS = 1e-05


def pair_sum(value, axis):
    if lax.axis_size(axis) == 2:
        return jax.tree.map(
            lambda v: v + lax.ppermute(v, axis, [(0, 1), (1, 0)]), value
        )
    return lax.psum(value, axis)


def gather_rep(w):
    size = lax.axis_size("rep")
    if size != 4:
        return lax.all_gather(w, "rep", axis=w.ndim - 1, tiled=True)
    index = lax.axis_index("rep")
    across = lax.ppermute(w, "rep", [(k, k ^ 2) for k in range(size)])
    partner = lax.ppermute(w, "rep", [(k, k ^ 1) for k in range(size)])
    diagonal = lax.ppermute(across, "rep", [(k, k ^ 1) for k in range(size)])
    held = [w, partner, across, diagonal]
    blocks = []
    for position in range(size):
        offset = index ^ position
        block = held[3]
        for d in (2, 1, 0):
            block = jnp.where(offset == d, held[d], block)
        blocks.append(block)
    return jnp.concatenate(blocks, axis=-1)


def local_vector(vec, frame_index, rep_size, frame_size):
    width = vec.shape[0] // (rep_size * frame_size)
    table = vec.reshape(rep_size, frame_size, width)
    return lax.dynamic_index_in_dim(table, frame_index, axis=1, keepdims=False).reshape(-1)


def silu_bf16(normed):
    return jax.nn.silu(normed).astype(jnp.bfloat16)


def temporal_wide(activations, second, temporal_w, temporal_bias):
    rep_size = lax.axis_size("rep")
    frame_size = lax.axis_size("frame")
    channels = activations.shape[-1]
    _, frames, rows, cols, local = second.shape
    shard_width = local // rep_size
    second_all = lax.all_gather(second, "frame", axis=4, tiled=True)
    rows_order = np.arange(channels).reshape(rep_size, frame_size, shard_width)
    rows_order = rows_order.transpose(1, 0, 2).reshape(-1)
    temporal_w = temporal_w[:, rows_order, :]
    lhs_t = second_all.reshape(frames, rows * cols, channels)[None]
    kernel_t = temporal_w.reshape(3, 1, channels, local)
    temporal = lax.conv_general_dilated(
        lhs_t,
        kernel_t,
        window_strides=(1, 1),
        padding=((1, 1), (0, 0)),
        dimension_numbers=("NHWC", "HWIO", "NHWC"),
        preferred_element_type=jnp.float32,
    )
    temporal = temporal.reshape(1, frames, rows, cols, local).astype(jnp.bfloat16)
    back = lax.all_to_all(temporal, "frame", split_axis=1, concat_axis=4, tiled=True)
    per_frame = frames // frame_size
    back = back.reshape(1, per_frame, rows, cols, frame_size, rep_size, shard_width)
    back = jnp.swapaxes(back, 4, 5).reshape(1, per_frame, rows, cols, channels)
    return activations.astype(jnp.float32) + back.astype(jnp.float32) + temporal_bias


def shards(
    activations,
    spatial_weight,
    temporal_weight,
    first_gain,
    first_shift,
    spatial_bias,
    second_gain,
    second_shift,
    temporal_bias,
):
    rep_size = lax.axis_size("rep")
    frame_size = lax.axis_size("frame")
    row_size = lax.axis_size("row")
    frame_index = lax.axis_index("frame")
    row_index = lax.axis_index("row")
    channels = activations.shape[-1]
    rows = activations.shape[2]
    cols = activations.shape[3]
    width = channels // GROUPS
    shard_width = spatial_weight.shape[-1]

    spatial_w = gather_rep(spatial_weight)
    temporal_w = gather_rep(temporal_weight)
    local = spatial_w.shape[-1]

    raw = lax.all_gather(activations, "frame", axis=1, tiled=True)
    frames = raw.shape[1]

    if row_size > 1:
        down = [(i, i + 1) for i in range(row_size - 1)]
        up = [(i + 1, i) for i in range(row_size - 1)]
        above = lax.ppermute(raw[:, :, rows - 1 :], "row", down)
        below = lax.ppermute(raw[:, :, :1], "row", up)
    else:
        above = jnp.zeros_like(raw[:, :, :1])
        below = jnp.zeros_like(raw[:, :, :1])

    inputs = raw.astype(jnp.float32)
    grouped = inputs.reshape(1, -1, GROUPS, width)
    sums = jnp.sum(grouped, axis=(1, 3))
    squares = jnp.sum(grouped * grouped, axis=(1, 3))
    sums, squares = pair_sum((sums, squares), "row")
    count = grouped.shape[1] * width * row_size
    mean = sums / count
    variance = squares / count - mean * mean
    inverse = lax.rsqrt(variance + EPS)
    mean_full = jnp.repeat(mean, width, axis=1)[:, None, None, None, :]
    inverse_full = jnp.repeat(inverse, width, axis=1)[:, None, None, None, :]

    def first_norm(x):
        normed = (x.astype(jnp.float32) - mean_full) * inverse_full * first_gain + first_shift
        return silu_bf16(normed)

    first_mid = first_norm(raw)
    first_above = jnp.where(row_index > 0, first_norm(above), jnp.zeros((), jnp.bfloat16))
    first_below = jnp.where(
        row_index < row_size - 1, first_norm(below), jnp.zeros((), jnp.bfloat16)
    )
    padded = jnp.concatenate([first_above, first_mid, first_below], axis=2)

    field = lax.optimization_barrier(padded[0])
    spatial = None
    for col_tap in range(3):
        product = None
        for row_tap in range(3):
            term = jnp.einsum(
                "frxc,cn->frxn",
                field[:, row_tap : row_tap + rows],
                spatial_w[3 * row_tap + col_tap],
                preferred_element_type=jnp.float32,
            )
            product = term if product is None else product + term
        if col_tap == 0:
            product = jnp.pad(product[:, :, :-1], ((0, 0), (0, 0), (1, 0), (0, 0)))
        elif col_tap == 2:
            product = jnp.pad(product[:, :, 1:], ((0, 0), (0, 0), (0, 1), (0, 0)))
        spatial = product if spatial is None else spatial + product
    spatial = spatial[None]
    spatial = spatial + local_vector(spatial_bias, frame_index, rep_size, frame_size)

    g2 = local_vector(second_gain, frame_index, rep_size, frame_size)
    s2 = local_vector(second_shift, frame_index, rep_size, frame_size)
    if shard_width % width == 0:
        grouped2 = spatial.reshape(-1, local // width, width)
        sums2 = jnp.sum(grouped2, axis=(0, 2))
        squares2 = jnp.sum(grouped2 * grouped2, axis=(0, 2))
        sums2, squares2 = pair_sum((sums2, squares2), "row")
        count2 = grouped2.shape[0] * width * row_size
        mean2 = sums2 / count2
        variance2 = squares2 / count2 - mean2 * mean2
        inverse2 = lax.rsqrt(variance2 + EPS)
        mean2_full = jnp.repeat(mean2, width)
        inverse2_full = jnp.repeat(inverse2, width)
    else:
        flat = spatial.reshape(-1, local)
        csum = jnp.sum(flat, axis=0)
        csq = jnp.sum(flat * flat, axis=0)
        csum, csq = pair_sum((csum, csq), "row")
        both = lax.all_gather(jnp.stack([csum, csq]), "frame", axis=0)
        both = both.reshape(frame_size, 2, rep_size, shard_width)
        both = jnp.transpose(both, (1, 2, 0, 3)).reshape(2, GROUPS, -1)
        gsum = jnp.sum(both, axis=2)
        count2 = flat.shape[0] * row_size * width
        gmean = gsum[0] / count2
        gvar = gsum[1] / count2 - gmean * gmean
        ginv = lax.rsqrt(gvar + EPS)
        mean2_full = local_vector(jnp.repeat(gmean, width), frame_index, rep_size, frame_size)
        inverse2_full = local_vector(jnp.repeat(ginv, width), frame_index, rep_size, frame_size)
    second = silu_bf16((spatial - mean2_full) * inverse2_full * g2 + s2)

    if frame_size > 8:
        return temporal_wide(activations, second, temporal_w, temporal_bias)
    second_all = lax.all_gather(second[0], "frame", axis=0, tiled=False)
    taps = temporal_w.reshape(3, rep_size, frame_size, shard_width, local)
    temporal = None
    for group in range(frame_size):
        block = second_all[group]
        weights = taps[:, :, group].reshape(3, rep_size * shard_width, local)
        for tap in range(3):
            if tap == 1:
                source = block
            elif tap == 0:
                source = block[:-1]
            else:
                source = block[1:]
            if source.shape[0] == 0:
                continue
            term = jnp.einsum(
                "frxc,cn->frxn", source, weights[tap], preferred_element_type=jnp.float32
            )
            if tap == 0:
                term = jnp.pad(term, ((1, 0), (0, 0), (0, 0), (0, 0)))
            elif tap == 2:
                term = jnp.pad(term, ((0, 1), (0, 0), (0, 0), (0, 0)))
            temporal = term if temporal is None else temporal + term
    temporal = temporal.astype(jnp.bfloat16)

    per_frame = frames // frame_size
    result = jnp.zeros((per_frame, rows, cols, rep_size, frame_size, shard_width), jnp.float32)
    for shift in range(frame_size):
        target = (frame_index + shift) % frame_size
        piece = lax.dynamic_slice_in_dim(temporal, target * per_frame, per_frame, axis=0)
        if shift:
            piece = lax.ppermute(
                piece, "frame", [(k, (k + shift) % frame_size) for k in range(frame_size)]
            )
        source = (frame_index - shift) % frame_size
        piece = piece.reshape(per_frame, rows, cols, rep_size, 1, shard_width)
        result = lax.dynamic_update_slice_in_dim(
            result, piece.astype(jnp.float32), source, axis=4
        )
    result = result.reshape(1, per_frame, rows, cols, channels)
    return activations.astype(jnp.float32) + result + temporal_bias


def solution(mesh):
    placed = (
        P("rep", "frame", "row", None, None),
        P(None, None, ("rep", "frame")),
        P(None, None, ("rep", "frame")),
        P(),
        P(),
        P(),
        P(),
        P(),
        P(),
    )
    return jax.shard_map(
        shards,
        mesh=mesh,
        in_specs=placed,
        out_specs=P("rep", "frame", "row", None, None),
        check_vma=False,
    )
```

time: 382 us -> 288 us (0.75)
  waiting for transfers between devices: 217 us -> 143 us
  blocking collectives: 23 us -> 0 us
  other arithmetic: 32.9 us -> 27 us
  starting transfers between devices: 13.6 us -> 18.4 us
    all_gather x1, waiting for transfers between devices: 149 us -> 39.5 us  [shards(): second_all = lax.all_gather(second[0], 'frame', axis=0, tiled=False)]
    dynamic_update_slice x0 -> x4, local copies, waits for them, and re-layouts: none -> 45.8 us  [shards(): lax.dynamic_update_slice_in_dim(result, piece.astype(jnp.float32), source...]
    all_gather x1, waiting for transfers between devices: 10.8 us -> 42.8 us  [shards(): raw = lax.all_gather(activations, 'frame', axis=1, tiled=True)]
    conv_general_dilated x2 -> x0, matrix products: 24 us -> none  [the longest x1 17.7 us: shards(): lax.conv_general_dilated(lhs, kernel, window_strides=(1, 1), padding=((0,...]
    all_to_all x1 -> x0, blocking collectives: 23 us -> none  [shards(): lax.all_to_all(temporal, 'frame', split_axis=1, concat_axis=4, tiled=True)]
    dot_general x0 -> x17, matrix products: none -> 21.8 us  [the longest x9 15.8 us: shards(): jnp.einsum('frxc,cn->frxn', field[:, row_tap:row_tap + rows], spatial_w[3...]
    gather x5 -> x0, local copies, waits for them, and re-layouts: 14.5 us -> none  [the longest x1 12 us: shards(): temporal_w = temporal_w[:, rows_order, :]]
    all_gather x1 -> x0, local copies, waits for them, and re-layouts: 12.8 us -> none  [shards(): second_all = lax.all_gather(second, 'frame', axis=3, tiled=True)]
  transfers between devices with their start and end apart: 12 -> 17, of which waited for: 9 -> 9; matrix products, arithmetic and copies ran while one was open for 12% -> 21% of each run, Pallas kernels for 0% -> 0%
where the time goes in v2:
time: 288 us
  waiting for transfers between devices  143 us (50%)
  local copies, waits for them, and re-layouts  59.6 us (21%)
  other arithmetic  27 us (9%)
  matrix products  25.5 us (9%)
  starting transfers between devices  18.4 us (6%)
  between operations  14 us (5%)
    ppermute x2, waiting for transfers between devices, gather_rep(): across = lax.ppermute(w, 'rep', [(k, k ^ 2) for k in range(size)])  51.6 us
    dynamic_update_slice x4, local copies, waits for them, and re-layouts, shards(): lax.dynamic_update_slice_in_dim(result, piece.astype(jnp.float32), source...  45.8 us
    all_gather x1, waiting for transfers between devices, shards(): raw = lax.all_gather(activations, 'frame', axis=1, tiled=True)  42.8 us
    all_gather x1, waiting for transfers between devices, shards(): second_all = lax.all_gather(second[0], 'frame', axis=0, tiled=False)  39.5 us
    dot_general x9, matrix products, shards(): jnp.einsum('frxc,cn->frxn', field[:, row_tap:row_tap + rows], spatial_w[3...  15.8 us
    concatenate x2, other arithmetic, gather_rep(): return jnp.concatenate(blocks, axis=-1)  9.57 us
    dot_general x8, matrix products, shards(): jnp.einsum('frxc,cn->frxn', source, weights[tap], preferred_element_type=...  6.05 us
  transfers between devices with their start and end apart: 17, of which 9 were waited for; matrix products, arithmetic and copies ran while one was open for 21% of the time, Pallas kernels for 0%

profile of v2, /device:TPU:0, one launch (start us, length us, event | category | flops | bytes accessed | tf_op | source)
XLA Modules:
  0.0 287.9 jit_solution(6336116725697258098)
XLA Ops:
  6.5 3.0 %collective-permute-start.5 = (bf16[9,1280,80]{1,2,0:T(8,128)(2,1)}, bf16[9,1280,80]{1,2,0:T(8,128)(2,1)S(1)}, u32[]{:S(2)}, u32[]{:S(2)}) collective-permute-start(bf16[9,1280,80]{1,2,0:T(8,128)(2,1)} %param.10), channel_id=1, source_target_pairs={{0,16},{8,24},{16,0},{24,8},{1,17},{9,25},{17,1},{25,9},{2,18},{10... | collective-permute-start | bytes 5529608 | tf_op jit(solution)/shard_map/ppermute | solution.py:27
  9.5 40.4 %collective-permute-done.5 = bf16[9,1280,80]{1,2,0:T(8,128)(2,1)S(1)} collective-permute-done((bf16[9,1280,80]{1,2,0:T(8,128)(2,1)}, bf16[9,1280,80]{1,2,0:T(8,128)(2,1)S(1)}, u32[]{:S(2)}, u32[]{:S(2)}) %collective-permute-start.5) | collective-permute-done | bytes 1843232 | tf_op jit(solution)/shard_map/ppermute | solution.py:27
  53.8 3.0 %select_select_fusion.3 = (bf16[9,1280,80]{1,2,0:T(8,128)(2,1)S(1)}, bf16[9,1280,80]{1,2,0:T(8,128)(2,1)S(1)}, bf16[9,1280,80]{1,2,0:T(8,128)(2,1)S(1)}, bf16[9,1280,80]{1,2,0:T(8,128)(2,1)S(1)}) fusion(bf16[9,1280,80]{1,2,0:T(8,128)(2,1)} %param.10, bf16[9,1280,80]{1,2,0:T(8,128)(2,1)} %collective-permute-done.4, ...), kind=kLoop, calls=%fused_computation.19 | loop fusion | flops 11059200 | bytes 14745612 | tf_op jit(solution)/shard_map/jit(_where)/select_n | solution.py:36
  56.9 6.8 %pad_maximum_fusion = bf16[9,1280,320]{1,2,0:T(8,128)(2,1)} fusion(bf16[9,1280,80]{1,2,0:T(8,128)(2,1)S(1)} %get-tuple-element.13, bf16[9,1280,80]{1,2,0:T(8,128)(2,1)S(1)} %get-tuple-element.14, bf16[9,1280,80]{1,2,0:T(8,128)(2,1)S(1)} %get-tuple-element.12, bf16[9,1280,80]{1,2,0:T(8,128)(2,1)S(1)} %get-tuple-element.11), kind=kLoop, calls=%fused_computation.3 | loop fusion | flops 29491200 | bytes 14745600 | tf_op jit(solution)/shard_map/concatenate | solution.py:38
  63.7 42.8 %all-gather.4.cloned.1.call-done = bf16[1,4,8,32,1280]{4,3,2,0,1:T(8,128)(2,1)} async-done(((bf16[1,1,8,32,1280]{4,3,2,0,1:T(8,128)(2,1)}), bf16[1,4,8,32,1280]{4,3,2,0,1:T(8,128)(2,1)}) %all-gather.4.cloned.1.call-update) | async-done | bytes 2621456 | tf_op jit(solution)/shard_map/all_gather | solution.py:105
  106.5 2.6 convert_reduce_fusion
  109.3 1.5 collective-permute-start.1
  111.7 4.1 %collective-permute-start = (bf16[1,4,1,32,1280]{4,3,2,1,0:T(8,128)(2,1)S(1)}, bf16[1,4,1,32,1280]{4,3,2,1,0:T(8,128)(2,1)}, u32[]{:S(2)}, u32[]{:S(2)}) collective-permute-start(bf16[1,4,1,32,1280]{4,3,2,1,0:T(8,128)(2,1)S(1)} %get-tuple-element.31), channel_id=1, source_target_pairs={{0,1},{2,3},{4,5},{6,7},{8,9},{10,11},{12,13},{14,15},{16,17},{18,... | collective-permute-start | bytes 983048 | tf_op jit(solution)/shard_map/ppermute | solution.py:111
  117.7 1.8 fusion.9
  119.5 1.9 collective-permute-done
  121.3 4.9 %collective-permute-done.3 = bf16[1,4,1,32,1280]{4,3,2,1,0:T(8,128)(2,1)} collective-permute-done((bf16[1,4,1,32,1280]{4,3,2,1,0:T(8,128)(2,1)S(1)}, bf16[1,4,1,32,1280]{4,3,2,1,0:T(8,128)(2,1)}, u32[]{:S(2)}, u32[]{:S(2)}) %collective-permute-start.3) | collective-permute-done | bytes 327712 | tf_op jit(solution)/shard_map/ppermute | solution.py:112
  126.3 1.7 fusion.26
  128.4 2.9 fusion.13
  143.1 2.2 multiply_reduce_fusion
  145.8 2.1 collective-permute-start.8
  151.2 1.5 collective-permute-start.10
  152.7 11.2 %collective-permute-done.10 = bf16[3,1280,80]{1,2,0:T(8,128)(2,1)} collective-permute-done((bf16[3,1280,80]{1,2,0:T(8,128)(2,1)S(1)}, bf16[3,1280,80]{1,2,0:T(8,128)(2,1)}, u32[]{:S(2)}, u32[]{:S(2)}) %collective-permute-start.10) | collective-permute-done | bytes 614432 | tf_op jit(solution)/shard_map/ppermute | solution.py:27
  164.6 1.5 copy.64
  166.2 1.5 copy.66
  167.8 2.2 copy.65
  169.9 1.7 select_select_fusion.7
  171.6 2.8 pad_maximum_fusion.1
  174.8 39.5 %all-gather.6.cloned.1.call-done = bf16[16,8,32,320]{3,2,1,0:T(8,128)(2,1)} async-done(((bf16[4,8,32,320]{3,2,1,0:T(8,128)(2,1)}), bf16[16,8,32,320]{3,2,1,0:T(8,128)(2,1)}) %all-gather.6.cloned.1.call-update) | async-done | bytes 2621456 | tf_op jit(solution)/shard_map/all_gather | solution.py:192
  214.3 1.8 fusion.25
  216.1 1.6 fusion.24
  226.3 2.7 collective-permute-start.14
  229.7 11.4 %dynamic_update_slice.12 = f32[1,8,32,4,4,80]{5,4,3,2,1,0:T(4,128)S(1)} dynamic-update-slice(f32[1,8,32,4,4,80]{5,4,3,2,1,0:T(4,128)S(1)} %broadcast_in_dim.32, f32[1,8,32,4,1,80]{5,4,3,2,1,0:T(1,128)S(1)} %bitcast.222, s32[]{:T(128)} %constant.81.clone.1, s32[]{:T(128)} %constant.81.clone.1, s32[]{:T(128)} %constant.81.clone.1, s32[]{:T(128)} %constant.81.clone.1, s32[]{:T(128)S(6)} %select_n.277, ...) | dynamic-update-slice | bytes 655364 | tf_op jit(solution)/shard_map/dynamic_update_slice | solution.py:228
  241.5 11.4 %dynamic_update_slice.13 = f32[1,8,32,4,4,80]{5,4,3,2,1,0:T(4,128)S(1)} dynamic-update-slice(f32[1,8,32,4,4,80]{5,4,3,2,1,0:T(4,128)S(1)} %dynamic_update_slice.12, f32[1,8,32,4,1,80]{5,4,3,2,1,0:T(1,128)S(1)} %bitcast.224, s32[]{:T(128)} %constant.81.clone.1, s32[]{:T(128)} %constant.81.clone.1, s32[]{:T(128)} %constant.81.clone.1, s32[]{:T(128)} %constant.81.clone.1, s32[]{:T(128)S(6)} %select_n.281, ...) | dynamic-update-slice | bytes 655364 | tf_op jit(solution)/shard_map/dynamic_update_slice | solution.py:228
  253.3 11.4 %dynamic_update_slice.14 = f32[1,8,32,4,4,80]{5,4,3,2,1,0:T(4,128)S(1)} dynamic-update-slice(f32[1,8,32,4,4,80]{5,4,3,2,1,0:T(4,128)S(1)} %dynamic_update_slice.13, f32[1,8,32,4,1,80]{5,4,3,2,1,0:T(1,128)S(1)} %bitcast.225, s32[]{:T(128)} %constant.81.clone.1, s32[]{:T(128)} %constant.81.clone.1, s32[]{:T(128)} %constant.81.clone.1, s32[]{:T(128)} %constant.81.clone.1, s32[]{:T(128)S(6)} %select_n.285, ...) | dynamic-update-slice | bytes 655364 | tf_op jit(solution)/shard_map/dynamic_update_slice | solution.py:228
  265.1 11.4 %dynamic_update_slice.15 = f32[1,8,32,4,4,80]{5,4,3,2,1,0:T(4,128)S(1)} dynamic-update-slice(f32[1,8,32,4,4,80]{5,4,3,2,1,0:T(4,128)S(1)} %dynamic_update_slice.14, f32[1,8,32,4,1,80]{5,4,3,2,1,0:T(1,128)S(1)} %bitcast.223, s32[]{:T(128)} %constant.81.clone.1, s32[]{:T(128)} %constant.81.clone.1, s32[]{:T(128)} %constant.81.clone.1, s32[]{:T(128)} %constant.81.clone.1, s32[]{:T(128)S(6)} %select_n.289, ...) | dynamic-update-slice | bytes 655364 | tf_op jit(solution)/shard_map/dynamic_update_slice | solution.py:228
  276.5 2.2 reshape.184
  278.8 2.3 add_add_fusion.1
  (96 shorter events, 33.9 us)
Async XLA Ops:
  6.5 99.9 %all-gather.4.cloned.1.call-start = ((), (), s32[]{:S(2)}) async-start(), calls=%async_computation | async-start | bytes 3276800 | tf_op jit(solution)/shard_map/all_gather | solution.py:105
  6.5 43.4 %collective-permute-start.5 = (bf16[9,1280,80]{1,2,0:T(8,128)(2,1)}, bf16[9,1280,80]{1,2,0:T(8,128)(2,1)S(1)}, u32[]{:S(2)}, u32[]{:S(2)}) collective-permute-start(bf16[9,1280,80]{1,2,0:T(8,128)(2,1)} %param.10), channel_id=1, source_target_pairs={{0,16},{8,24},{16,0},{24,8},{1,17},{9,25},{17,1},{25,9},{2,18},{10... | collective-permute-start | bytes 5529608 | tf_op jit(solution)/shard_map/ppermute | solution.py:27
  9.5 43.2 %collective-permute-start.4 = (bf16[9,1280,80]{1,2,0:T(8,128)(2,1)}, bf16[9,1280,80]{1,2,0:T(8,128)(2,1)}, u32[]{:S(2)}, u32[]{:S(2)}) collective-permute-start(bf16[9,1280,80]{1,2,0:T(8,128)(2,1)} %param.10), channel_id=1, source_target_pairs={{0,8},{8,0},{16,24},{24,16},{1,9},{9,1},{17,25},{25,17},{2,10},{10... | collective-permute-start | bytes 5529608 | tf_op jit(solution)/shard_map/ppermute | solution.py:28
  49.9 3.9 %collective-permute-start.6 = (bf16[9,1280,80]{1,2,0:T(8,128)(2,1)S(1)}, bf16[9,1280,80]{1,2,0:T(8,128)(2,1)}, u32[]{:S(2)}, u32[]{:S(2)}) collective-permute-start(bf16[9,1280,80]{1,2,0:T(8,128)(2,1)S(1)} %collective-permute-done.5), channel_id=1, source_target_pairs={{0,8},{8,0},{16,24},{24,16},{1,9},{9,1},{17,25},{25,17},{2,10},{10... | collective-permute-start | bytes 5529608 | tf_op jit(solution)/shard_map/ppermute | solution.py:29
  49.9 164.4 %all-gather.6.cloned.1.call-start = ((), (), s32[]{:S(2)}) async-start(), calls=%async_computation.1 | async-start | bytes 3932160 | tf_op jit(solution)/shard_map/all_gather | solution.py:192
  63.6 54.0 %copy-start.3 = (f32[1280]{0:T(1024)S(1)}, f32[1280]{0:T(1024)}, u32[]{:S(2)}) copy-start(f32[1280]{0:T(1024)} %param.13) | copy-start | bytes 15364
  63.6 54.0 %copy-start.4 = (f32[1280]{0:T(1024)S(1)}, f32[1280]{0:T(1024)}, u32[]{:S(2)}) copy-start(f32[1280]{0:T(1024)} %param.12) | copy-start | bytes 15364
  106.5 5.2 %copy-start.1 = (bf16[1,4,8,32,1280]{4,3,2,0,1:T(8,128)(2,1)S(1)}, bf16[1,4,8,32,1280]{4,3,2,0,1:T(8,128)(2,1)}, u32[]{:S(2)}) copy-start(bf16[1,4,8,32,1280]{4,3,2,0,1:T(8,128)(2,1)} %all-gather.4.cloned.1.call-done) | copy-start | bytes 7864324
  109.3 8.0 %collective-permute-start.1 = (f32[1,32]{1,0:T(1,128)S(1)}, f32[1,32]{1,0:T(1,128)S(1)}, u32[]{:S(2)}, u32[]{:S(2)}) collective-permute-start(f32[1,32]{1,0:T(1,128)S(1)} %bitcast.238), channel_id=1, source_target_pairs={{0,1},{1,0},{2,3},{3,2},{4,5},{5,4},{6,7},{7,6},{8,9},{9,8},{10,11... | collective-permute-start | bytes 392 | tf_op jit(solution)/shard_map/ppermute | solution.py:17
  111.1 6.2 %collective-permute-start.2 = (f32[1,32]{1,0:T(1,128)S(1)}, f32[1,32]{1,0:T(1,128)S(1)}, u32[]{:S(2)}, u32[]{:S(2)}) collective-permute-start(f32[1,32]{1,0:T(1,128)S(1)} %bitcast.239), channel_id=1, source_target_pairs={{0,1},{1,0},{2,3},{3,2},{4,5},{5,4},{6,7},{7,6},{8,9},{9,8},{10,11... | collective-permute-start | bytes 392 | tf_op jit(solution)/shard_map/ppermute | solution.py:17
  111.7 9.6 %collective-permute-start = (bf16[1,4,1,32,1280]{4,3,2,1,0:T(8,128)(2,1)S(1)}, bf16[1,4,1,32,1280]{4,3,2,1,0:T(8,128)(2,1)}, u32[]{:S(2)}, u32[]{:S(2)}) collective-permute-start(bf16[1,4,1,32,1280]{4,3,2,1,0:T(8,128)(2,1)S(1)} %get-tuple-element.31), channel_id=1, source_target_pairs={{0,1},{2,3},{4,5},{6,7},{8,9},{10,11},{12,13},{14,15},{16,17},{18,... | collective-permute-start | bytes 983048 | tf_op jit(solution)/shard_map/ppermute | solution.py:111
  115.8 10.4 %collective-permute-start.3 = (bf16[1,4,1,32,1280]{4,3,2,1,0:T(8,128)(2,1)S(1)}, bf16[1,4,1,32,1280]{4,3,2,1,0:T(8,128)(2,1)}, u32[]{:S(2)}, u32[]{:S(2)}) collective-permute-start(bf16[1,4,1,32,1280]{4,3,2,1,0:T(8,128)(2,1)S(1)} %get-tuple-element.32), channel_id=1, source_target_pairs={{1,0},{3,2},{5,4},{7,6},{9,8},{11,10},{13,12},{15,14},{17,16},{19,... | collective-permute-start | bytes 983048 | tf_op jit(solution)/shard_map/ppermute | solution.py:112
  126.3 5.0 %slice-start = ((s8[7372800]{0:T(1024)(128)(4,1)}), s8[4194304]{0:T(1024)(128)(4,1)S(1)}, s32[]{:S(2)}) async-start(s8[7372800]{0:T(1024)(128)(4,1)} %bitcast.219), calls=%async_computation.2 | async-start | bytes 8388608
  128.0 3.3 %slice-start.1 = ((s8[7372800]{0:T(1024)(128)(4,1)}), s8[3178496]{0:T(1024)(128)(4,1)S(1)}, s32[]{:S(2)}) async-start(s8[7372800]{0:T(1024)(128)(4,1)} %bitcast.219), calls=%async_computation.3 | async-start | bytes 6356992
  145.3 5.9 %copy-start.2 = (bf16[3,1280,80]{1,2,0:T(8,128)(2,1)S(1)}, bf16[3,1280,80]{1,2,0:T(8,128)(2,1)}, u32[]{:S(2)}) copy-start(bf16[3,1280,80]{1,2,0:T(8,128)(2,1)} %param.11) | copy-start | bytes 1843204
  145.5 3.6 %collective-permute-start.7 = (f32[8]{0:T(128)S(1)}, f32[8]{0:T(128)S(1)}, u32[]{:S(2)}, u32[]{:S(2)}) collective-permute-start(f32[8]{0:T(128)S(1)} %reduce_sum.78), channel_id=1, source_target_pairs={{0,1},{1,0},{2,3},{3,2},{4,5},{5,4},{6,7},{7,6},{8,9},{9,8},{10,11... | collective-permute-start | bytes 104 | tf_op jit(solution)/shard_map/ppermute | solution.py:17
  145.8 3.6 %collective-permute-start.8 = (f32[8]{0:T(128)S(1)}, f32[8]{0:T(128)S(1)}, u32[]{:S(2)}, u32[]{:S(2)}) collective-permute-start(f32[8]{0:T(128)S(1)} %reduce_sum.81), channel_id=1, source_target_pairs={{0,1},{1,0},{2,3},{3,2},{4,5},{5,4},{6,7},{7,6},{8,9},{9,8},{10,11... | collective-permute-start | bytes 104 | tf_op jit(solution)/shard_map/ppermute | solution.py:17
  151.2 12.7 %collective-permute-start.10 = (bf16[3,1280,80]{1,2,0:T(8,128)(2,1)S(1)}, bf16[3,1280,80]{1,2,0:T(8,128)(2,1)}, u32[]{:S(2)}, u32[]{:S(2)}) collective-permute-start(bf16[3,1280,80]{1,2,0:T(8,128)(2,1)S(1)} %copy-done.2), channel_id=1, source_target_pairs={{0,16},{8,24},{16,0},{24,8},{1,17},{9,25},{17,1},{25,9},{2,18},{10... | collective-permute-start | bytes 1843208 | tf_op jit(solution)/shard_map/ppermute | solution.py:27
  152.7 13.5 %collective-permute-start.9 = (bf16[3,1280,80]{1,2,0:T(8,128)(2,1)S(1)}, bf16[3,1280,80]{1,2,0:T(8,128)(2,1)}, u32[]{:S(2)}, u32[]{:S(2)}) collective-permute-start(bf16[3,1280,80]{1,2,0:T(8,128)(2,1)S(1)} %copy-done.2), channel_id=1, source_target_pairs={{0,8},{8,0},{16,24},{24,16},{1,9},{9,1},{17,25},{25,17},{2,10},{10... | collective-permute-start | bytes 1843208 | tf_op jit(solution)/shard_map/ppermute | solution.py:28
  163.9 3.8 %collective-permute-start.11 = (bf16[3,1280,80]{1,2,0:T(8,128)(2,1)}, bf16[3,1280,80]{1,2,0:T(8,128)(2,1)}, u32[]{:S(2)}, u32[]{:S(2)}) collective-permute-start(bf16[3,1280,80]{1,2,0:T(8,128)(2,1)} %collective-permute-done.10), channel_id=1, source_target_pairs={{0,8},{8,0},{16,24},{24,16},{1,9},{9,1},{17,25},{25,17},{2,10},{10... | collective-permute-start | bytes 1843208 | tf_op jit(solution)/shard_map/ppermute | solution.py:29
  214.3 3.4 %copy-start = (bf16[16,8,32,320]{3,2,1,0:T(8,128)(2,1)S(1)}, bf16[16,8,32,320]{3,2,1,0:T(8,128)(2,1)}, u32[]{:S(2)}) copy-start(bf16[16,8,32,320]{3,2,1,0:T(8,128)(2,1)} %all-gather.6.cloned.1.call-done) | copy-start | bytes 7864324
  225.0 16.1 %collective-permute-start.12 = (bf16[1,8,32,320]{3,2,1,0:T(8,128)(2,1)}, bf16[1,8,32,320]{3,2,1,0:T(8,128)(2,1)S(1)}, u32[]{:S(2)}, u32[]{:S(2)}) collective-permute-start(bf16[1,8,32,320]{3,2,1,0:T(8,128)(2,1)} %get-tuple-element.35), channel_id=1, source_target_pairs={{0,2},{2,4},{4,6},{6,0},{1,3},{3,5},{5,7},{7,1},{8,10},{10,12},{12... | collective-permute-start | bytes 491528 | tf_op jit(solution)/shard_map/ppermute | solution.py:223
  225.0 27.9 %collective-permute-start.13 = (bf16[1,8,32,320]{3,2,1,0:T(8,128)(2,1)}, bf16[1,8,32,320]{3,2,1,0:T(8,128)(2,1)S(1)}, u32[]{:S(2)}, u32[]{:S(2)}) collective-permute-start(bf16[1,8,32,320]{3,2,1,0:T(8,128)(2,1)} %get-tuple-element.34), channel_id=1, source_target_pairs={{0,4},{2,6},{4,0},{6,2},{1,5},{3,7},{5,1},{7,3},{8,12},{10,14},{12... | collective-permute-start | bytes 491528 | tf_op jit(solution)/shard_map/ppermute | solution.py:223
  226.3 38.4 %collective-permute-start.14 = (bf16[1,8,32,320]{3,2,1,0:T(8,128)(2,1)S(1)}, bf16[1,8,32,320]{3,2,1,0:T(8,128)(2,1)S(1)}, u32[]{:S(2)}, u32[]{:S(2)}) collective-permute-start(bf16[1,8,32,320]{3,2,1,0:T(8,128)(2,1)S(1)} %get-tuple-element.33), channel_id=1, source_target_pairs={{0,6},{2,0},{4,2},{6,4},{1,7},{3,1},{5,3},{7,5},{8,14},{10,8},{12,... | collective-permute-start | bytes 491528 | tf_op jit(solution)/shard_map/ppermute | solution.py:223
  276.5 2.3 copy-start.5
Sparse Core Ops, SparseCore 0:
  50.0 56.3 all-gather.3
  151.3 62.9 all-gather.5

commit v3 on v2

--- a/solution.py
+++ b/solution.py
@@ -4,6 +4,7 @@
 import jax.numpy as jnp
 from jax import lax
 from jax.sharding import PartitionSpec as P
+
 
 GROUPS = 32
 
@@ -215,7 +216,7 @@
     temporal = temporal.astype(jnp.bfloat16)
 
     per_frame = frames // frame_size
-    result = jnp.zeros((per_frame, rows, cols, rep_size, frame_size, shard_width), jnp.float32)
+    pieces = []
     for shift in range(frame_size):
         target = (frame_index + shift) % frame_size
         piece = lax.dynamic_slice_in_dim(temporal, target * per_frame, per_frame, axis=0)
@@ -223,13 +224,16 @@
             piece = lax.ppermute(
                 piece, "frame", [(k, (k + shift) % frame_size) for k in range(frame_size)]
             )
-        source = (frame_index - shift) % frame_size
-        piece = piece.reshape(per_frame, rows, cols, rep_size, 1, shard_width)
-        result = lax.dynamic_update_slice_in_dim(
-            result, piece.astype(jnp.float32), source, axis=4
-        )
-    result = result.reshape(1, per_frame, rows, cols, channels)
-    return activations.astype(jnp.float32) + result + temporal_bias
+        pieces.append(piece.reshape(per_frame, rows, cols, rep_size, shard_width))
+    slots = []
+    for group in range(frame_size):
+        wanted = (frame_index - group) % frame_size
+        slot = pieces[frame_size - 1]
+        for shift in range(frame_size - 2, -1, -1):
+            slot = jnp.where(wanted == shift, pieces[shift], slot)
+        slots.append(slot)
+    result = jnp.stack(slots, axis=4).reshape(1, per_frame, rows, cols, channels)
+    return activations.astype(jnp.float32) + result.astype(jnp.float32) + temporal_bias
 
 
 def solution(mesh):
@@ -244,6 +248,7 @@
         P(),
         P(),
     )
+
     return jax.shard_map(
         shards,
         mesh=mesh,

time: 288 us -> 258 us (0.90)
  local copies, waits for them, and re-layouts: 59.6 us -> 15.7 us
  waiting for transfers between devices: 143 us -> 156 us
    dynamic_update_slice x4 -> x0, local copies, waits for them, and re-layouts: 45.8 us -> none  [shards(): lax.dynamic_update_slice_in_dim(result, piece.astype(jnp.float32), source...]
    ppermute x3, waiting for transfers between devices: 0.01 us -> 12.9 us  [shards(): lax.ppermute(piece, 'frame', [(k, (k + shift) % frame_size) for k in rang...]
  transfers between devices with their start and end apart: 17 -> 17, of which waited for: 9 -> 11; matrix products, arithmetic and copies ran while one was open for 21% -> 11% of each run, Pallas kernels for 0% -> 0%
where the time goes in v3:
time: 258 us; the launch traced here: 256 us
  waiting for transfers between devices  156 us (60%)
  other arithmetic  26.5 us (10%)
  matrix products  25.5 us (10%)
  starting transfers between devices  18.4 us (7%)
  local copies, waits for them, and re-layouts  15.7 us (6%)
  between operations  14 us (5%)
    ppermute x2, waiting for transfers between devices, gather_rep(): across = lax.ppermute(w, 'rep', [(k, k ^ 2) for k in range(size)])  51.6 us
    all_gather x1, waiting for transfers between devices, shards(): raw = lax.all_gather(activations, 'frame', axis=1, tiled=True)  42.8 us
    all_gather x1, waiting for transfers between devices, shards(): second_all = lax.all_gather(second[0], 'frame', axis=0, tiled=False)  39.5 us
    dot_general x9, matrix products, shards(): jnp.einsum('frxc,cn->frxn', field[:, row_tap:row_tap + rows], spatial_w[3...  15.7 us
    ppermute x3, waiting for transfers between devices, shards(): lax.ppermute(piece, 'frame', [(k, (k + shift) % frame_size) for k in rang...  12.9 us
    concatenate x2, other arithmetic, gather_rep(): return jnp.concatenate(blocks, axis=-1)  9.64 us
    ppermute x1, waiting for transfers between devices, shards(): below = lax.ppermute(raw[:, :, :1], 'row', up)  6.69 us
    dot_general x8, matrix products, shards(): jnp.einsum('frxc,cn->frxn', source, weights[tap], preferred_element_type=...  6.2 us
  transfers between devices with their start and end apart: 17, of which 11 were waited for; matrix products, arithmetic and copies ran while one was open for 11% of the time, Pallas kernels for 0%

profile of v3, /device:TPU:0, one launch (start us, length us, event | category | flops | bytes accessed | tf_op | source)
XLA Modules:
  0.0 256.4 jit_solution(18157739977730701644)
XLA Ops:
  6.5 3.0 %collective-permute-start.5 = (bf16[9,1280,80]{1,2,0:T(8,128)(2,1)}, bf16[9,1280,80]{1,2,0:T(8,128)(2,1)S(1)}, u32[]{:S(2)}, u32[]{:S(2)}) collective-permute-start(bf16[9,1280,80]{1,2,0:T(8,128)(2,1)} %param.10), channel_id=1, source_target_pairs={{0,16},{8,24},{16,0},{24,8},{1,17},{9,25},{17,1},{25,9},{2,18},{10... | collective-permute-start | bytes 5529608 | tf_op jit(solution)/shard_map/ppermute | solution.py:28
  9.5 40.4 %collective-permute-done.5 = bf16[9,1280,80]{1,2,0:T(8,128)(2,1)S(1)} collective-permute-done((bf16[9,1280,80]{1,2,0:T(8,128)(2,1)}, bf16[9,1280,80]{1,2,0:T(8,128)(2,1)S(1)}, u32[]{:S(2)}, u32[]{:S(2)}) %collective-permute-start.5) | collective-permute-done | bytes 1843232 | tf_op jit(solution)/shard_map/ppermute | solution.py:28
  53.8 3.0 %select_select_fusion.3 = (bf16[9,1280,80]{1,2,0:T(8,128)(2,1)S(1)}, bf16[9,1280,80]{1,2,0:T(8,128)(2,1)S(1)}, bf16[9,1280,80]{1,2,0:T(8,128)(2,1)S(1)}, bf16[9,1280,80]{1,2,0:T(8,128)(2,1)S(1)}) fusion(bf16[9,1280,80]{1,2,0:T(8,128)(2,1)} %param.10, bf16[9,1280,80]{1,2,0:T(8,128)(2,1)} %collective-permute-done.4, ...), kind=kLoop, calls=%fused_computation.19 | loop fusion | flops 11059200 | bytes 14745612 | tf_op jit(solution)/shard_map/jit(_where)/select_n | solution.py:37
  56.9 6.9 %pad_maximum_fusion = bf16[9,1280,320]{1,2,0:T(8,128)(2,1)} fusion(bf16[9,1280,80]{1,2,0:T(8,128)(2,1)S(1)} %get-tuple-element.13, bf16[9,1280,80]{1,2,0:T(8,128)(2,1)S(1)} %get-tuple-element.14, bf16[9,1280,80]{1,2,0:T(8,128)(2,1)S(1)} %get-tuple-element.12, bf16[9,1280,80]{1,2,0:T(8,128)(2,1)S(1)} %get-tuple-element.11), kind=kLoop, calls=%fused_computation.3 | loop fusion | flops 29491200 | bytes 14745600 | tf_op jit(solution)/shard_map/concatenate | solution.py:39
  63.7 42.8 %all-gather.4.cloned.1.call-done = bf16[1,4,8,32,1280]{4,3,2,0,1:T(8,128)(2,1)} async-done(((bf16[1,1,8,32,1280]{4,3,2,0,1:T(8,128)(2,1)}), bf16[1,4,8,32,1280]{4,3,2,0,1:T(8,128)(2,1)}) %all-gather.4.cloned.1.call-update) | async-done | bytes 2621456 | tf_op jit(solution)/shard_map/all_gather | solution.py:106
  107.8 4.1 %collective-permute-start = (bf16[1,4,1,32,1280]{4,3,2,1,0:T(8,128)(2,1)S(1)}, bf16[1,4,1,32,1280]{4,3,2,1,0:T(8,128)(2,1)}, u32[]{:S(2)}, u32[]{:S(2)}) collective-permute-start(bf16[1,4,1,32,1280]{4,3,2,1,0:T(8,128)(2,1)S(1)} %get-tuple-element.31), channel_id=1, source_target_pairs={{0,1},{2,3},{4,5},{6,7},{8,9},{10,11},{12,13},{14,15},{16,17},{18,... | collective-permute-start | bytes 983048 | tf_op jit(solution)/shard_map/ppermute | solution.py:112
  111.9 2.5 convert_reduce_fusion
  114.8 2.1 collective-permute-start.2
  118.8 1.8 fusion.9
  120.6 6.7 %collective-permute-done.3 = bf16[1,4,1,32,1280]{4,3,2,1,0:T(8,128)(2,1)} collective-permute-done((bf16[1,4,1,32,1280]{4,3,2,1,0:T(8,128)(2,1)S(1)}, bf16[1,4,1,32,1280]{4,3,2,1,0:T(8,128)(2,1)}, u32[]{:S(2)}, u32[]{:S(2)}) %collective-permute-start.3) | collective-permute-done | bytes 327712 | tf_op jit(solution)/shard_map/ppermute | solution.py:113
  127.3 1.7 fusion.26
  129.5 2.9 %fusion.10 = f32[4,8,32,320]{3,2,1,0:T(8,128)S(1)} fusion(bf16[4,10,32,1280]{3,2,1,0:T(8,128)(2,1)S(1)} %maximum_bitcast_fusion, bf16[9,1280,320]{1,2,0:T(8,128)(2,1)} %pad_maximum_fusion), kind=kOutput, calls=%fused_computation.35 | convolution fusion | flops 838860800 | bytes 5406720 | tf_op jit(solution)/shard_map/frxc,cn->frxn/dot_general | solution.py:146
  132.4 1.5 fusion.11
  133.9 1.5 fusion.12
  135.4 1.5 fusion.15
  144.2 2.2 multiply_reduce_fusion
  146.9 2.1 collective-permute-start.7
  152.3 1.5 collective-permute-start.10
  153.8 11.2 %collective-permute-done.10 = bf16[3,1280,80]{1,2,0:T(8,128)(2,1)} collective-permute-done((bf16[3,1280,80]{1,2,0:T(8,128)(2,1)S(1)}, bf16[3,1280,80]{1,2,0:T(8,128)(2,1)}, u32[]{:S(2)}, u32[]{:S(2)}) %collective-permute-start.10) | collective-permute-done | bytes 614432 | tf_op jit(solution)/shard_map/ppermute | solution.py:28
  165.7 1.5 copy.96
  167.3 1.5 copy.98
  168.8 2.2 copy.97
  171.0 1.7 select_select_fusion.7
  172.7 2.8 %pad_maximum_fusion.1 = bf16[3,1280,320]{2,1,0:T(8,128)(2,1)S(1)} fusion(bf16[3,1280,80]{2,1,0:T(8,128)(2,1)S(1)} %get-tuple-element.16, bf16[3,1280,80]{2,1,0:T(8,128)(2,1)S(1)} %get-tuple-element.17, bf16[3,1280,80]{2,1,0:T(8,128)(2,1)S(1)} %get-tuple-element.18, bf16[3,1280,80]{2,1,0:T(8,128)(2,1)S(1)} %get-tuple-element.15), kind=kLoop, calls=%fused_computation.15 | loop fusion | flops 9830400 | bytes 4915200 | tf_op jit(solution)/shard_map/concatenate | solution.py:39
  175.9 39.5 %all-gather.6.cloned.1.call-done = bf16[16,8,32,320]{3,2,1,0:T(8,128)(2,1)} async-done(((bf16[4,8,32,320]{3,2,1,0:T(8,128)(2,1)}), bf16[16,8,32,320]{3,2,1,0:T(8,128)(2,1)}) %all-gather.6.cloned.1.call-update) | async-done | bytes 2621456 | tf_op jit(solution)/shard_map/all_gather | solution.py:193
  215.4 1.7 fusion.18
  217.1 1.7 fusion.19
  226.7 2.7 %collective-permute-start.14 = (bf16[1,8,32,320]{3,2,1,0:T(8,128)(2,1)S(1)}, bf16[1,8,32,320]{3,2,1,0:T(8,128)(2,1)S(1)}, u32[]{:S(2)}, u32[]{:S(2)}) collective-permute-start(bf16[1,8,32,320]{3,2,1,0:T(8,128)(2,1)S(1)} %get-tuple-element.37), channel_id=1, source_target_pairs={{0,6},{2,0},{4,2},{6,4},{1,7},{3,1},{5,3},{7,5},{8,14},{10,8},{12,... | collective-permute-start | bytes 491528 | tf_op jit(solution)/shard_map/ppermute | solution.py:224
  229.4 5.7 %collective-permute-done.12 = bf16[1,8,32,320]{3,2,1,0:T(8,128)(2,1)S(1)} collective-permute-done((bf16[1,8,32,320]{3,2,1,0:T(8,128)(2,1)S(1)}, bf16[1,8,32,320]{3,2,1,0:T(8,128)(2,1)S(1)}, u32[]{:S(2)}, u32[]{:S(2)}) %collective-permute-start.12) | collective-permute-done | bytes 163872 | tf_op jit(solution)/shard_map/ppermute | solution.py:224
  235.0 7.2 %collective-permute-done.13 = bf16[1,8,32,320]{3,2,1,0:T(8,128)(2,1)S(1)} collective-permute-done((bf16[1,8,32,320]{3,2,1,0:T(8,128)(2,1)S(1)}, bf16[1,8,32,320]{3,2,1,0:T(8,128)(2,1)S(1)}, u32[]{:S(2)}, u32[]{:S(2)}) %collective-permute-start.13) | collective-permute-done | bytes 163872 | tf_op jit(solution)/shard_map/ppermute | solution.py:224
  245.0 2.2 reshape.356
  247.2 2.3 add_add_fusion.1
  (98 shorter events, 30.4 us)
Async XLA Ops:
  6.5 99.9 %all-gather.4.cloned.1.call-start = ((), (), s32[]{:S(2)}) async-start(), calls=%async_computation | async-start | bytes 3276800 | tf_op jit(solution)/shard_map/all_gather | solution.py:106
  6.5 43.4 %collective-permute-start.5 = (bf16[9,1280,80]{1,2,0:T(8,128)(2,1)}, bf16[9,1280,80]{1,2,0:T(8,128)(2,1)S(1)}, u32[]{:S(2)}, u32[]{:S(2)}) collective-permute-start(bf16[9,1280,80]{1,2,0:T(8,128)(2,1)} %param.10), channel_id=1, source_target_pairs={{0,16},{8,24},{16,0},{24,8},{1,17},{9,25},{17,1},{25,9},{2,18},{10... | collective-permute-start | bytes 5529608 | tf_op jit(solution)/shard_map/ppermute | solution.py:28
  9.5 43.2 %collective-permute-start.4 = (bf16[9,1280,80]{1,2,0:T(8,128)(2,1)}, bf16[9,1280,80]{1,2,0:T(8,128)(2,1)}, u32[]{:S(2)}, u32[]{:S(2)}) collective-permute-start(bf16[9,1280,80]{1,2,0:T(8,128)(2,1)} %param.10), channel_id=1, source_target_pairs={{0,8},{8,0},{16,24},{24,16},{1,9},{9,1},{17,25},{25,17},{2,10},{10... | collective-permute-start | bytes 5529608 | tf_op jit(solution)/shard_map/ppermute | solution.py:29
  49.9 3.9 %collective-permute-start.6 = (bf16[9,1280,80]{1,2,0:T(8,128)(2,1)S(1)}, bf16[9,1280,80]{1,2,0:T(8,128)(2,1)}, u32[]{:S(2)}, u32[]{:S(2)}) collective-permute-start(bf16[9,1280,80]{1,2,0:T(8,128)(2,1)S(1)} %collective-permute-done.5), channel_id=1, source_target_pairs={{0,8},{8,0},{16,24},{24,16},{1,9},{9,1},{17,25},{25,17},{2,10},{10... | collective-permute-start | bytes 5529608 | tf_op jit(solution)/shard_map/ppermute | solution.py:30
  49.9 165.5 %all-gather.6.cloned.1.call-start = ((), (), s32[]{:S(2)}) async-start(), calls=%async_computation.1 | async-start | bytes 3932160 | tf_op jit(solution)/shard_map/all_gather | solution.py:193
  106.5 12.3 %copy-start.1 = (bf16[1,4,8,32,1280]{4,3,2,0,1:T(8,128)(2,1)S(1)}, bf16[1,4,8,32,1280]{4,3,2,0,1:T(8,128)(2,1)}, u32[]{:S(2)}) copy-start(bf16[1,4,8,32,1280]{4,3,2,0,1:T(8,128)(2,1)} %all-gather.4.cloned.1.call-done) | copy-start | bytes 7864324
  106.5 12.3 %copy-start.3 = (f32[1280]{0:T(1024)S(1)}, f32[1280]{0:T(1024)}, u32[]{:S(2)}) copy-start(f32[1280]{0:T(1024)} %param.13) | copy-start | bytes 15364
  106.5 12.3 %copy-start.4 = (f32[1280]{0:T(1024)S(1)}, f32[1280]{0:T(1024)}, u32[]{:S(2)}) copy-start(f32[1280]{0:T(1024)} %param.12) | copy-start | bytes 15364
  107.8 12.9 %collective-permute-start = (bf16[1,4,1,32,1280]{4,3,2,1,0:T(8,128)(2,1)S(1)}, bf16[1,4,1,32,1280]{4,3,2,1,0:T(8,128)(2,1)}, u32[]{:S(2)}, u32[]{:S(2)}) collective-permute-start(bf16[1,4,1,32,1280]{4,3,2,1,0:T(8,128)(2,1)S(1)} %get-tuple-element.31), channel_id=1, source_target_pairs={{0,1},{2,3},{4,5},{6,7},{8,9},{10,11},{12,13},{14,15},{16,17},{18,... | collective-permute-start | bytes 983048 | tf_op jit(solution)/shard_map/ppermute | solution.py:112
  114.6 3.8 %collective-permute-start.1 = (f32[1,32]{1,0:T(1,128)S(1)}, f32[1,32]{1,0:T(1,128)S(1)}, u32[]{:S(2)}, u32[]{:S(2)}) collective-permute-start(f32[1,32]{1,0:T(1,128)S(1)} %bitcast.230), channel_id=1, source_target_pairs={{0,1},{1,0},{2,3},{3,2},{4,5},{5,4},{6,7},{7,6},{8,9},{9,8},{10,11... | collective-permute-start | bytes 392 | tf_op jit(solution)/shard_map/ppermute | solution.py:18
  114.8 3.6 %collective-permute-start.2 = (f32[1,32]{1,0:T(1,128)S(1)}, f32[1,32]{1,0:T(1,128)S(1)}, u32[]{:S(2)}, u32[]{:S(2)}) collective-permute-start(f32[1,32]{1,0:T(1,128)S(1)} %bitcast.231), channel_id=1, source_target_pairs={{0,1},{1,0},{2,3},{3,2},{4,5},{5,4},{6,7},{7,6},{8,9},{9,8},{10,11... | collective-permute-start | bytes 392 | tf_op jit(solution)/shard_map/ppermute | solution.py:18
  116.9 10.4 %collective-permute-start.3 = (bf16[1,4,1,32,1280]{4,3,2,1,0:T(8,128)(2,1)S(1)}, bf16[1,4,1,32,1280]{4,3,2,1,0:T(8,128)(2,1)}, u32[]{:S(2)}, u32[]{:S(2)}) collective-permute-start(bf16[1,4,1,32,1280]{4,3,2,1,0:T(8,128)(2,1)S(1)} %get-tuple-element.32), channel_id=1, source_target_pairs={{1,0},{3,2},{5,4},{7,6},{9,8},{11,10},{13,12},{15,14},{17,16},{19,... | collective-permute-start | bytes 983048 | tf_op jit(solution)/shard_map/ppermute | solution.py:113
  127.3 5.0 %slice-start = ((s8[7372800]{0:T(1024)(128)(4,1)}), s8[4194304]{0:T(1024)(128)(4,1)S(1)}, s32[]{:S(2)}) async-start(s8[7372800]{0:T(1024)(128)(4,1)} %bitcast.215), calls=%async_computation.2 | async-start | bytes 8388608
  129.1 3.3 %slice-start.1 = ((s8[7372800]{0:T(1024)(128)(4,1)}), s8[3178496]{0:T(1024)(128)(4,1)S(1)}, s32[]{:S(2)}) async-start(s8[7372800]{0:T(1024)(128)(4,1)} %bitcast.215), calls=%async_computation.3 | async-start | bytes 6356992
  146.4 5.9 %copy-start.2 = (bf16[3,1280,80]{1,2,0:T(8,128)(2,1)S(1)}, bf16[3,1280,80]{1,2,0:T(8,128)(2,1)}, u32[]{:S(2)}) copy-start(bf16[3,1280,80]{1,2,0:T(8,128)(2,1)} %param.11) | copy-start | bytes 1843204
  146.6 3.6 %collective-permute-start.8 = (f32[8]{0:T(128)S(1)}, f32[8]{0:T(128)S(1)}, u32[]{:S(2)}, u32[]{:S(2)}) collective-permute-start(f32[8]{0:T(128)S(1)} %reduce_sum.81), channel_id=1, source_target_pairs={{0,1},{1,0},{2,3},{3,2},{4,5},{5,4},{6,7},{7,6},{8,9},{9,8},{10,11... | collective-permute-start | bytes 104 | tf_op jit(solution)/shard_map/ppermute | solution.py:18
  146.9 3.6 %collective-permute-start.7 = (f32[8]{0:T(128)S(1)}, f32[8]{0:T(128)S(1)}, u32[]{:S(2)}, u32[]{:S(2)}) collective-permute-start(f32[8]{0:T(128)S(1)} %reduce_sum.78), channel_id=1, source_target_pairs={{0,1},{1,0},{2,3},{3,2},{4,5},{5,4},{6,7},{7,6},{8,9},{9,8},{10,11... | collective-permute-start | bytes 104 | tf_op jit(solution)/shard_map/ppermute | solution.py:18
  152.3 12.8 %collective-permute-start.10 = (bf16[3,1280,80]{1,2,0:T(8,128)(2,1)S(1)}, bf16[3,1280,80]{1,2,0:T(8,128)(2,1)}, u32[]{:S(2)}, u32[]{:S(2)}) collective-permute-start(bf16[3,1280,80]{1,2,0:T(8,128)(2,1)S(1)} %copy-done.2), channel_id=1, source_target_pairs={{0,16},{8,24},{16,0},{24,8},{1,17},{9,25},{17,1},{25,9},{2,18},{10... | collective-permute-start | bytes 1843208 | tf_op jit(solution)/shard_map/ppermute | solution.py:28
  153.8 13.5 %collective-permute-start.9 = (bf16[3,1280,80]{1,2,0:T(8,128)(2,1)S(1)}, bf16[3,1280,80]{1,2,0:T(8,128)(2,1)}, u32[]{:S(2)}, u32[]{:S(2)}) collective-permute-start(bf16[3,1280,80]{1,2,0:T(8,128)(2,1)S(1)} %copy-done.2), channel_id=1, source_target_pairs={{0,8},{8,0},{16,24},{24,16},{1,9},{9,1},{17,25},{25,17},{2,10},{10... | collective-permute-start | bytes 1843208 | tf_op jit(solution)/shard_map/ppermute | solution.py:29
  165.0 3.8 %collective-permute-start.11 = (bf16[3,1280,80]{1,2,0:T(8,128)(2,1)}, bf16[3,1280,80]{1,2,0:T(8,128)(2,1)}, u32[]{:S(2)}, u32[]{:S(2)}) collective-permute-start(bf16[3,1280,80]{1,2,0:T(8,128)(2,1)} %collective-permute-done.10), channel_id=1, source_target_pairs={{0,8},{8,0},{16,24},{24,16},{1,9},{9,1},{17,25},{25,17},{2,10},{10... | collective-permute-start | bytes 1843208 | tf_op jit(solution)/shard_map/ppermute | solution.py:30
  215.4 3.4 %copy-start = (bf16[16,8,32,320]{3,2,1,0:T(8,128)(2,1)S(1)}, bf16[16,8,32,320]{3,2,1,0:T(8,128)(2,1)}, u32[]{:S(2)}) copy-start(bf16[16,8,32,320]{3,2,1,0:T(8,128)(2,1)} %all-gather.6.cloned.1.call-done) | copy-start | bytes 7864324
  225.3 9.7 %collective-permute-start.12 = (bf16[1,8,32,320]{3,2,1,0:T(8,128)(2,1)S(1)}, bf16[1,8,32,320]{3,2,1,0:T(8,128)(2,1)S(1)}, u32[]{:S(2)}, u32[]{:S(2)}) collective-permute-start(bf16[1,8,32,320]{3,2,1,0:T(8,128)(2,1)S(1)} %get-tuple-element.39), channel_id=1, source_target_pairs={{0,2},{2,4},{4,6},{6,0},{1,3},{3,5},{5,7},{7,1},{8,10},{10,12},{12... | collective-permute-start | bytes 491528 | tf_op jit(solution)/shard_map/ppermute | solution.py:224
  225.4 16.8 %collective-permute-start.13 = (bf16[1,8,32,320]{3,2,1,0:T(8,128)(2,1)S(1)}, bf16[1,8,32,320]{3,2,1,0:T(8,128)(2,1)S(1)}, u32[]{:S(2)}, u32[]{:S(2)}) collective-permute-start(bf16[1,8,32,320]{3,2,1,0:T(8,128)(2,1)S(1)} %get-tuple-element.38), channel_id=1, source_target_pairs={{0,4},{2,6},{4,0},{6,2},{1,5},{3,7},{5,1},{7,3},{8,12},{10,14},{12... | collective-permute-start | bytes 491528 | tf_op jit(solution)/shard_map/ppermute | solution.py:224
  226.7 15.5 %collective-permute-start.14 = (bf16[1,8,32,320]{3,2,1,0:T(8,128)(2,1)S(1)}, bf16[1,8,32,320]{3,2,1,0:T(8,128)(2,1)S(1)}, u32[]{:S(2)}, u32[]{:S(2)}) collective-permute-start(bf16[1,8,32,320]{3,2,1,0:T(8,128)(2,1)S(1)} %get-tuple-element.37), channel_id=1, source_target_pairs={{0,6},{2,0},{4,2},{6,4},{1,7},{3,1},{5,3},{7,5},{8,14},{10,8},{12,... | collective-permute-start | bytes 491528 | tf_op jit(solution)/shard_map/ppermute | solution.py:224
  245.0 2.3 copy-start.5
Sparse Core Ops, SparseCore 0:
  50.0 56.3 all-gather.3
  152.4 62.9 all-gather.5

commit v4 on v3

--- a/solution.py
+++ b/solution.py
@@ -18,6 +18,18 @@
             lambda v: v + lax.ppermute(v, axis, [(0, 1), (1, 0)]), value
         )
     return lax.psum(value, axis)
+
+
+def butterfly_sum(value, axis):
+    size = lax.axis_size(axis)
+    if size & (size - 1) != 0:
+        return lax.psum(value, axis)
+    step = 1
+    while step < size:
+        pairs = [(k, k ^ step) for k in range(size)]
+        value = jax.tree.map(lambda v: v + lax.ppermute(v, axis, pairs), value)
+        step *= 2
+    return value
 
 
 def gather_rep(w):
@@ -115,12 +127,12 @@
         above = jnp.zeros_like(raw[:, :, :1])
         below = jnp.zeros_like(raw[:, :, :1])
 
-    inputs = raw.astype(jnp.float32)
-    grouped = inputs.reshape(1, -1, GROUPS, width)
+    grouped = activations.astype(jnp.float32).reshape(1, -1, GROUPS, width)
     sums = jnp.sum(grouped, axis=(1, 3))
     squares = jnp.sum(grouped * grouped, axis=(1, 3))
-    sums, squares = pair_sum((sums, squares), "row")
-    count = grouped.shape[1] * width * row_size
+    sums, squares = butterfly_sum((sums, squares), "frame")
+    sums, squares = butterfly_sum((sums, squares), "row")
+    count = grouped.shape[1] * width * frame_size * row_size
     mean = sums / count
     variance = squares / count - mean * mean
     inverse = lax.rsqrt(variance + EPS)
@@ -139,23 +151,20 @@
     padded = jnp.concatenate([first_above, first_mid, first_below], axis=2)
 
     field = lax.optimization_barrier(padded[0])
-    spatial = None
-    for col_tap in range(3):
-        product = None
-        for row_tap in range(3):
-            term = jnp.einsum(
-                "frxc,cn->frxn",
-                field[:, row_tap : row_tap + rows],
-                spatial_w[3 * row_tap + col_tap],
-                preferred_element_type=jnp.float32,
-            )
-            product = term if product is None else product + term
-        if col_tap == 0:
-            product = jnp.pad(product[:, :, :-1], ((0, 0), (0, 0), (1, 0), (0, 0)))
-        elif col_tap == 2:
-            product = jnp.pad(product[:, :, 1:], ((0, 0), (0, 0), (0, 1), (0, 0)))
-        spatial = product if spatial is None else spatial + product
-    spatial = spatial[None]
+    wide = spatial_w.reshape(3, 3, channels, local).transpose(0, 2, 1, 3)
+    wide = wide.reshape(3, channels, 3 * local)
+    product = None
+    for row_tap in range(3):
+        term = jnp.einsum(
+            "frxc,cn->frxn",
+            field[:, row_tap : row_tap + rows],
+            wide[row_tap],
+            preferred_element_type=jnp.float32,
+        )
+        product = term if product is None else product + term
+    left = jnp.pad(product[:, :, :-1, :local], ((0, 0), (0, 0), (1, 0), (0, 0)))
+    right = jnp.pad(product[:, :, 1:, 2 * local :], ((0, 0), (0, 0), (0, 1), (0, 0)))
+    spatial = (left + product[..., local : 2 * local] + right)[None]
     spatial = spatial + local_vector(spatial_bias, frame_index, rep_size, frame_size)
 
     g2 = local_vector(second_gain, frame_index, rep_size, frame_size)
@@ -192,27 +201,19 @@
         return temporal_wide(activations, second, temporal_w, temporal_bias)
     second_all = lax.all_gather(second[0], "frame", axis=0, tiled=False)
     taps = temporal_w.reshape(3, rep_size, frame_size, shard_width, local)
-    temporal = None
+    total = None
     for group in range(frame_size):
-        block = second_all[group]
         weights = taps[:, :, group].reshape(3, rep_size * shard_width, local)
-        for tap in range(3):
-            if tap == 1:
-                source = block
-            elif tap == 0:
-                source = block[:-1]
-            else:
-                source = block[1:]
-            if source.shape[0] == 0:
-                continue
-            term = jnp.einsum(
-                "frxc,cn->frxn", source, weights[tap], preferred_element_type=jnp.float32
-            )
-            if tap == 0:
-                term = jnp.pad(term, ((1, 0), (0, 0), (0, 0), (0, 0)))
-            elif tap == 2:
-                term = jnp.pad(term, ((0, 1), (0, 0), (0, 0), (0, 0)))
-            temporal = term if temporal is None else temporal + term
+        weights = weights.transpose(1, 0, 2).reshape(rep_size * shard_width, 3 * local)
+        term = jnp.einsum(
+            "frxc,cn->frxn", second_all[group], weights, preferred_element_type=jnp.float32
+        )
+        total = term if total is None else total + term
+    temporal = total[..., local : 2 * local]
+    if frames > 1:
+        before = jnp.pad(total[:-1, ..., :local], ((1, 0), (0, 0), (0, 0), (0, 0)))
+        after = jnp.pad(total[1:, ..., 2 * local :], ((0, 1), (0, 0), (0, 0), (0, 0)))
+        temporal = before + temporal + after
     temporal = temporal.astype(jnp.bfloat16)
 
     per_frame = frames // frame_size

time: 258 us -> 244 us (0.946)
  waiting for transfers between devices: 156 us -> 140 us
  matrix products: 25.5 us -> 15.2 us
  local copies, waits for them, and re-layouts: 15.7 us -> 24.4 us
  starting transfers between devices: 18.4 us -> 24.4 us
    all_gather x1, waiting for transfers between devices: 42.8 us -> 27.4 us  [shards(): raw = lax.all_gather(activations, 'frame', axis=1, tiled=True)]
    ppermute x0 -> x6, starting transfers between devices: none -> 8.82 us  [butterfly_sum(): value = jax.tree.map(lambda v: v + lax.ppermute(v, axis, pairs), value)]
    dot_general x17 -> x7, matrix products: 21.9 us -> 15.2 us  [the longest x3 8.71 us: shards(): jnp.einsum('frxc,cn->frxn', field[:, row_tap:row_tap + rows], wide[row_ta...]
    ppermute x0 -> x6, waiting for transfers between devices: none -> 4.29 us  [butterfly_sum(): value = jax.tree.map(lambda v: v + lax.ppermute(v, axis, pairs), value)]
    all_gather x1, waiting for transfers between devices: 39.5 us -> 35.9 us  [shards(): second_all = lax.all_gather(second[0], 'frame', axis=0, tiled=False)]
    pad x4 -> x0, matrix products: 3.54 us -> none  [shards(): term = jnp.pad(term, ((1, 0), (0, 0), (0, 0), (0, 0)))]
    slice x1 -> x4, local copies, waits for them, and re-layouts: 0.43 us -> 3.82 us  [the longest x1 2.72 us: shards(): wide[row_tap]]
    another operation x0 -> x4, local copies, waits for them, and re-layouts: none -> 3.07 us  [shards(): weights = taps[:, :, group].reshape(3, rep_size * shard_width, local)]
  transfers between devices with their start and end apart: 17 -> 21, of which waited for: 11 -> 13; matrix products, arithmetic and copies ran while one was open for 11% -> 14% of each run, Pallas kernels for 0% -> 0%
where the time goes in v4:
time: 244 us; the launch traced here: 243 us
  waiting for transfers between devices  140 us (57%)
  other arithmetic  25 us (10%)
  starting transfers between devices  24.4 us (10%)
  local copies, waits for them, and re-layouts  24.4 us (10%)
  matrix products  15.2 us (6%)
  between operations  13.9 us (6%)
    ppermute x2, waiting for transfers between devices, gather_rep(): across = lax.ppermute(w, 'rep', [(k, k ^ 2) for k in range(size)])  52.2 us
    all_gather x1, waiting for transfers between devices, shards(): second_all = lax.all_gather(second[0], 'frame', axis=0, tiled=False)  35.9 us
    all_gather x1, waiting for transfers between devices, shards(): raw = lax.all_gather(activations, 'frame', axis=1, tiled=True)  27.4 us
    ppermute x3, waiting for transfers between devices, shards(): lax.ppermute(piece, 'frame', [(k, (k + shift) % frame_size) for k in rang...  12.9 us
    ppermute x6, starting transfers between devices, butterfly_sum(): value = jax.tree.map(lambda v: v + lax.ppermute(v, axis, pairs), value)  8.82 us
    dot_general x3, matrix products, shards(): jnp.einsum('frxc,cn->frxn', field[:, row_tap:row_tap + rows], wide[row_ta...  8.71 us
    concatenate x2, other arithmetic, gather_rep(): return jnp.concatenate(blocks, axis=-1)  8.28 us
    dot_general x4, matrix products, shards(): jnp.einsum('frxc,cn->frxn', second_all[group], weights, preferred_element...  6.53 us
  transfers between devices with their start and end apart: 21, of which 13 were waited for; matrix products, arithmetic and copies ran while one was open for 14% of the time, Pallas kernels for 0%

profile of v4, /device:TPU:0, one launch (start us, length us, event | category | flops | bytes accessed | tf_op | source)
XLA Modules:
  0.0 242.9 jit_solution(16393990067617087164)
XLA Ops:
  6.5 3.0 %collective-permute-start.9 = (bf16[9,1280,80]{1,2,0:T(8,128)(2,1)}, bf16[9,1280,80]{1,2,0:T(8,128)(2,1)S(1)}, u32[]{:S(2)}, u32[]{:S(2)}) collective-permute-start(bf16[9,1280,80]{1,2,0:T(8,128)(2,1)} %param.10), channel_id=1, source_target_pairs={{0,16},{8,24},{16,0},{24,8},{1,17},{9,25},{17,1},{25,9},{2,18},{10... | collective-permute-start | bytes 5529608 | tf_op jit(solution)/shard_map/ppermute | solution.py:40
  9.5 40.4 %collective-permute-done.9 = bf16[9,1280,80]{1,2,0:T(8,128)(2,1)S(1)} collective-permute-done((bf16[9,1280,80]{1,2,0:T(8,128)(2,1)}, bf16[9,1280,80]{1,2,0:T(8,128)(2,1)S(1)}, u32[]{:S(2)}, u32[]{:S(2)}) %collective-permute-start.9) | collective-permute-done | bytes 1843232 | tf_op jit(solution)/shard_map/ppermute | solution.py:40
  51.5 1.9 collective-permute-start.1
  56.4 2.9 %collective-permute-start.2 = (f32[1,32]{1,0:T(1,128)S(1)}, f32[1,32]{1,0:T(1,128)S(1)}, u32[]{:S(2)}, u32[]{:S(2)}) collective-permute-start(f32[1,32]{1,0:T(1,128)S(1)} %bitcast_add_fusion.1), channel_id=1, source_target_pairs={{0,4},{2,6},{4,0},{6,2},{1,5},{3,7},{5,1},{7,3},{8,12},{10,14},{12... | collective-permute-start | bytes 392 | tf_op jit(solution)/shard_map/ppermute | solution.py:30
  60.9 1.8 collective-permute-start.3
  65.5 2.0 collective-permute-done.6
  67.8 3.1 %select_select_fusion.3 = (bf16[9,1280,80]{1,2,0:T(8,128)(2,1)S(1)}, bf16[9,1280,80]{1,2,0:T(8,128)(2,1)S(1)}, bf16[9,1280,80]{1,2,0:T(8,128)(2,1)S(1)}, bf16[9,1280,80]{1,2,0:T(8,128)(2,1)S(1)}) fusion(bf16[9,1280,80]{1,2,0:T(8,128)(2,1)} %param.10, bf16[9,1280,80]{1,2,0:T(8,128)(2,1)} %collective-permute-done.8, ...), kind=kLoop, calls=%fused_computation.12 | loop fusion | flops 11059200 | bytes 14745612 | tf_op jit(solution)/shard_map/jit(_where)/select_n | solution.py:49
  70.9 5.5 %pad_maximum_fusion = bf16[9,1280,320]{1,2,0:T(8,128)(2,1)S(1)} fusion(bf16[9,1280,80]{1,2,0:T(8,128)(2,1)S(1)} %get-tuple-element.17, bf16[9,1280,80]{1,2,0:T(8,128)(2,1)S(1)} %get-tuple-element.18, bf16[9,1280,80]{1,2,0:T(8,128)(2,1)S(1)} %get-tuple-element.16, bf16[9,1280,80]{1,2,0:T(8,128)(2,1)S(1)} %get-tuple-element.15), kind=kLoop, calls=%fused_computation | loop fusion | flops 29491200 | bytes 14745600 | tf_op jit(solution)/shard_map/concatenate | solution.py:51
  76.4 2.7 %fusion.10 = (bf16[1,1280,3,320]{1,3,2,0:T(8,128)(2,1)S(1)}, bf16[1,1280,3,320]{1,3,2,0:T(8,128)(2,1)}, bf16[1,1280,3,320]{1,3,2,0:T(8,128)(2,1)}) fusion(bf16[3,1280,3,320]{1,3,2,0:T(8,128)(2,1)S(1)} %bitcast.80), kind=kLoop, calls=%fused_computation.49 | loop fusion | bytes 14745600 | tf_op jit(solution)/shard_map/slice | solution.py:161
  79.1 27.4 %all-gather.4.cloned.1.call-done = bf16[1,4,8,32,1280]{4,3,2,0,1:T(8,128)(2,1)} async-done(((bf16[1,1,8,32,1280]{4,3,2,0,1:T(8,128)(2,1)}), bf16[1,4,8,32,1280]{4,3,2,0,1:T(8,128)(2,1)}) %all-gather.4.cloned.1.call-update) | async-done | bytes 2621456 | tf_op jit(solution)/shard_map/all_gather | solution.py:118
  107.6 3.4 %collective-permute-start = (bf16[1,4,1,32,1280]{4,3,2,1,0:T(8,128)(2,1)S(1)}, bf16[1,4,1,32,1280]{4,3,2,1,0:T(8,128)(2,1)S(1)}, u32[]{:S(2)}, u32[]{:S(2)}) collective-permute-start(bf16[1,4,1,32,1280]{4,3,2,1,0:T(8,128)(2,1)S(1)} %get-tuple-element.31), channel_id=1, source_target_pairs={{0,1},{2,3},{4,5},{6,7},{8,9},{10,11},{12,13},{14,15},{16,17},{18,... | collective-permute-start | bytes 983048 | tf_op jit(solution)/shard_map/ppermute | solution.py:124
  112.5 3.5 %multiply_convert_fusion = bf16[1,4,8,32,1280]{4,3,2,1,0:T(8,128)(2,1)S(1)} fusion(f32[1280]{0:T(1024)S(1)} %copy-done.7, f32[1280]{0:T(1024)S(1)} %copy-done.8, f32[1280]{0:T(1024)S(1)} %broadcast_in_dim.32, f32[1280]{0:T(1024)S(1)} %broadcast_in_dim.30, bf16[1,4,8,32,1280]{4,3,2,0,1:T(8,128)(2,1)} %all-gather.4.cloned.1.call-done), kind=kLoop, calls=%fused_computation.1 | loop fusion | flops 13107200 | bytes 5263360 | tf_op jit(solution)/shard_map/convert_element_type | solution.py:61
  116.1 1.7 collective-permute-done
  117.8 4.1 %collective-permute-done.7 = bf16[1,4,1,32,1280]{4,3,2,1,0:T(8,128)(2,1)S(1)} collective-permute-done((bf16[1,4,1,32,1280]{4,3,2,1,0:T(8,128)(2,1)S(1)}, bf16[1,4,1,32,1280]{4,3,2,1,0:T(8,128)(2,1)S(1)}, u32[]{:S(2)}, u32[]{:S(2)}) %collective-permute-start.7) | collective-permute-done | bytes 327712 | tf_op jit(solution)/shard_map/ppermute | solution.py:125
  124.1 2.9 %fusion.16 = f32[4,8,32,960]{3,2,1,0:T(8,128)S(1)} fusion(bf16[4,10,32,1280]{3,2,1,0:T(8,128)(2,1)S(1)} %maximum_bitcast_fusion, bf16[1280,960,1,1]{0,1,3,2:T(8,128)(2,1)S(1)} %bitcast.94), kind=kOutput, calls=%fused_computation.55 | convolution fusion | flops 2516582400 | bytes 9666560 | tf_op jit(solution)/shard_map/frxc,cn->frxn/dot_general | solution.py:158
  127.0 2.9 %fusion.15 = f32[4,8,32,960]{3,2,1,0:T(8,128)S(1)} fusion(bf16[4,10,32,1280]{3,2,1,0:T(8,128)(2,1)S(1)} %maximum_bitcast_fusion, bf16[1280,960,1,1]{0,1,3,2:T(8,128)(2,1)S(1)} %bitcast.93), kind=kOutput, calls=%fused_computation.54 | convolution fusion | flops 2516582400 | bytes 9666560 | tf_op jit(solution)/shard_map/frxc,cn->frxn/dot_general | solution.py:158
  129.9 2.9 %add_add_fusion.1 = f32[4,8,32,960]{3,2,1,0:T(8,128)S(1)} fusion(f32[4,8,32,960]{3,2,1,0:T(8,128)S(1)} %fusion.15, f32[4,8,32,960]{3,2,1,0:T(8,128)S(1)} %fusion.16, bf16[4,10,32,1280]{3,2,1,0:T(8,128)(2,1)S(1)} %maximum_bitcast_fusion, bf16[1280,960,1,1]{0,1,3,2:T(8,128)(2,1)S(1)} %bitcast.92), kind=kOutput, calls=%fused_computation.3 | convolution fusion | flops 2518548480 | bytes 17530880 | tf_op jit(solution)/shard_map/frxc,cn->frxn/dot_general | solution.py:158
  134.5 2.1 collective-permute-start.12
  139.9 1.5 collective-permute-start.14
  141.5 11.8 %collective-permute-done.14 = bf16[3,1280,80]{1,2,0:T(8,128)(2,1)} collective-permute-done((bf16[3,1280,80]{1,2,0:T(8,128)(2,1)S(1)}, bf16[3,1280,80]{1,2,0:T(8,128)(2,1)}, u32[]{:S(2)}, u32[]{:S(2)}) %collective-permute-start.14) | collective-permute-done | bytes 614432 | tf_op jit(solution)/shard_map/ppermute | solution.py:40
  153.9 1.5 copy.120
  155.5 1.5 copy.122
  157.0 2.2 copy.121
  159.2 1.7 select_select_fusion.7
  160.9 2.8 %pad_maximum_fusion.1 = bf16[3,1280,320]{2,1,0:T(8,128)(2,1)S(1)} fusion(bf16[3,1280,80]{2,1,0:T(8,128)(2,1)S(1)} %get-tuple-element.24, bf16[3,1280,80]{2,1,0:T(8,128)(2,1)S(1)} %get-tuple-element.25, bf16[3,1280,80]{2,1,0:T(8,128)(2,1)S(1)} %get-tuple-element.26, bf16[3,1280,80]{2,1,0:T(8,128)(2,1)S(1)} %get-tuple-element.23), kind=kLoop, calls=%fused_computation.5 | loop fusion | flops 9830400 | bytes 4915200 | tf_op jit(solution)/shard_map/concatenate | solution.py:51
  167.2 35.9 %all-gather.6.cloned.1.call-done = bf16[16,8,32,320]{3,2,1,0:T(8,128)(2,1)} async-done(((bf16[4,8,32,320]{3,2,1,0:T(8,128)(2,1)}), bf16[16,8,32,320]{3,2,1,0:T(8,128)(2,1)}) %all-gather.6.cloned.1.call-update) | async-done | bytes 2621456 | tf_op jit(solution)/shard_map/all_gather | solution.py:202
  203.0 2.6 %fusion.18 = f32[4,8,32,960]{3,2,1,0:T(8,128)S(1)} fusion(bf16[16,8,32,320]{3,2,1,0:T(8,128)(2,1)} %all-gather.6.cloned.1.call-done, bf16[320,960,1,1]{0,1,3,2:T(8,128)(2,1)S(1)} %bitcast.88), kind=kOutput, calls=%fused_computation.57 | convolution fusion | flops 629145600 | bytes 7168000 | tf_op jit(solution)/shard_map/frxc,cn->frxn/dot_general | solution.py:208
  211.9 2.7 %collective-permute-start.18 = (bf16[1,8,32,320]{3,2,1,0:T(8,128)(2,1)S(1)}, bf16[1,8,32,320]{3,2,1,0:T(8,128)(2,1)S(1)}, u32[]{:S(2)}, u32[]{:S(2)}) collective-permute-start(bf16[1,8,32,320]{3,2,1,0:T(8,128)(2,1)S(1)} %get-tuple-element.37), channel_id=1, source_target_pairs={{0,6},{2,0},{4,2},{6,4},{1,7},{3,1},{5,3},{7,5},{8,14},{10,8},{12,... | collective-permute-start | bytes 491528 | tf_op jit(solution)/shard_map/ppermute | solution.py:225
  214.6 5.7 %collective-permute-done.16 = bf16[1,8,32,320]{3,2,1,0:T(8,128)(2,1)S(1)} collective-permute-done((bf16[1,8,32,320]{3,2,1,0:T(8,128)(2,1)S(1)}, bf16[1,8,32,320]{3,2,1,0:T(8,128)(2,1)S(1)}, u32[]{:S(2)}, u32[]{:S(2)}) %collective-permute-start.16) | collective-permute-done | bytes 163872 | tf_op jit(solution)/shard_map/ppermute | solution.py:225
  220.3 7.2 %collective-permute-done.17 = bf16[1,8,32,320]{3,2,1,0:T(8,128)(2,1)S(1)} collective-permute-done((bf16[1,8,32,320]{3,2,1,0:T(8,128)(2,1)S(1)}, bf16[1,8,32,320]{3,2,1,0:T(8,128)(2,1)S(1)}, u32[]{:S(2)}, u32[]{:S(2)}) %collective-permute-start.17) | collective-permute-done | bytes 163872 | tf_op jit(solution)/shard_map/ppermute | solution.py:225
  230.3 3.3 %reshape.351 = f32[1,1,8,32,1280]{4,3,2,1,0:T(8,128)} reshape(f32[1,8,32,4,4,80]{5,4,3,2,1,0:T(4,128)S(1)} %copy.148) | data formatting | bytes 2621440 | tf_op jit(solution)/shard_map/convert_element_type | solution.py:237
  233.6 2.5 %fusion.5 = f32[1,1,8,32,1280]{4,3,2,1,0:T(8,128)} fusion(f32[1,1,8,32,1280]{4,3,2,1,0:T(8,128)} %reshape.351, bf16[1,1,8,32,1280]{4,3,2,1,0:T(8,128)(2,1)S(1)} %copy-done.1, f32[1280]{0:T(1024)S(1)} %copy-done.9), kind=kLoop, calls=%fused_computation.22 | loop fusion | flops 983040 | bytes 3281920 | tf_op jit(solution)/shard_map/add | solution.py:237
  (107 shorter events, 32.1 us)
Async XLA Ops:
  6.5 100.0 %all-gather.4.cloned.1.call-start = ((), (), s32[]{:S(2)}) async-start(), calls=%async_computation | async-start | bytes 3276800 | tf_op jit(solution)/shard_map/all_gather | solution.py:118
  6.5 43.4 %collective-permute-start.9 = (bf16[9,1280,80]{1,2,0:T(8,128)(2,1)}, bf16[9,1280,80]{1,2,0:T(8,128)(2,1)S(1)}, u32[]{:S(2)}, u32[]{:S(2)}) collective-permute-start(bf16[9,1280,80]{1,2,0:T(8,128)(2,1)} %param.10), channel_id=1, source_target_pairs={{0,16},{8,24},{16,0},{24,8},{1,17},{9,25},{17,1},{25,9},{2,18},{10... | collective-permute-start | bytes 5529608 | tf_op jit(solution)/shard_map/ppermute | solution.py:40
  9.5 58.3 %collective-permute-start.8 = (bf16[9,1280,80]{1,2,0:T(8,128)(2,1)}, bf16[9,1280,80]{1,2,0:T(8,128)(2,1)}, u32[]{:S(2)}, u32[]{:S(2)}) collective-permute-start(bf16[9,1280,80]{1,2,0:T(8,128)(2,1)} %param.10), channel_id=1, source_target_pairs={{0,8},{8,0},{16,24},{24,16},{1,9},{9,1},{17,25},{25,17},{2,10},{10... | collective-permute-start | bytes 5529608 | tf_op jit(solution)/shard_map/ppermute | solution.py:41
  49.9 17.9 %collective-permute-start.10 = (bf16[9,1280,80]{1,2,0:T(8,128)(2,1)S(1)}, bf16[9,1280,80]{1,2,0:T(8,128)(2,1)}, u32[]{:S(2)}, u32[]{:S(2)}) collective-permute-start(bf16[9,1280,80]{1,2,0:T(8,128)(2,1)S(1)} %collective-permute-done.9), channel_id=1, source_target_pairs={{0,8},{8,0},{16,24},{24,16},{1,9},{9,1},{17,25},{25,17},{2,10},{10... | collective-permute-start | bytes 5529608 | tf_op jit(solution)/shard_map/ppermute | solution.py:42
  49.9 153.1 %all-gather.6.cloned.1.call-start = ((), (), s32[]{:S(2)}) async-start(), calls=%async_computation.1 | async-start | bytes 3932160 | tf_op jit(solution)/shard_map/all_gather | solution.py:202
  51.5 4.9 %collective-permute-start.1 = (f32[1,32]{1,0:T(1,128)S(1)}, f32[1,32]{1,0:T(1,128)S(1)}, u32[]{:S(2)}, u32[]{:S(2)}) collective-permute-start(f32[1,32]{1,0:T(1,128)S(1)} %bitcast.96), channel_id=1, source_target_pairs={{0,2},{2,0},{4,6},{6,4},{1,3},{3,1},{5,7},{7,5},{8,10},{10,8},{12,... | collective-permute-start | bytes 392 | tf_op jit(solution)/shard_map/ppermute | solution.py:30
  53.5 5.7 %collective-permute-start.4 = (f32[1,32]{1,0:T(1,128)S(1)}, f32[1,32]{1,0:T(1,128)S(1)}, u32[]{:S(2)}, u32[]{:S(2)}) collective-permute-start(f32[1,32]{1,0:T(1,128)S(1)} %bitcast.95), channel_id=1, source_target_pairs={{0,2},{2,0},{4,6},{6,4},{1,3},{3,1},{5,7},{7,5},{8,10},{10,8},{12,... | collective-permute-start | bytes 392 | tf_op jit(solution)/shard_map/ppermute | solution.py:30
  56.4 4.5 %collective-permute-start.2 = (f32[1,32]{1,0:T(1,128)S(1)}, f32[1,32]{1,0:T(1,128)S(1)}, u32[]{:S(2)}, u32[]{:S(2)}) collective-permute-start(f32[1,32]{1,0:T(1,128)S(1)} %bitcast_add_fusion.1), channel_id=1, source_target_pairs={{0,4},{2,6},{4,0},{6,2},{1,5},{3,7},{5,1},{7,3},{8,12},{10,14},{12... | collective-permute-start | bytes 392 | tf_op jit(solution)/shard_map/ppermute | solution.py:30
  59.3 4.6 %collective-permute-start.5 = (f32[1,32]{1,0:T(1,128)S(1)}, f32[1,32]{1,0:T(1,128)S(1)}, u32[]{:S(2)}, u32[]{:S(2)}) collective-permute-start(f32[1,32]{1,0:T(1,128)S(1)} %bitcast_add_fusion), channel_id=1, source_target_pairs={{0,4},{2,6},{4,0},{6,2},{1,5},{3,7},{5,1},{7,3},{8,12},{10,14},{12... | collective-permute-start | bytes 392 | tf_op jit(solution)/shard_map/ppermute | solution.py:30
  60.9 4.6 %collective-permute-start.3 = (f32[1,32]{1,0:T(1,128)S(1)}, f32[1,32]{1,0:T(1,128)S(1)}, u32[]{:S(2)}, u32[]{:S(2)}) collective-permute-start(f32[1,32]{1,0:T(1,128)S(1)} %add.194), channel_id=1, source_target_pairs={{0,1},{1,0},{2,3},{3,2},{4,5},{5,4},{6,7},{7,6},{8,9},{9,8},{10,11... | collective-permute-start | bytes 392 | tf_op jit(solution)/shard_map/ppermute | solution.py:30
  63.9 3.6 %collective-permute-start.6 = (f32[1,32]{1,0:T(1,128)S(1)}, f32[1,32]{1,0:T(1,128)S(1)}, u32[]{:S(2)}, u32[]{:S(2)}) collective-permute-start(f32[1,32]{1,0:T(1,128)S(1)} %add.197), channel_id=1, source_target_pairs={{0,1},{1,0},{2,3},{3,2},{4,5},{5,4},{6,7},{7,6},{8,9},{9,8},{10,11... | collective-permute-start | bytes 392 | tf_op jit(solution)/shard_map/ppermute | solution.py:30
  76.4 36.1 %copy-start.7 = (f32[1280]{0:T(1024)S(1)}, f32[1280]{0:T(1024)}, u32[]{:S(2)}) copy-start(f32[1280]{0:T(1024)} %param.13) | copy-start | bytes 15364
  76.4 36.1 %copy-start.8 = (f32[1280]{0:T(1024)S(1)}, f32[1280]{0:T(1024)}, u32[]{:S(2)}) copy-start(f32[1280]{0:T(1024)} %param.12) | copy-start | bytes 15364
  107.6 10.2 %collective-permute-start = (bf16[1,4,1,32,1280]{4,3,2,1,0:T(8,128)(2,1)S(1)}, bf16[1,4,1,32,1280]{4,3,2,1,0:T(8,128)(2,1)S(1)}, u32[]{:S(2)}, u32[]{:S(2)}) collective-permute-start(bf16[1,4,1,32,1280]{4,3,2,1,0:T(8,128)(2,1)S(1)} %get-tuple-element.31), channel_id=1, source_target_pairs={{0,1},{2,3},{4,5},{6,7},{8,9},{10,11},{12,13},{14,15},{16,17},{18,... | collective-permute-start | bytes 983048 | tf_op jit(solution)/shard_map/ppermute | solution.py:124
  111.0 10.9 %collective-permute-start.7 = (bf16[1,4,1,32,1280]{4,3,2,1,0:T(8,128)(2,1)S(1)}, bf16[1,4,1,32,1280]{4,3,2,1,0:T(8,128)(2,1)S(1)}, u32[]{:S(2)}, u32[]{:S(2)}) collective-permute-start(bf16[1,4,1,32,1280]{4,3,2,1,0:T(8,128)(2,1)S(1)} %get-tuple-element.32), channel_id=1, source_target_pairs={{1,0},{3,2},{5,4},{7,6},{9,8},{11,10},{13,12},{15,14},{17,16},{19,... | collective-permute-start | bytes 983048 | tf_op jit(solution)/shard_map/ppermute | solution.py:125
  122.4 1.7 copy-start.5
  124.1 2.9 %copy-start.4 = (bf16[1,1280,3,320]{1,3,2,0:T(8,128)(2,1)S(1)}, bf16[1,1280,3,320]{1,3,2,0:T(8,128)(2,1)}, u32[]{:S(2)}) copy-start(bf16[1,1280,3,320]{1,3,2,0:T(8,128)(2,1)} %get-tuple-element.14) | copy-start | bytes 7372804
  134.0 5.9 %copy-start.6 = (bf16[3,1280,80]{1,2,0:T(8,128)(2,1)S(1)}, bf16[3,1280,80]{1,2,0:T(8,128)(2,1)}, u32[]{:S(2)}) copy-start(bf16[3,1280,80]{1,2,0:T(8,128)(2,1)} %param.11) | copy-start | bytes 1843204
  134.2 3.6 %collective-permute-start.11 = (f32[8]{0:T(128)S(1)}, f32[8]{0:T(128)S(1)}, u32[]{:S(2)}, u32[]{:S(2)}) collective-permute-start(f32[8]{0:T(128)S(1)} %reduce_sum.78), channel_id=1, source_target_pairs={{0,1},{1,0},{2,3},{3,2},{4,5},{5,4},{6,7},{7,6},{8,9},{9,8},{10,11... | collective-permute-start | bytes 104 | tf_op jit(solution)/shard_map/ppermute | solution.py:18
  134.5 3.6 %collective-permute-start.12 = (f32[8]{0:T(128)S(1)}, f32[8]{0:T(128)S(1)}, u32[]{:S(2)}, u32[]{:S(2)}) collective-permute-start(f32[8]{0:T(128)S(1)} %reduce_sum.81), channel_id=1, source_target_pairs={{0,1},{1,0},{2,3},{3,2},{4,5},{5,4},{6,7},{7,6},{8,9},{9,8},{10,11... | collective-permute-start | bytes 104 | tf_op jit(solution)/shard_map/ppermute | solution.py:18
  139.9 13.3 %collective-permute-start.14 = (bf16[3,1280,80]{1,2,0:T(8,128)(2,1)S(1)}, bf16[3,1280,80]{1,2,0:T(8,128)(2,1)}, u32[]{:S(2)}, u32[]{:S(2)}) collective-permute-start(bf16[3,1280,80]{1,2,0:T(8,128)(2,1)S(1)} %copy-done.6), channel_id=1, source_target_pairs={{0,16},{8,24},{16,0},{24,8},{1,17},{9,25},{17,1},{25,9},{2,18},{10... | collective-permute-start | bytes 1843208 | tf_op jit(solution)/shard_map/ppermute | solution.py:40
  141.5 14.0 %collective-permute-start.13 = (bf16[3,1280,80]{1,2,0:T(8,128)(2,1)S(1)}, bf16[3,1280,80]{1,2,0:T(8,128)(2,1)}, u32[]{:S(2)}, u32[]{:S(2)}) collective-permute-start(bf16[3,1280,80]{1,2,0:T(8,128)(2,1)S(1)} %copy-done.6), channel_id=1, source_target_pairs={{0,8},{8,0},{16,24},{24,16},{1,9},{9,1},{17,25},{25,17},{2,10},{10... | collective-permute-start | bytes 1843208 | tf_op jit(solution)/shard_map/ppermute | solution.py:41
  153.2 3.8 %collective-permute-start.15 = (bf16[3,1280,80]{1,2,0:T(8,128)(2,1)}, bf16[3,1280,80]{1,2,0:T(8,128)(2,1)}, u32[]{:S(2)}, u32[]{:S(2)}) collective-permute-start(bf16[3,1280,80]{1,2,0:T(8,128)(2,1)} %collective-permute-done.14), channel_id=1, source_target_pairs={{0,8},{8,0},{16,24},{24,16},{1,9},{9,1},{17,25},{25,17},{2,10},{10... | collective-permute-start | bytes 1843208 | tf_op jit(solution)/shard_map/ppermute | solution.py:42
  165.3 37.8 %copy-start.2 = (bf16[3,320,320]{1,2,0:T(8,128)(2,1)S(1)}, bf16[3,320,320]{1,2,0:T(8,128)(2,1)}, u32[]{:S(2)}) copy-start(bf16[3,320,320]{1,2,0:T(8,128)(2,1)} %copy.138) | copy-start | bytes 1843204
  203.0 2.6 %copy-start = (bf16[16,8,32,320]{3,2,1,0:T(8,128)(2,1)S(1)}, bf16[16,8,32,320]{3,2,1,0:T(8,128)(2,1)}, u32[]{:S(2)}) copy-start(bf16[16,8,32,320]{3,2,1,0:T(8,128)(2,1)} %all-gather.6.cloned.1.call-done) | copy-start | bytes 7864324
  203.0 2.6 %copy-start.3 = (bf16[3,320,320]{1,2,0:T(8,128)(2,1)S(1)}, bf16[3,320,320]{1,2,0:T(8,128)(2,1)}, u32[]{:S(2)}) copy-start(bf16[3,320,320]{1,2,0:T(8,128)(2,1)} %copy.136) | copy-start | bytes 1843204
  210.6 9.7 %collective-permute-start.16 = (bf16[1,8,32,320]{3,2,1,0:T(8,128)(2,1)S(1)}, bf16[1,8,32,320]{3,2,1,0:T(8,128)(2,1)S(1)}, u32[]{:S(2)}, u32[]{:S(2)}) collective-permute-start(bf16[1,8,32,320]{3,2,1,0:T(8,128)(2,1)S(1)} %get-tuple-element.39), channel_id=1, source_target_pairs={{0,2},{2,4},{4,6},{6,0},{1,3},{3,5},{5,7},{7,1},{8,10},{10,12},{12... | collective-permute-start | bytes 491528 | tf_op jit(solution)/shard_map/ppermute | solution.py:225
  210.7 16.8 %collective-permute-start.17 = (bf16[1,8,32,320]{3,2,1,0:T(8,128)(2,1)S(1)}, bf16[1,8,32,320]{3,2,1,0:T(8,128)(2,1)S(1)}, u32[]{:S(2)}, u32[]{:S(2)}) collective-permute-start(bf16[1,8,32,320]{3,2,1,0:T(8,128)(2,1)S(1)} %get-tuple-element.38), channel_id=1, source_target_pairs={{0,4},{2,6},{4,0},{6,2},{1,5},{3,7},{5,1},{7,3},{8,12},{10,14},{12... | collective-permute-start | bytes 491528 | tf_op jit(solution)/shard_map/ppermute | solution.py:225
  211.9 15.5 %collective-permute-start.18 = (bf16[1,8,32,320]{3,2,1,0:T(8,128)(2,1)S(1)}, bf16[1,8,32,320]{3,2,1,0:T(8,128)(2,1)S(1)}, u32[]{:S(2)}, u32[]{:S(2)}) collective-permute-start(bf16[1,8,32,320]{3,2,1,0:T(8,128)(2,1)S(1)} %get-tuple-element.37), channel_id=1, source_target_pairs={{0,6},{2,0},{4,2},{6,4},{1,7},{3,1},{5,3},{7,5},{8,14},{10,8},{12,... | collective-permute-start | bytes 491528 | tf_op jit(solution)/shard_map/ppermute | solution.py:225
  230.2 3.3 %copy-start.1 = (bf16[1,1,8,32,1280]{4,3,2,1,0:T(8,128)(2,1)S(1)}, bf16[1,1,8,32,1280]{4,3,2,1,0:T(8,128)(2,1)}, u32[]{:S(2)}) copy-start(bf16[1,1,8,32,1280]{4,3,2,1,0:T(8,128)(2,1)} %param.9) | copy-start | bytes 1966084
  230.3 3.3 %copy-start.9 = (f32[1280]{0:T(1024)S(1)}, f32[1280]{0:T(1024)}, u32[]{:S(2)}) copy-start(f32[1280]{0:T(1024)} %param.17) | copy-start | bytes 15364
Sparse Core Ops, SparseCore 0:
  50.0 56.3 all-gather.3
  140.0 62.9 all-gather.5

commit v5 on v4

--- a/solution.py
+++ b/solution.py
@@ -111,9 +111,10 @@
     width = channels // GROUPS
     shard_width = spatial_weight.shape[-1]
 
-    spatial_w = gather_rep(spatial_weight)
+    spatial_shard = spatial_weight.reshape(3, 3, channels, shard_width).transpose(0, 2, 1, 3)
+    spatial_w = gather_rep(spatial_shard)
     temporal_w = gather_rep(temporal_weight)
-    local = spatial_w.shape[-1]
+    local = rep_size * shard_width
 
     raw = lax.all_gather(activations, "frame", axis=1, tiled=True)
     frames = raw.shape[1]
@@ -128,10 +129,11 @@
         below = jnp.zeros_like(raw[:, :, :1])
 
     grouped = activations.astype(jnp.float32).reshape(1, -1, GROUPS, width)
-    sums = jnp.sum(grouped, axis=(1, 3))
-    squares = jnp.sum(grouped * grouped, axis=(1, 3))
-    sums, squares = butterfly_sum((sums, squares), "frame")
-    sums, squares = butterfly_sum((sums, squares), "row")
+    stats = jnp.concatenate(
+        [jnp.sum(grouped, axis=(1, 3)), jnp.sum(grouped * grouped, axis=(1, 3))]
+    )
+    stats = butterfly_sum(butterfly_sum(stats, "frame"), "row")
+    sums, squares = stats[:1], stats[1:]
     count = grouped.shape[1] * width * frame_size * row_size
     mean = sums / count
     variance = squares / count - mean * mean
@@ -151,8 +153,7 @@
     padded = jnp.concatenate([first_above, first_mid, first_below], axis=2)
 
     field = lax.optimization_barrier(padded[0])
-    wide = spatial_w.reshape(3, 3, channels, local).transpose(0, 2, 1, 3)
-    wide = wide.reshape(3, channels, 3 * local)
+    wide = spatial_w.reshape(3, channels, 3 * local)
     product = None
     for row_tap in range(3):
         term = jnp.einsum(
@@ -171,9 +172,11 @@
     s2 = local_vector(second_shift, frame_index, rep_size, frame_size)
     if shard_width % width == 0:
         grouped2 = spatial.reshape(-1, local // width, width)
-        sums2 = jnp.sum(grouped2, axis=(0, 2))
-        squares2 = jnp.sum(grouped2 * grouped2, axis=(0, 2))
-        sums2, squares2 = pair_sum((sums2, squares2), "row")
+        stats2 = jnp.stack(
+            [jnp.sum(grouped2, axis=(0, 2)), jnp.sum(grouped2 * grouped2, axis=(0, 2))]
+        )
+        stats2 = pair_sum(stats2, "row")
+        sums2, squares2 = stats2[0], stats2[1]
         count2 = grouped2.shape[0] * width * row_size
         mean2 = sums2 / count2
         variance2 = squares2 / count2 - mean2 * mean2

time: 244 us -> 243 us (level)
  starting transfers between devices: 24.4 us -> 20.2 us
  waiting for transfers between devices: 140 us -> 143 us
    all_gather x1, waiting for transfers between devices: 27.4 us -> 31.3 us  [shards(): raw = lax.all_gather(activations, 'frame', axis=1, tiled=True)]
    ppermute x6 -> x3, starting transfers between devices: 8.82 us -> 6.63 us  [butterfly_sum(): value = jax.tree.map(lambda v: v + lax.ppermute(v, axis, pairs), value)]
  transfers between devices with their start and end apart: 21 -> 17, of which waited for: 13 -> 12; matrix products, arithmetic and copies ran while one was open for 14% -> 14% of each run, Pallas kernels for 0% -> 0%
where the time goes in v5:
time: 243 us; the launch traced here: 241 us
  waiting for transfers between devices  143 us (59%)
  other arithmetic  25 us (10%)
  local copies, waits for them, and re-layouts  24.4 us (10%)
  starting transfers between devices  20.2 us (8%)
  matrix products  15.2 us (6%)
  between operations  13.9 us (6%)
    ppermute x2, waiting for transfers between devices, gather_rep(): across = lax.ppermute(w, 'rep', [(k, k ^ 2) for k in range(size)])  52.2 us
    all_gather x1, waiting for transfers between devices, shards(): second_all = lax.all_gather(second[0], 'frame', axis=0, tiled=False)  34.4 us
    all_gather x1, waiting for transfers between devices, shards(): raw = lax.all_gather(activations, 'frame', axis=1, tiled=True)  31.3 us
    ppermute x3, waiting for transfers between devices, shards(): lax.ppermute(piece, 'frame', [(k, (k + shift) % frame_size) for k in rang...  12.9 us
    dot_general x3, matrix products, shards(): jnp.einsum('frxc,cn->frxn', field[:, row_tap:row_tap + rows], wide[row_ta...  8.71 us
    concatenate x2, other arithmetic, gather_rep(): return jnp.concatenate(blocks, axis=-1)  8.27 us
    ppermute x3, starting transfers between devices, butterfly_sum(): value = jax.tree.map(lambda v: v + lax.ppermute(v, axis, pairs), value)  6.63 us
    dot_general x4, matrix products, shards(): jnp.einsum('frxc,cn->frxn', second_all[group], weights, preferred_element...  6.53 us
  transfers between devices with their start and end apart: 17, of which 12 were waited for; matrix products, arithmetic and copies ran while one was open for 14% of the time, Pallas kernels for 0%

profile of v5, /device:TPU:0, one launch (start us, length us, event | category | flops | bytes accessed | tf_op | source)
XLA Modules:
  0.0 241.4 jit_solution(3068218465588520655)
XLA Ops:
  6.5 3.0 %collective-permute-start.6 = (bf16[3,1280,3,80]{1,3,2,0:T(8,128)(2,1)}, bf16[3,1280,3,80]{1,3,2,0:T(8,128)(2,1)S(1)}, u32[]{:S(2)}, u32[]{:S(2)}) collective-permute-start(bf16[3,1280,3,80]{1,3,2,0:T(8,128)(2,1)} %bitcast.104), channel_id=1, source_target_pairs={{0,16},{8,24},{16,0},{24,8},{1,17},{9,25},{17,1},{25,9},{2,18},{10... | collective-permute-start | bytes 5529608 | tf_op jit(solution)/shard_map/ppermute | solution.py:40
  9.5 40.4 %collective-permute-done.6 = bf16[3,1280,3,80]{1,3,2,0:T(8,128)(2,1)S(1)} collective-permute-done((bf16[3,1280,3,80]{1,3,2,0:T(8,128)(2,1)}, bf16[3,1280,3,80]{1,3,2,0:T(8,128)(2,1)S(1)}, u32[]{:S(2)}, u32[]{:S(2)}) %collective-permute-start.6) | collective-permute-done | bytes 1843232 | tf_op jit(solution)/shard_map/ppermute | solution.py:40
  51.7 1.9 collective-permute-start.1
  55.3 2.9 %collective-permute-start.2 = (f32[2,32]{1,0:T(2,128)S(1)}, f32[2,32]{1,0:T(2,128)S(1)}, u32[]{:S(2)}, u32[]{:S(2)}) collective-permute-start(f32[2,32]{1,0:T(2,128)S(1)} %fusion.12), channel_id=1, source_target_pairs={{0,4},{2,6},{4,0},{6,2},{1,5},{3,7},{5,1},{7,3},{8,12},{10,14},{12... | collective-permute-start | bytes 776 | tf_op jit(solution)/shard_map/ppermute | solution.py:30
  59.9 1.8 collective-permute-start.3
  61.9 1.6 collective-permute-done.3
  63.9 3.1 %select_select_fusion.3 = (bf16[3,1280,3,80]{1,3,2,0:T(8,128)(2,1)S(1)}, bf16[3,1280,3,80]{1,3,2,0:T(8,128)(2,1)S(1)}, bf16[3,1280,3,80]{1,3,2,0:T(8,128)(2,1)S(1)}, bf16[3,1280,3,80]{1,3,2,0:T(8,128)(2,1)S(1)}) fusion(bf16[3,1280,3,80]{1,3,2,0:T(8,128)(2,1)} %bitcast.106, bf16[3,1280,3,80]{1,3,2,0:T(8,128)(2,1)} %collective-permute-done.5, ...), kind=kLoop, calls=%fused_computation.12 | loop fusion | flops 11059200 | bytes 14745612 | tf_op jit(solution)/shard_map/jit(_where)/select_n | solution.py:49
  66.9 5.5 %pad_maximum_fusion = bf16[3,1280,3,320]{1,3,2,0:T(8,128)(2,1)S(1)} fusion(bf16[3,1280,3,80]{1,3,2,0:T(8,128)(2,1)S(1)} %get-tuple-element.14, bf16[3,1280,3,80]{1,3,2,0:T(8,128)(2,1)S(1)} %get-tuple-element.15, bf16[3,1280,3,80]{1,3,2,0:T(8,128)(2,1)S(1)} %get-tuple-element.16, bf16[3,1280,3,80]{1,3,2,0:T(8,128)(2,1)S(1)} %get-tuple-element.13), kind=kLoop, calls=%fused_computation | loop fusion | flops 29491200 | bytes 14745600 | tf_op jit(solution)/shard_map/concatenate | solution.py:51
  72.5 2.7 %fusion.15 = (bf16[1,1280,3,320]{1,3,2,0:T(8,128)(2,1)S(1)}, bf16[1,1280,3,320]{1,3,2,0:T(8,128)(2,1)}, bf16[1,1280,3,320]{1,3,2,0:T(8,128)(2,1)}) fusion(bf16[3,1280,3,320]{1,3,2,0:T(8,128)(2,1)S(1)} %pad_maximum_fusion), kind=kLoop, calls=%fused_computation.54 | loop fusion | bytes 14745600 | tf_op jit(solution)/shard_map/slice | solution.py:162
  75.2 31.3 %all-gather.4.cloned.1.call-done = bf16[1,4,8,32,1280]{4,3,2,0,1:T(8,128)(2,1)} async-done(((bf16[1,1,8,32,1280]{4,3,2,0,1:T(8,128)(2,1)}), bf16[1,4,8,32,1280]{4,3,2,0,1:T(8,128)(2,1)}) %all-gather.4.cloned.1.call-update) | async-done | bytes 2621456 | tf_op jit(solution)/shard_map/all_gather | solution.py:119
  107.6 3.4 %collective-permute-start = (bf16[1,4,1,32,1280]{4,3,2,1,0:T(8,128)(2,1)S(1)}, bf16[1,4,1,32,1280]{4,3,2,1,0:T(8,128)(2,1)S(1)}, u32[]{:S(2)}, u32[]{:S(2)}) collective-permute-start(bf16[1,4,1,32,1280]{4,3,2,1,0:T(8,128)(2,1)S(1)} %get-tuple-element.29), channel_id=1, source_target_pairs={{0,1},{2,3},{4,5},{6,7},{8,9},{10,11},{12,13},{14,15},{16,17},{18,... | collective-permute-start | bytes 983048 | tf_op jit(solution)/shard_map/ppermute | solution.py:125
  112.5 3.5 %multiply_convert_fusion = bf16[1,4,8,32,1280]{4,3,2,1,0:T(8,128)(2,1)S(1)} fusion(f32[1280]{0:T(1024)S(1)} %copy-done.7, f32[1280]{0:T(1024)S(1)} %copy-done.8, f32[1280]{0:T(1024)S(1)} %broadcast_in_dim.32, f32[1280]{0:T(1024)S(1)} %broadcast_in_dim.30, bf16[1,4,8,32,1280]{4,3,2,0,1:T(8,128)(2,1)} %all-gather.4.cloned.1.call-done), kind=kLoop, calls=%fused_computation.1 | loop fusion | flops 13107200 | bytes 5263360 | tf_op jit(solution)/shard_map/convert_element_type | solution.py:61
  116.0 1.7 collective-permute-done
  117.8 4.1 %collective-permute-done.4 = bf16[1,4,1,32,1280]{4,3,2,1,0:T(8,128)(2,1)S(1)} collective-permute-done((bf16[1,4,1,32,1280]{4,3,2,1,0:T(8,128)(2,1)S(1)}, bf16[1,4,1,32,1280]{4,3,2,1,0:T(8,128)(2,1)S(1)}, u32[]{:S(2)}, u32[]{:S(2)}) %collective-permute-start.4) | collective-permute-done | bytes 327712 | tf_op jit(solution)/shard_map/ppermute | solution.py:126
  124.1 2.9 %fusion.21 = f32[4,8,32,960]{3,2,1,0:T(8,128)S(1)} fusion(bf16[4,10,32,1280]{3,2,1,0:T(8,128)(2,1)S(1)} %maximum_bitcast_fusion, bf16[1280,960,1,1]{0,1,3,2:T(8,128)(2,1)S(1)} %bitcast.103), kind=kOutput, calls=%fused_computation.60 | convolution fusion | flops 2516582400 | bytes 9666560 | tf_op jit(solution)/shard_map/frxc,cn->frxn/dot_general | solution.py:159
  127.0 2.9 %fusion.20 = f32[4,8,32,960]{3,2,1,0:T(8,128)S(1)} fusion(bf16[4,10,32,1280]{3,2,1,0:T(8,128)(2,1)S(1)} %maximum_bitcast_fusion, bf16[1280,960,1,1]{0,1,3,2:T(8,128)(2,1)S(1)} %bitcast.102), kind=kOutput, calls=%fused_computation.59 | convolution fusion | flops 2516582400 | bytes 9666560 | tf_op jit(solution)/shard_map/frxc,cn->frxn/dot_general | solution.py:159
  129.9 2.9 %add_add_fusion.1 = f32[4,8,32,960]{3,2,1,0:T(8,128)S(1)} fusion(f32[4,8,32,960]{3,2,1,0:T(8,128)S(1)} %fusion.20, f32[4,8,32,960]{3,2,1,0:T(8,128)S(1)} %fusion.21, bf16[4,10,32,1280]{3,2,1,0:T(8,128)(2,1)S(1)} %maximum_bitcast_fusion, bf16[1280,960,1,1]{0,1,3,2:T(8,128)(2,1)S(1)} %bitcast.101), kind=kOutput, calls=%fused_computation.3 | convolution fusion | flops 2518548480 | bytes 17530880 | tf_op jit(solution)/shard_map/frxc,cn->frxn/dot_general | solution.py:159
  134.6 3.5 %collective-permute-done.8 = f32[2,8]{1,0:T(2,128)S(1)} collective-permute-done((f32[2,8]{1,0:T(2,128)S(1)}, f32[2,8]{1,0:T(2,128)S(1)}, u32[]{:S(2)}, u32[]{:S(2)}) %collective-permute-start.8) | collective-permute-done | bytes 96 | tf_op jit(solution)/shard_map/ppermute | solution.py:18
  139.9 1.5 collective-permute-start.10
  141.4 11.8 %collective-permute-done.10 = bf16[3,1280,80]{1,2,0:T(8,128)(2,1)} collective-permute-done((bf16[3,1280,80]{1,2,0:T(8,128)(2,1)S(1)}, bf16[3,1280,80]{1,2,0:T(8,128)(2,1)}, u32[]{:S(2)}, u32[]{:S(2)}) %collective-permute-start.10) | collective-permute-done | bytes 614432 | tf_op jit(solution)/shard_map/ppermute | solution.py:40
  153.9 1.5 copy.120
  155.4 1.5 copy.122
  157.0 2.2 copy.121
  159.2 1.7 select_select_fusion.7
  160.8 2.8 %pad_maximum_fusion.1 = bf16[3,1280,320]{2,1,0:T(8,128)(2,1)S(1)} fusion(bf16[3,1280,80]{2,1,0:T(8,128)(2,1)S(1)} %get-tuple-element.22, bf16[3,1280,80]{2,1,0:T(8,128)(2,1)S(1)} %get-tuple-element.23, bf16[3,1280,80]{2,1,0:T(8,128)(2,1)S(1)} %get-tuple-element.24, bf16[3,1280,80]{2,1,0:T(8,128)(2,1)S(1)} %get-tuple-element.21), kind=kLoop, calls=%fused_computation.5 | loop fusion | flops 9830400 | bytes 4915200 | tf_op jit(solution)/shard_map/concatenate | solution.py:51
  167.1 34.4 %all-gather.6.cloned.1.call-done = bf16[16,8,32,320]{3,2,1,0:T(8,128)(2,1)} async-done(((bf16[4,8,32,320]{3,2,1,0:T(8,128)(2,1)}), bf16[16,8,32,320]{3,2,1,0:T(8,128)(2,1)}) %all-gather.6.cloned.1.call-update) | async-done | bytes 2621456 | tf_op jit(solution)/shard_map/all_gather | solution.py:205
  201.5 2.6 %fusion.23 = f32[4,8,32,960]{3,2,1,0:T(8,128)S(1)} fusion(bf16[16,8,32,320]{3,2,1,0:T(8,128)(2,1)} %all-gather.6.cloned.1.call-done, bf16[320,960,1,1]{0,1,3,2:T(8,128)(2,1)S(1)} %bitcast.97), kind=kOutput, calls=%fused_computation.62 | convolution fusion | flops 629145600 | bytes 7168000 | tf_op jit(solution)/shard_map/frxc,cn->frxn/dot_general | solution.py:211
  210.4 2.7 %collective-permute-start.14 = (bf16[1,8,32,320]{3,2,1,0:T(8,128)(2,1)S(1)}, bf16[1,8,32,320]{3,2,1,0:T(8,128)(2,1)S(1)}, u32[]{:S(2)}, u32[]{:S(2)}) collective-permute-start(bf16[1,8,32,320]{3,2,1,0:T(8,128)(2,1)S(1)} %get-tuple-element.35), channel_id=1, source_target_pairs={{0,6},{2,0},{4,2},{6,4},{1,7},{3,1},{5,3},{7,5},{8,14},{10,8},{12,... | collective-permute-start | bytes 491528 | tf_op jit(solution)/shard_map/ppermute | solution.py:228
  213.1 5.7 %collective-permute-done.12 = bf16[1,8,32,320]{3,2,1,0:T(8,128)(2,1)S(1)} collective-permute-done((bf16[1,8,32,320]{3,2,1,0:T(8,128)(2,1)S(1)}, bf16[1,8,32,320]{3,2,1,0:T(8,128)(2,1)S(1)}, u32[]{:S(2)}, u32[]{:S(2)}) %collective-permute-start.12) | collective-permute-done | bytes 163872 | tf_op jit(solution)/shard_map/ppermute | solution.py:228
  218.8 7.2 %collective-permute-done.13 = bf16[1,8,32,320]{3,2,1,0:T(8,128)(2,1)S(1)} collective-permute-done((bf16[1,8,32,320]{3,2,1,0:T(8,128)(2,1)S(1)}, bf16[1,8,32,320]{3,2,1,0:T(8,128)(2,1)S(1)}, u32[]{:S(2)}, u32[]{:S(2)}) %collective-permute-start.13) | collective-permute-done | bytes 163872 | tf_op jit(solution)/shard_map/ppermute | solution.py:228
  228.8 3.3 %reshape.355 = f32[1,1,8,32,1280]{4,3,2,1,0:T(8,128)} reshape(f32[1,8,32,4,4,80]{5,4,3,2,1,0:T(4,128)S(1)} %copy.148) | data formatting | bytes 2621440 | tf_op jit(solution)/shard_map/convert_element_type | solution.py:240
  232.1 2.5 %fusion.5 = f32[1,1,8,32,1280]{4,3,2,1,0:T(8,128)} fusion(f32[1,1,8,32,1280]{4,3,2,1,0:T(8,128)} %reshape.355, bf16[1,1,8,32,1280]{4,3,2,1,0:T(8,128)(2,1)S(1)} %copy-done.1, f32[1280]{0:T(1024)S(1)} %copy-done.9), kind=kLoop, calls=%fused_computation.22 | loop fusion | flops 983040 | bytes 3281920 | tf_op jit(solution)/shard_map/add | solution.py:240
  (102 shorter events, 27.0 us)
Async XLA Ops:
  6.5 100.0 %all-gather.4.cloned.1.call-start = ((), (), s32[]{:S(2)}) async-start(), calls=%async_computation | async-start | bytes 3276800 | tf_op jit(solution)/shard_map/all_gather | solution.py:119
  6.5 43.4 %collective-permute-start.6 = (bf16[3,1280,3,80]{1,3,2,0:T(8,128)(2,1)}, bf16[3,1280,3,80]{1,3,2,0:T(8,128)(2,1)S(1)}, u32[]{:S(2)}, u32[]{:S(2)}) collective-permute-start(bf16[3,1280,3,80]{1,3,2,0:T(8,128)(2,1)} %bitcast.104), channel_id=1, source_target_pairs={{0,16},{8,24},{16,0},{24,8},{1,17},{9,25},{17,1},{25,9},{2,18},{10... | collective-permute-start | bytes 5529608 | tf_op jit(solution)/shard_map/ppermute | solution.py:40
  9.5 54.4 %collective-permute-start.5 = (bf16[3,1280,3,80]{1,3,2,0:T(8,128)(2,1)}, bf16[3,1280,3,80]{1,3,2,0:T(8,128)(2,1)}, u32[]{:S(2)}, u32[]{:S(2)}) collective-permute-start(bf16[3,1280,3,80]{1,3,2,0:T(8,128)(2,1)} %bitcast.105), channel_id=1, source_target_pairs={{0,8},{8,0},{16,24},{24,16},{1,9},{9,1},{17,25},{25,17},{2,10},{10... | collective-permute-start | bytes 5529608 | tf_op jit(solution)/shard_map/ppermute | solution.py:41
  49.9 14.0 %collective-permute-start.7 = (bf16[3,1280,3,80]{1,3,2,0:T(8,128)(2,1)S(1)}, bf16[3,1280,3,80]{1,3,2,0:T(8,128)(2,1)}, u32[]{:S(2)}, u32[]{:S(2)}) collective-permute-start(bf16[3,1280,3,80]{1,3,2,0:T(8,128)(2,1)S(1)} %collective-permute-done.6), channel_id=1, source_target_pairs={{0,8},{8,0},{16,24},{24,16},{1,9},{9,1},{17,25},{25,17},{2,10},{10... | collective-permute-start | bytes 5529608 | tf_op jit(solution)/shard_map/ppermute | solution.py:42
  49.9 151.6 %all-gather.6.cloned.1.call-start = ((), (), s32[]{:S(2)}) async-start(), calls=%async_computation.1 | async-start | bytes 3932160 | tf_op jit(solution)/shard_map/all_gather | solution.py:205
  51.7 3.6 %collective-permute-start.1 = (f32[2,32]{1,0:T(2,128)S(1)}, f32[2,32]{1,0:T(2,128)S(1)}, u32[]{:S(2)}, u32[]{:S(2)}) collective-permute-start(f32[2,32]{1,0:T(2,128)S(1)} %pad_maximum_fusion.2), channel_id=1, source_target_pairs={{0,2},{2,0},{4,6},{6,4},{1,3},{3,1},{5,7},{7,5},{8,10},{10,8},{12,... | collective-permute-start | bytes 776 | tf_op jit(solution)/shard_map/ppermute | solution.py:30
  55.3 4.5 %collective-permute-start.2 = (f32[2,32]{1,0:T(2,128)S(1)}, f32[2,32]{1,0:T(2,128)S(1)}, u32[]{:S(2)}, u32[]{:S(2)}) collective-permute-start(f32[2,32]{1,0:T(2,128)S(1)} %fusion.12), channel_id=1, source_target_pairs={{0,4},{2,6},{4,0},{6,2},{1,5},{3,7},{5,1},{7,3},{8,12},{10,14},{12... | collective-permute-start | bytes 776 | tf_op jit(solution)/shard_map/ppermute | solution.py:30
  59.9 3.6 %collective-permute-start.3 = (f32[2,32]{1,0:T(2,128)S(1)}, f32[2,32]{1,0:T(2,128)S(1)}, u32[]{:S(2)}, u32[]{:S(2)}) collective-permute-start(f32[2,32]{1,0:T(2,128)S(1)} %fusion.39), channel_id=1, source_target_pairs={{0,1},{1,0},{2,3},{3,2},{4,5},{5,4},{6,7},{7,6},{8,9},{9,8},{10,11... | collective-permute-start | bytes 776 | tf_op jit(solution)/shard_map/ppermute | solution.py:30
  72.4 40.1 %copy-start.7 = (f32[1280]{0:T(1024)S(1)}, f32[1280]{0:T(1024)}, u32[]{:S(2)}) copy-start(f32[1280]{0:T(1024)} %param.13) | copy-start | bytes 15364
  72.5 40.0 %copy-start.8 = (f32[1280]{0:T(1024)S(1)}, f32[1280]{0:T(1024)}, u32[]{:S(2)}) copy-start(f32[1280]{0:T(1024)} %param.12) | copy-start | bytes 15364
  107.6 10.2 %collective-permute-start = (bf16[1,4,1,32,1280]{4,3,2,1,0:T(8,128)(2,1)S(1)}, bf16[1,4,1,32,1280]{4,3,2,1,0:T(8,128)(2,1)S(1)}, u32[]{:S(2)}, u32[]{:S(2)}) collective-permute-start(bf16[1,4,1,32,1280]{4,3,2,1,0:T(8,128)(2,1)S(1)} %get-tuple-element.29), channel_id=1, source_target_pairs={{0,1},{2,3},{4,5},{6,7},{8,9},{10,11},{12,13},{14,15},{16,17},{18,... | collective-permute-start | bytes 983048 | tf_op jit(solution)/shard_map/ppermute | solution.py:125
  111.0 10.9 %collective-permute-start.4 = (bf16[1,4,1,32,1280]{4,3,2,1,0:T(8,128)(2,1)S(1)}, bf16[1,4,1,32,1280]{4,3,2,1,0:T(8,128)(2,1)S(1)}, u32[]{:S(2)}, u32[]{:S(2)}) collective-permute-start(bf16[1,4,1,32,1280]{4,3,2,1,0:T(8,128)(2,1)S(1)} %get-tuple-element.30), channel_id=1, source_target_pairs={{1,0},{3,2},{5,4},{7,6},{9,8},{11,10},{13,12},{15,14},{17,16},{19,... | collective-permute-start | bytes 983048 | tf_op jit(solution)/shard_map/ppermute | solution.py:126
  122.4 1.7 copy-start.5
  124.1 2.9 %copy-start.4 = (bf16[1,1280,3,320]{1,3,2,0:T(8,128)(2,1)S(1)}, bf16[1,1280,3,320]{1,3,2,0:T(8,128)(2,1)}, u32[]{:S(2)}) copy-start(bf16[1,1280,3,320]{1,3,2,0:T(8,128)(2,1)} %get-tuple-element.12) | copy-start | bytes 7372804
  134.0 5.9 %copy-start.6 = (bf16[3,1280,80]{1,2,0:T(8,128)(2,1)S(1)}, bf16[3,1280,80]{1,2,0:T(8,128)(2,1)}, u32[]{:S(2)}) copy-start(bf16[3,1280,80]{1,2,0:T(8,128)(2,1)} %param.11) | copy-start | bytes 1843204
  134.4 3.6 %collective-permute-start.8 = (f32[2,8]{1,0:T(2,128)S(1)}, f32[2,8]{1,0:T(2,128)S(1)}, u32[]{:S(2)}, u32[]{:S(2)}) collective-permute-start(f32[2,8]{1,0:T(2,128)S(1)} %pad_maximum_fusion.3), channel_id=1, source_target_pairs={{0,1},{1,0},{2,3},{3,2},{4,5},{5,4},{6,7},{7,6},{8,9},{9,8},{10,11... | collective-permute-start | bytes 200 | tf_op jit(solution)/shard_map/ppermute | solution.py:18
  139.9 13.3 %collective-permute-start.10 = (bf16[3,1280,80]{1,2,0:T(8,128)(2,1)S(1)}, bf16[3,1280,80]{1,2,0:T(8,128)(2,1)}, u32[]{:S(2)}, u32[]{:S(2)}) collective-permute-start(bf16[3,1280,80]{1,2,0:T(8,128)(2,1)S(1)} %copy-done.6), channel_id=1, source_target_pairs={{0,16},{8,24},{16,0},{24,8},{1,17},{9,25},{17,1},{25,9},{2,18},{10... | collective-permute-start | bytes 1843208 | tf_op jit(solution)/shard_map/ppermute | solution.py:40
  141.4 14.0 %collective-permute-start.9 = (bf16[3,1280,80]{1,2,0:T(8,128)(2,1)S(1)}, bf16[3,1280,80]{1,2,0:T(8,128)(2,1)}, u32[]{:S(2)}, u32[]{:S(2)}) collective-permute-start(bf16[3,1280,80]{1,2,0:T(8,128)(2,1)S(1)} %copy-done.6), channel_id=1, source_target_pairs={{0,8},{8,0},{16,24},{24,16},{1,9},{9,1},{17,25},{25,17},{2,10},{10... | collective-permute-start | bytes 1843208 | tf_op jit(solution)/shard_map/ppermute | solution.py:41
  153.2 3.8 %collective-permute-start.11 = (bf16[3,1280,80]{1,2,0:T(8,128)(2,1)}, bf16[3,1280,80]{1,2,0:T(8,128)(2,1)}, u32[]{:S(2)}, u32[]{:S(2)}) collective-permute-start(bf16[3,1280,80]{1,2,0:T(8,128)(2,1)} %collective-permute-done.10), channel_id=1, source_target_pairs={{0,8},{8,0},{16,24},{24,16},{1,9},{9,1},{17,25},{25,17},{2,10},{10... | collective-permute-start | bytes 1843208 | tf_op jit(solution)/shard_map/ppermute | solution.py:42
  165.2 36.3 %copy-start.2 = (bf16[3,320,320]{1,2,0:T(8,128)(2,1)S(1)}, bf16[3,320,320]{1,2,0:T(8,128)(2,1)}, u32[]{:S(2)}) copy-start(bf16[3,320,320]{1,2,0:T(8,128)(2,1)} %copy.138) | copy-start | bytes 1843204
  201.5 2.6 %copy-start = (bf16[16,8,32,320]{3,2,1,0:T(8,128)(2,1)S(1)}, bf16[16,8,32,320]{3,2,1,0:T(8,128)(2,1)}, u32[]{:S(2)}) copy-start(bf16[16,8,32,320]{3,2,1,0:T(8,128)(2,1)} %all-gather.6.cloned.1.call-done) | copy-start | bytes 7864324
  201.5 2.6 %copy-start.3 = (bf16[3,320,320]{1,2,0:T(8,128)(2,1)S(1)}, bf16[3,320,320]{1,2,0:T(8,128)(2,1)}, u32[]{:S(2)}) copy-start(bf16[3,320,320]{1,2,0:T(8,128)(2,1)} %copy.136) | copy-start | bytes 1843204
  209.1 9.7 %collective-permute-start.12 = (bf16[1,8,32,320]{3,2,1,0:T(8,128)(2,1)S(1)}, bf16[1,8,32,320]{3,2,1,0:T(8,128)(2,1)S(1)}, u32[]{:S(2)}, u32[]{:S(2)}) collective-permute-start(bf16[1,8,32,320]{3,2,1,0:T(8,128)(2,1)S(1)} %get-tuple-element.37), channel_id=1, source_target_pairs={{0,2},{2,4},{4,6},{6,0},{1,3},{3,5},{5,7},{7,1},{8,10},{10,12},{12... | collective-permute-start | bytes 491528 | tf_op jit(solution)/shard_map/ppermute | solution.py:228
  209.2 16.8 %collective-permute-start.13 = (bf16[1,8,32,320]{3,2,1,0:T(8,128)(2,1)S(1)}, bf16[1,8,32,320]{3,2,1,0:T(8,128)(2,1)S(1)}, u32[]{:S(2)}, u32[]{:S(2)}) collective-permute-start(bf16[1,8,32,320]{3,2,1,0:T(8,128)(2,1)S(1)} %get-tuple-element.36), channel_id=1, source_target_pairs={{0,4},{2,6},{4,0},{6,2},{1,5},{3,7},{5,1},{7,3},{8,12},{10,14},{12... | collective-permute-start | bytes 491528 | tf_op jit(solution)/shard_map/ppermute | solution.py:228
  210.4 15.5 %collective-permute-start.14 = (bf16[1,8,32,320]{3,2,1,0:T(8,128)(2,1)S(1)}, bf16[1,8,32,320]{3,2,1,0:T(8,128)(2,1)S(1)}, u32[]{:S(2)}, u32[]{:S(2)}) collective-permute-start(bf16[1,8,32,320]{3,2,1,0:T(8,128)(2,1)S(1)} %get-tuple-element.35), channel_id=1, source_target_pairs={{0,6},{2,0},{4,2},{6,4},{1,7},{3,1},{5,3},{7,5},{8,14},{10,8},{12,... | collective-permute-start | bytes 491528 | tf_op jit(solution)/shard_map/ppermute | solution.py:228
  228.8 3.3 %copy-start.1 = (bf16[1,1,8,32,1280]{4,3,2,1,0:T(8,128)(2,1)S(1)}, bf16[1,1,8,32,1280]{4,3,2,1,0:T(8,128)(2,1)}, u32[]{:S(2)}) copy-start(bf16[1,1,8,32,1280]{4,3,2,1,0:T(8,128)(2,1)} %param.9) | copy-start | bytes 1966084
  228.8 3.3 %copy-start.9 = (f32[1280]{0:T(1024)S(1)}, f32[1280]{0:T(1024)}, u32[]{:S(2)}) copy-start(f32[1280]{0:T(1024)} %param.17) | copy-start | bytes 15364
Sparse Core Ops, SparseCore 0:
  50.0 56.3 all-gather.3
  140.0 61.5 all-gather.5

commit v6 on v5

--- a/solution.py
+++ b/solution.py
@@ -18,18 +18,6 @@
             lambda v: v + lax.ppermute(v, axis, [(0, 1), (1, 0)]), value
         )
     return lax.psum(value, axis)
-
-
-def butterfly_sum(value, axis):
-    size = lax.axis_size(axis)
-    if size & (size - 1) != 0:
-        return lax.psum(value, axis)
-    step = 1
-    while step < size:
-        pairs = [(k, k ^ step) for k in range(size)]
-        value = jax.tree.map(lambda v: v + lax.ppermute(v, axis, pairs), value)
-        step *= 2
-    return value
 
 
 def gather_rep(w):
@@ -128,13 +116,13 @@
         above = jnp.zeros_like(raw[:, :, :1])
         below = jnp.zeros_like(raw[:, :, :1])
 
-    grouped = activations.astype(jnp.float32).reshape(1, -1, GROUPS, width)
+    grouped = raw.astype(jnp.float32).reshape(1, -1, GROUPS, width)
     stats = jnp.concatenate(
         [jnp.sum(grouped, axis=(1, 3)), jnp.sum(grouped * grouped, axis=(1, 3))]
     )
-    stats = butterfly_sum(butterfly_sum(stats, "frame"), "row")
+    stats = pair_sum(stats, "row")
     sums, squares = stats[:1], stats[1:]
-    count = grouped.shape[1] * width * frame_size * row_size
+    count = grouped.shape[1] * width * row_size
     mean = sums / count
     variance = squares / count - mean * mean
     inverse = lax.rsqrt(variance + EPS)

time: 243 us -> 246 us (1.012)
  waiting for transfers between devices: 143 us -> 152 us
  starting transfers between devices: 20.2 us -> 14.8 us
    all_gather x1, waiting for transfers between devices: 31.3 us -> 40.9 us  [shards(): raw = lax.all_gather(activations, 'frame', axis=1, tiled=True)]
    ppermute x3 -> x0, starting transfers between devices: 6.63 us -> none  [butterfly_sum(): value = jax.tree.map(lambda v: v + lax.ppermute(v, axis, pairs), value)]
    ppermute x3 -> x0, waiting for transfers between devices: 2.6 us -> none  [butterfly_sum(): value = jax.tree.map(lambda v: v + lax.ppermute(v, axis, pairs), value)]
  transfers between devices with their start and end apart: 17 -> 15, of which waited for: 12 -> 10; matrix products, arithmetic and copies ran while one was open for 14% -> 12% of each run, Pallas kernels for 0% -> 0%
where the time goes in v6:
time: 246 us; the launch traced here: 244 us
  waiting for transfers between devices  152 us (62%)
  other arithmetic  25.3 us (10%)
  local copies, waits for them, and re-layouts  22.8 us (9%)
  matrix products  15.2 us (6%)
  starting transfers between devices  14.8 us (6%)
  between operations  14 us (6%)
    ppermute x2, waiting for transfers between devices, gather_rep(): across = lax.ppermute(w, 'rep', [(k, k ^ 2) for k in range(size)])  51.9 us
    all_gather x1, waiting for transfers between devices, shards(): raw = lax.all_gather(activations, 'frame', axis=1, tiled=True)  40.9 us
    all_gather x1, waiting for transfers between devices, shards(): second_all = lax.all_gather(second[0], 'frame', axis=0, tiled=False)  34.7 us
    ppermute x3, waiting for transfers between devices, shards(): lax.ppermute(piece, 'frame', [(k, (k + shift) % frame_size) for k in rang...  12.9 us
    dot_general x3, matrix products, shards(): jnp.einsum('frxc,cn->frxn', field[:, row_tap:row_tap + rows], wide[row_ta...  8.69 us
    concatenate x2, other arithmetic, gather_rep(): return jnp.concatenate(blocks, axis=-1)  8.27 us
    dot_general x4, matrix products, shards(): jnp.einsum('frxc,cn->frxn', second_all[group], weights, preferred_element...  6.53 us
    ppermute x1, waiting for transfers between devices, shards(): below = lax.ppermute(raw[:, :, :1], 'row', up)  4.93 us
  transfers between devices with their start and end apart: 15, of which 10 were waited for; matrix products, arithmetic and copies ran while one was open for 12% of the time, Pallas kernels for 0%

profile of v6, /device:TPU:0, one launch (start us, length us, event | category | flops | bytes accessed | tf_op | source)
XLA Modules:
  0.0 244.3 jit_solution(3794884922333357173)
XLA Ops:
  6.5 3.0 %collective-permute-start.4 = (bf16[3,1280,3,80]{1,3,2,0:T(8,128)(2,1)}, bf16[3,1280,3,80]{1,3,2,0:T(8,128)(2,1)S(1)}, u32[]{:S(2)}, u32[]{:S(2)}) collective-permute-start(bf16[3,1280,3,80]{1,3,2,0:T(8,128)(2,1)} %bitcast.106), channel_id=1, source_target_pairs={{0,16},{8,24},{16,0},{24,8},{1,17},{9,25},{17,1},{25,9},{2,18},{10... | collective-permute-start | bytes 5529608 | tf_op jit(solution)/shard_map/ppermute | solution.py:28
  9.5 40.4 %collective-permute-done.4 = bf16[3,1280,3,80]{1,3,2,0:T(8,128)(2,1)S(1)} collective-permute-done((bf16[3,1280,3,80]{1,3,2,0:T(8,128)(2,1)}, bf16[3,1280,3,80]{1,3,2,0:T(8,128)(2,1)S(1)}, u32[]{:S(2)}, u32[]{:S(2)}) %collective-permute-start.4) | collective-permute-done | bytes 1843232 | tf_op jit(solution)/shard_map/ppermute | solution.py:28
  53.8 3.0 %select_select_fusion.3 = (bf16[3,1280,3,80]{1,3,2,0:T(8,128)(2,1)S(1)}, bf16[3,1280,3,80]{1,3,2,0:T(8,128)(2,1)S(1)}, bf16[3,1280,3,80]{1,3,2,0:T(8,128)(2,1)S(1)}, bf16[3,1280,3,80]{1,3,2,0:T(8,128)(2,1)S(1)}) fusion(bf16[3,1280,3,80]{1,3,2,0:T(8,128)(2,1)} %bitcast.108, bf16[3,1280,3,80]{1,3,2,0:T(8,128)(2,1)} %collective-permute-done.3, ...), kind=kLoop, calls=%fused_computation.21 | loop fusion | flops 11059200 | bytes 14745612 | tf_op jit(solution)/shard_map/jit(_where)/select_n | solution.py:37
  56.9 5.5 %pad_maximum_fusion = bf16[3,1280,3,320]{1,3,2,0:T(8,128)(2,1)S(1)} fusion(bf16[3,1280,3,80]{1,3,2,0:T(8,128)(2,1)S(1)} %get-tuple-element.14, bf16[3,1280,3,80]{1,3,2,0:T(8,128)(2,1)S(1)} %get-tuple-element.15, bf16[3,1280,3,80]{1,3,2,0:T(8,128)(2,1)S(1)} %get-tuple-element.16, bf16[3,1280,3,80]{1,3,2,0:T(8,128)(2,1)S(1)} %get-tuple-element.13), kind=kLoop, calls=%fused_computation.3 | loop fusion | flops 29491200 | bytes 14745600 | tf_op jit(solution)/shard_map/concatenate | solution.py:39
  62.4 3.2 %fusion.23 = (bf16[1,1280,3,320]{1,3,2,0:T(8,128)(2,1)}, bf16[1,1280,3,320]{1,3,2,0:T(8,128)(2,1)}, bf16[1,1280,3,320]{1,3,2,0:T(8,128)(2,1)}) fusion(bf16[3,1280,3,320]{1,3,2,0:T(8,128)(2,1)S(1)} %pad_maximum_fusion), kind=kLoop, calls=%fused_computation.62 | loop fusion | bytes 14745600 | tf_op jit(solution)/shard_map/slice | solution.py:150
  65.6 40.9 %all-gather.4.cloned.1.call-done = bf16[1,4,8,32,1280]{4,3,2,0,1:T(8,128)(2,1)} async-done(((bf16[1,1,8,32,1280]{4,3,2,0,1:T(8,128)(2,1)}), bf16[1,4,8,32,1280]{4,3,2,0,1:T(8,128)(2,1)}) %all-gather.4.cloned.1.call-update) | async-done | bytes 2621456 | tf_op jit(solution)/shard_map/all_gather | solution.py:107
  106.5 2.6 %convert_reduce_fusion = (f32[1280]{0:T(1024)S(1)}, f32[1280]{0:T(1024)S(1)}) fusion(bf16[1,4,8,32,1280]{4,3,2,0,1:T(8,128)(2,1)} %all-gather.4.cloned.1.call-done), kind=kLoop, calls=%fused_computation.2 | loop fusion | flops 5240320 | bytes 2631680 | tf_op jit(solution)/shard_map/reduce_sum | solution.py:121
  109.5 1.5 collective-permute-start.1
  111.1 3.2 %collective-permute-start = (bf16[1,4,1,32,1280]{4,3,2,1,0:T(8,128)(2,1)S(1)}, bf16[1,4,1,32,1280]{4,3,2,1,0:T(8,128)(2,1)}, u32[]{:S(2)}, u32[]{:S(2)}) collective-permute-start(bf16[1,4,1,32,1280]{4,3,2,1,0:T(8,128)(2,1)S(1)} %get-tuple-element.29), channel_id=1, source_target_pairs={{0,1},{2,3},{4,5},{6,7},{8,9},{10,11},{12,13},{14,15},{16,17},{18,... | collective-permute-start | bytes 983048 | tf_op jit(solution)/shard_map/ppermute | solution.py:113
  114.3 1.5 collective-permute-start.2
  116.2 1.8 fusion.9
  118.0 2.1 collective-permute-done
  120.1 4.9 %collective-permute-done.2 = bf16[1,4,1,32,1280]{4,3,2,1,0:T(8,128)(2,1)} collective-permute-done((bf16[1,4,1,32,1280]{4,3,2,1,0:T(8,128)(2,1)S(1)}, bf16[1,4,1,32,1280]{4,3,2,1,0:T(8,128)(2,1)}, u32[]{:S(2)}, u32[]{:S(2)}) %collective-permute-start.2) | collective-permute-done | bytes 327712 | tf_op jit(solution)/shard_map/ppermute | solution.py:114
  125.0 1.6 fusion.14
  128.3 2.9 %fusion.29 = f32[4,8,32,960]{3,2,1,0:T(8,128)S(1)} fusion(bf16[4,10,32,1280]{3,2,1,0:T(8,128)(2,1)S(1)} %maximum_bitcast_fusion, bf16[1280,960,1,1]{0,1,3,2:T(8,128)(2,1)S(1)} %bitcast.105), kind=kOutput, calls=%fused_computation.68 | convolution fusion | flops 2516582400 | bytes 9666560 | tf_op jit(solution)/shard_map/frxc,cn->frxn/dot_general | solution.py:147
  131.2 2.9 %fusion.28 = f32[4,8,32,960]{3,2,1,0:T(8,128)S(1)} fusion(bf16[4,10,32,1280]{3,2,1,0:T(8,128)(2,1)S(1)} %maximum_bitcast_fusion, bf16[1280,960,1,1]{0,1,3,2:T(8,128)(2,1)S(1)} %bitcast.104), kind=kOutput, calls=%fused_computation.67 | convolution fusion | flops 2516582400 | bytes 9666560 | tf_op jit(solution)/shard_map/frxc,cn->frxn/dot_general | solution.py:147
  134.1 2.9 %add_add_fusion.1 = f32[4,8,32,960]{3,2,1,0:T(8,128)S(1)} fusion(f32[4,8,32,960]{3,2,1,0:T(8,128)S(1)} %fusion.28, f32[4,8,32,960]{3,2,1,0:T(8,128)S(1)} %fusion.29, bf16[4,10,32,1280]{3,2,1,0:T(8,128)(2,1)S(1)} %maximum_bitcast_fusion, bf16[1280,960,1,1]{0,1,3,2:T(8,128)(2,1)S(1)} %bitcast.103), kind=kOutput, calls=%fused_computation.15 | convolution fusion | flops 2518548480 | bytes 17530880 | tf_op jit(solution)/shard_map/frxc,cn->frxn/dot_general | solution.py:147
  138.8 3.5 %collective-permute-done.6 = f32[2,8]{1,0:T(2,128)S(1)} collective-permute-done((f32[2,8]{1,0:T(2,128)S(1)}, f32[2,8]{1,0:T(2,128)S(1)}, u32[]{:S(2)}, u32[]{:S(2)}) %collective-permute-start.6) | collective-permute-done | bytes 96 | tf_op jit(solution)/shard_map/ppermute | solution.py:18
  144.1 1.5 collective-permute-start.8
  145.6 11.5 %collective-permute-done.8 = bf16[3,1280,80]{1,2,0:T(8,128)(2,1)} collective-permute-done((bf16[3,1280,80]{1,2,0:T(8,128)(2,1)S(1)}, bf16[3,1280,80]{1,2,0:T(8,128)(2,1)}, u32[]{:S(2)}, u32[]{:S(2)}) %collective-permute-start.8) | collective-permute-done | bytes 614432 | tf_op jit(solution)/shard_map/ppermute | solution.py:28
  157.8 1.5 copy.120
  159.3 1.5 copy.122
  160.9 2.2 copy.121
  163.1 1.7 select_select_fusion.7
  164.7 2.8 %pad_maximum_fusion.1 = bf16[3,1280,320]{2,1,0:T(8,128)(2,1)S(1)} fusion(bf16[3,1280,80]{2,1,0:T(8,128)(2,1)S(1)} %get-tuple-element.22, bf16[3,1280,80]{2,1,0:T(8,128)(2,1)S(1)} %get-tuple-element.23, bf16[3,1280,80]{2,1,0:T(8,128)(2,1)S(1)} %get-tuple-element.24, bf16[3,1280,80]{2,1,0:T(8,128)(2,1)S(1)} %get-tuple-element.21), kind=kLoop, calls=%fused_computation.17 | loop fusion | flops 9830400 | bytes 4915200 | tf_op jit(solution)/shard_map/concatenate | solution.py:39
  171.1 34.7 %all-gather.6.cloned.1.call-done = bf16[16,8,32,320]{3,2,1,0:T(8,128)(2,1)} async-done(((bf16[4,8,32,320]{3,2,1,0:T(8,128)(2,1)}), bf16[16,8,32,320]{3,2,1,0:T(8,128)(2,1)}) %all-gather.6.cloned.1.call-update) | async-done | bytes 2621456 | tf_op jit(solution)/shard_map/all_gather | solution.py:193
  205.7 2.6 %fusion.31 = f32[4,8,32,960]{3,2,1,0:T(8,128)S(1)} fusion(bf16[16,8,32,320]{3,2,1,0:T(8,128)(2,1)} %all-gather.6.cloned.1.call-done, bf16[320,960,1,1]{0,1,3,2:T(8,128)(2,1)S(1)} %bitcast.98), kind=kOutput, calls=%fused_computation.70 | convolution fusion | flops 629145600 | bytes 7168000 | tf_op jit(solution)/shard_map/frxc,cn->frxn/dot_general | solution.py:199
  214.6 2.7 %collective-permute-start.12 = (bf16[1,8,32,320]{3,2,1,0:T(8,128)(2,1)S(1)}, bf16[1,8,32,320]{3,2,1,0:T(8,128)(2,1)S(1)}, u32[]{:S(2)}, u32[]{:S(2)}) collective-permute-start(bf16[1,8,32,320]{3,2,1,0:T(8,128)(2,1)S(1)} %get-tuple-element.35), channel_id=1, source_target_pairs={{0,6},{2,0},{4,2},{6,4},{1,7},{3,1},{5,3},{7,5},{8,14},{10,8},{12,... | collective-permute-start | bytes 491528 | tf_op jit(solution)/shard_map/ppermute | solution.py:216
  217.3 5.7 %collective-permute-done.10 = bf16[1,8,32,320]{3,2,1,0:T(8,128)(2,1)S(1)} collective-permute-done((bf16[1,8,32,320]{3,2,1,0:T(8,128)(2,1)S(1)}, bf16[1,8,32,320]{3,2,1,0:T(8,128)(2,1)S(1)}, u32[]{:S(2)}, u32[]{:S(2)}) %collective-permute-start.10) | collective-permute-done | bytes 163872 | tf_op jit(solution)/shard_map/ppermute | solution.py:216
  222.9 7.2 %collective-permute-done.11 = bf16[1,8,32,320]{3,2,1,0:T(8,128)(2,1)S(1)} collective-permute-done((bf16[1,8,32,320]{3,2,1,0:T(8,128)(2,1)S(1)}, bf16[1,8,32,320]{3,2,1,0:T(8,128)(2,1)S(1)}, u32[]{:S(2)}, u32[]{:S(2)}) %collective-permute-start.11) | collective-permute-done | bytes 163872 | tf_op jit(solution)/shard_map/ppermute | solution.py:216
  232.9 2.2 reshape.355
  235.1 2.3 add_add_fusion.2
  (98 shorter events, 22.9 us)
Async XLA Ops:
  6.5 99.9 %all-gather.4.cloned.1.call-start = ((), (), s32[]{:S(2)}) async-start(), calls=%async_computation | async-start | bytes 3276800 | tf_op jit(solution)/shard_map/all_gather | solution.py:107
  6.5 43.4 %collective-permute-start.4 = (bf16[3,1280,3,80]{1,3,2,0:T(8,128)(2,1)}, bf16[3,1280,3,80]{1,3,2,0:T(8,128)(2,1)S(1)}, u32[]{:S(2)}, u32[]{:S(2)}) collective-permute-start(bf16[3,1280,3,80]{1,3,2,0:T(8,128)(2,1)} %bitcast.106), channel_id=1, source_target_pairs={{0,16},{8,24},{16,0},{24,8},{1,17},{9,25},{17,1},{25,9},{2,18},{10... | collective-permute-start | bytes 5529608 | tf_op jit(solution)/shard_map/ppermute | solution.py:28
  9.5 43.1 %collective-permute-start.3 = (bf16[3,1280,3,80]{1,3,2,0:T(8,128)(2,1)}, bf16[3,1280,3,80]{1,3,2,0:T(8,128)(2,1)}, u32[]{:S(2)}, u32[]{:S(2)}) collective-permute-start(bf16[3,1280,3,80]{1,3,2,0:T(8,128)(2,1)} %bitcast.107), channel_id=1, source_target_pairs={{0,8},{8,0},{16,24},{24,16},{1,9},{9,1},{17,25},{25,17},{2,10},{10... | collective-permute-start | bytes 5529608 | tf_op jit(solution)/shard_map/ppermute | solution.py:29
  49.9 3.9 %collective-permute-start.5 = (bf16[3,1280,3,80]{1,3,2,0:T(8,128)(2,1)S(1)}, bf16[3,1280,3,80]{1,3,2,0:T(8,128)(2,1)}, u32[]{:S(2)}, u32[]{:S(2)}) collective-permute-start(bf16[3,1280,3,80]{1,3,2,0:T(8,128)(2,1)S(1)} %collective-permute-done.4), channel_id=1, source_target_pairs={{0,8},{8,0},{16,24},{24,16},{1,9},{9,1},{17,25},{25,17},{2,10},{10... | collective-permute-start | bytes 5529608 | tf_op jit(solution)/shard_map/ppermute | solution.py:30
  49.9 155.8 %all-gather.6.cloned.1.call-start = ((), (), s32[]{:S(2)}) async-start(), calls=%async_computation.1 | async-start | bytes 3932160 | tf_op jit(solution)/shard_map/all_gather | solution.py:193
  65.6 50.6 %copy-start.8 = (f32[1280]{0:T(1024)S(1)}, f32[1280]{0:T(1024)}, u32[]{:S(2)}) copy-start(f32[1280]{0:T(1024)} %param.13) | copy-start | bytes 15364
  65.6 50.6 %copy-start.9 = (f32[1280]{0:T(1024)S(1)}, f32[1280]{0:T(1024)}, u32[]{:S(2)}) copy-start(f32[1280]{0:T(1024)} %param.12) | copy-start | bytes 15364
  106.5 4.6 %copy-start = (bf16[1,4,8,32,1280]{4,3,2,0,1:T(8,128)(2,1)S(1)}, bf16[1,4,8,32,1280]{4,3,2,0,1:T(8,128)(2,1)}, u32[]{:S(2)}) copy-start(bf16[1,4,8,32,1280]{4,3,2,0,1:T(8,128)(2,1)} %all-gather.4.cloned.1.call-done) | copy-start | bytes 7864324
  109.5 6.3 %collective-permute-start.1 = (f32[2,32]{1,0:T(2,128)S(1)}, f32[2,32]{1,0:T(2,128)S(1)}, u32[]{:S(2)}, u32[]{:S(2)}) collective-permute-start(f32[2,32]{1,0:T(2,128)S(1)} %pad_maximum_fusion.2), channel_id=1, source_target_pairs={{0,1},{1,0},{2,3},{3,2},{4,5},{5,4},{6,7},{7,6},{8,9},{9,8},{10,11... | collective-permute-start | bytes 776 | tf_op jit(solution)/shard_map/ppermute | solution.py:18
  111.1 9.0 %collective-permute-start = (bf16[1,4,1,32,1280]{4,3,2,1,0:T(8,128)(2,1)S(1)}, bf16[1,4,1,32,1280]{4,3,2,1,0:T(8,128)(2,1)}, u32[]{:S(2)}, u32[]{:S(2)}) collective-permute-start(bf16[1,4,1,32,1280]{4,3,2,1,0:T(8,128)(2,1)S(1)} %get-tuple-element.29), channel_id=1, source_target_pairs={{0,1},{2,3},{4,5},{6,7},{8,9},{10,11},{12,13},{14,15},{16,17},{18,... | collective-permute-start | bytes 983048 | tf_op jit(solution)/shard_map/ppermute | solution.py:113
  114.3 10.7 %collective-permute-start.2 = (bf16[1,4,1,32,1280]{4,3,2,1,0:T(8,128)(2,1)S(1)}, bf16[1,4,1,32,1280]{4,3,2,1,0:T(8,128)(2,1)}, u32[]{:S(2)}, u32[]{:S(2)}) collective-permute-start(bf16[1,4,1,32,1280]{4,3,2,1,0:T(8,128)(2,1)S(1)} %get-tuple-element.30), channel_id=1, source_target_pairs={{1,0},{3,2},{5,4},{7,6},{9,8},{11,10},{13,12},{15,14},{17,16},{19,... | collective-permute-start | bytes 983048 | tf_op jit(solution)/shard_map/ppermute | solution.py:114
  126.6 1.7 copy-start.6
  128.3 2.9 %copy-start.5 = (bf16[1,1280,3,320]{1,3,2,0:T(8,128)(2,1)S(1)}, bf16[1,1280,3,320]{1,3,2,0:T(8,128)(2,1)}, u32[]{:S(2)}) copy-start(bf16[1,1280,3,320]{1,3,2,0:T(8,128)(2,1)} %get-tuple-element.12) | copy-start | bytes 7372804
  131.2 2.9 %copy-start.4 = (bf16[1,1280,3,320]{1,3,2,0:T(8,128)(2,1)S(1)}, bf16[1,1280,3,320]{1,3,2,0:T(8,128)(2,1)}, u32[]{:S(2)}) copy-start(bf16[1,1280,3,320]{1,3,2,0:T(8,128)(2,1)} %get-tuple-element.10) | copy-start | bytes 7372804
  138.2 5.8 %copy-start.7 = (bf16[3,1280,80]{1,2,0:T(8,128)(2,1)S(1)}, bf16[3,1280,80]{1,2,0:T(8,128)(2,1)}, u32[]{:S(2)}) copy-start(bf16[3,1280,80]{1,2,0:T(8,128)(2,1)} %param.11) | copy-start | bytes 1843204
  138.6 3.6 %collective-permute-start.6 = (f32[2,8]{1,0:T(2,128)S(1)}, f32[2,8]{1,0:T(2,128)S(1)}, u32[]{:S(2)}, u32[]{:S(2)}) collective-permute-start(f32[2,8]{1,0:T(2,128)S(1)} %pad_maximum_fusion.3), channel_id=1, source_target_pairs={{0,1},{1,0},{2,3},{3,2},{4,5},{5,4},{6,7},{7,6},{8,9},{9,8},{10,11... | collective-permute-start | bytes 200 | tf_op jit(solution)/shard_map/ppermute | solution.py:18
  144.1 13.0 %collective-permute-start.8 = (bf16[3,1280,80]{1,2,0:T(8,128)(2,1)S(1)}, bf16[3,1280,80]{1,2,0:T(8,128)(2,1)}, u32[]{:S(2)}, u32[]{:S(2)}) collective-permute-start(bf16[3,1280,80]{1,2,0:T(8,128)(2,1)S(1)} %copy-done.7), channel_id=1, source_target_pairs={{0,16},{8,24},{16,0},{24,8},{1,17},{9,25},{17,1},{25,9},{2,18},{10... | collective-permute-start | bytes 1843208 | tf_op jit(solution)/shard_map/ppermute | solution.py:28
  145.6 13.7 %collective-permute-start.7 = (bf16[3,1280,80]{1,2,0:T(8,128)(2,1)S(1)}, bf16[3,1280,80]{1,2,0:T(8,128)(2,1)}, u32[]{:S(2)}, u32[]{:S(2)}) collective-permute-start(bf16[3,1280,80]{1,2,0:T(8,128)(2,1)S(1)} %copy-done.7), channel_id=1, source_target_pairs={{0,8},{8,0},{16,24},{24,16},{1,9},{9,1},{17,25},{25,17},{2,10},{10... | collective-permute-start | bytes 1843208 | tf_op jit(solution)/shard_map/ppermute | solution.py:29
  157.1 3.8 %collective-permute-start.9 = (bf16[3,1280,80]{1,2,0:T(8,128)(2,1)}, bf16[3,1280,80]{1,2,0:T(8,128)(2,1)}, u32[]{:S(2)}, u32[]{:S(2)}) collective-permute-start(bf16[3,1280,80]{1,2,0:T(8,128)(2,1)} %collective-permute-done.8), channel_id=1, source_target_pairs={{0,8},{8,0},{16,24},{24,16},{1,9},{9,1},{17,25},{25,17},{2,10},{10... | collective-permute-start | bytes 1843208 | tf_op jit(solution)/shard_map/ppermute | solution.py:30
  169.1 36.6 %copy-start.2 = (bf16[3,320,320]{1,2,0:T(8,128)(2,1)S(1)}, bf16[3,320,320]{1,2,0:T(8,128)(2,1)}, u32[]{:S(2)}) copy-start(bf16[3,320,320]{1,2,0:T(8,128)(2,1)} %copy.138) | copy-start | bytes 1843204
  205.7 2.6 %copy-start.1 = (bf16[16,8,32,320]{3,2,1,0:T(8,128)(2,1)S(1)}, bf16[16,8,32,320]{3,2,1,0:T(8,128)(2,1)}, u32[]{:S(2)}) copy-start(bf16[16,8,32,320]{3,2,1,0:T(8,128)(2,1)} %all-gather.6.cloned.1.call-done) | copy-start | bytes 7864324
  205.7 2.6 %copy-start.3 = (bf16[3,320,320]{1,2,0:T(8,128)(2,1)S(1)}, bf16[3,320,320]{1,2,0:T(8,128)(2,1)}, u32[]{:S(2)}) copy-start(bf16[3,320,320]{1,2,0:T(8,128)(2,1)} %copy.136) | copy-start | bytes 1843204
  213.2 9.7 %collective-permute-start.10 = (bf16[1,8,32,320]{3,2,1,0:T(8,128)(2,1)S(1)}, bf16[1,8,32,320]{3,2,1,0:T(8,128)(2,1)S(1)}, u32[]{:S(2)}, u32[]{:S(2)}) collective-permute-start(bf16[1,8,32,320]{3,2,1,0:T(8,128)(2,1)S(1)} %get-tuple-element.37), channel_id=1, source_target_pairs={{0,2},{2,4},{4,6},{6,0},{1,3},{3,5},{5,7},{7,1},{8,10},{10,12},{12... | collective-permute-start | bytes 491528 | tf_op jit(solution)/shard_map/ppermute | solution.py:216
  213.3 16.8 %collective-permute-start.11 = (bf16[1,8,32,320]{3,2,1,0:T(8,128)(2,1)S(1)}, bf16[1,8,32,320]{3,2,1,0:T(8,128)(2,1)S(1)}, u32[]{:S(2)}, u32[]{:S(2)}) collective-permute-start(bf16[1,8,32,320]{3,2,1,0:T(8,128)(2,1)S(1)} %get-tuple-element.36), channel_id=1, source_target_pairs={{0,4},{2,6},{4,0},{6,2},{1,5},{3,7},{5,1},{7,3},{8,12},{10,14},{12... | collective-permute-start | bytes 491528 | tf_op jit(solution)/shard_map/ppermute | solution.py:216
  214.6 15.5 %collective-permute-start.12 = (bf16[1,8,32,320]{3,2,1,0:T(8,128)(2,1)S(1)}, bf16[1,8,32,320]{3,2,1,0:T(8,128)(2,1)S(1)}, u32[]{:S(2)}, u32[]{:S(2)}) collective-permute-start(bf16[1,8,32,320]{3,2,1,0:T(8,128)(2,1)S(1)} %get-tuple-element.35), channel_id=1, source_target_pairs={{0,6},{2,0},{4,2},{6,4},{1,7},{3,1},{5,3},{7,5},{8,14},{10,8},{12,... | collective-permute-start | bytes 491528 | tf_op jit(solution)/shard_map/ppermute | solution.py:216
  231.5 3.6 %copy-start.10 = (f32[1280]{0:T(1024)S(1)}, f32[1280]{0:T(1024)}, u32[]{:S(2)}) copy-start(f32[1280]{0:T(1024)} %param.17) | copy-start | bytes 15364
Sparse Core Ops, SparseCore 0:
  50.0 56.3 all-gather.3
  144.2 61.5 all-gather.5

commit v7 on v6

--- a/solution.py
+++ b/solution.py
@@ -190,16 +190,24 @@
 
     if frame_size > 8:
         return temporal_wide(activations, second, temporal_w, temporal_bias)
-    second_all = lax.all_gather(second[0], "frame", axis=0, tiled=False)
     taps = temporal_w.reshape(3, rep_size, frame_size, shard_width, local)
-    total = None
-    for group in range(frame_size):
-        weights = taps[:, :, group].reshape(3, rep_size * shard_width, local)
-        weights = weights.transpose(1, 0, 2).reshape(rep_size * shard_width, 3 * local)
-        term = jnp.einsum(
-            "frxc,cn->frxn", second_all[group], weights, preferred_element_type=jnp.float32
-        )
-        total = term if total is None else total + term
+    wide_t = taps.transpose(2, 1, 3, 0, 4).reshape(frame_size, rep_size * shard_width, 3 * local)
+    block = second[0]
+
+    def product(source, group):
+        weights = lax.dynamic_index_in_dim(wide_t, group, axis=0, keepdims=False)
+        return jnp.einsum("frxc,cn->frxn", source, weights, preferred_element_type=jnp.float32)
+
+    total = product(block, frame_index)
+    for distance in range(1, frame_size):
+        for sign in (1, -1):
+            offset = sign * distance
+            pairs = [
+                (k + offset, k) for k in range(frame_size) if 0 <= k + offset < frame_size
+            ]
+            received = lax.ppermute(block, "frame", pairs)
+            group = jnp.clip(frame_index + offset, 0, frame_size - 1)
+            total = total + product(received, group)
     temporal = total[..., local : 2 * local]
     if frames > 1:
         before = jnp.pad(total[:-1, ..., :local], ((1, 0), (0, 0), (0, 0), (0, 0)))

time: 246 us -> 287 us (1.17)
  starting transfers between devices: 14.8 us -> 47.9 us
  waiting for transfers between devices: 152 us -> 133 us
  local copies, waits for them, and re-layouts: 22.8 us -> 34.1 us
  matrix products: 15.2 us -> 26.3 us
  other arithmetic: 25.3 us -> 31.1 us
    ppermute x0 -> x6, waiting for transfers between devices: none -> 37.2 us  [shards(): received = lax.ppermute(block, 'frame', pairs)]
    all_gather x1 -> x0, waiting for transfers between devices: 34.7 us -> none  [shards(): second_all = lax.all_gather(second[0], 'frame', axis=0, tiled=False)]
    all_gather x1, waiting for transfers between devices: 40.9 us -> 18.3 us  [shards(): raw = lax.all_gather(activations, 'frame', axis=1, tiled=True)]
    ppermute x0 -> x6, starting transfers between devices: none -> 18.9 us  [shards(): received = lax.ppermute(block, 'frame', pairs)]
    ppermute x3, starting transfers between devices: 4.03 us -> 17.7 us  [shards(): lax.ppermute(piece, 'frame', [(k, (k + shift) % frame_size) for k in rang...]
    dot_general x4 -> x7, matrix products: 6.53 us -> 17.6 us  [product(): jnp.einsum('frxc,cn->frxn', source, weights, preferred_element_type=jnp.f...]
    reshape x0 -> x1, local copies, waits for them, and re-layouts: none -> 6.85 us  [shards(): taps.transpose(2, 1, 3, 0, 4)]
    transpose x0 -> x1, local copies, waits for them, and re-layouts: none -> 4.38 us  [shards(): taps.transpose(2, 1, 3, 0, 4)]
  transfers between devices with their start and end apart: 15 -> 20, of which waited for: 10 -> 9; matrix products, arithmetic and copies ran while one was open for 12% -> 19% of each run, Pallas kernels for 0% -> 0%
where the time goes in v7:
time: 287 us; the launch traced here: 286 us
  waiting for transfers between devices  133 us (46%)
  starting transfers between devices  47.9 us (17%)
  local copies, waits for them, and re-layouts  34.1 us (12%)
  other arithmetic  31.1 us (11%)
  matrix products  26.3 us (9%)
  between operations  13.9 us (5%)
    ppermute x2, waiting for transfers between devices, gather_rep(): across = lax.ppermute(w, 'rep', [(k, k ^ 2) for k in range(size)])  54.9 us
    ppermute x6, waiting for transfers between devices, shards(): received = lax.ppermute(block, 'frame', pairs)  37.2 us
    ppermute x6, starting transfers between devices, shards(): received = lax.ppermute(block, 'frame', pairs)  18.9 us
    all_gather x1, waiting for transfers between devices, shards(): raw = lax.all_gather(activations, 'frame', axis=1, tiled=True)  18.3 us
    ppermute x3, starting transfers between devices, shards(): lax.ppermute(piece, 'frame', [(k, (k + shift) % frame_size) for k in rang...  17.7 us
    dot_general x7, matrix products, product(): jnp.einsum('frxc,cn->frxn', source, weights, preferred_element_type=jnp.f...  17.6 us
    ppermute x3, waiting for transfers between devices, shards(): lax.ppermute(piece, 'frame', [(k, (k + shift) % frame_size) for k in rang...  15.7 us
    concatenate x2, other arithmetic, gather_rep(): return jnp.concatenate(blocks, axis=-1)  9.45 us
  transfers between devices with their start and end apart: 20, of which 9 were waited for; matrix products, arithmetic and copies ran while one was open for 19% of the time, Pallas kernels for 0%

profile of v7, /device:TPU:0, one launch (start us, length us, event | category | flops | bytes accessed | tf_op | source)
XLA Modules:
  0.0 286.4 jit_solution(730104086492099424)
XLA Ops:
  6.5 3.0 %collective-permute-start.4 = (bf16[3,1280,3,80]{1,3,2,0:T(8,128)(2,1)}, bf16[3,1280,3,80]{1,3,2,0:T(8,128)(2,1)}, u32[]{:S(2)}, u32[]{:S(2)}) collective-permute-start(bf16[3,1280,3,80]{1,3,2,0:T(8,128)(2,1)} %bitcast.126), channel_id=1, source_target_pairs={{0,16},{8,24},{16,0},{24,8},{1,17},{9,25},{17,1},{25,9},{2,18},{10... | collective-permute-start | bytes 5529608 | tf_op jit(solution)/shard_map/ppermute | solution.py:28
  9.5 40.5 %collective-permute-done.4 = bf16[3,1280,3,80]{1,3,2,0:T(8,128)(2,1)} collective-permute-done((bf16[3,1280,3,80]{1,3,2,0:T(8,128)(2,1)}, bf16[3,1280,3,80]{1,3,2,0:T(8,128)(2,1)}, u32[]{:S(2)}, u32[]{:S(2)}) %collective-permute-start.4) | collective-permute-done | bytes 1843232 | tf_op jit(solution)/shard_map/ppermute | solution.py:28
  52.1 14.4 %collective-permute-done.8 = bf16[3,1280,80]{1,2,0:T(8,128)(2,1)S(1)} collective-permute-done((bf16[3,1280,80]{1,2,0:T(8,128)(2,1)}, bf16[3,1280,80]{1,2,0:T(8,128)(2,1)S(1)}, u32[]{:S(2)}, u32[]{:S(2)}) %collective-permute-start.8) | collective-permute-done | bytes 614432 | tf_op jit(solution)/shard_map/ppermute | solution.py:28
  74.6 2.2 copy.90
  76.8 3.1 %select_select_fusion.3 = (bf16[3,1280,3,80]{1,3,2,0:T(8,128)(2,1)S(1)}, bf16[3,1280,3,80]{1,3,2,0:T(8,128)(2,1)S(1)}, bf16[3,1280,3,80]{1,3,2,0:T(8,128)(2,1)S(1)}, bf16[3,1280,3,80]{1,3,2,0:T(8,128)(2,1)S(1)}) fusion(bf16[3,1280,3,80]{1,3,2,0:T(8,128)(2,1)S(1)} %bitcast.128, bf16[3,1280,3,80]{1,3,2,0:T(8,128)(2,1)} %collective-permute-done.3, ...), kind=kLoop, calls=%fused_computation.21 | loop fusion | flops 11059200 | bytes 14745612 | tf_op jit(solution)/shard_map/jit(_where)/select_n | solution.py:37
  79.9 5.5 %pad_maximum_fusion = bf16[3,1280,3,320]{1,3,2,0:T(8,128)(2,1)S(1)} fusion(bf16[3,1280,3,80]{1,3,2,0:T(8,128)(2,1)S(1)} %get-tuple-element.14, bf16[3,1280,3,80]{1,3,2,0:T(8,128)(2,1)S(1)} %get-tuple-element.15, bf16[3,1280,3,80]{1,3,2,0:T(8,128)(2,1)S(1)} %get-tuple-element.16, bf16[3,1280,3,80]{1,3,2,0:T(8,128)(2,1)S(1)} %get-tuple-element.13), kind=kLoop, calls=%fused_computation.3 | loop fusion | flops 29491200 | bytes 14745600 | tf_op jit(solution)/shard_map/concatenate | solution.py:39
  85.4 3.3 %fusion.56 = (bf16[1,1280,3,320]{1,3,2,0:T(8,128)(2,1)}, bf16[1,1280,3,320]{1,3,2,0:T(8,128)(2,1)}, bf16[1,1280,3,320]{1,3,2,0:T(8,128)(2,1)}) fusion(bf16[3,1280,3,320]{1,3,2,0:T(8,128)(2,1)S(1)} %pad_maximum_fusion), kind=kLoop, calls=%fused_computation.93 | loop fusion | bytes 14745600 | tf_op jit(solution)/shard_map/slice | solution.py:150
  88.7 18.3 %all-gather.2.cloned.1.call-done = bf16[1,4,8,32,1280]{4,3,2,0,1:T(8,128)(2,1)} async-done(((bf16[1,1,8,32,1280]{4,3,2,0,1:T(8,128)(2,1)}), bf16[1,4,8,32,1280]{4,3,2,0,1:T(8,128)(2,1)}) %all-gather.2.cloned.1.call-update) | async-done | bytes 2621456 | tf_op jit(solution)/shard_map/all_gather | solution.py:107
  107.0 2.6 convert_reduce_fusion
  111.6 3.2 %collective-permute-start = (bf16[1,4,1,32,1280]{4,3,2,1,0:T(8,128)(2,1)S(1)}, bf16[1,4,1,32,1280]{4,3,2,1,0:T(8,128)(2,1)}, u32[]{:S(2)}, u32[]{:S(2)}) collective-permute-start(bf16[1,4,1,32,1280]{4,3,2,1,0:T(8,128)(2,1)S(1)} %get-tuple-element.25), channel_id=1, source_target_pairs={{0,1},{2,3},{4,5},{6,7},{8,9},{10,11},{12,13},{14,15},{16,17},{18,... | collective-permute-start | bytes 983048 | tf_op jit(solution)/shard_map/ppermute | solution.py:113
  120.6 4.9 %collective-permute-done.2 = bf16[1,4,1,32,1280]{4,3,2,1,0:T(8,128)(2,1)} collective-permute-done((bf16[1,4,1,32,1280]{4,3,2,1,0:T(8,128)(2,1)S(1)}, bf16[1,4,1,32,1280]{4,3,2,1,0:T(8,128)(2,1)}, u32[]{:S(2)}, u32[]{:S(2)}) %collective-permute-start.2) | collective-permute-done | bytes 327712 | tf_op jit(solution)/shard_map/ppermute | solution.py:114
  128.8 2.9 %fusion.61 = f32[4,8,32,960]{3,2,1,0:T(8,128)S(1)} fusion(bf16[4,10,32,1280]{3,2,1,0:T(8,128)(2,1)S(1)} %maximum_bitcast_fusion, bf16[1280,960,1,1]{0,1,3,2:T(8,128)(2,1)S(1)} %bitcast.125), kind=kOutput, calls=%fused_computation.98 | convolution fusion | flops 2516582400 | bytes 9666560 | tf_op jit(solution)/shard_map/frxc,cn->frxn/dot_general | solution.py:147
  131.7 2.9 %fusion.60 = f32[4,8,32,960]{3,2,1,0:T(8,128)S(1)} fusion(bf16[4,10,32,1280]{3,2,1,0:T(8,128)(2,1)S(1)} %maximum_bitcast_fusion, bf16[1280,960,1,1]{0,1,3,2:T(8,128)(2,1)S(1)} %bitcast.124), kind=kOutput, calls=%fused_computation.97 | convolution fusion | flops 2516582400 | bytes 9666560 | tf_op jit(solution)/shard_map/frxc,cn->frxn/dot_general | solution.py:147
  134.7 2.9 %add_add_fusion.1 = f32[4,8,32,960]{3,2,1,0:T(8,128)S(1)} fusion(f32[4,8,32,960]{3,2,1,0:T(8,128)S(1)} %fusion.60, f32[4,8,32,960]{3,2,1,0:T(8,128)S(1)} %fusion.61, bf16[4,10,32,1280]{3,2,1,0:T(8,128)(2,1)S(1)} %maximum_bitcast_fusion, bf16[1280,960,1,1]{0,1,3,2:T(8,128)(2,1)S(1)} %bitcast.123), kind=kOutput, calls=%fused_computation.15 | convolution fusion | flops 2518548480 | bytes 17530880 | tf_op jit(solution)/shard_map/frxc,cn->frxn/dot_general | solution.py:147
  139.5 3.6 %select_select_fusion.7 = (bf16[3,1280,80]{2,1,0:T(8,128)(2,1)}, bf16[3,1280,80]{2,1,0:T(8,128)(2,1)}, bf16[3,1280,80]{2,1,0:T(8,128)(2,1)}, bf16[3,1280,80]{2,1,0:T(8,128)(2,1)}) fusion(bf16[3,1280,80]{2,1,0:T(8,128)(2,1)S(1)} %copy-done.1, bf16[3,1280,80]{2,1,0:T(8,128)(2,1)} %copy.91, bf16[3,1280,80]{2,1,0:T(8,128)(2,1)S(1)} %copy-done.2, ...), kind=kLoop, calls=%fused_computation.35 | loop fusion | flops 3686400 | bytes 4915212 | tf_op jit(solution)/shard_map/jit(_where)/select_n | solution.py:37
  143.5 2.3 multiply_convert_fusion
  147.3 4.0 %pad_maximum_fusion.1 = bf16[3,1280,320]{2,1,0:T(8,128)(2,1)S(1)} fusion(bf16[3,1280,80]{2,1,0:T(8,128)(2,1)S(1)} %copy-done.4, bf16[3,1280,80]{2,1,0:T(8,128)(2,1)} %get-tuple-element.23, bf16[3,1280,80]{2,1,0:T(8,128)(2,1)} %get-tuple-element.24, bf16[3,1280,80]{2,1,0:T(8,128)(2,1)S(1)} %copy-done.3), kind=kLoop, calls=%fused_computation.17 | loop fusion | flops 9830400 | bytes 4915200 | tf_op jit(solution)/shard_map/concatenate | solution.py:39
  151.2 4.4 %copy.105 = bf16[4,4,80,3,320]{4,3,2,1,0:T(4,128)(2,1)} copy(bf16[4,4,80,3,320]{4,2,0,1,3:T(8,128)(2,1)S(1)} %bitcast.121) | data formatting | bytes 4915200 | tf_op jit(solution)/shard_map/transpose | solution.py:194
  155.6 6.8 %reshape.343 = bf16[4,320,960]{2,1,0:T(8,128)(2,1)S(1)} reshape(bf16[4,4,80,3,320]{4,3,2,1,0:T(4,128)(2,1)} %copy.105) | data formatting | bytes 4915200 | tf_op jit(solution)/shard_map/reshape | solution.py:194
  162.5 5.9 %collective-permute-start.15 = (bf16[4,8,32,320]{3,2,1,0:T(8,128)(2,1)}, bf16[4,8,32,320]{3,2,1,0:T(8,128)(2,1)S(1)}, u32[]{:S(2)}, u32[]{:S(2)}) collective-permute-start(bf16[4,8,32,320]{3,2,1,0:T(8,128)(2,1)} %multiply_convert_fusion), channel_id=1, source_target_pairs={{0,6},{1,7},{8,14},{9,15},{16,22},{17,23},{24,30},{25,31}} | collective-permute-start | bytes 1966088 | tf_op jit(solution)/shard_map/ppermute | solution.py:208
  171.0 7.6 %collective-permute-start.11 = (bf16[4,8,32,320]{3,2,1,0:T(8,128)(2,1)}, bf16[4,8,32,320]{3,2,1,0:T(8,128)(2,1)S(1)}, u32[]{:S(2)}, u32[]{:S(2)}) collective-permute-start(bf16[4,8,32,320]{3,2,1,0:T(8,128)(2,1)} %multiply_convert_fusion), channel_id=1, source_target_pairs={{0,2},{2,4},{4,6},{1,3},{3,5},{5,7},{8,10},{10,12},{12,14},{9,11},... | collective-permute-start | bytes 1966088 | tf_op jit(solution)/shard_map/ppermute | solution.py:208
  178.6 2.4 fusion.28
  182.3 2.4 fusion.26
  184.7 32.6 %collective-permute-done.11 = bf16[4,8,32,320]{3,2,1,0:T(8,128)(2,1)S(1)} collective-permute-done((bf16[4,8,32,320]{3,2,1,0:T(8,128)(2,1)}, bf16[4,8,32,320]{3,2,1,0:T(8,128)(2,1)S(1)}, u32[]{:S(2)}, u32[]{:S(2)}) %collective-permute-start.11) | collective-permute-done | bytes 655392 | tf_op jit(solution)/shard_map/ppermute | solution.py:208
  218.6 4.5 %collective-permute-done.12 = bf16[4,8,32,320]{3,2,1,0:T(8,128)(2,1)S(1)} collective-permute-done((bf16[4,8,32,320]{3,2,1,0:T(8,128)(2,1)}, bf16[4,8,32,320]{3,2,1,0:T(8,128)(2,1)S(1)}, u32[]{:S(2)}, u32[]{:S(2)}) %collective-permute-start.12) | collective-permute-done | bytes 655392 | tf_op jit(solution)/shard_map/ppermute | solution.py:208
  225.6 3.2 %fusion.18 = f32[4,8,32,960]{3,2,1,0:T(8,128)} fusion(bf16[4,8,32,320]{3,2,1,0:T(8,128)(2,1)S(1)} %collective-permute-done.14, bf16[4,320,960]{2,1,0:T(8,128)(2,1)S(1)} %reshape.343, s32[]{:T(128)S(6)} %min.23), kind=kOutput, calls=%fused_computation.38 | convolution fusion | flops 629145600 | bytes 5373956 | tf_op jit(solution)/shard_map/frxc,cn->frxn/dot_general | solution.py:199
  228.8 5.9 %add_add_fusion = f32[4,8,32,960]{3,2,1,0:T(8,128)} fusion(f32[4,8,32,960]{3,2,1,0:T(8,128)} %fusion.18, f32[4,8,32,960]{3,2,1,0:T(8,128)S(1)} %fusion.20, f32[4,8,32,960]{3,2,1,0:T(8,128)S(1)} %fusion.22, f32[4,8,32,960]{3,2,1,0:T(8,128)S(1)} %fusion.24, f32[4,8,32,960]{3,2,1,0:T(8,128)S(1)} %fusion.28, f32[4,8,32,960]{3,2,1,0:T(8,128)S(1)} %fusion.26, ...), kind=kOutput, calls=%fused_computation.14 | convolution fusion | flops 635043840 | bytes 30277636 | tf_op jit(solution)/shard_map/frxc,cn->frxn/dot_general | solution.py:199
  236.6 2.2 fusion.11
  238.9 15.7 %collective-permute-start.17 = (bf16[1,8,32,320]{3,2,1,0:T(8,128)(2,1)S(1)}, bf16[1,8,32,320]{3,2,1,0:T(8,128)(2,1)S(1)}, u32[]{:S(2)}, u32[]{:S(2)}) collective-permute-start(bf16[1,8,32,320]{3,2,1,0:T(8,128)(2,1)S(1)} %get-tuple-element.32), channel_id=1, source_target_pairs={{0,4},{2,6},{4,0},{6,2},{1,5},{3,7},{5,1},{7,3},{8,12},{10,14},{12... | collective-permute-start | bytes 491528 | tf_op jit(solution)/shard_map/ppermute | solution.py:224
  257.8 14.5 %collective-permute-done.17 = bf16[1,8,32,320]{3,2,1,0:T(8,128)(2,1)S(1)} collective-permute-done((bf16[1,8,32,320]{3,2,1,0:T(8,128)(2,1)S(1)}, bf16[1,8,32,320]{3,2,1,0:T(8,128)(2,1)S(1)}, u32[]{:S(2)}, u32[]{:S(2)}) %collective-permute-start.17) | collective-permute-done | bytes 163872 | tf_op jit(solution)/shard_map/ppermute | solution.py:224
  275.0 2.2 reshape.344
  277.3 2.3 add_add_fusion.2
  (109 shorter events, 40.4 us)
Async XLA Ops:
  6.5 100.5 %all-gather.2.cloned.1.call-start = ((), (), s32[]{:S(2)}) async-start(), calls=%async_computation | async-start | bytes 3276800 | tf_op jit(solution)/shard_map/all_gather | solution.py:107
  6.5 43.5 %collective-permute-start.4 = (bf16[3,1280,3,80]{1,3,2,0:T(8,128)(2,1)}, bf16[3,1280,3,80]{1,3,2,0:T(8,128)(2,1)}, u32[]{:S(2)}, u32[]{:S(2)}) collective-permute-start(bf16[3,1280,3,80]{1,3,2,0:T(8,128)(2,1)} %bitcast.126), channel_id=1, source_target_pairs={{0,16},{8,24},{16,0},{24,8},{1,17},{9,25},{17,1},{25,9},{2,18},{10... | collective-permute-start | bytes 5529608 | tf_op jit(solution)/shard_map/ppermute | solution.py:28
  9.5 67.3 %collective-permute-start.3 = (bf16[3,1280,3,80]{1,3,2,0:T(8,128)(2,1)}, bf16[3,1280,3,80]{1,3,2,0:T(8,128)(2,1)}, u32[]{:S(2)}, u32[]{:S(2)}) collective-permute-start(bf16[3,1280,3,80]{1,3,2,0:T(8,128)(2,1)} %bitcast.127), channel_id=1, source_target_pairs={{0,8},{8,0},{16,24},{24,16},{1,9},{9,1},{17,25},{25,17},{2,10},{10... | collective-permute-start | bytes 5529608 | tf_op jit(solution)/shard_map/ppermute | solution.py:29
  50.0 26.8 %collective-permute-start.5 = (bf16[3,1280,3,80]{1,3,2,0:T(8,128)(2,1)}, bf16[3,1280,3,80]{1,3,2,0:T(8,128)(2,1)}, u32[]{:S(2)}, u32[]{:S(2)}) collective-permute-start(bf16[3,1280,3,80]{1,3,2,0:T(8,128)(2,1)} %collective-permute-done.4), channel_id=1, source_target_pairs={{0,8},{8,0},{16,24},{24,16},{1,9},{9,1},{17,25},{25,17},{2,10},{10... | collective-permute-start | bytes 5529608 | tf_op jit(solution)/shard_map/ppermute | solution.py:30
  50.0 16.5 %collective-permute-start.8 = (bf16[3,1280,80]{1,2,0:T(8,128)(2,1)}, bf16[3,1280,80]{1,2,0:T(8,128)(2,1)S(1)}, u32[]{:S(2)}, u32[]{:S(2)}) collective-permute-start(bf16[3,1280,80]{1,2,0:T(8,128)(2,1)} %param.11), channel_id=1, source_target_pairs={{0,16},{8,24},{16,0},{24,8},{1,17},{9,25},{17,1},{25,9},{2,18},{10... | collective-permute-start | bytes 1843208 | tf_op jit(solution)/shard_map/ppermute | solution.py:28
  51.8 21.6 %collective-permute-start.7 = (bf16[3,1280,80]{1,2,0:T(8,128)(2,1)}, bf16[3,1280,80]{1,2,0:T(8,128)(2,1)S(1)}, u32[]{:S(2)}, u32[]{:S(2)}) collective-permute-start(bf16[3,1280,80]{1,2,0:T(8,128)(2,1)} %param.11), channel_id=1, source_target_pairs={{0,8},{8,0},{16,24},{24,16},{1,9},{9,1},{17,25},{25,17},{2,10},{10... | collective-permute-start | bytes 1843208 | tf_op jit(solution)/shard_map/ppermute | solution.py:29
  66.5 8.1 %collective-permute-start.9 = (bf16[3,1280,80]{1,2,0:T(8,128)(2,1)S(1)}, bf16[3,1280,80]{1,2,0:T(8,128)(2,1)}, u32[]{:S(2)}, u32[]{:S(2)}) collective-permute-start(bf16[3,1280,80]{1,2,0:T(8,128)(2,1)S(1)} %collective-permute-done.8), channel_id=1, source_target_pairs={{0,8},{8,0},{16,24},{24,16},{1,9},{9,1},{17,25},{25,17},{2,10},{10... | collective-permute-start | bytes 1843208 | tf_op jit(solution)/shard_map/ppermute | solution.py:30
  68.7 8.2 %copy-start.8 = (bf16[9,1280,80]{1,2,0:T(8,128)(2,1)S(1)}, bf16[9,1280,80]{1,2,0:T(8,128)(2,1)}, u32[]{:S(2)}) copy-start(bf16[9,1280,80]{1,2,0:T(8,128)(2,1)} %param.10) | copy-start | bytes 5529604
  88.7 28.0 %copy-start.9 = (f32[1280]{0:T(1024)S(1)}, f32[1280]{0:T(1024)}, u32[]{:S(2)}) copy-start(f32[1280]{0:T(1024)} %param.13) | copy-start | bytes 15364
  88.7 28.0 %copy-start.10 = (f32[1280]{0:T(1024)S(1)}, f32[1280]{0:T(1024)}, u32[]{:S(2)}) copy-start(f32[1280]{0:T(1024)} %param.12) | copy-start | bytes 15364
  107.0 4.6 %copy-start = (bf16[1,4,8,32,1280]{4,3,2,0,1:T(8,128)(2,1)S(1)}, bf16[1,4,8,32,1280]{4,3,2,0,1:T(8,128)(2,1)}, u32[]{:S(2)}) copy-start(bf16[1,4,8,32,1280]{4,3,2,0,1:T(8,128)(2,1)} %all-gather.2.cloned.1.call-done) | copy-start | bytes 7864324
  110.1 6.2 %collective-permute-start.1 = (f32[2,32]{1,0:T(2,128)S(1)}, f32[2,32]{1,0:T(2,128)S(1)}, u32[]{:S(2)}, u32[]{:S(2)}) collective-permute-start(f32[2,32]{1,0:T(2,128)S(1)} %pad_maximum_fusion.2), channel_id=1, source_target_pairs={{0,1},{1,0},{2,3},{3,2},{4,5},{5,4},{6,7},{7,6},{8,9},{9,8},{10,11... | collective-permute-start | bytes 776 | tf_op jit(solution)/shard_map/ppermute | solution.py:18
  111.6 9.0 %collective-permute-start = (bf16[1,4,1,32,1280]{4,3,2,1,0:T(8,128)(2,1)S(1)}, bf16[1,4,1,32,1280]{4,3,2,1,0:T(8,128)(2,1)}, u32[]{:S(2)}, u32[]{:S(2)}) collective-permute-start(bf16[1,4,1,32,1280]{4,3,2,1,0:T(8,128)(2,1)S(1)} %get-tuple-element.25), channel_id=1, source_target_pairs={{0,1},{2,3},{4,5},{6,7},{8,9},{10,11},{12,13},{14,15},{16,17},{18,... | collective-permute-start | bytes 983048 | tf_op jit(solution)/shard_map/ppermute | solution.py:113
  114.8 10.7 %collective-permute-start.2 = (bf16[1,4,1,32,1280]{4,3,2,1,0:T(8,128)(2,1)S(1)}, bf16[1,4,1,32,1280]{4,3,2,1,0:T(8,128)(2,1)}, u32[]{:S(2)}, u32[]{:S(2)}) collective-permute-start(bf16[1,4,1,32,1280]{4,3,2,1,0:T(8,128)(2,1)S(1)} %get-tuple-element.26), channel_id=1, source_target_pairs={{1,0},{3,2},{5,4},{7,6},{9,8},{11,10},{13,12},{15,14},{17,16},{19,... | collective-permute-start | bytes 983048 | tf_op jit(solution)/shard_map/ppermute | solution.py:114
  127.1 1.7 copy-start.7
  128.8 2.9 %copy-start.6 = (bf16[1,1280,3,320]{1,3,2,0:T(8,128)(2,1)S(1)}, bf16[1,1280,3,320]{1,3,2,0:T(8,128)(2,1)}, u32[]{:S(2)}) copy-start(bf16[1,1280,3,320]{1,3,2,0:T(8,128)(2,1)} %get-tuple-element.12) | copy-start | bytes 7372804
  131.7 2.9 %copy-start.5 = (bf16[1,1280,3,320]{1,3,2,0:T(8,128)(2,1)S(1)}, bf16[1,1280,3,320]{1,3,2,0:T(8,128)(2,1)}, u32[]{:S(2)}) copy-start(bf16[1,1280,3,320]{1,3,2,0:T(8,128)(2,1)} %get-tuple-element.10) | copy-start | bytes 7372804
  137.9 1.3 copy-start.1
  138.0 1.5 copy-start.2
  139.2 3.9 %collective-permute-start.6 = (f32[2,8]{1,0:T(2,128)S(1)}, f32[2,8]{1,0:T(2,128)S(1)}, u32[]{:S(2)}, u32[]{:S(2)}) collective-permute-start(f32[2,8]{1,0:T(2,128)S(1)} %pad_maximum_fusion.3), channel_id=1, source_target_pairs={{0,1},{1,0},{2,3},{3,2},{4,5},{5,4},{6,7},{7,6},{8,9},{9,8},{10,11... | collective-permute-start | bytes 200 | tf_op jit(solution)/shard_map/ppermute | solution.py:18
  143.1 4.1 %copy-start.3 = (bf16[3,1280,80]{2,1,0:T(8,128)(2,1)S(1)}, bf16[3,1280,80]{2,1,0:T(8,128)(2,1)}, u32[]{:S(2)}) copy-start(bf16[3,1280,80]{2,1,0:T(8,128)(2,1)} %get-tuple-element.21) | copy-start | bytes 1843204
  143.1 4.2 %copy-start.4 = (bf16[3,1280,80]{2,1,0:T(8,128)(2,1)S(1)}, bf16[3,1280,80]{2,1,0:T(8,128)(2,1)}, u32[]{:S(2)}) copy-start(bf16[3,1280,80]{2,1,0:T(8,128)(2,1)} %get-tuple-element.22) | copy-start | bytes 1843204
  145.7 35.3 %collective-permute-start.10 = (bf16[4,8,32,320]{3,2,1,0:T(8,128)(2,1)}, bf16[4,8,32,320]{3,2,1,0:T(8,128)(2,1)}, u32[]{:S(2)}, u32[]{:S(2)}) collective-permute-start(bf16[4,8,32,320]{3,2,1,0:T(8,128)(2,1)} %multiply_convert_fusion), channel_id=1, source_target_pairs={{2,0},{4,2},{6,4},{3,1},{5,3},{7,5},{10,8},{12,10},{14,12},{11,9},... | collective-permute-start | bytes 1966088 | tf_op jit(solution)/shard_map/ppermute | solution.py:208
  162.5 66.4 %collective-permute-start.15 = (bf16[4,8,32,320]{3,2,1,0:T(8,128)(2,1)}, bf16[4,8,32,320]{3,2,1,0:T(8,128)(2,1)S(1)}, u32[]{:S(2)}, u32[]{:S(2)}) collective-permute-start(bf16[4,8,32,320]{3,2,1,0:T(8,128)(2,1)} %multiply_convert_fusion), channel_id=1, source_target_pairs={{0,6},{1,7},{8,14},{9,15},{16,22},{17,23},{24,30},{25,31}} | collective-permute-start | bytes 1966088 | tf_op jit(solution)/shard_map/ppermute | solution.py:208
  168.4 57.3 %collective-permute-start.14 = (bf16[4,8,32,320]{3,2,1,0:T(8,128)(2,1)}, bf16[4,8,32,320]{3,2,1,0:T(8,128)(2,1)S(1)}, u32[]{:S(2)}, u32[]{:S(2)}) collective-permute-start(bf16[4,8,32,320]{3,2,1,0:T(8,128)(2,1)} %multiply_convert_fusion), channel_id=1, source_target_pairs={{6,0},{7,1},{14,8},{15,9},{22,16},{23,17},{30,24},{31,25}} | collective-permute-start | bytes 1966088 | tf_op jit(solution)/shard_map/ppermute | solution.py:208
  169.7 54.7 %collective-permute-start.13 = (bf16[4,8,32,320]{3,2,1,0:T(8,128)(2,1)}, bf16[4,8,32,320]{3,2,1,0:T(8,128)(2,1)S(1)}, u32[]{:S(2)}, u32[]{:S(2)}) collective-permute-start(bf16[4,8,32,320]{3,2,1,0:T(8,128)(2,1)} %multiply_convert_fusion), channel_id=1, source_target_pairs={{0,4},{2,6},{1,5},{3,7},{8,12},{10,14},{9,13},{11,15},{16,20},{18,... | collective-permute-start | bytes 1966088 | tf_op jit(solution)/shard_map/ppermute | solution.py:208
  171.0 46.3 %collective-permute-start.11 = (bf16[4,8,32,320]{3,2,1,0:T(8,128)(2,1)}, bf16[4,8,32,320]{3,2,1,0:T(8,128)(2,1)S(1)}, u32[]{:S(2)}, u32[]{:S(2)}) collective-permute-start(bf16[4,8,32,320]{3,2,1,0:T(8,128)(2,1)} %multiply_convert_fusion), channel_id=1, source_target_pairs={{0,2},{2,4},{4,6},{1,3},{3,5},{5,7},{8,10},{10,12},{12,14},{9,11},... | collective-permute-start | bytes 1966088 | tf_op jit(solution)/shard_map/ppermute | solution.py:208
  181.0 42.1 %collective-permute-start.12 = (bf16[4,8,32,320]{3,2,1,0:T(8,128)(2,1)}, bf16[4,8,32,320]{3,2,1,0:T(8,128)(2,1)S(1)}, u32[]{:S(2)}, u32[]{:S(2)}) collective-permute-start(bf16[4,8,32,320]{3,2,1,0:T(8,128)(2,1)} %multiply_convert_fusion), channel_id=1, source_target_pairs={{4,0},{6,2},{5,1},{7,3},{12,8},{14,10},{13,9},{15,11},{20,16},{22,... | collective-permute-start | bytes 1966088 | tf_op jit(solution)/shard_map/ppermute | solution.py:208
  238.9 18.9 %collective-permute-start.18 = (bf16[1,8,32,320]{3,2,1,0:T(8,128)(2,1)S(1)}, bf16[1,8,32,320]{3,2,1,0:T(8,128)(2,1)S(1)}, u32[]{:S(2)}, u32[]{:S(2)}) collective-permute-start(bf16[1,8,32,320]{3,2,1,0:T(8,128)(2,1)S(1)} %get-tuple-element.31), channel_id=1, source_target_pairs={{0,6},{2,0},{4,2},{6,4},{1,7},{3,1},{5,3},{7,5},{8,14},{10,8},{12,... | collective-permute-start | bytes 491528 | tf_op jit(solution)/shard_map/ppermute | solution.py:224
  238.9 33.3 %collective-permute-start.17 = (bf16[1,8,32,320]{3,2,1,0:T(8,128)(2,1)S(1)}, bf16[1,8,32,320]{3,2,1,0:T(8,128)(2,1)S(1)}, u32[]{:S(2)}, u32[]{:S(2)}) collective-permute-start(bf16[1,8,32,320]{3,2,1,0:T(8,128)(2,1)S(1)} %get-tuple-element.32), channel_id=1, source_target_pairs={{0,4},{2,6},{4,0},{6,2},{1,5},{3,7},{5,1},{7,3},{8,12},{10,14},{12... | collective-permute-start | bytes 491528 | tf_op jit(solution)/shard_map/ppermute | solution.py:224
  254.6 17.6 %collective-permute-start.16 = (bf16[1,8,32,320]{3,2,1,0:T(8,128)(2,1)S(1)}, bf16[1,8,32,320]{3,2,1,0:T(8,128)(2,1)S(1)}, u32[]{:S(2)}, u32[]{:S(2)}) collective-permute-start(bf16[1,8,32,320]{3,2,1,0:T(8,128)(2,1)S(1)} %get-tuple-element.33), channel_id=1, source_target_pairs={{0,2},{2,4},{4,6},{6,0},{1,3},{3,5},{5,7},{7,1},{8,10},{10,12},{12... | collective-permute-start | bytes 491528 | tf_op jit(solution)/shard_map/ppermute | solution.py:224
  275.0 2.3 copy-start.11
Sparse Core Ops, SparseCore 0:
  51.9 55.0 all-gather.1

commit v8 on v6

--- a/solution.py
+++ b/solution.py
@@ -133,24 +133,24 @@
         normed = (x.astype(jnp.float32) - mean_full) * inverse_full * first_gain + first_shift
         return silu_bf16(normed)
 
-    first_mid = first_norm(raw)
-    first_above = jnp.where(row_index > 0, first_norm(above), jnp.zeros((), jnp.bfloat16))
+    first_mid = lax.optimization_barrier(first_norm(raw)[0])
+    first_above = jnp.where(row_index > 0, first_norm(above), jnp.zeros((), jnp.bfloat16))[0]
     first_below = jnp.where(
         row_index < row_size - 1, first_norm(below), jnp.zeros((), jnp.bfloat16)
-    )
-    padded = jnp.concatenate([first_above, first_mid, first_below], axis=2)
-
-    field = lax.optimization_barrier(padded[0])
+    )[0]
+
     wide = spatial_w.reshape(3, channels, 3 * local)
-    product = None
-    for row_tap in range(3):
-        term = jnp.einsum(
-            "frxc,cn->frxn",
-            field[:, row_tap : row_tap + rows],
-            wide[row_tap],
-            preferred_element_type=jnp.float32,
-        )
-        product = term if product is None else product + term
+
+    def tap(field, row_tap):
+        return jnp.einsum(
+            "frxc,cn->frxn", field, wide[row_tap], preferred_element_type=jnp.float32
+        )
+
+    product = tap(first_mid, 1)
+    product = product + jnp.pad(tap(first_mid[:, :-1], 0), ((0, 0), (1, 0), (0, 0), (0, 0)))
+    product = product + jnp.pad(tap(first_mid[:, 1:], 2), ((0, 0), (0, 1), (0, 0), (0, 0)))
+    product = product + jnp.pad(tap(first_above, 0), ((0, 0), (0, rows - 1), (0, 0), (0, 0)))
+    product = product + jnp.pad(tap(first_below, 2), ((0, 0), (rows - 1, 0), (0, 0), (0, 0)))
     left = jnp.pad(product[:, :, :-1, :local], ((0, 0), (0, 0), (1, 0), (0, 0)))
     right = jnp.pad(product[:, :, 1:, 2 * local :], ((0, 0), (0, 0), (0, 1), (0, 0)))
     spatial = (left + product[..., local : 2 * local] + right)[None]

time: 246 us -> 241 us (0.980)
  waiting for transfers between devices: 152 us -> 145 us
  matrix products: 15.2 us -> 18.8 us
  starting transfers between devices: 14.8 us -> 17.5 us
    ppermute x1, waiting for transfers between devices: 4.93 us -> 0.01 us  [shards(): below = lax.ppermute(raw[:, :, :1], 'row', up)]
    pad x0 -> x1, matrix products: none -> 2.9 us  [shards(): jnp.pad(tap(first_mid[:, :-1], 0), ((0, 0), (1, 0), (0, 0), (0, 0)))]
    ppermute x1, starting transfers between devices: 3.19 us -> 6 us  [shards(): above = lax.ppermute(raw[:, :, rows - 1:], 'row', down)]
    dot_general x3 -> x4, matrix products: 8.69 us -> 9.37 us  [tap(): jnp.einsum('frxc,cn->frxn', field, wide[row_tap], preferred_element_type=...]
  transfers between devices with their start and end apart: 15 -> 15, of which waited for: 10 -> 8; matrix products, arithmetic and copies ran while one was open for 12% -> 16% of each run, Pallas kernels for 0% -> 0%
where the time goes in v8:
time: 241 us; the launch traced here: 240 us
  waiting for transfers between devices  145 us (60%)
  other arithmetic  23.4 us (10%)
  local copies, waits for them, and re-layouts  21.5 us (9%)
  matrix products  18.8 us (8%)
  starting transfers between devices  17.5 us (7%)
  between operations  14 us (6%)
    ppermute x2, waiting for transfers between devices, gather_rep(): across = lax.ppermute(w, 'rep', [(k, k ^ 2) for k in range(size)])  52.5 us
    all_gather x1, waiting for transfers between devices, shards(): raw = lax.all_gather(activations, 'frame', axis=1, tiled=True)  40.9 us
    all_gather x1, waiting for transfers between devices, shards(): second_all = lax.all_gather(second[0], 'frame', axis=0, tiled=False)  33.9 us
    ppermute x3, waiting for transfers between devices, shards(): lax.ppermute(piece, 'frame', [(k, (k + shift) % frame_size) for k in rang...  12.9 us
    dot_general x4, matrix products, tap(): jnp.einsum('frxc,cn->frxn', field, wide[row_tap], preferred_element_type=...  9.37 us
    concatenate x2, other arithmetic, gather_rep(): return jnp.concatenate(blocks, axis=-1)  8.27 us
    dot_general x4, matrix products, shards(): jnp.einsum('frxc,cn->frxn', second_all[group], weights, preferred_element...  6.53 us
    ppermute x1, starting transfers between devices, shards(): above = lax.ppermute(raw[:, :, rows - 1:], 'row', down)  6 us
  transfers between devices with their start and end apart: 15, of which 8 were waited for; matrix products, arithmetic and copies ran while one was open for 16% of the time, Pallas kernels for 0%

profile of v8, /device:TPU:0, one launch (start us, length us, event | category | flops | bytes accessed | tf_op | source)
XLA Modules:
  0.0 240.0 jit_solution(1474166999226615005)
XLA Ops:
  6.5 3.0 %collective-permute-start.2 = (bf16[3,1280,3,80]{1,3,2,0:T(8,128)(2,1)}, bf16[3,1280,3,80]{1,3,2,0:T(8,128)(2,1)S(1)}, u32[]{:S(2)}, u32[]{:S(2)}) collective-permute-start(bf16[3,1280,3,80]{1,3,2,0:T(8,128)(2,1)} %bitcast.120), channel_id=1, source_target_pairs={{0,16},{8,24},{16,0},{24,8},{1,17},{9,25},{17,1},{25,9},{2,18},{10... | collective-permute-start | bytes 5529608 | tf_op jit(solution)/shard_map/ppermute | solution.py:28
  9.5 40.4 %collective-permute-done.2 = bf16[3,1280,3,80]{1,3,2,0:T(8,128)(2,1)S(1)} collective-permute-done((bf16[3,1280,3,80]{1,3,2,0:T(8,128)(2,1)}, bf16[3,1280,3,80]{1,3,2,0:T(8,128)(2,1)S(1)}, u32[]{:S(2)}, u32[]{:S(2)}) %collective-permute-start.2) | collective-permute-done | bytes 1843232 | tf_op jit(solution)/shard_map/ppermute | solution.py:28
  53.8 3.0 %select_select_fusion.3 = (bf16[3,1280,3,80]{1,3,2,0:T(8,128)(2,1)S(1)}, bf16[3,1280,3,80]{1,3,2,0:T(8,128)(2,1)S(1)}, bf16[3,1280,3,80]{1,3,2,0:T(8,128)(2,1)S(1)}, bf16[3,1280,3,80]{1,3,2,0:T(8,128)(2,1)S(1)}) fusion(bf16[3,1280,3,80]{1,3,2,0:T(8,128)(2,1)} %bitcast.122, bf16[3,1280,3,80]{1,3,2,0:T(8,128)(2,1)} %collective-permute-done.1, ...), kind=kLoop, calls=%fused_computation.23 | loop fusion | flops 11059200 | bytes 14745612 | tf_op jit(solution)/shard_map/jit(_where)/select_n | solution.py:37
  56.9 5.5 %pad_maximum_fusion = bf16[3,1280,3,320]{1,3,2,0:T(8,128)(2,1)S(1)} fusion(bf16[3,1280,3,80]{1,3,2,0:T(8,128)(2,1)S(1)} %get-tuple-element.14, bf16[3,1280,3,80]{1,3,2,0:T(8,128)(2,1)S(1)} %get-tuple-element.15, bf16[3,1280,3,80]{1,3,2,0:T(8,128)(2,1)S(1)} %get-tuple-element.16, bf16[3,1280,3,80]{1,3,2,0:T(8,128)(2,1)S(1)} %get-tuple-element.13), kind=kLoop, calls=%fused_computation.3 | loop fusion | flops 29491200 | bytes 14745600 | tf_op jit(solution)/shard_map/concatenate | solution.py:39
  62.4 3.2 %fusion.48 = (bf16[1,1280,3,320]{1,3,2,0:T(8,128)(2,1)}, bf16[1,1280,3,320]{1,3,2,0:T(8,128)(2,1)}, bf16[1,1280,3,320]{1,3,2,0:T(8,128)(2,1)}) fusion(bf16[3,1280,3,320]{1,3,2,0:T(8,128)(2,1)S(1)} %pad_maximum_fusion), kind=kLoop, calls=%fused_computation.86 | loop fusion | bytes 14745600 | tf_op jit(solution)/shard_map/slice | solution.py:146
  65.6 40.9 %all-gather.4.cloned.1.call-done = bf16[1,4,8,32,1280]{4,3,2,0,1:T(8,128)(2,1)} async-done(((bf16[1,1,8,32,1280]{4,3,2,0,1:T(8,128)(2,1)}), bf16[1,4,8,32,1280]{4,3,2,0,1:T(8,128)(2,1)}) %all-gather.4.cloned.1.call-update) | async-done | bytes 2621456 | tf_op jit(solution)/shard_map/all_gather | solution.py:107
  106.5 2.6 %convert_reduce_fusion = (f32[1280]{0:T(1024)S(1)}, f32[1280]{0:T(1024)S(1)}) fusion(bf16[1,4,8,32,1280]{4,3,2,0,1:T(8,128)(2,1)} %all-gather.4.cloned.1.call-done), kind=kLoop, calls=%fused_computation.2 | loop fusion | flops 5240320 | bytes 2631680 | tf_op jit(solution)/shard_map/reduce_sum | solution.py:121
  109.5 1.5 collective-permute-start
  112.4 6.0 %collective-permute-start.4 = (bf16[1,4,1,32,1280]{4,3,2,0,1:T(8,128)(2,1)S(1)}, bf16[1,4,1,32,1280]{4,3,2,0,1:T(8,128)(2,1)}, u32[]{:S(2)}, u32[]{:S(2)}) collective-permute-start(bf16[1,4,1,32,1280]{4,3,2,0,1:T(8,128)(2,1)S(1)} %get-tuple-element.29), channel_id=1, source_target_pairs={{0,1},{2,3},{4,5},{6,7},{8,9},{10,11},{12,13},{14,15},{16,17},{18,... | collective-permute-start | bytes 983048 | tf_op jit(solution)/shard_map/ppermute | solution.py:113
  118.8 1.8 fusion.10
  120.6 2.6 %fusion.53 = f32[4,7,32,960]{3,2,1,0:T(8,128)S(1)} fusion(bf16[4,8,32,1280]{3,2,1,0:T(8,128)(2,1)S(1)} %fusion.10, bf16[1280,960,1,1]{0,1,3,2:T(8,128)(2,1)S(1)} %bitcast.118), kind=kOutput, calls=%fused_computation.91 | convolution fusion | flops 2202009600 | bytes 8519680 | tf_op jit(solution)/shard_map/frxc,cn->frxn/dot_general | solution.py:145
  123.2 2.9 %fusion.11 = f32[4,8,32,960]{3,2,1,0:T(8,128)S(1)} fusion(bf16[1280,960,1,1]{0,1,3,2:T(8,128)(2,1)S(1)} %bitcast.116, bf16[4,8,32,1280]{3,2,1,0:T(8,128)(2,1)S(1)} %fusion.10), kind=kOutput, calls=%fused_computation.18 | convolution fusion | flops 2202009600 | bytes 8683520 | tf_op jit(solution)/shard_map/jit(_pad)/pad | solution.py:150
  126.1 1.9 convolution_bitcast_fusion
  128.0 2.0 convolution_bitcast_fusion.1
  130.1 2.9 %pad_add_fusion = f32[4,8,32,960]{3,2,1,0:T(8,128)S(1)} fusion(f32[4,1,32,960]{3,2,1,0:T(8,128)S(1)} %convolution_bitcast_fusion, f32[4,1,32,960]{3,2,1,0:T(8,128)S(1)} %convolution_bitcast_fusion.1, f32[4,7,32,960]{3,2,1,0:T(8,128)S(1)} %fusion.53, f32[4,8,32,960]{3,2,1,0:T(8,128)S(1)} %fusion.11, bf16[4,8,32,1280]{3,2,1,0:T(8,128)(2,1)S(1)} %fusion.10, ...), kind=kOutput, calls=%fused_computation.15 | convolution fusion | flops 2520514560 | bytes 17367040 | tf_op jit(solution)/shard_map/frxc,cn->frxn/dot_general | solution.py:145
  134.7 3.5 %collective-permute-done.6 = f32[2,8]{1,0:T(2,128)S(1)} collective-permute-done((f32[2,8]{1,0:T(2,128)S(1)}, f32[2,8]{1,0:T(2,128)S(1)}, u32[]{:S(2)}, u32[]{:S(2)}) %collective-permute-start.6) | collective-permute-done | bytes 96 | tf_op jit(solution)/shard_map/ppermute | solution.py:18
  138.6 1.4 multiply_convert_fusion
  140.0 1.5 collective-permute-start.8
  141.5 12.1 %collective-permute-done.8 = bf16[3,1280,80]{1,2,0:T(8,128)(2,1)} collective-permute-done((bf16[3,1280,80]{1,2,0:T(8,128)(2,1)S(1)}, bf16[3,1280,80]{1,2,0:T(8,128)(2,1)}, u32[]{:S(2)}, u32[]{:S(2)}) %collective-permute-start.8) | collective-permute-done | bytes 614432 | tf_op jit(solution)/shard_map/ppermute | solution.py:28
  154.3 1.5 copy.112
  155.9 1.5 copy.114
  157.4 2.2 copy.113
  159.6 1.7 select_select_fusion.7
  161.3 2.8 %pad_maximum_fusion.1 = bf16[3,1280,320]{2,1,0:T(8,128)(2,1)S(1)} fusion(bf16[3,1280,80]{2,1,0:T(8,128)(2,1)S(1)} %get-tuple-element.22, bf16[3,1280,80]{2,1,0:T(8,128)(2,1)S(1)} %get-tuple-element.23, bf16[3,1280,80]{2,1,0:T(8,128)(2,1)S(1)} %get-tuple-element.24, bf16[3,1280,80]{2,1,0:T(8,128)(2,1)S(1)} %get-tuple-element.21), kind=kLoop, calls=%fused_computation.16 | loop fusion | flops 9830400 | bytes 4915200 | tf_op jit(solution)/shard_map/concatenate | solution.py:39
  167.6 33.9 %all-gather.6.cloned.1.call-done = bf16[16,8,32,320]{3,2,1,0:T(8,128)(2,1)} async-done(((bf16[4,8,32,320]{3,2,1,0:T(8,128)(2,1)}), bf16[16,8,32,320]{3,2,1,0:T(8,128)(2,1)}) %all-gather.6.cloned.1.call-update) | async-done | bytes 2621456 | tf_op jit(solution)/shard_map/all_gather | solution.py:193
  201.4 2.6 %fusion.56 = f32[4,8,32,960]{3,2,1,0:T(8,128)S(1)} fusion(bf16[16,8,32,320]{3,2,1,0:T(8,128)(2,1)} %all-gather.6.cloned.1.call-done, bf16[320,960,1,1]{0,1,3,2:T(8,128)(2,1)S(1)} %bitcast.110), kind=kOutput, calls=%fused_computation.94 | convolution fusion | flops 629145600 | bytes 7168000 | tf_op jit(solution)/shard_map/frxc,cn->frxn/dot_general | solution.py:199
  206.6 1.4 add_add_fusion
  210.3 2.7 %collective-permute-start.12 = (bf16[1,8,32,320]{3,2,1,0:T(8,128)(2,1)S(1)}, bf16[1,8,32,320]{3,2,1,0:T(8,128)(2,1)S(1)}, u32[]{:S(2)}, u32[]{:S(2)}) collective-permute-start(bf16[1,8,32,320]{3,2,1,0:T(8,128)(2,1)S(1)} %get-tuple-element.35), channel_id=1, source_target_pairs={{0,6},{2,0},{4,2},{6,4},{1,7},{3,1},{5,3},{7,5},{8,14},{10,8},{12,... | collective-permute-start | bytes 491528 | tf_op jit(solution)/shard_map/ppermute | solution.py:216
  213.0 5.7 %collective-permute-done.10 = bf16[1,8,32,320]{3,2,1,0:T(8,128)(2,1)S(1)} collective-permute-done((bf16[1,8,32,320]{3,2,1,0:T(8,128)(2,1)S(1)}, bf16[1,8,32,320]{3,2,1,0:T(8,128)(2,1)S(1)}, u32[]{:S(2)}, u32[]{:S(2)}) %collective-permute-start.10) | collective-permute-done | bytes 163872 | tf_op jit(solution)/shard_map/ppermute | solution.py:216
  218.6 7.2 %collective-permute-done.11 = bf16[1,8,32,320]{3,2,1,0:T(8,128)(2,1)S(1)} collective-permute-done((bf16[1,8,32,320]{3,2,1,0:T(8,128)(2,1)S(1)}, bf16[1,8,32,320]{3,2,1,0:T(8,128)(2,1)S(1)}, u32[]{:S(2)}, u32[]{:S(2)}) %collective-permute-start.11) | collective-permute-done | bytes 163872 | tf_op jit(solution)/shard_map/ppermute | solution.py:216
  228.6 2.2 reshape.369
  230.8 2.3 add_add_fusion.1
  (98 shorter events, 19.7 us)
Async XLA Ops:
  6.5 99.9 %all-gather.4.cloned.1.call-start = ((), (), s32[]{:S(2)}) async-start(), calls=%async_computation | async-start | bytes 3276800 | tf_op jit(solution)/shard_map/all_gather | solution.py:107
  6.5 43.4 %collective-permute-start.2 = (bf16[3,1280,3,80]{1,3,2,0:T(8,128)(2,1)}, bf16[3,1280,3,80]{1,3,2,0:T(8,128)(2,1)S(1)}, u32[]{:S(2)}, u32[]{:S(2)}) collective-permute-start(bf16[3,1280,3,80]{1,3,2,0:T(8,128)(2,1)} %bitcast.120), channel_id=1, source_target_pairs={{0,16},{8,24},{16,0},{24,8},{1,17},{9,25},{17,1},{25,9},{2,18},{10... | collective-permute-start | bytes 5529608 | tf_op jit(solution)/shard_map/ppermute | solution.py:28
  9.5 43.1 %collective-permute-start.1 = (bf16[3,1280,3,80]{1,3,2,0:T(8,128)(2,1)}, bf16[3,1280,3,80]{1,3,2,0:T(8,128)(2,1)}, u32[]{:S(2)}, u32[]{:S(2)}) collective-permute-start(bf16[3,1280,3,80]{1,3,2,0:T(8,128)(2,1)} %bitcast.121), channel_id=1, source_target_pairs={{0,8},{8,0},{16,24},{24,16},{1,9},{9,1},{17,25},{25,17},{2,10},{10... | collective-permute-start | bytes 5529608 | tf_op jit(solution)/shard_map/ppermute | solution.py:29
  49.9 3.9 %collective-permute-start.3 = (bf16[3,1280,3,80]{1,3,2,0:T(8,128)(2,1)S(1)}, bf16[3,1280,3,80]{1,3,2,0:T(8,128)(2,1)}, u32[]{:S(2)}, u32[]{:S(2)}) collective-permute-start(bf16[3,1280,3,80]{1,3,2,0:T(8,128)(2,1)S(1)} %collective-permute-done.2), channel_id=1, source_target_pairs={{0,8},{8,0},{16,24},{24,16},{1,9},{9,1},{17,25},{25,17},{2,10},{10... | collective-permute-start | bytes 5529608 | tf_op jit(solution)/shard_map/ppermute | solution.py:30
  49.9 151.5 %all-gather.6.cloned.1.call-start = ((), (), s32[]{:S(2)}) async-start(), calls=%async_computation.1 | async-start | bytes 3932160 | tf_op jit(solution)/shard_map/all_gather | solution.py:193
  65.5 53.2 %copy-start.8 = (f32[1280]{0:T(1024)S(1)}, f32[1280]{0:T(1024)}, u32[]{:S(2)}) copy-start(f32[1280]{0:T(1024)} %param.13) | copy-start | bytes 15364
  65.5 53.2 %copy-start.9 = (f32[1280]{0:T(1024)S(1)}, f32[1280]{0:T(1024)}, u32[]{:S(2)}) copy-start(f32[1280]{0:T(1024)} %param.12) | copy-start | bytes 15364
  106.5 4.6 %copy-start = (bf16[1,4,8,32,1280]{4,3,2,0,1:T(8,128)(2,1)S(1)}, bf16[1,4,8,32,1280]{4,3,2,0,1:T(8,128)(2,1)}, u32[]{:S(2)}) copy-start(bf16[1,4,8,32,1280]{4,3,2,0,1:T(8,128)(2,1)} %all-gather.4.cloned.1.call-done) | copy-start | bytes 7864324
  109.5 8.9 %collective-permute-start = (f32[2,32]{1,0:T(2,128)S(1)}, f32[2,32]{1,0:T(2,128)S(1)}, u32[]{:S(2)}, u32[]{:S(2)}) collective-permute-start(f32[2,32]{1,0:T(2,128)S(1)} %pad_maximum_fusion.2), channel_id=1, source_target_pairs={{0,1},{1,0},{2,3},{3,2},{4,5},{5,4},{6,7},{7,6},{8,9},{9,8},{10,11... | collective-permute-start | bytes 776 | tf_op jit(solution)/shard_map/ppermute | solution.py:18
  111.1 15.0 %collective-permute-start.5 = (bf16[1,4,1,32,1280]{4,3,2,0,1:T(8,128)(2,1)S(1)}, bf16[1,4,1,32,1280]{4,3,2,0,1:T(8,128)(2,1)}, u32[]{:S(2)}, u32[]{:S(2)}) collective-permute-start(bf16[1,4,1,32,1280]{4,3,2,0,1:T(8,128)(2,1)S(1)} %get-tuple-element.30), channel_id=1, source_target_pairs={{1,0},{3,2},{5,4},{7,6},{9,8},{11,10},{13,12},{15,14},{17,16},{19,... | collective-permute-start | bytes 983048 | tf_op jit(solution)/shard_map/ppermute | solution.py:114
  112.4 15.6 %collective-permute-start.4 = (bf16[1,4,1,32,1280]{4,3,2,0,1:T(8,128)(2,1)S(1)}, bf16[1,4,1,32,1280]{4,3,2,0,1:T(8,128)(2,1)}, u32[]{:S(2)}, u32[]{:S(2)}) collective-permute-start(bf16[1,4,1,32,1280]{4,3,2,0,1:T(8,128)(2,1)S(1)} %get-tuple-element.29), channel_id=1, source_target_pairs={{0,1},{2,3},{4,5},{6,7},{8,9},{10,11},{12,13},{14,15},{16,17},{18,... | collective-permute-start | bytes 983048 | tf_op jit(solution)/shard_map/ppermute | solution.py:113
  118.8 1.8 copy-start.6
  120.6 2.6 %copy-start.5 = (bf16[1,1280,3,320]{1,3,2,0:T(8,128)(2,1)S(1)}, bf16[1,1280,3,320]{1,3,2,0:T(8,128)(2,1)}, u32[]{:S(2)}) copy-start(bf16[1,1280,3,320]{1,3,2,0:T(8,128)(2,1)} %get-tuple-element.12) | copy-start | bytes 7372804
  128.0 2.1 copy-start.4
  134.1 5.8 %copy-start.7 = (bf16[3,1280,80]{1,2,0:T(8,128)(2,1)S(1)}, bf16[3,1280,80]{1,2,0:T(8,128)(2,1)}, u32[]{:S(2)}) copy-start(bf16[3,1280,80]{1,2,0:T(8,128)(2,1)} %param.11) | copy-start | bytes 1843204
  134.6 3.6 %collective-permute-start.6 = (f32[2,8]{1,0:T(2,128)S(1)}, f32[2,8]{1,0:T(2,128)S(1)}, u32[]{:S(2)}, u32[]{:S(2)}) collective-permute-start(f32[2,8]{1,0:T(2,128)S(1)} %pad_maximum_fusion.3), channel_id=1, source_target_pairs={{0,1},{1,0},{2,3},{3,2},{4,5},{5,4},{6,7},{7,6},{8,9},{9,8},{10,11... | collective-permute-start | bytes 200 | tf_op jit(solution)/shard_map/ppermute | solution.py:18
  140.0 13.6 %collective-permute-start.8 = (bf16[3,1280,80]{1,2,0:T(8,128)(2,1)S(1)}, bf16[3,1280,80]{1,2,0:T(8,128)(2,1)}, u32[]{:S(2)}, u32[]{:S(2)}) collective-permute-start(bf16[3,1280,80]{1,2,0:T(8,128)(2,1)S(1)} %copy-done.7), channel_id=1, source_target_pairs={{0,16},{8,24},{16,0},{24,8},{1,17},{9,25},{17,1},{25,9},{2,18},{10... | collective-permute-start | bytes 1843208 | tf_op jit(solution)/shard_map/ppermute | solution.py:28
  141.5 14.3 %collective-permute-start.7 = (bf16[3,1280,80]{1,2,0:T(8,128)(2,1)S(1)}, bf16[3,1280,80]{1,2,0:T(8,128)(2,1)}, u32[]{:S(2)}, u32[]{:S(2)}) collective-permute-start(bf16[3,1280,80]{1,2,0:T(8,128)(2,1)S(1)} %copy-done.7), channel_id=1, source_target_pairs={{0,8},{8,0},{16,24},{24,16},{1,9},{9,1},{17,25},{25,17},{2,10},{10... | collective-permute-start | bytes 1843208 | tf_op jit(solution)/shard_map/ppermute | solution.py:29
  153.6 3.8 %collective-permute-start.9 = (bf16[3,1280,80]{1,2,0:T(8,128)(2,1)}, bf16[3,1280,80]{1,2,0:T(8,128)(2,1)}, u32[]{:S(2)}, u32[]{:S(2)}) collective-permute-start(bf16[3,1280,80]{1,2,0:T(8,128)(2,1)} %collective-permute-done.8), channel_id=1, source_target_pairs={{0,8},{8,0},{16,24},{24,16},{1,9},{9,1},{17,25},{25,17},{2,10},{10... | collective-permute-start | bytes 1843208 | tf_op jit(solution)/shard_map/ppermute | solution.py:30
  165.6 35.8 %copy-start.2 = (bf16[3,320,320]{1,2,0:T(8,128)(2,1)S(1)}, bf16[3,320,320]{1,2,0:T(8,128)(2,1)}, u32[]{:S(2)}) copy-start(bf16[3,320,320]{1,2,0:T(8,128)(2,1)} %copy.132) | copy-start | bytes 1843204
  201.4 2.6 %copy-start.1 = (bf16[16,8,32,320]{3,2,1,0:T(8,128)(2,1)S(1)}, bf16[16,8,32,320]{3,2,1,0:T(8,128)(2,1)}, u32[]{:S(2)}) copy-start(bf16[16,8,32,320]{3,2,1,0:T(8,128)(2,1)} %all-gather.6.cloned.1.call-done) | copy-start | bytes 7864324
  201.4 2.6 %copy-start.3 = (bf16[3,320,320]{1,2,0:T(8,128)(2,1)S(1)}, bf16[3,320,320]{1,2,0:T(8,128)(2,1)}, u32[]{:S(2)}) copy-start(bf16[3,320,320]{1,2,0:T(8,128)(2,1)} %copy.128) | copy-start | bytes 1843204
  208.9 9.7 %collective-permute-start.10 = (bf16[1,8,32,320]{3,2,1,0:T(8,128)(2,1)S(1)}, bf16[1,8,32,320]{3,2,1,0:T(8,128)(2,1)S(1)}, u32[]{:S(2)}, u32[]{:S(2)}) collective-permute-start(bf16[1,8,32,320]{3,2,1,0:T(8,128)(2,1)S(1)} %get-tuple-element.37), channel_id=1, source_target_pairs={{0,2},{2,4},{4,6},{6,0},{1,3},{3,5},{5,7},{7,1},{8,10},{10,12},{12... | collective-permute-start | bytes 491528 | tf_op jit(solution)/shard_map/ppermute | solution.py:216
  209.0 16.8 %collective-permute-start.11 = (bf16[1,8,32,320]{3,2,1,0:T(8,128)(2,1)S(1)}, bf16[1,8,32,320]{3,2,1,0:T(8,128)(2,1)S(1)}, u32[]{:S(2)}, u32[]{:S(2)}) collective-permute-start(bf16[1,8,32,320]{3,2,1,0:T(8,128)(2,1)S(1)} %get-tuple-element.36), channel_id=1, source_target_pairs={{0,4},{2,6},{4,0},{6,2},{1,5},{3,7},{5,1},{7,3},{8,12},{10,14},{12... | collective-permute-start | bytes 491528 | tf_op jit(solution)/shard_map/ppermute | solution.py:216
  210.3 15.5 %collective-permute-start.12 = (bf16[1,8,32,320]{3,2,1,0:T(8,128)(2,1)S(1)}, bf16[1,8,32,320]{3,2,1,0:T(8,128)(2,1)S(1)}, u32[]{:S(2)}, u32[]{:S(2)}) collective-permute-start(bf16[1,8,32,320]{3,2,1,0:T(8,128)(2,1)S(1)} %get-tuple-element.35), channel_id=1, source_target_pairs={{0,6},{2,0},{4,2},{6,4},{1,7},{3,1},{5,3},{7,5},{8,14},{10,8},{12,... | collective-permute-start | bytes 491528 | tf_op jit(solution)/shard_map/ppermute | solution.py:216
  228.6 2.3 copy-start.10
Sparse Core Ops, SparseCore 0:
  50.0 56.3 all-gather.3
  140.1 61.2 all-gather.5

commit v9 on v8

--- a/solution.py
+++ b/solution.py
@@ -224,7 +224,10 @@
         for shift in range(frame_size - 2, -1, -1):
             slot = jnp.where(wanted == shift, pieces[shift], slot)
         slots.append(slot)
-    result = jnp.stack(slots, axis=4).reshape(1, per_frame, rows, cols, channels)
+    result = jnp.concatenate(
+        [slots[group][..., block, :] for block in range(rep_size) for group in range(frame_size)],
+        axis=-1,
+    )[None]
     return activations.astype(jnp.float32) + result.astype(jnp.float32) + temporal_bias
 
 

time: 241 us -> 239 us (level)
    convert_element_type x2 -> x0, local copies, waits for them, and re-layouts: 3.6 us -> none  [shards(): result.astype(jnp.float32)]
where the time goes in v9:
time: 239 us; the launch traced here: 238 us
  waiting for transfers between devices  145 us (61%)
  other arithmetic  22.1 us (9%)
  local copies, waits for them, and re-layouts  20.7 us (9%)
  matrix products  18.8 us (8%)
  starting transfers between devices  17.5 us (7%)
  between operations  14.1 us (6%)
    ppermute x2, waiting for transfers between devices, gather_rep(): across = lax.ppermute(w, 'rep', [(k, k ^ 2) for k in range(size)])  52.5 us
    all_gather x1, waiting for transfers between devices, shards(): raw = lax.all_gather(activations, 'frame', axis=1, tiled=True)  40.9 us
    all_gather x1, waiting for transfers between devices, shards(): second_all = lax.all_gather(second[0], 'frame', axis=0, tiled=False)  33.9 us
    ppermute x3, waiting for transfers between devices, shards(): lax.ppermute(piece, 'frame', [(k, (k + shift) % frame_size) for k in rang...  12.8 us
    dot_general x4, matrix products, tap(): jnp.einsum('frxc,cn->frxn', field, wide[row_tap], preferred_element_type=...  9.38 us
    concatenate x2, other arithmetic, gather_rep(): return jnp.concatenate(blocks, axis=-1)  8.27 us
    dot_general x4, matrix products, shards(): jnp.einsum('frxc,cn->frxn', second_all[group], weights, preferred_element...  6.53 us
    ppermute x1, starting transfers between devices, shards(): above = lax.ppermute(raw[:, :, rows - 1:], 'row', down)  5.99 us
  transfers between devices with their start and end apart: 15, of which 8 were waited for; matrix products, arithmetic and copies ran while one was open for 16% of the time, Pallas kernels for 0%

profile of v9, /device:TPU:0, one launch (start us, length us, event | category | flops | bytes accessed | tf_op | source)
XLA Modules:
  0.0 238.0 jit_solution(15791598303261674717)
XLA Ops:
  6.5 3.0 %collective-permute-start.2 = (bf16[3,1280,3,80]{1,3,2,0:T(8,128)(2,1)}, bf16[3,1280,3,80]{1,3,2,0:T(8,128)(2,1)S(1)}, u32[]{:S(2)}, u32[]{:S(2)}) collective-permute-start(bf16[3,1280,3,80]{1,3,2,0:T(8,128)(2,1)} %bitcast.171), channel_id=1, source_target_pairs={{0,16},{8,24},{16,0},{24,8},{1,17},{9,25},{17,1},{25,9},{2,18},{10... | collective-permute-start | bytes 5529608 | tf_op jit(solution)/shard_map/ppermute | solution.py:28
  9.5 40.4 %collective-permute-done.2 = bf16[3,1280,3,80]{1,3,2,0:T(8,128)(2,1)S(1)} collective-permute-done((bf16[3,1280,3,80]{1,3,2,0:T(8,128)(2,1)}, bf16[3,1280,3,80]{1,3,2,0:T(8,128)(2,1)S(1)}, u32[]{:S(2)}, u32[]{:S(2)}) %collective-permute-start.2) | collective-permute-done | bytes 1843232 | tf_op jit(solution)/shard_map/ppermute | solution.py:28
  53.8 3.0 %select_select_fusion.3 = (bf16[3,1280,3,80]{1,3,2,0:T(8,128)(2,1)S(1)}, bf16[3,1280,3,80]{1,3,2,0:T(8,128)(2,1)S(1)}, bf16[3,1280,3,80]{1,3,2,0:T(8,128)(2,1)S(1)}, bf16[3,1280,3,80]{1,3,2,0:T(8,128)(2,1)S(1)}) fusion(bf16[3,1280,3,80]{1,3,2,0:T(8,128)(2,1)} %bitcast.173, bf16[3,1280,3,80]{1,3,2,0:T(8,128)(2,1)} %collective-permute-done.1, ...), kind=kLoop, calls=%fused_computation.23 | loop fusion | flops 11059200 | bytes 14745612 | tf_op jit(solution)/shard_map/jit(_where)/select_n | solution.py:37
  56.9 5.5 %pad_maximum_fusion = bf16[3,1280,3,320]{1,3,2,0:T(8,128)(2,1)S(1)} fusion(bf16[3,1280,3,80]{1,3,2,0:T(8,128)(2,1)S(1)} %get-tuple-element.14, bf16[3,1280,3,80]{1,3,2,0:T(8,128)(2,1)S(1)} %get-tuple-element.15, bf16[3,1280,3,80]{1,3,2,0:T(8,128)(2,1)S(1)} %get-tuple-element.16, bf16[3,1280,3,80]{1,3,2,0:T(8,128)(2,1)S(1)} %get-tuple-element.13), kind=kLoop, calls=%fused_computation.3 | loop fusion | flops 29491200 | bytes 14745600 | tf_op jit(solution)/shard_map/concatenate | solution.py:39
  62.4 3.2 %fusion.49 = (bf16[1,1280,3,320]{1,3,2,0:T(8,128)(2,1)}, bf16[1,1280,3,320]{1,3,2,0:T(8,128)(2,1)}, bf16[1,1280,3,320]{1,3,2,0:T(8,128)(2,1)}) fusion(bf16[3,1280,3,320]{1,3,2,0:T(8,128)(2,1)S(1)} %pad_maximum_fusion), kind=kLoop, calls=%fused_computation.102 | loop fusion | bytes 14745600 | tf_op jit(solution)/shard_map/slice | solution.py:146
  65.6 40.9 %all-gather.4.cloned.1.call-done = bf16[1,4,8,32,1280]{4,3,2,0,1:T(8,128)(2,1)} async-done(((bf16[1,1,8,32,1280]{4,3,2,0,1:T(8,128)(2,1)}), bf16[1,4,8,32,1280]{4,3,2,0,1:T(8,128)(2,1)}) %all-gather.4.cloned.1.call-update) | async-done | bytes 2621456 | tf_op jit(solution)/shard_map/all_gather | solution.py:107
  106.5 2.6 %convert_reduce_fusion = (f32[1280]{0:T(1024)S(1)}, f32[1280]{0:T(1024)S(1)}) fusion(bf16[1,4,8,32,1280]{4,3,2,0,1:T(8,128)(2,1)} %all-gather.4.cloned.1.call-done), kind=kLoop, calls=%fused_computation.2 | loop fusion | flops 5240320 | bytes 2631680 | tf_op jit(solution)/shard_map/reduce_sum | solution.py:121
  109.5 1.5 collective-permute-start
  111.1 1.3 collective-permute-start.5
  112.4 6.0 %collective-permute-start.4 = (bf16[1,4,1,32,1280]{4,3,2,0,1:T(8,128)(2,1)S(1)}, bf16[1,4,1,32,1280]{4,3,2,0,1:T(8,128)(2,1)}, u32[]{:S(2)}, u32[]{:S(2)}) collective-permute-start(bf16[1,4,1,32,1280]{4,3,2,0,1:T(8,128)(2,1)S(1)} %get-tuple-element.29), channel_id=1, source_target_pairs={{0,1},{2,3},{4,5},{6,7},{8,9},{10,11},{12,13},{14,15},{16,17},{18,... | collective-permute-start | bytes 983048 | tf_op jit(solution)/shard_map/ppermute | solution.py:113
  118.8 1.8 fusion.10
  120.6 2.6 %fusion.58 = f32[4,7,32,960]{3,2,1,0:T(8,128)S(1)} fusion(bf16[4,8,32,1280]{3,2,1,0:T(8,128)(2,1)S(1)} %fusion.10, bf16[1280,960,1,1]{0,1,3,2:T(8,128)(2,1)S(1)} %bitcast.169), kind=kOutput, calls=%fused_computation.111 | convolution fusion | flops 2202009600 | bytes 8519680 | tf_op jit(solution)/shard_map/frxc,cn->frxn/dot_general | solution.py:145
  123.2 2.9 %fusion.11 = f32[4,8,32,960]{3,2,1,0:T(8,128)S(1)} fusion(bf16[1280,960,1,1]{0,1,3,2:T(8,128)(2,1)S(1)} %bitcast.167, bf16[4,8,32,1280]{3,2,1,0:T(8,128)(2,1)S(1)} %fusion.10), kind=kOutput, calls=%fused_computation.18 | convolution fusion | flops 2202009600 | bytes 8683520 | tf_op jit(solution)/shard_map/jit(_pad)/pad | solution.py:150
  126.1 1.9 convolution_bitcast_fusion
  128.0 2.0 convolution_bitcast_fusion.1
  130.1 2.9 %pad_add_fusion = f32[4,8,32,960]{3,2,1,0:T(8,128)S(1)} fusion(f32[4,1,32,960]{3,2,1,0:T(8,128)S(1)} %convolution_bitcast_fusion, f32[4,1,32,960]{3,2,1,0:T(8,128)S(1)} %convolution_bitcast_fusion.1, f32[4,7,32,960]{3,2,1,0:T(8,128)S(1)} %fusion.58, f32[4,8,32,960]{3,2,1,0:T(8,128)S(1)} %fusion.11, bf16[4,8,32,1280]{3,2,1,0:T(8,128)(2,1)S(1)} %fusion.10, ...), kind=kOutput, calls=%fused_computation.15 | convolution fusion | flops 2520514560 | bytes 17367040 | tf_op jit(solution)/shard_map/frxc,cn->frxn/dot_general | solution.py:145
  134.7 3.5 %collective-permute-done.6 = f32[2,8]{1,0:T(2,128)S(1)} collective-permute-done((f32[2,8]{1,0:T(2,128)S(1)}, f32[2,8]{1,0:T(2,128)S(1)}, u32[]{:S(2)}, u32[]{:S(2)}) %collective-permute-start.6) | collective-permute-done | bytes 96 | tf_op jit(solution)/shard_map/ppermute | solution.py:18
  138.5 1.4 multiply_convert_fusion
  140.0 1.5 collective-permute-start.8
  141.5 12.1 %collective-permute-done.8 = bf16[3,1280,80]{1,2,0:T(8,128)(2,1)} collective-permute-done((bf16[3,1280,80]{1,2,0:T(8,128)(2,1)S(1)}, bf16[3,1280,80]{1,2,0:T(8,128)(2,1)}, u32[]{:S(2)}, u32[]{:S(2)}) %collective-permute-start.8) | collective-permute-done | bytes 614432 | tf_op jit(solution)/shard_map/ppermute | solution.py:28
  154.3 1.5 copy.104
  155.9 1.5 copy.106
  157.4 2.2 copy.105
  159.6 1.7 select_select_fusion.7
  161.3 2.8 %pad_maximum_fusion.1 = bf16[3,1280,320]{2,1,0:T(8,128)(2,1)S(1)} fusion(bf16[3,1280,80]{2,1,0:T(8,128)(2,1)S(1)} %get-tuple-element.22, bf16[3,1280,80]{2,1,0:T(8,128)(2,1)S(1)} %get-tuple-element.23, bf16[3,1280,80]{2,1,0:T(8,128)(2,1)S(1)} %get-tuple-element.24, bf16[3,1280,80]{2,1,0:T(8,128)(2,1)S(1)} %get-tuple-element.21), kind=kLoop, calls=%fused_computation.16 | loop fusion | flops 9830400 | bytes 4915200 | tf_op jit(solution)/shard_map/concatenate | solution.py:39
  167.6 33.9 %all-gather.6.cloned.1.call-done = bf16[16,8,32,320]{3,2,1,0:T(8,128)(2,1)} async-done(((bf16[4,8,32,320]{3,2,1,0:T(8,128)(2,1)}), bf16[16,8,32,320]{3,2,1,0:T(8,128)(2,1)}) %all-gather.6.cloned.1.call-update) | async-done | bytes 2621456 | tf_op jit(solution)/shard_map/all_gather | solution.py:193
  201.5 2.6 %fusion.61 = f32[4,8,32,960]{3,2,1,0:T(8,128)S(1)} fusion(bf16[16,8,32,320]{3,2,1,0:T(8,128)(2,1)} %all-gather.6.cloned.1.call-done, bf16[320,960,1,1]{0,1,3,2:T(8,128)(2,1)S(1)} %bitcast.161), kind=kOutput, calls=%fused_computation.114 | convolution fusion | flops 629145600 | bytes 7168000 | tf_op jit(solution)/shard_map/frxc,cn->frxn/dot_general | solution.py:199
  206.6 1.4 add_add_fusion
  209.1 1.3 collective-permute-start.11
  210.4 2.7 %collective-permute-start.12 = (bf16[1,8,32,320]{3,2,1,0:T(8,128)(2,1)S(1)}, bf16[1,8,32,320]{3,2,1,0:T(8,128)(2,1)S(1)}, u32[]{:S(2)}, u32[]{:S(2)}) collective-permute-start(bf16[1,8,32,320]{3,2,1,0:T(8,128)(2,1)S(1)} %get-tuple-element.35), channel_id=1, source_target_pairs={{0,6},{2,0},{4,2},{6,4},{1,7},{3,1},{5,3},{7,5},{8,14},{10,8},{12,... | collective-permute-start | bytes 491528 | tf_op jit(solution)/shard_map/ppermute | solution.py:216
  213.0 5.7 %collective-permute-done.10 = bf16[1,8,32,320]{3,2,1,0:T(8,128)(2,1)S(1)} collective-permute-done((bf16[1,8,32,320]{3,2,1,0:T(8,128)(2,1)S(1)}, bf16[1,8,32,320]{3,2,1,0:T(8,128)(2,1)S(1)}, u32[]{:S(2)}, u32[]{:S(2)}) %collective-permute-start.10) | collective-permute-done | bytes 163872 | tf_op jit(solution)/shard_map/ppermute | solution.py:216
  218.7 7.2 %collective-permute-done.11 = bf16[1,8,32,320]{3,2,1,0:T(8,128)(2,1)S(1)} collective-permute-done((bf16[1,8,32,320]{3,2,1,0:T(8,128)(2,1)S(1)}, bf16[1,8,32,320]{3,2,1,0:T(8,128)(2,1)S(1)}, u32[]{:S(2)}, u32[]{:S(2)}) %collective-permute-start.11) | collective-permute-done | bytes 163872 | tf_op jit(solution)/shard_map/ppermute | solution.py:216
  (114 shorter events, 19.5 us)
Async XLA Ops:
  6.5 99.9 %all-gather.4.cloned.1.call-start = ((), (), s32[]{:S(2)}) async-start(), calls=%async_computation | async-start | bytes 3276800 | tf_op jit(solution)/shard_map/all_gather | solution.py:107
  6.5 43.4 %collective-permute-start.2 = (bf16[3,1280,3,80]{1,3,2,0:T(8,128)(2,1)}, bf16[3,1280,3,80]{1,3,2,0:T(8,128)(2,1)S(1)}, u32[]{:S(2)}, u32[]{:S(2)}) collective-permute-start(bf16[3,1280,3,80]{1,3,2,0:T(8,128)(2,1)} %bitcast.171), channel_id=1, source_target_pairs={{0,16},{8,24},{16,0},{24,8},{1,17},{9,25},{17,1},{25,9},{2,18},{10... | collective-permute-start | bytes 5529608 | tf_op jit(solution)/shard_map/ppermute | solution.py:28
  9.5 43.1 %collective-permute-start.1 = (bf16[3,1280,3,80]{1,3,2,0:T(8,128)(2,1)}, bf16[3,1280,3,80]{1,3,2,0:T(8,128)(2,1)}, u32[]{:S(2)}, u32[]{:S(2)}) collective-permute-start(bf16[3,1280,3,80]{1,3,2,0:T(8,128)(2,1)} %bitcast.172), channel_id=1, source_target_pairs={{0,8},{8,0},{16,24},{24,16},{1,9},{9,1},{17,25},{25,17},{2,10},{10... | collective-permute-start | bytes 5529608 | tf_op jit(solution)/shard_map/ppermute | solution.py:29
  49.9 3.9 %collective-permute-start.3 = (bf16[3,1280,3,80]{1,3,2,0:T(8,128)(2,1)S(1)}, bf16[3,1280,3,80]{1,3,2,0:T(8,128)(2,1)}, u32[]{:S(2)}, u32[]{:S(2)}) collective-permute-start(bf16[3,1280,3,80]{1,3,2,0:T(8,128)(2,1)S(1)} %collective-permute-done.2), channel_id=1, source_target_pairs={{0,8},{8,0},{16,24},{24,16},{1,9},{9,1},{17,25},{25,17},{2,10},{10... | collective-permute-start | bytes 5529608 | tf_op jit(solution)/shard_map/ppermute | solution.py:30
  49.9 151.5 %all-gather.6.cloned.1.call-start = ((), (), s32[]{:S(2)}) async-start(), calls=%async_computation.1 | async-start | bytes 3932160 | tf_op jit(solution)/shard_map/all_gather | solution.py:193
  65.6 53.2 %copy-start.9 = (f32[1280]{0:T(1024)S(1)}, f32[1280]{0:T(1024)}, u32[]{:S(2)}) copy-start(f32[1280]{0:T(1024)} %param.13) | copy-start | bytes 15364
  65.6 53.2 %copy-start.10 = (f32[1280]{0:T(1024)S(1)}, f32[1280]{0:T(1024)}, u32[]{:S(2)}) copy-start(f32[1280]{0:T(1024)} %param.12) | copy-start | bytes 15364
  106.5 4.6 %copy-start = (bf16[1,4,8,32,1280]{4,3,2,0,1:T(8,128)(2,1)S(1)}, bf16[1,4,8,32,1280]{4,3,2,0,1:T(8,128)(2,1)}, u32[]{:S(2)}) copy-start(bf16[1,4,8,32,1280]{4,3,2,0,1:T(8,128)(2,1)} %all-gather.4.cloned.1.call-done) | copy-start | bytes 7864324
  109.5 8.9 %collective-permute-start = (f32[2,32]{1,0:T(2,128)S(1)}, f32[2,32]{1,0:T(2,128)S(1)}, u32[]{:S(2)}, u32[]{:S(2)}) collective-permute-start(f32[2,32]{1,0:T(2,128)S(1)} %pad_maximum_fusion.2), channel_id=1, source_target_pairs={{0,1},{1,0},{2,3},{3,2},{4,5},{5,4},{6,7},{7,6},{8,9},{9,8},{10,11... | collective-permute-start | bytes 776 | tf_op jit(solution)/shard_map/ppermute | solution.py:18
  111.1 15.0 %collective-permute-start.5 = (bf16[1,4,1,32,1280]{4,3,2,0,1:T(8,128)(2,1)S(1)}, bf16[1,4,1,32,1280]{4,3,2,0,1:T(8,128)(2,1)}, u32[]{:S(2)}, u32[]{:S(2)}) collective-permute-start(bf16[1,4,1,32,1280]{4,3,2,0,1:T(8,128)(2,1)S(1)} %get-tuple-element.30), channel_id=1, source_target_pairs={{1,0},{3,2},{5,4},{7,6},{9,8},{11,10},{13,12},{15,14},{17,16},{19,... | collective-permute-start | bytes 983048 | tf_op jit(solution)/shard_map/ppermute | solution.py:114
  112.4 15.6 %collective-permute-start.4 = (bf16[1,4,1,32,1280]{4,3,2,0,1:T(8,128)(2,1)S(1)}, bf16[1,4,1,32,1280]{4,3,2,0,1:T(8,128)(2,1)}, u32[]{:S(2)}, u32[]{:S(2)}) collective-permute-start(bf16[1,4,1,32,1280]{4,3,2,0,1:T(8,128)(2,1)S(1)} %get-tuple-element.29), channel_id=1, source_target_pairs={{0,1},{2,3},{4,5},{6,7},{8,9},{10,11},{12,13},{14,15},{16,17},{18,... | collective-permute-start | bytes 983048 | tf_op jit(solution)/shard_map/ppermute | solution.py:113
  118.8 1.8 copy-start.7
  120.6 2.6 %copy-start.6 = (bf16[1,1280,3,320]{1,3,2,0:T(8,128)(2,1)S(1)}, bf16[1,1280,3,320]{1,3,2,0:T(8,128)(2,1)}, u32[]{:S(2)}) copy-start(bf16[1,1280,3,320]{1,3,2,0:T(8,128)(2,1)} %get-tuple-element.12) | copy-start | bytes 7372804
  128.0 2.0 copy-start.5
  134.1 5.9 %copy-start.8 = (bf16[3,1280,80]{1,2,0:T(8,128)(2,1)S(1)}, bf16[3,1280,80]{1,2,0:T(8,128)(2,1)}, u32[]{:S(2)}) copy-start(bf16[3,1280,80]{1,2,0:T(8,128)(2,1)} %param.11) | copy-start | bytes 1843204
  134.6 3.6 %collective-permute-start.6 = (f32[2,8]{1,0:T(2,128)S(1)}, f32[2,8]{1,0:T(2,128)S(1)}, u32[]{:S(2)}, u32[]{:S(2)}) collective-permute-start(f32[2,8]{1,0:T(2,128)S(1)} %pad_maximum_fusion.3), channel_id=1, source_target_pairs={{0,1},{1,0},{2,3},{3,2},{4,5},{5,4},{6,7},{7,6},{8,9},{9,8},{10,11... | collective-permute-start | bytes 200 | tf_op jit(solution)/shard_map/ppermute | solution.py:18
  140.0 13.6 %collective-permute-start.8 = (bf16[3,1280,80]{1,2,0:T(8,128)(2,1)S(1)}, bf16[3,1280,80]{1,2,0:T(8,128)(2,1)}, u32[]{:S(2)}, u32[]{:S(2)}) collective-permute-start(bf16[3,1280,80]{1,2,0:T(8,128)(2,1)S(1)} %copy-done.8), channel_id=1, source_target_pairs={{0,16},{8,24},{16,0},{24,8},{1,17},{9,25},{17,1},{25,9},{2,18},{10... | collective-permute-start | bytes 1843208 | tf_op jit(solution)/shard_map/ppermute | solution.py:28
  141.5 14.3 %collective-permute-start.7 = (bf16[3,1280,80]{1,2,0:T(8,128)(2,1)S(1)}, bf16[3,1280,80]{1,2,0:T(8,128)(2,1)}, u32[]{:S(2)}, u32[]{:S(2)}) collective-permute-start(bf16[3,1280,80]{1,2,0:T(8,128)(2,1)S(1)} %copy-done.8), channel_id=1, source_target_pairs={{0,8},{8,0},{16,24},{24,16},{1,9},{9,1},{17,25},{25,17},{2,10},{10... | collective-permute-start | bytes 1843208 | tf_op jit(solution)/shard_map/ppermute | solution.py:29
  153.6 3.8 %collective-permute-start.9 = (bf16[3,1280,80]{1,2,0:T(8,128)(2,1)}, bf16[3,1280,80]{1,2,0:T(8,128)(2,1)}, u32[]{:S(2)}, u32[]{:S(2)}) collective-permute-start(bf16[3,1280,80]{1,2,0:T(8,128)(2,1)} %collective-permute-done.8), channel_id=1, source_target_pairs={{0,8},{8,0},{16,24},{24,16},{1,9},{9,1},{17,25},{25,17},{2,10},{10... | collective-permute-start | bytes 1843208 | tf_op jit(solution)/shard_map/ppermute | solution.py:30
  165.7 35.8 %copy-start.2 = (bf16[3,320,320]{1,2,0:T(8,128)(2,1)S(1)}, bf16[3,320,320]{1,2,0:T(8,128)(2,1)}, u32[]{:S(2)}) copy-start(bf16[3,320,320]{1,2,0:T(8,128)(2,1)} %copy.124) | copy-start | bytes 1843204
  201.4 2.6 %copy-start.1 = (bf16[16,8,32,320]{3,2,1,0:T(8,128)(2,1)S(1)}, bf16[16,8,32,320]{3,2,1,0:T(8,128)(2,1)}, u32[]{:S(2)}) copy-start(bf16[16,8,32,320]{3,2,1,0:T(8,128)(2,1)} %all-gather.6.cloned.1.call-done) | copy-start | bytes 7864324
  201.5 2.6 %copy-start.3 = (bf16[3,320,320]{1,2,0:T(8,128)(2,1)S(1)}, bf16[3,320,320]{1,2,0:T(8,128)(2,1)}, u32[]{:S(2)}) copy-start(bf16[3,320,320]{1,2,0:T(8,128)(2,1)} %copy.120) | copy-start | bytes 1843204
  209.0 9.7 %collective-permute-start.10 = (bf16[1,8,32,320]{3,2,1,0:T(8,128)(2,1)S(1)}, bf16[1,8,32,320]{3,2,1,0:T(8,128)(2,1)S(1)}, u32[]{:S(2)}, u32[]{:S(2)}) collective-permute-start(bf16[1,8,32,320]{3,2,1,0:T(8,128)(2,1)S(1)} %get-tuple-element.37), channel_id=1, source_target_pairs={{0,2},{2,4},{4,6},{6,0},{1,3},{3,5},{5,7},{7,1},{8,10},{10,12},{12... | collective-permute-start | bytes 491528 | tf_op jit(solution)/shard_map/ppermute | solution.py:216
  209.1 16.8 %collective-permute-start.11 = (bf16[1,8,32,320]{3,2,1,0:T(8,128)(2,1)S(1)}, bf16[1,8,32,320]{3,2,1,0:T(8,128)(2,1)S(1)}, u32[]{:S(2)}, u32[]{:S(2)}) collective-permute-start(bf16[1,8,32,320]{3,2,1,0:T(8,128)(2,1)S(1)} %get-tuple-element.36), channel_id=1, source_target_pairs={{0,4},{2,6},{4,0},{6,2},{1,5},{3,7},{5,1},{7,3},{8,12},{10,14},{12... | collective-permute-start | bytes 491528 | tf_op jit(solution)/shard_map/ppermute | solution.py:216
  210.4 15.5 %collective-permute-start.12 = (bf16[1,8,32,320]{3,2,1,0:T(8,128)(2,1)S(1)}, bf16[1,8,32,320]{3,2,1,0:T(8,128)(2,1)S(1)}, u32[]{:S(2)}, u32[]{:S(2)}) collective-permute-start(bf16[1,8,32,320]{3,2,1,0:T(8,128)(2,1)S(1)} %get-tuple-element.35), channel_id=1, source_target_pairs={{0,6},{2,0},{4,2},{6,4},{1,7},{3,1},{5,3},{7,5},{8,14},{10,8},{12,... | collective-permute-start | bytes 491528 | tf_op jit(solution)/shard_map/ppermute | solution.py:216
  228.5 1.4 copy-start.4
  228.5 1.4 copy-start.11
Sparse Core Ops, SparseCore 0:
  50.0 56.3 all-gather.3
  140.1 61.2 all-gather.5

commit v10 on v9

--- a/solution.py
+++ b/solution.py
@@ -18,6 +18,18 @@
             lambda v: v + lax.ppermute(v, axis, [(0, 1), (1, 0)]), value
         )
     return lax.psum(value, axis)
+
+
+def butterfly_sum(value, axis):
+    size = lax.axis_size(axis)
+    if size & (size - 1) != 0:
+        return lax.psum(value, axis)
+    step = 1
+    while step < size:
+        pairs = [(k, k ^ step) for k in range(size)]
+        value = jax.tree.map(lambda v: v + lax.ppermute(v, axis, pairs), value)
+        step *= 2
+    return value
 
 
 def gather_rep(w):
@@ -116,13 +128,13 @@
         above = jnp.zeros_like(raw[:, :, :1])
         below = jnp.zeros_like(raw[:, :, :1])
 
-    grouped = raw.astype(jnp.float32).reshape(1, -1, GROUPS, width)
+    grouped = activations.astype(jnp.float32).reshape(1, -1, GROUPS, width)
     stats = jnp.concatenate(
         [jnp.sum(grouped, axis=(1, 3)), jnp.sum(grouped * grouped, axis=(1, 3))]
     )
-    stats = pair_sum(stats, "row")
-    sums, squares = stats[:1], stats[1:]
-    count = grouped.shape[1] * width * row_size
+    stats = butterfly_sum(butterfly_sum(stats, "frame"), "row")
+    sums, squares = stats[:1] * 1.0, stats[1:]
+    count = grouped.shape[1] * width * frame_size * row_size
     mean = sums / count
     variance = squares / count - mean * mean
     inverse = lax.rsqrt(variance + EPS)

time: 239 us -> 234 us (0.979)
  waiting for transfers between devices: 145 us -> 137 us
  starting transfers between devices: 17.5 us -> 21 us
    all_gather x1, waiting for transfers between devices: 40.9 us -> 30.6 us  [shards(): raw = lax.all_gather(activations, 'frame', axis=1, tiled=True)]
    ppermute x0 -> x3, starting transfers between devices: none -> 6.13 us  [butterfly_sum(): value = jax.tree.map(lambda v: v + lax.ppermute(v, axis, pairs), value)]
    ppermute x0 -> x3, waiting for transfers between devices: none -> 3.75 us  [butterfly_sum(): value = jax.tree.map(lambda v: v + lax.ppermute(v, axis, pairs), value)]
  transfers between devices with their start and end apart: 15 -> 17, of which waited for: 8 -> 9; matrix products, arithmetic and copies ran while one was open for 16% -> 17% of each run, Pallas kernels for 0% -> 0%
where the time goes in v10:
time: 234 us; the launch traced here: 233 us
  waiting for transfers between devices  137 us (59%)
  other arithmetic  22.5 us (10%)
  local copies, waits for them, and re-layouts  21.3 us (9%)
  starting transfers between devices  21 us (9%)
  matrix products  16.7 us (7%)
  between operations  14.1 us (6%)
    ppermute x2, waiting for transfers between devices, gather_rep(): across = lax.ppermute(w, 'rep', [(k, k ^ 2) for k in range(size)])  52.8 us
    all_gather x1, waiting for transfers between devices, shards(): second_all = lax.all_gather(second[0], 'frame', axis=0, tiled=False)  33.6 us
    all_gather x1, waiting for transfers between devices, shards(): raw = lax.all_gather(activations, 'frame', axis=1, tiled=True)  30.6 us
    ppermute x3, waiting for transfers between devices, shards(): lax.ppermute(piece, 'frame', [(k, (k + shift) % frame_size) for k in rang...  12.9 us
    concatenate x2, other arithmetic, gather_rep(): return jnp.concatenate(blocks, axis=-1)  8.27 us
    dot_general x4, matrix products, tap(): jnp.einsum('frxc,cn->frxn', field, wide[row_tap], preferred_element_type=...  7.32 us
    dot_general x4, matrix products, shards(): jnp.einsum('frxc,cn->frxn', second_all[group], weights, preferred_element...  6.53 us
    ppermute x3, starting transfers between devices, butterfly_sum(): value = jax.tree.map(lambda v: v + lax.ppermute(v, axis, pairs), value)  6.13 us
  transfers between devices with their start and end apart: 17, of which 9 were waited for; matrix products, arithmetic and copies ran while one was open for 17% of the time, Pallas kernels for 0%

profile of v10, /device:TPU:0, one launch (start us, length us, event | category | flops | bytes accessed | tf_op | source)
XLA Modules:
  0.0 232.7 jit_solution(14292458992353890672)
XLA Ops:
  6.5 3.0 %collective-permute-start.4 = (bf16[3,1280,3,80]{1,3,2,0:T(8,128)(2,1)}, bf16[3,1280,3,80]{1,3,2,0:T(8,128)(2,1)S(1)}, u32[]{:S(2)}, u32[]{:S(2)}) collective-permute-start(bf16[3,1280,3,80]{1,3,2,0:T(8,128)(2,1)} %bitcast.169), channel_id=1, source_target_pairs={{0,16},{8,24},{16,0},{24,8},{1,17},{9,25},{17,1},{25,9},{2,18},{10... | collective-permute-start | bytes 5529608 | tf_op jit(solution)/shard_map/ppermute | solution.py:40
  9.5 40.4 %collective-permute-done.4 = bf16[3,1280,3,80]{1,3,2,0:T(8,128)(2,1)S(1)} collective-permute-done((bf16[3,1280,3,80]{1,3,2,0:T(8,128)(2,1)}, bf16[3,1280,3,80]{1,3,2,0:T(8,128)(2,1)S(1)}, u32[]{:S(2)}, u32[]{:S(2)}) %collective-permute-start.4) | collective-permute-done | bytes 1843232 | tf_op jit(solution)/shard_map/ppermute | solution.py:40
  51.7 1.9 collective-permute-start
  56.0 2.7 %collective-permute-start.1 = (f32[2,32]{1,0:T(2,128)S(1)}, f32[2,32]{1,0:T(2,128)S(1)}, u32[]{:S(2)}, u32[]{:S(2)}) collective-permute-start(f32[2,32]{1,0:T(2,128)S(1)} %fusion.37), channel_id=1, source_target_pairs={{0,4},{2,6},{4,0},{6,2},{1,5},{3,7},{5,1},{7,3},{8,12},{10,14},{12... | collective-permute-start | bytes 776 | tf_op jit(solution)/shard_map/ppermute | solution.py:30
  58.6 1.9 collective-permute-done.1
  60.5 1.6 collective-permute-start.2
  62.3 1.9 collective-permute-done.2
  64.5 3.1 %select_select_fusion.3 = (bf16[3,1280,3,80]{1,3,2,0:T(8,128)(2,1)S(1)}, bf16[3,1280,3,80]{1,3,2,0:T(8,128)(2,1)S(1)}, bf16[3,1280,3,80]{1,3,2,0:T(8,128)(2,1)S(1)}, bf16[3,1280,3,80]{1,3,2,0:T(8,128)(2,1)S(1)}) fusion(bf16[3,1280,3,80]{1,3,2,0:T(8,128)(2,1)} %bitcast.171, bf16[3,1280,3,80]{1,3,2,0:T(8,128)(2,1)} %collective-permute-done.3, ...), kind=kLoop, calls=%fused_computation.14 | loop fusion | flops 11059200 | bytes 14745612 | tf_op jit(solution)/shard_map/jit(_where)/select_n | solution.py:49
  67.6 5.5 %pad_maximum_fusion = bf16[3,1280,3,320]{1,3,2,0:T(8,128)(2,1)S(1)} fusion(bf16[3,1280,3,80]{1,3,2,0:T(8,128)(2,1)S(1)} %get-tuple-element.14, bf16[3,1280,3,80]{1,3,2,0:T(8,128)(2,1)S(1)} %get-tuple-element.15, bf16[3,1280,3,80]{1,3,2,0:T(8,128)(2,1)S(1)} %get-tuple-element.16, bf16[3,1280,3,80]{1,3,2,0:T(8,128)(2,1)S(1)} %get-tuple-element.13), kind=kLoop, calls=%fused_computation | loop fusion | flops 29491200 | bytes 14745600 | tf_op jit(solution)/shard_map/concatenate | solution.py:51
  73.1 2.7 %fusion.40 = (bf16[1,1280,3,320]{1,3,2,0:T(8,128)(2,1)S(1)}, bf16[1,1280,3,320]{1,3,2,0:T(8,128)(2,1)}, bf16[1,1280,3,320]{1,3,2,0:T(8,128)(2,1)}) fusion(bf16[3,1280,3,320]{1,3,2,0:T(8,128)(2,1)S(1)} %pad_maximum_fusion), kind=kLoop, calls=%fused_computation.93 | loop fusion | bytes 14745600 | tf_op jit(solution)/shard_map/slice | solution.py:158
  75.9 30.6 %all-gather.4.cloned.1.call-done = bf16[1,4,8,32,1280]{4,3,2,0,1:T(8,128)(2,1)} async-done(((bf16[1,1,8,32,1280]{4,3,2,0,1:T(8,128)(2,1)}), bf16[1,4,8,32,1280]{4,3,2,0,1:T(8,128)(2,1)}) %all-gather.4.cloned.1.call-update) | async-done | bytes 2621456 | tf_op jit(solution)/shard_map/all_gather | solution.py:119
  107.6 1.3 collective-permute-start.7
  108.9 4.9 %collective-permute-start.6 = (bf16[1,4,1,32,1280]{4,3,2,0,1:T(8,128)(2,1)S(1)}, bf16[1,4,1,32,1280]{4,3,2,0,1:T(8,128)(2,1)S(1)}, u32[]{:S(2)}, u32[]{:S(2)}) collective-permute-start(bf16[1,4,1,32,1280]{4,3,2,0,1:T(8,128)(2,1)S(1)} %get-tuple-element.29), channel_id=1, source_target_pairs={{0,1},{2,3},{4,5},{6,7},{8,9},{10,11},{12,13},{14,15},{16,17},{18,... | collective-permute-start | bytes 983048 | tf_op jit(solution)/shard_map/ppermute | solution.py:125
  113.8 3.5 %fusion = bf16[4,8,32,1280]{3,2,1,0:T(8,128)(2,1)S(1)} fusion(bf16[1,4,8,32,1280]{4,3,2,0,1:T(8,128)(2,1)} %all-gather.4.cloned.1.call-done, f32[1280]{0:T(1024)S(1)} %copy-done.7, f32[1280]{0:T(1024)S(1)} %copy-done.8, f32[1280]{0:T(1024)S(1)} %mul.103, f32[1280]{0:T(1024)S(1)} %sub.50), kind=kLoop, calls=%fused_computation.5 | loop fusion | flops 13107200 | bytes 5263360 | tf_op jit(solution)/shard_map/squeeze | solution.py:148
  117.4 2.6 %fusion.49 = f32[4,7,32,960]{3,2,1,0:T(8,128)S(1)} fusion(bf16[4,8,32,1280]{3,2,1,0:T(8,128)(2,1)S(1)} %fusion, bf16[1280,960,1,1]{0,1,3,2:T(8,128)(2,1)S(1)} %bitcast.167), kind=kOutput, calls=%fused_computation.102 | convolution fusion | flops 2202009600 | bytes 8519680 | tf_op jit(solution)/shard_map/frxc,cn->frxn/dot_general | solution.py:157
  120.0 2.9 %fusion.1 = f32[4,8,32,960]{3,2,1,0:T(8,128)S(1)} fusion(bf16[1280,960,1,1]{0,1,3,2:T(8,128)(2,1)S(1)} %bitcast.165, bf16[4,8,32,1280]{3,2,1,0:T(8,128)(2,1)S(1)} %fusion), kind=kOutput, calls=%fused_computation.6 | convolution fusion | flops 2202009600 | bytes 8683520 | tf_op jit(solution)/shard_map/jit(_pad)/pad | solution.py:162
  124.7 2.9 %pad_add_fusion = f32[4,8,32,960]{3,2,1,0:T(8,128)S(1)} fusion(f32[4,1,32,960]{3,2,1,0:T(8,128)S(1)} %convolution_bitcast_fusion, f32[4,1,32,960]{3,2,1,0:T(8,128)S(1)} %convolution_bitcast_fusion.1, f32[4,7,32,960]{3,2,1,0:T(8,128)S(1)} %fusion.49, f32[4,8,32,960]{3,2,1,0:T(8,128)S(1)} %fusion.1, bf16[4,8,32,1280]{3,2,1,0:T(8,128)(2,1)S(1)} %fusion, ...), kind=kOutput, calls=%fused_computation.3 | convolution fusion | flops 2520514560 | bytes 17367040 | tf_op jit(solution)/shard_map/frxc,cn->frxn/dot_general | solution.py:157
  129.4 3.5 %collective-permute-done.8 = f32[2,8]{1,0:T(2,128)S(1)} collective-permute-done((f32[2,8]{1,0:T(2,128)S(1)}, f32[2,8]{1,0:T(2,128)S(1)}, u32[]{:S(2)}, u32[]{:S(2)}) %collective-permute-start.8) | collective-permute-done | bytes 96 | tf_op jit(solution)/shard_map/ppermute | solution.py:18
  133.2 1.4 multiply_convert_fusion.1
  134.7 1.5 collective-permute-start.10
  136.2 12.4 %collective-permute-done.10 = bf16[3,1280,80]{1,2,0:T(8,128)(2,1)} collective-permute-done((bf16[3,1280,80]{1,2,0:T(8,128)(2,1)S(1)}, bf16[3,1280,80]{1,2,0:T(8,128)(2,1)}, u32[]{:S(2)}, u32[]{:S(2)}) %collective-permute-start.10) | collective-permute-done | bytes 614432 | tf_op jit(solution)/shard_map/ppermute | solution.py:40
  149.3 1.5 copy.104
  150.8 1.5 copy.106
  152.4 2.2 copy.105
  154.6 1.7 select_select_fusion.7
  156.2 2.8 %pad_maximum_fusion.1 = bf16[3,1280,320]{2,1,0:T(8,128)(2,1)S(1)} fusion(bf16[3,1280,80]{2,1,0:T(8,128)(2,1)S(1)} %get-tuple-element.22, bf16[3,1280,80]{2,1,0:T(8,128)(2,1)S(1)} %get-tuple-element.23, bf16[3,1280,80]{2,1,0:T(8,128)(2,1)S(1)} %get-tuple-element.24, bf16[3,1280,80]{2,1,0:T(8,128)(2,1)S(1)} %get-tuple-element.21), kind=kLoop, calls=%fused_computation.4 | loop fusion | flops 9830400 | bytes 4915200 | tf_op jit(solution)/shard_map/concatenate | solution.py:51
  162.5 33.6 %all-gather.6.cloned.1.call-done = bf16[16,8,32,320]{3,2,1,0:T(8,128)(2,1)} async-done(((bf16[4,8,32,320]{3,2,1,0:T(8,128)(2,1)}), bf16[16,8,32,320]{3,2,1,0:T(8,128)(2,1)}) %all-gather.6.cloned.1.call-update) | async-done | bytes 2621456 | tf_op jit(solution)/shard_map/all_gather | solution.py:205
  196.1 2.6 %fusion.52 = f32[4,8,32,960]{3,2,1,0:T(8,128)S(1)} fusion(bf16[16,8,32,320]{3,2,1,0:T(8,128)(2,1)} %all-gather.6.cloned.1.call-done, bf16[320,960,1,1]{0,1,3,2:T(8,128)(2,1)S(1)} %bitcast.160), kind=kOutput, calls=%fused_computation.105 | convolution fusion | flops 629145600 | bytes 7168000 | tf_op jit(solution)/shard_map/frxc,cn->frxn/dot_general | solution.py:211
  201.3 1.4 add_add_fusion
  205.0 2.7 %collective-permute-start.14 = (bf16[1,8,32,320]{3,2,1,0:T(8,128)(2,1)S(1)}, bf16[1,8,32,320]{3,2,1,0:T(8,128)(2,1)S(1)}, u32[]{:S(2)}, u32[]{:S(2)}) collective-permute-start(bf16[1,8,32,320]{3,2,1,0:T(8,128)(2,1)S(1)} %get-tuple-element.35), channel_id=1, source_target_pairs={{0,6},{2,0},{4,2},{6,4},{1,7},{3,1},{5,3},{7,5},{8,14},{10,8},{12,... | collective-permute-start | bytes 491528 | tf_op jit(solution)/shard_map/ppermute | solution.py:228
  207.7 5.7 %collective-permute-done.12 = bf16[1,8,32,320]{3,2,1,0:T(8,128)(2,1)S(1)} collective-permute-done((bf16[1,8,32,320]{3,2,1,0:T(8,128)(2,1)S(1)}, bf16[1,8,32,320]{3,2,1,0:T(8,128)(2,1)S(1)}, u32[]{:S(2)}, u32[]{:S(2)}) %collective-permute-start.12) | collective-permute-done | bytes 163872 | tf_op jit(solution)/shard_map/ppermute | solution.py:228
  213.4 7.2 %collective-permute-done.13 = bf16[1,8,32,320]{3,2,1,0:T(8,128)(2,1)S(1)} collective-permute-done((bf16[1,8,32,320]{3,2,1,0:T(8,128)(2,1)S(1)}, bf16[1,8,32,320]{3,2,1,0:T(8,128)(2,1)S(1)}, u32[]{:S(2)}, u32[]{:S(2)}) %collective-permute-start.13) | collective-permute-done | bytes 163872 | tf_op jit(solution)/shard_map/ppermute | solution.py:228
  (116 shorter events, 23.8 us)
Async XLA Ops:
  6.5 100.0 %all-gather.4.cloned.1.call-start = ((), (), s32[]{:S(2)}) async-start(), calls=%async_computation | async-start | bytes 3276800 | tf_op jit(solution)/shard_map/all_gather | solution.py:119
  6.5 43.4 %collective-permute-start.4 = (bf16[3,1280,3,80]{1,3,2,0:T(8,128)(2,1)}, bf16[3,1280,3,80]{1,3,2,0:T(8,128)(2,1)S(1)}, u32[]{:S(2)}, u32[]{:S(2)}) collective-permute-start(bf16[3,1280,3,80]{1,3,2,0:T(8,128)(2,1)} %bitcast.169), channel_id=1, source_target_pairs={{0,16},{8,24},{16,0},{24,8},{1,17},{9,25},{17,1},{25,9},{2,18},{10... | collective-permute-start | bytes 5529608 | tf_op jit(solution)/shard_map/ppermute | solution.py:40
  9.5 55.0 %collective-permute-start.3 = (bf16[3,1280,3,80]{1,3,2,0:T(8,128)(2,1)}, bf16[3,1280,3,80]{1,3,2,0:T(8,128)(2,1)}, u32[]{:S(2)}, u32[]{:S(2)}) collective-permute-start(bf16[3,1280,3,80]{1,3,2,0:T(8,128)(2,1)} %bitcast.170), channel_id=1, source_target_pairs={{0,8},{8,0},{16,24},{24,16},{1,9},{9,1},{17,25},{25,17},{2,10},{10... | collective-permute-start | bytes 5529608 | tf_op jit(solution)/shard_map/ppermute | solution.py:41
  49.9 14.6 %collective-permute-start.5 = (bf16[3,1280,3,80]{1,3,2,0:T(8,128)(2,1)S(1)}, bf16[3,1280,3,80]{1,3,2,0:T(8,128)(2,1)}, u32[]{:S(2)}, u32[]{:S(2)}) collective-permute-start(bf16[3,1280,3,80]{1,3,2,0:T(8,128)(2,1)S(1)} %collective-permute-done.4), channel_id=1, source_target_pairs={{0,8},{8,0},{16,24},{24,16},{1,9},{9,1},{17,25},{25,17},{2,10},{10... | collective-permute-start | bytes 5529608 | tf_op jit(solution)/shard_map/ppermute | solution.py:42
  49.9 146.2 %all-gather.6.cloned.1.call-start = ((), (), s32[]{:S(2)}) async-start(), calls=%async_computation.1 | async-start | bytes 3932160 | tf_op jit(solution)/shard_map/all_gather | solution.py:205
  51.7 4.3 %collective-permute-start = (f32[2,32]{1,0:T(2,128)S(1)}, f32[2,32]{1,0:T(2,128)S(1)}, u32[]{:S(2)}, u32[]{:S(2)}) collective-permute-start(f32[2,32]{1,0:T(2,128)S(1)} %pad_maximum_fusion.2), channel_id=1, source_target_pairs={{0,2},{2,0},{4,6},{6,4},{1,3},{3,1},{5,7},{7,5},{8,10},{10,8},{12,... | collective-permute-start | bytes 776 | tf_op jit(solution)/shard_map/ppermute | solution.py:30
  56.0 4.5 %collective-permute-start.1 = (f32[2,32]{1,0:T(2,128)S(1)}, f32[2,32]{1,0:T(2,128)S(1)}, u32[]{:S(2)}, u32[]{:S(2)}) collective-permute-start(f32[2,32]{1,0:T(2,128)S(1)} %fusion.37), channel_id=1, source_target_pairs={{0,4},{2,6},{4,0},{6,2},{1,5},{3,7},{5,1},{7,3},{8,12},{10,14},{12... | collective-permute-start | bytes 776 | tf_op jit(solution)/shard_map/ppermute | solution.py:30
  60.5 3.6 %collective-permute-start.2 = (f32[2,32]{1,0:T(2,128)S(1)}, f32[2,32]{1,0:T(2,128)S(1)}, u32[]{:S(2)}, u32[]{:S(2)}) collective-permute-start(f32[2,32]{1,0:T(2,128)S(1)} %fusion.68), channel_id=1, source_target_pairs={{0,1},{1,0},{2,3},{3,2},{4,5},{5,4},{6,7},{7,6},{8,9},{9,8},{10,11... | collective-permute-start | bytes 776 | tf_op jit(solution)/shard_map/ppermute | solution.py:30
  73.1 40.7 %copy-start.7 = (f32[1280]{0:T(1024)S(1)}, f32[1280]{0:T(1024)}, u32[]{:S(2)}) copy-start(f32[1280]{0:T(1024)} %param.13) | copy-start | bytes 15364
  73.1 40.7 %copy-start.8 = (f32[1280]{0:T(1024)S(1)}, f32[1280]{0:T(1024)}, u32[]{:S(2)}) copy-start(f32[1280]{0:T(1024)} %param.12) | copy-start | bytes 15364
  107.6 15.3 %collective-permute-start.7 = (bf16[1,4,1,32,1280]{4,3,2,0,1:T(8,128)(2,1)S(1)}, bf16[1,4,1,32,1280]{4,3,2,0,1:T(8,128)(2,1)S(1)}, u32[]{:S(2)}, u32[]{:S(2)}) collective-permute-start(bf16[1,4,1,32,1280]{4,3,2,0,1:T(8,128)(2,1)S(1)} %get-tuple-element.30), channel_id=1, source_target_pairs={{1,0},{3,2},{5,4},{7,6},{9,8},{11,10},{13,12},{15,14},{17,16},{19,... | collective-permute-start | bytes 983048 | tf_op jit(solution)/shard_map/ppermute | solution.py:126
  108.9 8.5 %copy-start.5 = (bf16[1,1280,3,320]{1,3,2,0:T(8,128)(2,1)S(1)}, bf16[1,1280,3,320]{1,3,2,0:T(8,128)(2,1)}, u32[]{:S(2)}) copy-start(bf16[1,1280,3,320]{1,3,2,0:T(8,128)(2,1)} %get-tuple-element.11) | copy-start | bytes 7372804
  108.9 14.9 %collective-permute-start.6 = (bf16[1,4,1,32,1280]{4,3,2,0,1:T(8,128)(2,1)S(1)}, bf16[1,4,1,32,1280]{4,3,2,0,1:T(8,128)(2,1)S(1)}, u32[]{:S(2)}, u32[]{:S(2)}) collective-permute-start(bf16[1,4,1,32,1280]{4,3,2,0,1:T(8,128)(2,1)S(1)} %get-tuple-element.29), channel_id=1, source_target_pairs={{0,1},{2,3},{4,5},{6,7},{8,9},{10,11},{12,13},{14,15},{16,17},{18,... | collective-permute-start | bytes 983048 | tf_op jit(solution)/shard_map/ppermute | solution.py:125
  117.4 2.6 %copy-start.4 = (bf16[1,1280,3,320]{1,3,2,0:T(8,128)(2,1)S(1)}, bf16[1,1280,3,320]{1,3,2,0:T(8,128)(2,1)}, u32[]{:S(2)}) copy-start(bf16[1,1280,3,320]{1,3,2,0:T(8,128)(2,1)} %get-tuple-element.12) | copy-start | bytes 7372804
  128.8 5.9 %copy-start.6 = (bf16[3,1280,80]{1,2,0:T(8,128)(2,1)S(1)}, bf16[3,1280,80]{1,2,0:T(8,128)(2,1)}, u32[]{:S(2)}) copy-start(bf16[3,1280,80]{1,2,0:T(8,128)(2,1)} %param.11) | copy-start | bytes 1843204
  129.3 3.6 %collective-permute-start.8 = (f32[2,8]{1,0:T(2,128)S(1)}, f32[2,8]{1,0:T(2,128)S(1)}, u32[]{:S(2)}, u32[]{:S(2)}) collective-permute-start(f32[2,8]{1,0:T(2,128)S(1)} %pad_maximum_fusion.3), channel_id=1, source_target_pairs={{0,1},{1,0},{2,3},{3,2},{4,5},{5,4},{6,7},{7,6},{8,9},{9,8},{10,11... | collective-permute-start | bytes 200 | tf_op jit(solution)/shard_map/ppermute | solution.py:18
  134.7 13.9 %collective-permute-start.10 = (bf16[3,1280,80]{1,2,0:T(8,128)(2,1)S(1)}, bf16[3,1280,80]{1,2,0:T(8,128)(2,1)}, u32[]{:S(2)}, u32[]{:S(2)}) collective-permute-start(bf16[3,1280,80]{1,2,0:T(8,128)(2,1)S(1)} %copy-done.6), channel_id=1, source_target_pairs={{0,16},{8,24},{16,0},{24,8},{1,17},{9,25},{17,1},{25,9},{2,18},{10... | collective-permute-start | bytes 1843208 | tf_op jit(solution)/shard_map/ppermute | solution.py:40
  136.2 14.6 %collective-permute-start.9 = (bf16[3,1280,80]{1,2,0:T(8,128)(2,1)S(1)}, bf16[3,1280,80]{1,2,0:T(8,128)(2,1)}, u32[]{:S(2)}, u32[]{:S(2)}) collective-permute-start(bf16[3,1280,80]{1,2,0:T(8,128)(2,1)S(1)} %copy-done.6), channel_id=1, source_target_pairs={{0,8},{8,0},{16,24},{24,16},{1,9},{9,1},{17,25},{25,17},{2,10},{10... | collective-permute-start | bytes 1843208 | tf_op jit(solution)/shard_map/ppermute | solution.py:41
  148.6 3.8 %collective-permute-start.11 = (bf16[3,1280,80]{1,2,0:T(8,128)(2,1)}, bf16[3,1280,80]{1,2,0:T(8,128)(2,1)}, u32[]{:S(2)}, u32[]{:S(2)}) collective-permute-start(bf16[3,1280,80]{1,2,0:T(8,128)(2,1)} %collective-permute-done.10), channel_id=1, source_target_pairs={{0,8},{8,0},{16,24},{24,16},{1,9},{9,1},{17,25},{25,17},{2,10},{10... | collective-permute-start | bytes 1843208 | tf_op jit(solution)/shard_map/ppermute | solution.py:42
  160.6 35.5 %copy-start.2 = (bf16[3,320,320]{1,2,0:T(8,128)(2,1)S(1)}, bf16[3,320,320]{1,2,0:T(8,128)(2,1)}, u32[]{:S(2)}) copy-start(bf16[3,320,320]{1,2,0:T(8,128)(2,1)} %copy.124) | copy-start | bytes 1843204
  196.1 2.6 %copy-start = (bf16[16,8,32,320]{3,2,1,0:T(8,128)(2,1)S(1)}, bf16[16,8,32,320]{3,2,1,0:T(8,128)(2,1)}, u32[]{:S(2)}) copy-start(bf16[16,8,32,320]{3,2,1,0:T(8,128)(2,1)} %all-gather.6.cloned.1.call-done) | copy-start | bytes 7864324
  196.1 2.6 %copy-start.3 = (bf16[3,320,320]{1,2,0:T(8,128)(2,1)S(1)}, bf16[3,320,320]{1,2,0:T(8,128)(2,1)}, u32[]{:S(2)}) copy-start(bf16[3,320,320]{1,2,0:T(8,128)(2,1)} %copy.120) | copy-start | bytes 1843204
  203.7 9.7 %collective-permute-start.12 = (bf16[1,8,32,320]{3,2,1,0:T(8,128)(2,1)S(1)}, bf16[1,8,32,320]{3,2,1,0:T(8,128)(2,1)S(1)}, u32[]{:S(2)}, u32[]{:S(2)}) collective-permute-start(bf16[1,8,32,320]{3,2,1,0:T(8,128)(2,1)S(1)} %get-tuple-element.37), channel_id=1, source_target_pairs={{0,2},{2,4},{4,6},{6,0},{1,3},{3,5},{5,7},{7,1},{8,10},{10,12},{12... | collective-permute-start | bytes 491528 | tf_op jit(solution)/shard_map/ppermute | solution.py:228
  203.7 16.8 %collective-permute-start.13 = (bf16[1,8,32,320]{3,2,1,0:T(8,128)(2,1)S(1)}, bf16[1,8,32,320]{3,2,1,0:T(8,128)(2,1)S(1)}, u32[]{:S(2)}, u32[]{:S(2)}) collective-permute-start(bf16[1,8,32,320]{3,2,1,0:T(8,128)(2,1)S(1)} %get-tuple-element.36), channel_id=1, source_target_pairs={{0,4},{2,6},{4,0},{6,2},{1,5},{3,7},{5,1},{7,3},{8,12},{10,14},{12... | collective-permute-start | bytes 491528 | tf_op jit(solution)/shard_map/ppermute | solution.py:228
  205.0 15.5 %collective-permute-start.14 = (bf16[1,8,32,320]{3,2,1,0:T(8,128)(2,1)S(1)}, bf16[1,8,32,320]{3,2,1,0:T(8,128)(2,1)S(1)}, u32[]{:S(2)}, u32[]{:S(2)}) collective-permute-start(bf16[1,8,32,320]{3,2,1,0:T(8,128)(2,1)S(1)} %get-tuple-element.35), channel_id=1, source_target_pairs={{0,6},{2,0},{4,2},{6,4},{1,7},{3,1},{5,3},{7,5},{8,14},{10,8},{12,... | collective-permute-start | bytes 491528 | tf_op jit(solution)/shard_map/ppermute | solution.py:228
  223.2 1.4 copy-start.1
  223.2 1.4 copy-start.9
Sparse Core Ops, SparseCore 0:
  50.0 56.3 all-gather.3
  134.8 61.2 all-gather.5

commit v11 on v10

--- a/solution.py
+++ b/solution.py
@@ -122,8 +122,15 @@
     if row_size > 1:
         down = [(i, i + 1) for i in range(row_size - 1)]
         up = [(i + 1, i) for i in range(row_size - 1)]
-        above = lax.ppermute(raw[:, :, rows - 1 :], "row", down)
-        below = lax.ppermute(raw[:, :, :1], "row", up)
+        edges = jnp.concatenate(
+            [
+                lax.ppermute(activations[:, :, rows - 1 :], "row", down),
+                lax.ppermute(activations[:, :, :1], "row", up),
+            ],
+            axis=2,
+        )
+        edges = lax.all_gather(edges, "frame", axis=1, tiled=True)
+        above, below = edges[:, :, :1], edges[:, :, 1:]
     else:
         above = jnp.zeros_like(raw[:, :, :1])
         below = jnp.zeros_like(raw[:, :, :1])

time: 234 us -> 221 us (0.944)
  waiting for transfers between devices: 137 us -> 108 us
  blocking collectives: 0 us -> 16.9 us
    all_gather x1, waiting for transfers between devices: 30.6 us -> 0.01 us  [shards(): raw = lax.all_gather(activations, 'frame', axis=1, tiled=True)]
    all_gather x0 -> x1, blocking collectives: none -> 16.9 us  [shards(): edges = lax.all_gather(edges, 'frame', axis=1, tiled=True)]
    all_gather x1, waiting for transfers between devices: 33.6 us -> 37.7 us  [shards(): second_all = lax.all_gather(second[0], 'frame', axis=0, tiled=False)]
    ppermute x2, waiting for transfers between devices: 52.8 us -> 49.2 us  [gather_rep(): across = lax.ppermute(w, 'rep', [(k, k ^ 2) for k in range(size)])]
  transfers between devices with their start and end apart: 17 -> 17, of which waited for: 9 -> 8; matrix products, arithmetic and copies ran while one was open for 17% -> 14% of each run, Pallas kernels for 0% -> 0%
where the time goes in v11:
time: 221 us; the launch traced here: 219 us
  waiting for transfers between devices  108 us (49%)
  other arithmetic  23 us (10%)
  local copies, waits for them, and re-layouts  20.1 us (9%)
  starting transfers between devices  19.2 us (9%)
  matrix products  17.5 us (8%)
  blocking collectives  16.9 us (8%)
  between operations  14.1 us (6%)
    ppermute x2, waiting for transfers between devices, gather_rep(): across = lax.ppermute(w, 'rep', [(k, k ^ 2) for k in range(size)])  49.2 us
    all_gather x1, waiting for transfers between devices, shards(): second_all = lax.all_gather(second[0], 'frame', axis=0, tiled=False)  37.7 us
    all_gather x1, blocking collectives, shards(): edges = lax.all_gather(edges, 'frame', axis=1, tiled=True)  16.9 us
    ppermute x3, waiting for transfers between devices, shards(): lax.ppermute(piece, 'frame', [(k, (k + shift) % frame_size) for k in rang...  12.9 us
    concatenate x2, other arithmetic, gather_rep(): return jnp.concatenate(blocks, axis=-1)  8.68 us
    dot_general x4, matrix products, tap(): jnp.einsum('frxc,cn->frxn', field, wide[row_tap], preferred_element_type=...  8.09 us
    dot_general x4, matrix products, shards(): jnp.einsum('frxc,cn->frxn', second_all[group], weights, preferred_element...  6.53 us
    ppermute x3, waiting for transfers between devices, butterfly_sum(): value = jax.tree.map(lambda v: v + lax.ppermute(v, axis, pairs), value)  5.24 us
  transfers between devices with their start and end apart: 17, of which 8 were waited for; matrix products, arithmetic and copies ran while one was open for 14% of the time, Pallas kernels for 0%

profile of v11, /device:TPU:0, one launch (start us, length us, event | category | flops | bytes accessed | tf_op | source)
XLA Modules:
  0.0 219.4 jit_solution(8377870112088661056)
XLA Ops:
  6.5 3.0 %collective-permute-start.4 = (bf16[3,1280,3,80]{1,3,2,0:T(8,128)(2,1)}, bf16[3,1280,3,80]{1,3,2,0:T(8,128)(2,1)}, u32[]{:S(2)}, u32[]{:S(2)}) collective-permute-start(bf16[3,1280,3,80]{1,3,2,0:T(8,128)(2,1)} %bitcast.172), channel_id=1, source_target_pairs={{0,16},{8,24},{16,0},{24,8},{1,17},{9,25},{17,1},{25,9},{2,18},{10... | collective-permute-start | bytes 5529608 | tf_op jit(solution)/shard_map/ppermute | solution.py:40
  9.6 40.5 %collective-permute-done.4 = bf16[3,1280,3,80]{1,3,2,0:T(8,128)(2,1)} collective-permute-done((bf16[3,1280,3,80]{1,3,2,0:T(8,128)(2,1)}, bf16[3,1280,3,80]{1,3,2,0:T(8,128)(2,1)}, u32[]{:S(2)}, u32[]{:S(2)}) %collective-permute-start.4) | collective-permute-done | bytes 1843232 | tf_op jit(solution)/shard_map/ppermute | solution.py:40
  51.0 1.3 collective-permute-start.7
  52.3 4.6 %collective-permute-start.6 = (bf16[1,1,1,32,1280]{4,3,2,0,1:T(8,128)(2,1)S(1)}, bf16[1,1,1,32,1280]{4,3,2,0,1:T(8,128)(2,1)S(1)}, u32[]{:S(2)}, u32[]{:S(2)}) collective-permute-start(bf16[1,1,1,32,1280]{4,3,2,0,1:T(8,128)(2,1)S(1)} %get-tuple-element.36), channel_id=1, source_target_pairs={{0,1},{2,3},{4,5},{6,7},{8,9},{10,11},{12,13},{14,15},{16,17},{18,... | collective-permute-start | bytes 245768 | tf_op jit(solution)/shard_map/ppermute | solution.py:127
  58.6 1.8 collective-permute-start
  62.8 2.7 %collective-permute-start.1 = (f32[2,32]{1,0:T(2,128)S(1)}, f32[2,32]{1,0:T(2,128)S(1)}, u32[]{:S(2)}, u32[]{:S(2)}) collective-permute-start(f32[2,32]{1,0:T(2,128)S(1)} %fusion.39), channel_id=1, source_target_pairs={{0,4},{2,6},{4,0},{6,2},{1,5},{3,7},{5,1},{7,3},{8,12},{10,14},{12... | collective-permute-start | bytes 776 | tf_op jit(solution)/shard_map/ppermute | solution.py:30
  65.5 1.9 collective-permute-done.1
  67.6 3.4 %collective-permute-done.2 = f32[2,32]{1,0:T(2,128)S(1)} collective-permute-done((f32[2,32]{1,0:T(2,128)S(1)}, f32[2,32]{1,0:T(2,128)S(1)}, u32[]{:S(2)}, u32[]{:S(2)}) %collective-permute-start.2) | collective-permute-done | bytes 288 | tf_op jit(solution)/shard_map/ppermute | solution.py:30
  71.4 16.9 %all_gather.10 = bf16[1,4,2,32,1280]{4,3,2,0,1:T(8,128)(2,1)S(1)} all-gather(bf16[1,1,2,32,1280]{4,3,2,0,1:T(8,128)(2,1)S(1)} %pad_maximum_fusion.2), channel_id=1, replica_groups=mesh['rep'=4,'frame'=4,'row'=2] {'frame'}, dimensions={1}, use_global_device_ids=true | all-gather | bytes 819200 | tf_op jit(solution)/shard_map/all_gather | solution.py:132
  88.3 3.0 %select_select_fusion.3 = (bf16[3,1280,3,80]{1,3,2,0:T(8,128)(2,1)S(1)}, bf16[3,1280,3,80]{1,3,2,0:T(8,128)(2,1)S(1)}, bf16[3,1280,3,80]{1,3,2,0:T(8,128)(2,1)S(1)}, bf16[3,1280,3,80]{1,3,2,0:T(8,128)(2,1)S(1)}) fusion(bf16[3,1280,3,80]{1,3,2,0:T(8,128)(2,1)S(1)} %bitcast.174, bf16[3,1280,3,80]{1,3,2,0:T(8,128)(2,1)} %collective-permute-done.3, ...), kind=kLoop, calls=%fused_computation.14 | loop fusion | flops 11059200 | bytes 14745612 | tf_op jit(solution)/shard_map/jit(_where)/select_n | solution.py:49
  91.4 5.7 %pad_maximum_fusion = bf16[3,1280,3,320]{1,3,2,0:T(8,128)(2,1)S(1)} fusion(bf16[3,1280,3,80]{1,3,2,0:T(8,128)(2,1)S(1)} %get-tuple-element.14, bf16[3,1280,3,80]{1,3,2,0:T(8,128)(2,1)S(1)} %get-tuple-element.15, bf16[3,1280,3,80]{1,3,2,0:T(8,128)(2,1)S(1)} %get-tuple-element.16, bf16[3,1280,3,80]{1,3,2,0:T(8,128)(2,1)S(1)} %get-tuple-element.13), kind=kLoop, calls=%fused_computation | loop fusion | flops 29491200 | bytes 14745600 | tf_op jit(solution)/shard_map/concatenate | solution.py:51
  99.8 1.7 convolution_bitcast_fusion.1
  101.5 3.7 %fusion = bf16[4,8,32,1280]{3,2,1,0:T(8,128)(2,1)S(1)} fusion(bf16[1,4,8,32,1280]{4,3,2,0,1:T(8,128)(2,1)} %all-gather.4.cloned.1.call-done, f32[1280]{0:T(1024)S(1)} %copy-done.10, f32[1280]{0:T(1024)S(1)} %copy-done.11, f32[1280]{0:T(1024)S(1)} %mul.103, f32[1280]{0:T(1024)S(1)} %sub.50), kind=kLoop, calls=%fused_computation.5 | loop fusion | flops 13107200 | bytes 5263360 | tf_op jit(solution)/shard_map/squeeze | solution.py:155
  105.2 2.6 %fusion.51 = f32[4,7,32,960]{3,2,1,0:T(8,128)S(1)} fusion(bf16[4,8,32,1280]{3,2,1,0:T(8,128)(2,1)S(1)} %fusion, bf16[1280,960,1,1]{0,1,3,2:T(8,128)(2,1)S(1)} %bitcast.171), kind=kOutput, calls=%fused_computation.105 | convolution fusion | flops 2202009600 | bytes 8519680 | tf_op jit(solution)/shard_map/frxc,cn->frxn/dot_general | solution.py:164
  107.8 2.9 %fusion.1 = f32[4,8,32,960]{3,2,1,0:T(8,128)S(1)} fusion(bf16[1280,960,1,1]{0,1,3,2:T(8,128)(2,1)S(1)} %bitcast.169, bf16[4,8,32,1280]{3,2,1,0:T(8,128)(2,1)S(1)} %fusion), kind=kOutput, calls=%fused_computation.6 | convolution fusion | flops 2202009600 | bytes 8683520 | tf_op jit(solution)/shard_map/jit(_pad)/pad | solution.py:169
  110.7 2.9 %pad_add_fusion = f32[4,8,32,960]{3,2,1,0:T(8,128)S(1)} fusion(f32[4,1,32,960]{3,2,1,0:T(8,128)S(1)} %convolution_bitcast_fusion, f32[4,1,32,960]{3,2,1,0:T(8,128)S(1)} %copy-done.13, f32[4,7,32,960]{3,2,1,0:T(8,128)S(1)} %fusion.51, f32[4,8,32,960]{3,2,1,0:T(8,128)S(1)} %fusion.1, bf16[4,8,32,1280]{3,2,1,0:T(8,128)(2,1)S(1)} %fusion, ...), kind=kOutput, calls=%fused_computation.3 | convolution fusion | flops 2520514560 | bytes 17367040 | tf_op jit(solution)/shard_map/frxc,cn->frxn/dot_general | solution.py:164
  115.5 3.4 %collective-permute-done.8 = f32[2,8]{1,0:T(2,128)S(1)} collective-permute-done((f32[2,8]{1,0:T(2,128)S(1)}, f32[2,8]{1,0:T(2,128)S(1)}, u32[]{:S(2)}, u32[]{:S(2)}) %collective-permute-start.8) | collective-permute-done | bytes 96 | tf_op jit(solution)/shard_map/ppermute | solution.py:18
  119.2 1.4 multiply_convert_fusion.1
  120.7 1.6 collective-permute-start.10
  122.2 8.7 %collective-permute-done.10 = bf16[3,1280,80]{1,2,0:T(8,128)(2,1)} collective-permute-done((bf16[3,1280,80]{1,2,0:T(8,128)(2,1)S(1)}, bf16[3,1280,80]{1,2,0:T(8,128)(2,1)}, u32[]{:S(2)}, u32[]{:S(2)}) %collective-permute-start.10) | collective-permute-done | bytes 614432 | tf_op jit(solution)/shard_map/ppermute | solution.py:40
  131.7 1.5 copy.108
  133.2 1.5 copy.110
  134.8 2.2 copy.109
  137.0 1.7 select_select_fusion.7
  138.6 3.0 %pad_maximum_fusion.1 = bf16[3,1280,320]{2,1,0:T(8,128)(2,1)S(1)} fusion(bf16[3,1280,80]{2,1,0:T(8,128)(2,1)S(1)} %get-tuple-element.22, bf16[3,1280,80]{2,1,0:T(8,128)(2,1)S(1)} %get-tuple-element.23, bf16[3,1280,80]{2,1,0:T(8,128)(2,1)S(1)} %get-tuple-element.24, bf16[3,1280,80]{2,1,0:T(8,128)(2,1)S(1)} %get-tuple-element.21), kind=kLoop, calls=%fused_computation.4 | loop fusion | flops 9830400 | bytes 4915200 | tf_op jit(solution)/shard_map/concatenate | solution.py:51
  145.2 37.7 %all-gather.6.cloned.1.call-done = bf16[16,8,32,320]{3,2,1,0:T(8,128)(2,1)} async-done(((bf16[4,8,32,320]{3,2,1,0:T(8,128)(2,1)}), bf16[16,8,32,320]{3,2,1,0:T(8,128)(2,1)}) %all-gather.6.cloned.1.call-update) | async-done | bytes 2621456 | tf_op jit(solution)/shard_map/all_gather | solution.py:212
  182.9 2.6 %fusion.54 = f32[4,8,32,960]{3,2,1,0:T(8,128)S(1)} fusion(bf16[16,8,32,320]{3,2,1,0:T(8,128)(2,1)} %all-gather.6.cloned.1.call-done, bf16[320,960,1,1]{0,1,3,2:T(8,128)(2,1)S(1)} %bitcast.163), kind=kOutput, calls=%fused_computation.108 | convolution fusion | flops 629145600 | bytes 7168000 | tf_op jit(solution)/shard_map/frxc,cn->frxn/dot_general | solution.py:218
  188.0 1.4 add_add_fusion
  190.4 1.3 collective-permute-start.13
  191.7 2.7 %collective-permute-start.14 = (bf16[1,8,32,320]{3,2,1,0:T(8,128)(2,1)S(1)}, bf16[1,8,32,320]{3,2,1,0:T(8,128)(2,1)S(1)}, u32[]{:S(2)}, u32[]{:S(2)}) collective-permute-start(bf16[1,8,32,320]{3,2,1,0:T(8,128)(2,1)S(1)} %get-tuple-element.33), channel_id=1, source_target_pairs={{0,6},{2,0},{4,2},{6,4},{1,7},{3,1},{5,3},{7,5},{8,14},{10,8},{12,... | collective-permute-start | bytes 491528 | tf_op jit(solution)/shard_map/ppermute | solution.py:235
  194.4 5.7 %collective-permute-done.12 = bf16[1,8,32,320]{3,2,1,0:T(8,128)(2,1)S(1)} collective-permute-done((bf16[1,8,32,320]{3,2,1,0:T(8,128)(2,1)S(1)}, bf16[1,8,32,320]{3,2,1,0:T(8,128)(2,1)S(1)}, u32[]{:S(2)}, u32[]{:S(2)}) %collective-permute-start.12) | collective-permute-done | bytes 163872 | tf_op jit(solution)/shard_map/ppermute | solution.py:235
  200.1 7.2 %collective-permute-done.13 = bf16[1,8,32,320]{3,2,1,0:T(8,128)(2,1)S(1)} collective-permute-done((bf16[1,8,32,320]{3,2,1,0:T(8,128)(2,1)S(1)}, bf16[1,8,32,320]{3,2,1,0:T(8,128)(2,1)S(1)}, u32[]{:S(2)}, u32[]{:S(2)}) %collective-permute-start.13) | collective-permute-done | bytes 163872 | tf_op jit(solution)/shard_map/ppermute | solution.py:235
  (126 shorter events, 23.3 us)
Async XLA Ops:
  6.5 81.8 %copy-start.8 = (bf16[9,1280,80]{1,2,0:T(8,128)(2,1)S(1)}, bf16[9,1280,80]{1,2,0:T(8,128)(2,1)}, u32[]{:S(2)}) copy-start(bf16[9,1280,80]{1,2,0:T(8,128)(2,1)} %param.10) | copy-start | bytes 5529604
  6.5 94.9 %all-gather.4.cloned.1.call-start = ((), (), s32[]{:S(2)}) async-start(), calls=%async_computation | async-start | bytes 3276800 | tf_op jit(solution)/shard_map/all_gather | solution.py:119
  6.5 43.5 %collective-permute-start.4 = (bf16[3,1280,3,80]{1,3,2,0:T(8,128)(2,1)}, bf16[3,1280,3,80]{1,3,2,0:T(8,128)(2,1)}, u32[]{:S(2)}, u32[]{:S(2)}) collective-permute-start(bf16[3,1280,3,80]{1,3,2,0:T(8,128)(2,1)} %bitcast.172), channel_id=1, source_target_pairs={{0,16},{8,24},{16,0},{24,8},{1,17},{9,25},{17,1},{25,9},{2,18},{10... | collective-permute-start | bytes 5529608 | tf_op jit(solution)/shard_map/ppermute | solution.py:40
  9.5 78.8 %collective-permute-start.3 = (bf16[3,1280,3,80]{1,3,2,0:T(8,128)(2,1)}, bf16[3,1280,3,80]{1,3,2,0:T(8,128)(2,1)}, u32[]{:S(2)}, u32[]{:S(2)}) collective-permute-start(bf16[3,1280,3,80]{1,3,2,0:T(8,128)(2,1)} %bitcast.173), channel_id=1, source_target_pairs={{0,8},{8,0},{16,24},{24,16},{1,9},{9,1},{17,25},{25,17},{2,10},{10... | collective-permute-start | bytes 5529608 | tf_op jit(solution)/shard_map/ppermute | solution.py:41
  9.5 173.3 %all-gather.6.cloned.1.call-start = ((), (), s32[]{:S(2)}) async-start(), calls=%async_computation.1 | async-start | bytes 3932160 | tf_op jit(solution)/shard_map/all_gather | solution.py:212
  50.1 38.3 %collective-permute-start.5 = (bf16[3,1280,3,80]{1,3,2,0:T(8,128)(2,1)}, bf16[3,1280,3,80]{1,3,2,0:T(8,128)(2,1)}, u32[]{:S(2)}, u32[]{:S(2)}) collective-permute-start(bf16[3,1280,3,80]{1,3,2,0:T(8,128)(2,1)} %collective-permute-done.4), channel_id=1, source_target_pairs={{0,8},{8,0},{16,24},{24,16},{1,9},{9,1},{17,25},{25,17},{2,10},{10... | collective-permute-start | bytes 5529608 | tf_op jit(solution)/shard_map/ppermute | solution.py:42
  51.0 20.3 %collective-permute-start.7 = (bf16[1,1,1,32,1280]{4,3,2,0,1:T(8,128)(2,1)S(1)}, bf16[1,1,1,32,1280]{4,3,2,0,1:T(8,128)(2,1)S(1)}, u32[]{:S(2)}, u32[]{:S(2)}) collective-permute-start(bf16[1,1,1,32,1280]{4,3,2,0,1:T(8,128)(2,1)S(1)} %get-tuple-element.37), channel_id=1, source_target_pairs={{1,0},{3,2},{5,4},{7,6},{9,8},{11,10},{13,12},{15,14},{17,16},{19,... | collective-permute-start | bytes 245768 | tf_op jit(solution)/shard_map/ppermute | solution.py:128
  52.3 19.0 %collective-permute-start.6 = (bf16[1,1,1,32,1280]{4,3,2,0,1:T(8,128)(2,1)S(1)}, bf16[1,1,1,32,1280]{4,3,2,0,1:T(8,128)(2,1)S(1)}, u32[]{:S(2)}, u32[]{:S(2)}) collective-permute-start(bf16[1,1,1,32,1280]{4,3,2,0,1:T(8,128)(2,1)S(1)} %get-tuple-element.36), channel_id=1, source_target_pairs={{0,1},{2,3},{4,5},{6,7},{8,9},{10,11},{12,13},{14,15},{16,17},{18,... | collective-permute-start | bytes 245768 | tf_op jit(solution)/shard_map/ppermute | solution.py:127
  58.6 4.2 %collective-permute-start = (f32[2,32]{1,0:T(2,128)S(1)}, f32[2,32]{1,0:T(2,128)S(1)}, u32[]{:S(2)}, u32[]{:S(2)}) collective-permute-start(f32[2,32]{1,0:T(2,128)S(1)} %pad_maximum_fusion.3), channel_id=1, source_target_pairs={{0,2},{2,0},{4,6},{6,4},{1,3},{3,1},{5,7},{7,5},{8,10},{10,8},{12,... | collective-permute-start | bytes 776 | tf_op jit(solution)/shard_map/ppermute | solution.py:30
  62.8 4.5 %collective-permute-start.1 = (f32[2,32]{1,0:T(2,128)S(1)}, f32[2,32]{1,0:T(2,128)S(1)}, u32[]{:S(2)}, u32[]{:S(2)}) collective-permute-start(f32[2,32]{1,0:T(2,128)S(1)} %fusion.39), channel_id=1, source_target_pairs={{0,4},{2,6},{4,0},{6,2},{1,5},{3,7},{5,1},{7,3},{8,12},{10,14},{12... | collective-permute-start | bytes 776 | tf_op jit(solution)/shard_map/ppermute | solution.py:30
  67.4 3.6 %collective-permute-start.2 = (f32[2,32]{1,0:T(2,128)S(1)}, f32[2,32]{1,0:T(2,128)S(1)}, u32[]{:S(2)}, u32[]{:S(2)}) collective-permute-start(f32[2,32]{1,0:T(2,128)S(1)} %fusion.70), channel_id=1, source_target_pairs={{0,1},{1,0},{2,3},{3,2},{4,5},{5,4},{6,7},{7,6},{8,9},{9,8},{10,11... | collective-permute-start | bytes 776 | tf_op jit(solution)/shard_map/ppermute | solution.py:30
  97.1 0.7 copy-start.10
  97.1 0.7 copy-start.11
  97.6 1.5 copy-start.6
  97.6 2.2 copy-start.4
  101.5 3.7 %copy-start.7 = (bf16[1,1280,3,320]{1,3,2,0:T(8,128)(2,1)S(1)}, bf16[1,1280,3,320]{1,3,2,0:T(8,128)(2,1)}, u32[]{:S(2)}) copy-start(bf16[1,1280,3,320]{1,3,2,0:T(8,128)(2,1)} %copy-done.6) | copy-start | bytes 7372804
  105.2 2.6 %copy-start.5 = (bf16[1,1280,3,320]{1,3,2,0:T(8,128)(2,1)S(1)}, bf16[1,1280,3,320]{1,3,2,0:T(8,128)(2,1)}, u32[]{:S(2)}) copy-start(bf16[1,1280,3,320]{1,3,2,0:T(8,128)(2,1)} %copy-done.4) | copy-start | bytes 7372804
  107.8 2.9 %copy-start.13 = (f32[4,1,32,960]{3,2,1,0:T(8,128)S(1)}, f32[4,1,32,960]{3,2,1,0:T(8,128)}, u32[]{:S(2)}) copy-start(f32[4,1,32,960]{3,2,1,0:T(8,128)} %convolution_bitcast_fusion.1) | copy-start | bytes 1474564
  114.8 5.9 %copy-start.9 = (bf16[3,1280,80]{1,2,0:T(8,128)(2,1)S(1)}, bf16[3,1280,80]{1,2,0:T(8,128)(2,1)}, u32[]{:S(2)}) copy-start(bf16[3,1280,80]{1,2,0:T(8,128)(2,1)} %param.11) | copy-start | bytes 1843204
  115.2 3.6 %collective-permute-start.8 = (f32[2,8]{1,0:T(2,128)S(1)}, f32[2,8]{1,0:T(2,128)S(1)}, u32[]{:S(2)}, u32[]{:S(2)}) collective-permute-start(f32[2,8]{1,0:T(2,128)S(1)} %pad_maximum_fusion.4), channel_id=1, source_target_pairs={{0,1},{1,0},{2,3},{3,2},{4,5},{5,4},{6,7},{7,6},{8,9},{9,8},{10,11... | collective-permute-start | bytes 200 | tf_op jit(solution)/shard_map/ppermute | solution.py:18
  120.7 10.3 %collective-permute-start.10 = (bf16[3,1280,80]{1,2,0:T(8,128)(2,1)S(1)}, bf16[3,1280,80]{1,2,0:T(8,128)(2,1)}, u32[]{:S(2)}, u32[]{:S(2)}) collective-permute-start(bf16[3,1280,80]{1,2,0:T(8,128)(2,1)S(1)} %copy-done.9), channel_id=1, source_target_pairs={{0,16},{8,24},{16,0},{24,8},{1,17},{9,25},{17,1},{25,9},{2,18},{10... | collective-permute-start | bytes 1843208 | tf_op jit(solution)/shard_map/ppermute | solution.py:40
  122.2 11.0 %collective-permute-start.9 = (bf16[3,1280,80]{1,2,0:T(8,128)(2,1)S(1)}, bf16[3,1280,80]{1,2,0:T(8,128)(2,1)}, u32[]{:S(2)}, u32[]{:S(2)}) collective-permute-start(bf16[3,1280,80]{1,2,0:T(8,128)(2,1)S(1)} %copy-done.9), channel_id=1, source_target_pairs={{0,8},{8,0},{16,24},{24,16},{1,9},{9,1},{17,25},{25,17},{2,10},{10... | collective-permute-start | bytes 1843208 | tf_op jit(solution)/shard_map/ppermute | solution.py:41
  131.0 3.8 %collective-permute-start.11 = (bf16[3,1280,80]{1,2,0:T(8,128)(2,1)}, bf16[3,1280,80]{1,2,0:T(8,128)(2,1)}, u32[]{:S(2)}, u32[]{:S(2)}) collective-permute-start(bf16[3,1280,80]{1,2,0:T(8,128)(2,1)} %collective-permute-done.10), channel_id=1, source_target_pairs={{0,8},{8,0},{16,24},{24,16},{1,9},{9,1},{17,25},{25,17},{2,10},{10... | collective-permute-start | bytes 1843208 | tf_op jit(solution)/shard_map/ppermute | solution.py:42
  143.2 39.6 %copy-start.2 = (bf16[3,320,320]{1,2,0:T(8,128)(2,1)S(1)}, bf16[3,320,320]{1,2,0:T(8,128)(2,1)}, u32[]{:S(2)}) copy-start(bf16[3,320,320]{1,2,0:T(8,128)(2,1)} %copy.128) | copy-start | bytes 1843204
  182.8 2.6 %copy-start.1 = (bf16[16,8,32,320]{3,2,1,0:T(8,128)(2,1)S(1)}, bf16[16,8,32,320]{3,2,1,0:T(8,128)(2,1)}, u32[]{:S(2)}) copy-start(bf16[16,8,32,320]{3,2,1,0:T(8,128)(2,1)} %all-gather.6.cloned.1.call-done) | copy-start | bytes 7864324
  182.8 2.6 %copy-start.3 = (bf16[3,320,320]{1,2,0:T(8,128)(2,1)S(1)}, bf16[3,320,320]{1,2,0:T(8,128)(2,1)}, u32[]{:S(2)}) copy-start(bf16[3,320,320]{1,2,0:T(8,128)(2,1)} %copy.124) | copy-start | bytes 1843204
  190.3 9.7 %collective-permute-start.12 = (bf16[1,8,32,320]{3,2,1,0:T(8,128)(2,1)S(1)}, bf16[1,8,32,320]{3,2,1,0:T(8,128)(2,1)S(1)}, u32[]{:S(2)}, u32[]{:S(2)}) collective-permute-start(bf16[1,8,32,320]{3,2,1,0:T(8,128)(2,1)S(1)} %get-tuple-element.35), channel_id=1, source_target_pairs={{0,2},{2,4},{4,6},{6,0},{1,3},{3,5},{5,7},{7,1},{8,10},{10,12},{12... | collective-permute-start | bytes 491528 | tf_op jit(solution)/shard_map/ppermute | solution.py:235
  190.4 16.8 %collective-permute-start.13 = (bf16[1,8,32,320]{3,2,1,0:T(8,128)(2,1)S(1)}, bf16[1,8,32,320]{3,2,1,0:T(8,128)(2,1)S(1)}, u32[]{:S(2)}, u32[]{:S(2)}) collective-permute-start(bf16[1,8,32,320]{3,2,1,0:T(8,128)(2,1)S(1)} %get-tuple-element.34), channel_id=1, source_target_pairs={{0,4},{2,6},{4,0},{6,2},{1,5},{3,7},{5,1},{7,3},{8,12},{10,14},{12... | collective-permute-start | bytes 491528 | tf_op jit(solution)/shard_map/ppermute | solution.py:235
  191.7 15.5 %collective-permute-start.14 = (bf16[1,8,32,320]{3,2,1,0:T(8,128)(2,1)S(1)}, bf16[1,8,32,320]{3,2,1,0:T(8,128)(2,1)S(1)}, u32[]{:S(2)}, u32[]{:S(2)}) collective-permute-start(bf16[1,8,32,320]{3,2,1,0:T(8,128)(2,1)S(1)} %get-tuple-element.33), channel_id=1, source_target_pairs={{0,6},{2,0},{4,2},{6,4},{1,7},{3,1},{5,3},{7,5},{8,14},{10,8},{12,... | collective-permute-start | bytes 491528 | tf_op jit(solution)/shard_map/ppermute | solution.py:235
  209.8 1.4 copy-start
  209.9 1.4 copy-start.12
Sparse Core Ops, SparseCore 0:
  9.7 56.7 all-gather.3
  120.8 62.0 all-gather.5

commit v12 on v10

--- a/solution.py
+++ b/solution.py
@@ -204,14 +204,17 @@
         return temporal_wide(activations, second, temporal_w, temporal_bias)
     second_all = lax.all_gather(second[0], "frame", axis=0, tiled=False)
     taps = temporal_w.reshape(3, rep_size, frame_size, shard_width, local)
-    total = None
-    for group in range(frame_size):
-        weights = taps[:, :, group].reshape(3, rep_size * shard_width, local)
-        weights = weights.transpose(1, 0, 2).reshape(rep_size * shard_width, 3 * local)
-        term = jnp.einsum(
-            "frxc,cn->frxn", second_all[group], weights, preferred_element_type=jnp.float32
-        )
-        total = term if total is None else total + term
+    wide_t = taps.transpose(2, 1, 3, 0, 4).reshape(frame_size, rep_size * shard_width, 3 * local)
+
+    def product(source, group):
+        weights = lax.dynamic_index_in_dim(wide_t, group, axis=0, keepdims=False)
+        return jnp.einsum("frxc,cn->frxn", source, weights, preferred_element_type=jnp.float32)
+
+    total = product(second[0], frame_index)
+    for shift in range(1, frame_size):
+        group = (frame_index + shift) % frame_size
+        block = lax.dynamic_index_in_dim(second_all, group, axis=0, keepdims=False)
+        total = total + product(block, group)
     temporal = total[..., local : 2 * local]
     if frames > 1:
         before = jnp.pad(total[:-1, ..., :local], ((1, 0), (0, 0), (0, 0), (0, 0)))

time: 234 us -> 234 us (level)
  waiting for transfers between devices: 137 us -> 126 us
  local copies, waits for them, and re-layouts: 21.3 us -> 30 us
    all_gather x1, waiting for transfers between devices: 33.6 us -> 22.6 us  [shards(): second_all = lax.all_gather(second[0], 'frame', axis=0, tiled=False)]
    reshape x0 -> x1, local copies, waits for them, and re-layouts: none -> 6.93 us  [shards(): taps.transpose(2, 1, 3, 0, 4)]
    transpose x0 -> x1, local copies, waits for them, and re-layouts: none -> 4.38 us  [shards(): taps.transpose(2, 1, 3, 0, 4)]
    another operation x4 -> x0, local copies, waits for them, and re-layouts: 3.07 us -> none  [shards(): weights = taps[:, :, group].reshape(3, rep_size * shard_width, local)]
  transfers between devices with their start and end apart: 17 -> 17, of which waited for: 9 -> 9; matrix products, arithmetic and copies ran while one was open for 17% -> 22% of each run, Pallas kernels for 0% -> 0%
where the time goes in v12:
time: 234 us; the launch traced here: 232 us
  waiting for transfers between devices  126 us (54%)
  local copies, waits for them, and re-layouts  30 us (13%)
  other arithmetic  22.5 us (10%)
  starting transfers between devices  21 us (9%)
  matrix products  18.5 us (8%)
  between operations  14.1 us (6%)
    ppermute x2, waiting for transfers between devices, gather_rep(): across = lax.ppermute(w, 'rep', [(k, k ^ 2) for k in range(size)])  52.8 us
    all_gather x1, waiting for transfers between devices, shards(): raw = lax.all_gather(activations, 'frame', axis=1, tiled=True)  30.6 us
    all_gather x1, waiting for transfers between devices, shards(): second_all = lax.all_gather(second[0], 'frame', axis=0, tiled=False)  22.6 us
    ppermute x3, waiting for transfers between devices, shards(): lax.ppermute(piece, 'frame', [(k, (k + shift) % frame_size) for k in rang...  12.9 us
    dot_general x4, matrix products, product(): jnp.einsum('frxc,cn->frxn', source, weights, preferred_element_type=jnp.f...  8.29 us
    concatenate x2, other arithmetic, gather_rep(): return jnp.concatenate(blocks, axis=-1)  8.27 us
    dot_general x4, matrix products, tap(): jnp.einsum('frxc,cn->frxn', field, wide[row_tap], preferred_element_type=...  7.32 us
    reshape x1, local copies, waits for them, and re-layouts, shards(): taps.transpose(2, 1, 3, 0, 4)  6.93 us
  transfers between devices with their start and end apart: 17, of which 9 were waited for; matrix products, arithmetic and copies ran while one was open for 22% of the time, Pallas kernels for 0%

profile of v12, /device:TPU:0, one launch (start us, length us, event | category | flops | bytes accessed | tf_op | source)
XLA Modules:
  0.0 232.2 jit_solution(4245711567919403182)
XLA Ops:
  6.5 3.0 %collective-permute-start.4 = (bf16[3,1280,3,80]{1,3,2,0:T(8,128)(2,1)}, bf16[3,1280,3,80]{1,3,2,0:T(8,128)(2,1)S(1)}, u32[]{:S(2)}, u32[]{:S(2)}) collective-permute-start(bf16[3,1280,3,80]{1,3,2,0:T(8,128)(2,1)} %bitcast.170), channel_id=1, source_target_pairs={{0,16},{8,24},{16,0},{24,8},{1,17},{9,25},{17,1},{25,9},{2,18},{10... | collective-permute-start | bytes 5529608 | tf_op jit(solution)/shard_map/ppermute | solution.py:40
  9.5 40.4 %collective-permute-done.4 = bf16[3,1280,3,80]{1,3,2,0:T(8,128)(2,1)S(1)} collective-permute-done((bf16[3,1280,3,80]{1,3,2,0:T(8,128)(2,1)}, bf16[3,1280,3,80]{1,3,2,0:T(8,128)(2,1)S(1)}, u32[]{:S(2)}, u32[]{:S(2)}) %collective-permute-start.4) | collective-permute-done | bytes 1843232 | tf_op jit(solution)/shard_map/ppermute | solution.py:40
  51.7 1.9 collective-permute-start
  56.0 2.7 %collective-permute-start.1 = (f32[2,32]{1,0:T(2,128)S(1)}, f32[2,32]{1,0:T(2,128)S(1)}, u32[]{:S(2)}, u32[]{:S(2)}) collective-permute-start(f32[2,32]{1,0:T(2,128)S(1)} %fusion.61), channel_id=1, source_target_pairs={{0,4},{2,6},{4,0},{6,2},{1,5},{3,7},{5,1},{7,3},{8,12},{10,14},{12... | collective-permute-start | bytes 776 | tf_op jit(solution)/shard_map/ppermute | solution.py:30
  58.6 1.9 collective-permute-done.1
  60.5 1.6 collective-permute-start.2
  62.3 1.9 collective-permute-done.2
  64.5 3.1 %select_select_fusion.3 = (bf16[3,1280,3,80]{1,3,2,0:T(8,128)(2,1)S(1)}, bf16[3,1280,3,80]{1,3,2,0:T(8,128)(2,1)S(1)}, bf16[3,1280,3,80]{1,3,2,0:T(8,128)(2,1)S(1)}, bf16[3,1280,3,80]{1,3,2,0:T(8,128)(2,1)S(1)}) fusion(bf16[3,1280,3,80]{1,3,2,0:T(8,128)(2,1)} %bitcast.172, bf16[3,1280,3,80]{1,3,2,0:T(8,128)(2,1)} %collective-permute-done.3, ...), kind=kLoop, calls=%fused_computation.14 | loop fusion | flops 11059200 | bytes 14745612 | tf_op jit(solution)/shard_map/jit(_where)/select_n | solution.py:49
  67.6 5.5 %pad_maximum_fusion = bf16[3,1280,3,320]{1,3,2,0:T(8,128)(2,1)S(1)} fusion(bf16[3,1280,3,80]{1,3,2,0:T(8,128)(2,1)S(1)} %get-tuple-element.14, bf16[3,1280,3,80]{1,3,2,0:T(8,128)(2,1)S(1)} %get-tuple-element.15, bf16[3,1280,3,80]{1,3,2,0:T(8,128)(2,1)S(1)} %get-tuple-element.16, bf16[3,1280,3,80]{1,3,2,0:T(8,128)(2,1)S(1)} %get-tuple-element.13), kind=kLoop, calls=%fused_computation | loop fusion | flops 29491200 | bytes 14745600 | tf_op jit(solution)/shard_map/concatenate | solution.py:51
  73.1 2.7 %fusion.64 = (bf16[1,1280,3,320]{1,3,2,0:T(8,128)(2,1)S(1)}, bf16[1,1280,3,320]{1,3,2,0:T(8,128)(2,1)}, bf16[1,1280,3,320]{1,3,2,0:T(8,128)(2,1)}) fusion(bf16[3,1280,3,320]{1,3,2,0:T(8,128)(2,1)S(1)} %pad_maximum_fusion), kind=kLoop, calls=%fused_computation.117 | loop fusion | bytes 14745600 | tf_op jit(solution)/shard_map/slice | solution.py:158
  75.9 30.6 %all-gather.4.cloned.1.call-done = bf16[1,4,8,32,1280]{4,3,2,0,1:T(8,128)(2,1)} async-done(((bf16[1,1,8,32,1280]{4,3,2,0,1:T(8,128)(2,1)}), bf16[1,4,8,32,1280]{4,3,2,0,1:T(8,128)(2,1)}) %all-gather.4.cloned.1.call-update) | async-done | bytes 2621456 | tf_op jit(solution)/shard_map/all_gather | solution.py:119
  108.9 4.9 %collective-permute-start.6 = (bf16[1,4,1,32,1280]{4,3,2,0,1:T(8,128)(2,1)S(1)}, bf16[1,4,1,32,1280]{4,3,2,0,1:T(8,128)(2,1)S(1)}, u32[]{:S(2)}, u32[]{:S(2)}) collective-permute-start(bf16[1,4,1,32,1280]{4,3,2,0,1:T(8,128)(2,1)S(1)} %get-tuple-element.25), channel_id=1, source_target_pairs={{0,1},{2,3},{4,5},{6,7},{8,9},{10,11},{12,13},{14,15},{16,17},{18,... | collective-permute-start | bytes 983048 | tf_op jit(solution)/shard_map/ppermute | solution.py:125
  113.8 3.5 %fusion = bf16[4,8,32,1280]{3,2,1,0:T(8,128)(2,1)S(1)} fusion(bf16[1,4,8,32,1280]{4,3,2,0,1:T(8,128)(2,1)} %all-gather.4.cloned.1.call-done, f32[1280]{0:T(1024)S(1)} %copy-done.7, f32[1280]{0:T(1024)S(1)} %copy-done.8, f32[1280]{0:T(1024)S(1)} %mul.103, f32[1280]{0:T(1024)S(1)} %sub.50), kind=kLoop, calls=%fused_computation.5 | loop fusion | flops 13107200 | bytes 5263360 | tf_op jit(solution)/shard_map/squeeze | solution.py:148
  117.4 2.6 %fusion.72 = f32[4,7,32,960]{3,2,1,0:T(8,128)S(1)} fusion(bf16[4,8,32,1280]{3,2,1,0:T(8,128)(2,1)S(1)} %fusion, bf16[1280,960,1,1]{0,1,3,2:T(8,128)(2,1)S(1)} %bitcast.168), kind=kOutput, calls=%fused_computation.125 | convolution fusion | flops 2202009600 | bytes 8519680 | tf_op jit(solution)/shard_map/frxc,cn->frxn/dot_general | solution.py:157
  120.0 2.9 %fusion.1 = f32[4,8,32,960]{3,2,1,0:T(8,128)S(1)} fusion(bf16[1280,960,1,1]{0,1,3,2:T(8,128)(2,1)S(1)} %bitcast.166, bf16[4,8,32,1280]{3,2,1,0:T(8,128)(2,1)S(1)} %fusion), kind=kOutput, calls=%fused_computation.6 | convolution fusion | flops 2202009600 | bytes 8683520 | tf_op jit(solution)/shard_map/jit(_pad)/pad | solution.py:162
  124.7 2.9 %pad_add_fusion = f32[4,8,32,960]{3,2,1,0:T(8,128)S(1)} fusion(f32[4,1,32,960]{3,2,1,0:T(8,128)S(1)} %convolution_bitcast_fusion, f32[4,1,32,960]{3,2,1,0:T(8,128)S(1)} %convolution_bitcast_fusion.1, f32[4,7,32,960]{3,2,1,0:T(8,128)S(1)} %fusion.72, f32[4,8,32,960]{3,2,1,0:T(8,128)S(1)} %fusion.1, bf16[4,8,32,1280]{3,2,1,0:T(8,128)(2,1)S(1)} %fusion, ...), kind=kOutput, calls=%fused_computation.3 | convolution fusion | flops 2520514560 | bytes 17367040 | tf_op jit(solution)/shard_map/frxc,cn->frxn/dot_general | solution.py:157
  129.4 3.5 %collective-permute-done.8 = f32[2,8]{1,0:T(2,128)S(1)} collective-permute-done((f32[2,8]{1,0:T(2,128)S(1)}, f32[2,8]{1,0:T(2,128)S(1)}, u32[]{:S(2)}, u32[]{:S(2)}) %collective-permute-start.8) | collective-permute-done | bytes 96 | tf_op jit(solution)/shard_map/ppermute | solution.py:18
  134.7 1.5 collective-permute-start.10
  136.2 12.4 %collective-permute-done.10 = bf16[3,1280,80]{1,2,0:T(8,128)(2,1)} collective-permute-done((bf16[3,1280,80]{1,2,0:T(8,128)(2,1)S(1)}, bf16[3,1280,80]{1,2,0:T(8,128)(2,1)}, u32[]{:S(2)}, u32[]{:S(2)}) %collective-permute-start.10) | collective-permute-done | bytes 614432 | tf_op jit(solution)/shard_map/ppermute | solution.py:40
  149.3 1.5 copy.87
  150.8 1.5 copy.89
  152.4 2.2 copy.88
  154.6 1.7 select_select_fusion.7
  156.2 2.8 %pad_maximum_fusion.1 = bf16[3,1280,320]{2,1,0:T(8,128)(2,1)S(1)} fusion(bf16[3,1280,80]{2,1,0:T(8,128)(2,1)S(1)} %get-tuple-element.22, bf16[3,1280,80]{2,1,0:T(8,128)(2,1)S(1)} %get-tuple-element.23, bf16[3,1280,80]{2,1,0:T(8,128)(2,1)S(1)} %get-tuple-element.24, bf16[3,1280,80]{2,1,0:T(8,128)(2,1)S(1)} %get-tuple-element.21), kind=kLoop, calls=%fused_computation.4 | loop fusion | flops 9830400 | bytes 4915200 | tf_op jit(solution)/shard_map/concatenate | solution.py:51
  159.0 4.4 %copy.103 = bf16[4,4,80,3,320]{4,3,2,1,0:T(4,128)(2,1)} copy(bf16[4,4,80,3,320]{4,2,0,1,3:T(8,128)(2,1)S(1)} %bitcast.163) | data formatting | bytes 4915200 | tf_op jit(solution)/shard_map/transpose | solution.py:207
  163.4 6.9 %reshape.340 = bf16[4,320,960]{2,1,0:T(8,128)(2,1)S(1)} reshape(bf16[4,4,80,3,320]{4,3,2,1,0:T(4,128)(2,1)} %copy.103) | data formatting | bytes 4915200 | tf_op jit(solution)/shard_map/reshape | solution.py:207
  170.3 3.2 %fusion.20 = f32[4,8,32,960]{3,2,1,0:T(8,128)} fusion(bf16[4,8,32,320]{3,2,1,0:T(8,128)(2,1)S(1)} %copy-done.1, bf16[4,320,960]{2,1,0:T(8,128)(2,1)S(1)} %reshape.340, s32[]{:T(128)S(6)} %select_n.448), kind=kOutput, calls=%fused_computation.42 | convolution fusion | flops 629145600 | bytes 5373956 | tf_op jit(solution)/shard_map/frxc,cn->frxn/dot_general | solution.py:211
  173.6 22.6 %all-gather.6.cloned.1.call-done = bf16[16,8,32,320]{3,2,1,0:T(8,128)(2,1)} async-done(((bf16[4,8,32,320]{3,2,1,0:T(8,128)(2,1)}), bf16[16,8,32,320]{3,2,1,0:T(8,128)(2,1)}) %all-gather.6.cloned.1.call-update) | async-done | bytes 2621456 | tf_op jit(solution)/shard_map/all_gather | solution.py:205
  196.1 2.5 %fusion.10 = f32[4,8,32,960]{3,2,1,0:T(8,128)S(1)} fusion(bf16[4,4,8,32,320]{4,3,2,1,0:T(8,128)(2,1)} %bitcast.173, s32[]{:T(128)S(6)} %select_n.476, bf16[4,320,960]{2,1,0:T(8,128)(2,1)S(1)} %reshape.340), kind=kOutput, calls=%fused_computation.32 | convolution fusion | flops 629145600 | bytes 5374976 | tf_op jit(solution)/shard_map/frxc,cn->frxn/dot_general | solution.py:211
  204.5 2.7 %collective-permute-start.14 = (bf16[1,8,32,320]{3,2,1,0:T(8,128)(2,1)S(1)}, bf16[1,8,32,320]{3,2,1,0:T(8,128)(2,1)S(1)}, u32[]{:S(2)}, u32[]{:S(2)}) collective-permute-start(bf16[1,8,32,320]{3,2,1,0:T(8,128)(2,1)S(1)} %get-tuple-element.31), channel_id=1, source_target_pairs={{0,6},{2,0},{4,2},{6,4},{1,7},{3,1},{5,3},{7,5},{8,14},{10,8},{12,... | collective-permute-start | bytes 491528 | tf_op jit(solution)/shard_map/ppermute | solution.py:231
  207.2 5.7 %collective-permute-done.12 = bf16[1,8,32,320]{3,2,1,0:T(8,128)(2,1)S(1)} collective-permute-done((bf16[1,8,32,320]{3,2,1,0:T(8,128)(2,1)S(1)}, bf16[1,8,32,320]{3,2,1,0:T(8,128)(2,1)S(1)}, u32[]{:S(2)}, u32[]{:S(2)}) %collective-permute-start.12) | collective-permute-done | bytes 163872 | tf_op jit(solution)/shard_map/ppermute | solution.py:231
  212.9 7.2 %collective-permute-done.13 = bf16[1,8,32,320]{3,2,1,0:T(8,128)(2,1)S(1)} collective-permute-done((bf16[1,8,32,320]{3,2,1,0:T(8,128)(2,1)S(1)}, bf16[1,8,32,320]{3,2,1,0:T(8,128)(2,1)S(1)}, u32[]{:S(2)}, u32[]{:S(2)}) %collective-permute-start.13) | collective-permute-done | bytes 163872 | tf_op jit(solution)/shard_map/ppermute | solution.py:231
  (113 shorter events, 23.9 us)
Async XLA Ops:
  6.5 100.0 %all-gather.4.cloned.1.call-start = ((), (), s32[]{:S(2)}) async-start(), calls=%async_computation | async-start | bytes 3276800 | tf_op jit(solution)/shard_map/all_gather | solution.py:119
  6.5 43.4 %collective-permute-start.4 = (bf16[3,1280,3,80]{1,3,2,0:T(8,128)(2,1)}, bf16[3,1280,3,80]{1,3,2,0:T(8,128)(2,1)S(1)}, u32[]{:S(2)}, u32[]{:S(2)}) collective-permute-start(bf16[3,1280,3,80]{1,3,2,0:T(8,128)(2,1)} %bitcast.170), channel_id=1, source_target_pairs={{0,16},{8,24},{16,0},{24,8},{1,17},{9,25},{17,1},{25,9},{2,18},{10... | collective-permute-start | bytes 5529608 | tf_op jit(solution)/shard_map/ppermute | solution.py:40
  9.5 55.0 %collective-permute-start.3 = (bf16[3,1280,3,80]{1,3,2,0:T(8,128)(2,1)}, bf16[3,1280,3,80]{1,3,2,0:T(8,128)(2,1)}, u32[]{:S(2)}, u32[]{:S(2)}) collective-permute-start(bf16[3,1280,3,80]{1,3,2,0:T(8,128)(2,1)} %bitcast.171), channel_id=1, source_target_pairs={{0,8},{8,0},{16,24},{24,16},{1,9},{9,1},{17,25},{25,17},{2,10},{10... | collective-permute-start | bytes 5529608 | tf_op jit(solution)/shard_map/ppermute | solution.py:41
  49.9 14.6 %collective-permute-start.5 = (bf16[3,1280,3,80]{1,3,2,0:T(8,128)(2,1)S(1)}, bf16[3,1280,3,80]{1,3,2,0:T(8,128)(2,1)}, u32[]{:S(2)}, u32[]{:S(2)}) collective-permute-start(bf16[3,1280,3,80]{1,3,2,0:T(8,128)(2,1)S(1)} %collective-permute-done.4), channel_id=1, source_target_pairs={{0,8},{8,0},{16,24},{24,16},{1,9},{9,1},{17,25},{25,17},{2,10},{10... | collective-permute-start | bytes 5529608 | tf_op jit(solution)/shard_map/ppermute | solution.py:42
  49.9 146.2 %all-gather.6.cloned.1.call-start = ((), (), s32[]{:S(2)}) async-start(), calls=%async_computation.1 | async-start | bytes 3932160 | tf_op jit(solution)/shard_map/all_gather | solution.py:205
  51.7 4.3 %collective-permute-start = (f32[2,32]{1,0:T(2,128)S(1)}, f32[2,32]{1,0:T(2,128)S(1)}, u32[]{:S(2)}, u32[]{:S(2)}) collective-permute-start(f32[2,32]{1,0:T(2,128)S(1)} %pad_maximum_fusion.2), channel_id=1, source_target_pairs={{0,2},{2,0},{4,6},{6,4},{1,3},{3,1},{5,7},{7,5},{8,10},{10,8},{12,... | collective-permute-start | bytes 776 | tf_op jit(solution)/shard_map/ppermute | solution.py:30
  56.0 4.5 %collective-permute-start.1 = (f32[2,32]{1,0:T(2,128)S(1)}, f32[2,32]{1,0:T(2,128)S(1)}, u32[]{:S(2)}, u32[]{:S(2)}) collective-permute-start(f32[2,32]{1,0:T(2,128)S(1)} %fusion.61), channel_id=1, source_target_pairs={{0,4},{2,6},{4,0},{6,2},{1,5},{3,7},{5,1},{7,3},{8,12},{10,14},{12... | collective-permute-start | bytes 776 | tf_op jit(solution)/shard_map/ppermute | solution.py:30
  60.5 3.6 %collective-permute-start.2 = (f32[2,32]{1,0:T(2,128)S(1)}, f32[2,32]{1,0:T(2,128)S(1)}, u32[]{:S(2)}, u32[]{:S(2)}) collective-permute-start(f32[2,32]{1,0:T(2,128)S(1)} %fusion.81), channel_id=1, source_target_pairs={{0,1},{1,0},{2,3},{3,2},{4,5},{5,4},{6,7},{7,6},{8,9},{9,8},{10,11... | collective-permute-start | bytes 776 | tf_op jit(solution)/shard_map/ppermute | solution.py:30
  73.1 40.7 %copy-start.7 = (f32[1280]{0:T(1024)S(1)}, f32[1280]{0:T(1024)}, u32[]{:S(2)}) copy-start(f32[1280]{0:T(1024)} %param.13) | copy-start | bytes 15364
  73.1 40.7 %copy-start.8 = (f32[1280]{0:T(1024)S(1)}, f32[1280]{0:T(1024)}, u32[]{:S(2)}) copy-start(f32[1280]{0:T(1024)} %param.12) | copy-start | bytes 15364
  107.6 15.3 %collective-permute-start.7 = (bf16[1,4,1,32,1280]{4,3,2,0,1:T(8,128)(2,1)S(1)}, bf16[1,4,1,32,1280]{4,3,2,0,1:T(8,128)(2,1)S(1)}, u32[]{:S(2)}, u32[]{:S(2)}) collective-permute-start(bf16[1,4,1,32,1280]{4,3,2,0,1:T(8,128)(2,1)S(1)} %get-tuple-element.26), channel_id=1, source_target_pairs={{1,0},{3,2},{5,4},{7,6},{9,8},{11,10},{13,12},{15,14},{17,16},{19,... | collective-permute-start | bytes 983048 | tf_op jit(solution)/shard_map/ppermute | solution.py:126
  108.9 8.5 %copy-start.4 = (bf16[1,1280,3,320]{1,3,2,0:T(8,128)(2,1)S(1)}, bf16[1,1280,3,320]{1,3,2,0:T(8,128)(2,1)}, u32[]{:S(2)}) copy-start(bf16[1,1280,3,320]{1,3,2,0:T(8,128)(2,1)} %get-tuple-element.11) | copy-start | bytes 7372804
  108.9 14.9 %collective-permute-start.6 = (bf16[1,4,1,32,1280]{4,3,2,0,1:T(8,128)(2,1)S(1)}, bf16[1,4,1,32,1280]{4,3,2,0,1:T(8,128)(2,1)S(1)}, u32[]{:S(2)}, u32[]{:S(2)}) collective-permute-start(bf16[1,4,1,32,1280]{4,3,2,0,1:T(8,128)(2,1)S(1)} %get-tuple-element.25), channel_id=1, source_target_pairs={{0,1},{2,3},{4,5},{6,7},{8,9},{10,11},{12,13},{14,15},{16,17},{18,... | collective-permute-start | bytes 983048 | tf_op jit(solution)/shard_map/ppermute | solution.py:125
  117.4 2.6 %copy-start.3 = (bf16[1,1280,3,320]{1,3,2,0:T(8,128)(2,1)S(1)}, bf16[1,1280,3,320]{1,3,2,0:T(8,128)(2,1)}, u32[]{:S(2)}) copy-start(bf16[1,1280,3,320]{1,3,2,0:T(8,128)(2,1)} %get-tuple-element.12) | copy-start | bytes 7372804
  128.8 5.8 %copy-start.6 = (bf16[3,1280,80]{1,2,0:T(8,128)(2,1)S(1)}, bf16[3,1280,80]{1,2,0:T(8,128)(2,1)}, u32[]{:S(2)}) copy-start(bf16[3,1280,80]{1,2,0:T(8,128)(2,1)} %param.11) | copy-start | bytes 1843204
  129.3 3.6 %collective-permute-start.8 = (f32[2,8]{1,0:T(2,128)S(1)}, f32[2,8]{1,0:T(2,128)S(1)}, u32[]{:S(2)}, u32[]{:S(2)}) collective-permute-start(f32[2,8]{1,0:T(2,128)S(1)} %pad_maximum_fusion.3), channel_id=1, source_target_pairs={{0,1},{1,0},{2,3},{3,2},{4,5},{5,4},{6,7},{7,6},{8,9},{9,8},{10,11... | collective-permute-start | bytes 200 | tf_op jit(solution)/shard_map/ppermute | solution.py:18
  134.7 13.9 %collective-permute-start.10 = (bf16[3,1280,80]{1,2,0:T(8,128)(2,1)S(1)}, bf16[3,1280,80]{1,2,0:T(8,128)(2,1)}, u32[]{:S(2)}, u32[]{:S(2)}) collective-permute-start(bf16[3,1280,80]{1,2,0:T(8,128)(2,1)S(1)} %copy-done.6), channel_id=1, source_target_pairs={{0,16},{8,24},{16,0},{24,8},{1,17},{9,25},{17,1},{25,9},{2,18},{10... | collective-permute-start | bytes 1843208 | tf_op jit(solution)/shard_map/ppermute | solution.py:40
  136.2 14.6 %collective-permute-start.9 = (bf16[3,1280,80]{1,2,0:T(8,128)(2,1)S(1)}, bf16[3,1280,80]{1,2,0:T(8,128)(2,1)}, u32[]{:S(2)}, u32[]{:S(2)}) collective-permute-start(bf16[3,1280,80]{1,2,0:T(8,128)(2,1)S(1)} %copy-done.6), channel_id=1, source_target_pairs={{0,8},{8,0},{16,24},{24,16},{1,9},{9,1},{17,25},{25,17},{2,10},{10... | collective-permute-start | bytes 1843208 | tf_op jit(solution)/shard_map/ppermute | solution.py:41
  148.6 3.8 %collective-permute-start.11 = (bf16[3,1280,80]{1,2,0:T(8,128)(2,1)}, bf16[3,1280,80]{1,2,0:T(8,128)(2,1)}, u32[]{:S(2)}, u32[]{:S(2)}) collective-permute-start(bf16[3,1280,80]{1,2,0:T(8,128)(2,1)} %collective-permute-done.10), channel_id=1, source_target_pairs={{0,8},{8,0},{16,24},{24,16},{1,9},{9,1},{17,25},{25,17},{2,10},{10... | collective-permute-start | bytes 1843208 | tf_op jit(solution)/shard_map/ppermute | solution.py:42
  163.4 6.9 %copy-start.1 = (bf16[4,8,32,320]{3,2,1,0:T(8,128)(2,1)S(1)}, bf16[4,8,32,320]{3,2,1,0:T(8,128)(2,1)}, u32[]{:S(2)}) copy-start(bf16[4,8,32,320]{3,2,1,0:T(8,128)(2,1)} %multiply_convert_fusion.1) | copy-start | bytes 1966084
  196.1 2.5 %copy-start.5 = (bf16[16,8,32,320]{3,2,1,0:T(8,128)(2,1)S(1)}, bf16[16,8,32,320]{3,2,1,0:T(8,128)(2,1)}, u32[]{:S(2)}) copy-start(bf16[16,8,32,320]{3,2,1,0:T(8,128)(2,1)} %all-gather.6.cloned.1.call-done) | copy-start | bytes 7864324
  198.7 2.2 copy-start
  203.1 9.7 %collective-permute-start.12 = (bf16[1,8,32,320]{3,2,1,0:T(8,128)(2,1)S(1)}, bf16[1,8,32,320]{3,2,1,0:T(8,128)(2,1)S(1)}, u32[]{:S(2)}, u32[]{:S(2)}) collective-permute-start(bf16[1,8,32,320]{3,2,1,0:T(8,128)(2,1)S(1)} %get-tuple-element.33), channel_id=1, source_target_pairs={{0,2},{2,4},{4,6},{6,0},{1,3},{3,5},{5,7},{7,1},{8,10},{10,12},{12... | collective-permute-start | bytes 491528 | tf_op jit(solution)/shard_map/ppermute | solution.py:231
  203.2 16.8 %collective-permute-start.13 = (bf16[1,8,32,320]{3,2,1,0:T(8,128)(2,1)S(1)}, bf16[1,8,32,320]{3,2,1,0:T(8,128)(2,1)S(1)}, u32[]{:S(2)}, u32[]{:S(2)}) collective-permute-start(bf16[1,8,32,320]{3,2,1,0:T(8,128)(2,1)S(1)} %get-tuple-element.32), channel_id=1, source_target_pairs={{0,4},{2,6},{4,0},{6,2},{1,5},{3,7},{5,1},{7,3},{8,12},{10,14},{12... | collective-permute-start | bytes 491528 | tf_op jit(solution)/shard_map/ppermute | solution.py:231
  204.5 15.5 %collective-permute-start.14 = (bf16[1,8,32,320]{3,2,1,0:T(8,128)(2,1)S(1)}, bf16[1,8,32,320]{3,2,1,0:T(8,128)(2,1)S(1)}, u32[]{:S(2)}, u32[]{:S(2)}) collective-permute-start(bf16[1,8,32,320]{3,2,1,0:T(8,128)(2,1)S(1)} %get-tuple-element.31), channel_id=1, source_target_pairs={{0,6},{2,0},{4,2},{6,4},{1,7},{3,1},{5,3},{7,5},{8,14},{10,8},{12,... | collective-permute-start | bytes 491528 | tf_op jit(solution)/shard_map/ppermute | solution.py:231
  222.6 1.4 copy-start.2
  222.7 1.4 copy-start.9
Sparse Core Ops, SparseCore 0:
  50.0 56.3 all-gather.3
  134.8 61.2 all-gather.5

commit v13 on v12

--- a/solution.py
+++ b/solution.py
@@ -119,14 +119,7 @@
     raw = lax.all_gather(activations, "frame", axis=1, tiled=True)
     frames = raw.shape[1]
 
-    if row_size > 1:
-        down = [(i, i + 1) for i in range(row_size - 1)]
-        up = [(i + 1, i) for i in range(row_size - 1)]
-        above = lax.ppermute(raw[:, :, rows - 1 :], "row", down)
-        below = lax.ppermute(raw[:, :, :1], "row", up)
-    else:
-        above = jnp.zeros_like(raw[:, :, :1])
-        below = jnp.zeros_like(raw[:, :, :1])
+    edge_low, edge_high = raw[:, :, rows - 1 :], raw[:, :, :1]
 
     grouped = activations.astype(jnp.float32).reshape(1, -1, GROUPS, width)
     stats = jnp.concatenate(
@@ -146,19 +139,28 @@
         return silu_bf16(normed)
 
     first_mid = lax.optimization_barrier(first_norm(raw)[0])
+
+    wide = spatial_w.reshape(3, channels, 3 * local)
+
+    def tap(field, row_tap):
+        return jnp.einsum(
+            "frxc,cn->frxn", field, wide[row_tap], preferred_element_type=jnp.float32
+        )
+
+    product = tap(first_mid, 1)
+    (edge_low, edge_high), product = lax.optimization_barrier(((edge_low, edge_high), product))
+    if row_size > 1:
+        down = [(i, i + 1) for i in range(row_size - 1)]
+        up = [(i + 1, i) for i in range(row_size - 1)]
+        above = lax.ppermute(edge_low, "row", down)
+        below = lax.ppermute(edge_high, "row", up)
+    else:
+        above = jnp.zeros_like(edge_low)
+        below = jnp.zeros_like(edge_high)
     first_above = jnp.where(row_index > 0, first_norm(above), jnp.zeros((), jnp.bfloat16))[0]
     first_below = jnp.where(
         row_index < row_size - 1, first_norm(below), jnp.zeros((), jnp.bfloat16)
     )[0]
-
-    wide = spatial_w.reshape(3, channels, 3 * local)
-
-    def tap(field, row_tap):
-        return jnp.einsum(
-            "frxc,cn->frxn", field, wide[row_tap], preferred_element_type=jnp.float32
-        )
-
-    product = tap(first_mid, 1)
     product = product + jnp.pad(tap(first_mid[:, :-1], 0), ((0, 0), (1, 0), (0, 0), (0, 0)))
     product = product + jnp.pad(tap(first_mid[:, 1:], 2), ((0, 0), (0, 1), (0, 0), (0, 0)))
     product = product + jnp.pad(tap(first_above, 0), ((0, 0), (0, rows - 1), (0, 0), (0, 0)))

time: 234 us -> 238 us (1.017)
  waiting for transfers between devices: 126 us -> 129 us
    ppermute x2, waiting for transfers between devices: 0.01 us -> 2.82 us  [the longest x1 2.54 us: shards(): below = lax.ppermute(edge_high, 'row', up)]
    ppermute x1, starting transfers between devices: 0.07 us -> 2.55 us  [pair_sum(): lax.ppermute(v, axis, [(0, 1), (1, 0)])]
  transfers between devices with their start and end apart: 17 -> 17, of which waited for: 9 -> 11; matrix products, arithmetic and copies ran while one was open for 22% -> 19% of each run, Pallas kernels for 0% -> 0%
where the time goes in v13:
time: 238 us; the launch traced here: 237 us
  waiting for transfers between devices  129 us (54%)
  local copies, waits for them, and re-layouts  30 us (13%)
  starting transfers between devices  23.3 us (10%)
  other arithmetic  22.6 us (9%)
  matrix products  18.5 us (8%)
  between operations  14 us (6%)
    ppermute x2, waiting for transfers between devices, gather_rep(): across = lax.ppermute(w, 'rep', [(k, k ^ 2) for k in range(size)])  52.5 us
    all_gather x1, waiting for transfers between devices, shards(): raw = lax.all_gather(activations, 'frame', axis=1, tiled=True)  30.6 us
    all_gather x1, waiting for transfers between devices, shards(): second_all = lax.all_gather(second[0], 'frame', axis=0, tiled=False)  24.5 us
    ppermute x3, waiting for transfers between devices, shards(): lax.ppermute(piece, 'frame', [(k, (k + shift) % frame_size) for k in rang...  12.8 us
    dot_general x4, matrix products, product(): jnp.einsum('frxc,cn->frxn', source, weights, preferred_element_type=jnp.f...  8.29 us
    concatenate x2, other arithmetic, gather_rep(): return jnp.concatenate(blocks, axis=-1)  8.27 us
    dot_general x4, matrix products, tap(): jnp.einsum('frxc,cn->frxn', field, wide[row_tap], preferred_element_type=...  7.28 us
    reshape x1, local copies, waits for them, and re-layouts, shards(): taps.transpose(2, 1, 3, 0, 4)  6.93 us
  transfers between devices with their start and end apart: 17, of which 11 were waited for; matrix products, arithmetic and copies ran while one was open for 19% of the time, Pallas kernels for 0%

profile of v13, /device:TPU:0, one launch (start us, length us, event | category | flops | bytes accessed | tf_op | source)
XLA Modules:
  0.0 237.0 jit_solution(13811717126703076928)
XLA Ops:
  6.5 3.0 %collective-permute-start.4 = (bf16[3,1280,3,80]{1,3,2,0:T(8,128)(2,1)}, bf16[3,1280,3,80]{1,3,2,0:T(8,128)(2,1)S(1)}, u32[]{:S(2)}, u32[]{:S(2)}) collective-permute-start(bf16[3,1280,3,80]{1,3,2,0:T(8,128)(2,1)} %bitcast.170), channel_id=1, source_target_pairs={{0,16},{8,24},{16,0},{24,8},{1,17},{9,25},{17,1},{25,9},{2,18},{10... | collective-permute-start | bytes 5529608 | tf_op jit(solution)/shard_map/ppermute | solution.py:40
  9.5 40.4 %collective-permute-done.4 = bf16[3,1280,3,80]{1,3,2,0:T(8,128)(2,1)S(1)} collective-permute-done((bf16[3,1280,3,80]{1,3,2,0:T(8,128)(2,1)}, bf16[3,1280,3,80]{1,3,2,0:T(8,128)(2,1)S(1)}, u32[]{:S(2)}, u32[]{:S(2)}) %collective-permute-start.4) | collective-permute-done | bytes 1843232 | tf_op jit(solution)/shard_map/ppermute | solution.py:40
  51.7 1.9 collective-permute-start
  56.0 2.7 %collective-permute-start.1 = (f32[2,32]{1,0:T(2,128)S(1)}, f32[2,32]{1,0:T(2,128)S(1)}, u32[]{:S(2)}, u32[]{:S(2)}) collective-permute-start(f32[2,32]{1,0:T(2,128)S(1)} %fusion.63), channel_id=1, source_target_pairs={{0,4},{2,6},{4,0},{6,2},{1,5},{3,7},{5,1},{7,3},{8,12},{10,14},{12... | collective-permute-start | bytes 776 | tf_op jit(solution)/shard_map/ppermute | solution.py:30
  58.6 1.9 collective-permute-done.1
  60.5 1.6 collective-permute-start.2
  62.3 1.9 collective-permute-done.2
  64.5 3.1 %select_select_fusion.3 = (bf16[3,1280,3,80]{1,3,2,0:T(8,128)(2,1)S(1)}, bf16[3,1280,3,80]{1,3,2,0:T(8,128)(2,1)S(1)}, bf16[3,1280,3,80]{1,3,2,0:T(8,128)(2,1)S(1)}, bf16[3,1280,3,80]{1,3,2,0:T(8,128)(2,1)S(1)}) fusion(bf16[3,1280,3,80]{1,3,2,0:T(8,128)(2,1)} %bitcast.172, bf16[3,1280,3,80]{1,3,2,0:T(8,128)(2,1)} %collective-permute-done.3, ...), kind=kLoop, calls=%fused_computation.14 | loop fusion | flops 11059200 | bytes 14745612 | tf_op jit(solution)/shard_map/jit(_where)/select_n | solution.py:49
  67.6 5.5 %pad_maximum_fusion = bf16[3,1280,3,320]{1,3,2,0:T(8,128)(2,1)S(1)} fusion(bf16[3,1280,3,80]{1,3,2,0:T(8,128)(2,1)S(1)} %get-tuple-element.20, bf16[3,1280,3,80]{1,3,2,0:T(8,128)(2,1)S(1)} %get-tuple-element.21, bf16[3,1280,3,80]{1,3,2,0:T(8,128)(2,1)S(1)} %get-tuple-element.22, bf16[3,1280,3,80]{1,3,2,0:T(8,128)(2,1)S(1)} %get-tuple-element.19), kind=kLoop, calls=%fused_computation | loop fusion | flops 29491200 | bytes 14745600 | tf_op jit(solution)/shard_map/concatenate | solution.py:51
  73.1 2.7 %fusion.66 = (bf16[1,1280,3,320]{1,3,2,0:T(8,128)(2,1)S(1)}, bf16[1,1280,3,320]{1,3,2,0:T(8,128)(2,1)}, bf16[1,1280,3,320]{1,3,2,0:T(8,128)(2,1)}) fusion(bf16[3,1280,3,320]{1,3,2,0:T(8,128)(2,1)S(1)} %pad_maximum_fusion), kind=kLoop, calls=%fused_computation.117 | loop fusion | bytes 14745600 | tf_op jit(solution)/shard_map/slice | solution.py:147
  75.9 30.6 %all-gather.4.cloned.1.call-done = bf16[1,4,8,32,1280]{4,3,2,0,1:T(8,128)(2,1)} async-done(((bf16[1,1,8,32,1280]{4,3,2,0,1:T(8,128)(2,1)}), bf16[1,4,8,32,1280]{4,3,2,0,1:T(8,128)(2,1)}) %all-gather.4.cloned.1.call-update) | async-done | bytes 2621456 | tf_op jit(solution)/shard_map/all_gather | solution.py:119
  106.5 3.7 %fusion = bf16[4,8,32,1280]{3,2,1,0:T(8,128)(2,1)S(1)} fusion(bf16[1,4,8,32,1280]{4,3,2,0,1:T(8,128)(2,1)} %all-gather.4.cloned.1.call-done, f32[1280]{0:T(1024)S(1)} %copy-done.7, f32[1280]{0:T(1024)S(1)} %copy-done.8, f32[1280]{0:T(1024)S(1)} %mul.103, f32[1280]{0:T(1024)S(1)} %sub.50), kind=kLoop, calls=%fused_computation.5 | loop fusion | flops 13107200 | bytes 5263360 | tf_op jit(solution)/shard_map/squeeze | solution.py:141
  110.2 2.9 %fusion.74 = f32[4,8,32,960]{3,2,1,0:T(8,128)S(1)} fusion(bf16[4,8,32,1280]{3,2,1,0:T(8,128)(2,1)S(1)} %fusion, bf16[1280,960,1,1]{0,1,3,2:T(8,128)(2,1)S(1)} %bitcast.169), kind=kOutput, calls=%fused_computation.125 | convolution fusion | flops 2516582400 | bytes 9011200 | tf_op jit(solution)/shard_map/frxc,cn->frxn/dot_general | solution.py:146
  115.5 4.8 %collective-permute-start.6 = (bf16[1,4,1,32,1280]{4,3,2,0,1:T(8,128)(2,1)S(1)}, bf16[1,4,1,32,1280]{4,3,2,0,1:T(8,128)(2,1)S(1)}, u32[]{:S(2)}, u32[]{:S(2)}) collective-permute-start(bf16[1,4,1,32,1280]{4,3,2,0,1:T(8,128)(2,1)S(1)} %get-tuple-element.9), channel_id=1, source_target_pairs={{0,1},{2,3},{4,5},{6,7},{8,9},{10,11},{12,13},{14,15},{16,17},{18,... | collective-permute-start | bytes 983048 | tf_op jit(solution)/shard_map/ppermute | solution.py:155
  120.3 2.6 %fusion.75 = f32[4,7,32,960]{3,2,1,0:T(8,128)S(1)} fusion(bf16[4,8,32,1280]{3,2,1,0:T(8,128)(2,1)S(1)} %fusion, bf16[1280,960,1,1]{0,1,3,2:T(8,128)(2,1)S(1)} %bitcast.167), kind=kOutput, calls=%fused_computation.126 | convolution fusion | flops 2202009600 | bytes 8519680 | tf_op jit(solution)/shard_map/frxc,cn->frxn/dot_general | solution.py:146
  122.9 2.5 %collective-permute-done.7 = bf16[1,4,1,32,1280]{4,3,2,0,1:T(8,128)(2,1)S(1)} collective-permute-done((bf16[1,4,1,32,1280]{4,3,2,0,1:T(8,128)(2,1)S(1)}, bf16[1,4,1,32,1280]{4,3,2,0,1:T(8,128)(2,1)S(1)}, u32[]{:S(2)}, u32[]{:S(2)}) %collective-permute-start.7) | collective-permute-done | bytes 327712 | tf_op jit(solution)/shard_map/ppermute | solution.py:156
  127.5 2.9 %pad_add_fusion = f32[4,8,32,960]{3,2,1,0:T(8,128)S(1)} fusion(f32[4,1,32,960]{3,2,1,0:T(8,128)S(1)} %convolution_bitcast_fusion, f32[4,1,32,960]{3,2,1,0:T(8,128)S(1)} %convolution_bitcast_fusion.1, f32[4,7,32,960]{3,2,1,0:T(8,128)S(1)} %fusion.75, f32[4,8,32,960]{3,2,1,0:T(8,128)S(1)} %fusion.74, bf16[1280,960,1,1]{0,1,3,2:T(8,128)(2,1)S(1)} %bitcast.166, ...), kind=kOutput, calls=%fused_computation.3 | convolution fusion | flops 2205941760 | bytes 17596416 | tf_op jit(solution)/shard_map/jit(_pad)/pad | solution.py:164
  132.0 2.5 %collective-permute-start.8 = (f32[2,8]{1,0:T(2,128)S(1)}, f32[2,8]{1,0:T(2,128)S(1)}, u32[]{:S(2)}, u32[]{:S(2)}) collective-permute-start(f32[2,8]{1,0:T(2,128)S(1)} %pad_maximum_fusion.3), channel_id=1, source_target_pairs={{0,1},{1,0},{2,3},{3,2},{4,5},{5,4},{6,7},{7,6},{8,9},{9,8},{10,11... | collective-permute-start | bytes 200 | tf_op jit(solution)/shard_map/ppermute | solution.py:18
  139.4 12.1 %collective-permute-done.10 = bf16[3,1280,80]{1,2,0:T(8,128)(2,1)} collective-permute-done((bf16[3,1280,80]{1,2,0:T(8,128)(2,1)S(1)}, bf16[3,1280,80]{1,2,0:T(8,128)(2,1)}, u32[]{:S(2)}, u32[]{:S(2)}) %collective-permute-start.10) | collective-permute-done | bytes 614432 | tf_op jit(solution)/shard_map/ppermute | solution.py:40
  152.1 1.5 copy.87
  153.7 1.5 copy.89
  155.3 2.2 copy.88
  157.4 1.7 select_select_fusion.7
  159.1 2.8 %pad_maximum_fusion.1 = bf16[3,1280,320]{2,1,0:T(8,128)(2,1)S(1)} fusion(bf16[3,1280,80]{2,1,0:T(8,128)(2,1)S(1)} %get-tuple-element.28, bf16[3,1280,80]{2,1,0:T(8,128)(2,1)S(1)} %get-tuple-element.29, bf16[3,1280,80]{2,1,0:T(8,128)(2,1)S(1)} %get-tuple-element.30, bf16[3,1280,80]{2,1,0:T(8,128)(2,1)S(1)} %get-tuple-element.27), kind=kLoop, calls=%fused_computation.4 | loop fusion | flops 9830400 | bytes 4915200 | tf_op jit(solution)/shard_map/concatenate | solution.py:51
  161.9 4.4 %copy.103 = bf16[4,4,80,3,320]{4,3,2,1,0:T(4,128)(2,1)} copy(bf16[4,4,80,3,320]{4,2,0,1,3:T(8,128)(2,1)S(1)} %bitcast.163) | data formatting | bytes 4915200 | tf_op jit(solution)/shard_map/transpose | solution.py:209
  166.3 6.9 %reshape.340 = bf16[4,320,960]{2,1,0:T(8,128)(2,1)S(1)} reshape(bf16[4,4,80,3,320]{4,3,2,1,0:T(4,128)(2,1)} %copy.103) | data formatting | bytes 4915200 | tf_op jit(solution)/shard_map/reshape | solution.py:209
  173.2 3.2 %fusion.22 = f32[4,8,32,960]{3,2,1,0:T(8,128)} fusion(bf16[4,8,32,320]{3,2,1,0:T(8,128)(2,1)S(1)} %copy-done.1, bf16[4,320,960]{2,1,0:T(8,128)(2,1)S(1)} %reshape.340, s32[]{:T(128)S(6)} %select_n.448), kind=kOutput, calls=%fused_computation.42 | convolution fusion | flops 629145600 | bytes 5373956 | tf_op jit(solution)/shard_map/frxc,cn->frxn/dot_general | solution.py:213
  176.4 24.5 %all-gather.6.cloned.1.call-done = bf16[16,8,32,320]{3,2,1,0:T(8,128)(2,1)} async-done(((bf16[4,8,32,320]{3,2,1,0:T(8,128)(2,1)}), bf16[16,8,32,320]{3,2,1,0:T(8,128)(2,1)}) %all-gather.6.cloned.1.call-update) | async-done | bytes 2621456 | tf_op jit(solution)/shard_map/all_gather | solution.py:207
  201.0 2.5 %fusion.12 = f32[4,8,32,960]{3,2,1,0:T(8,128)S(1)} fusion(bf16[4,4,8,32,320]{4,3,2,1,0:T(8,128)(2,1)} %bitcast.173, s32[]{:T(128)S(6)} %select_n.476, bf16[4,320,960]{2,1,0:T(8,128)(2,1)S(1)} %reshape.340), kind=kOutput, calls=%fused_computation.32 | convolution fusion | flops 629145600 | bytes 5374976 | tf_op jit(solution)/shard_map/frxc,cn->frxn/dot_general | solution.py:213
  209.3 2.7 %collective-permute-start.14 = (bf16[1,8,32,320]{3,2,1,0:T(8,128)(2,1)S(1)}, bf16[1,8,32,320]{3,2,1,0:T(8,128)(2,1)S(1)}, u32[]{:S(2)}, u32[]{:S(2)}) collective-permute-start(bf16[1,8,32,320]{3,2,1,0:T(8,128)(2,1)S(1)} %get-tuple-element.37), channel_id=1, source_target_pairs={{0,6},{2,0},{4,2},{6,4},{1,7},{3,1},{5,3},{7,5},{8,14},{10,8},{12,... | collective-permute-start | bytes 491528 | tf_op jit(solution)/shard_map/ppermute | solution.py:233
  212.0 5.7 %collective-permute-done.12 = bf16[1,8,32,320]{3,2,1,0:T(8,128)(2,1)S(1)} collective-permute-done((bf16[1,8,32,320]{3,2,1,0:T(8,128)(2,1)S(1)}, bf16[1,8,32,320]{3,2,1,0:T(8,128)(2,1)S(1)}, u32[]{:S(2)}, u32[]{:S(2)}) %collective-permute-start.12) | collective-permute-done | bytes 163872 | tf_op jit(solution)/shard_map/ppermute | solution.py:233
  217.7 7.2 %collective-permute-done.13 = bf16[1,8,32,320]{3,2,1,0:T(8,128)(2,1)S(1)} collective-permute-done((bf16[1,8,32,320]{3,2,1,0:T(8,128)(2,1)S(1)}, bf16[1,8,32,320]{3,2,1,0:T(8,128)(2,1)S(1)}, u32[]{:S(2)}, u32[]{:S(2)}) %collective-permute-start.13) | collective-permute-done | bytes 163872 | tf_op jit(solution)/shard_map/ppermute | solution.py:233
  (113 shorter events, 27.0 us)
Async XLA Ops:
  6.5 100.0 %all-gather.4.cloned.1.call-start = ((), (), s32[]{:S(2)}) async-start(), calls=%async_computation | async-start | bytes 3276800 | tf_op jit(solution)/shard_map/all_gather | solution.py:119
  6.5 43.4 %collective-permute-start.4 = (bf16[3,1280,3,80]{1,3,2,0:T(8,128)(2,1)}, bf16[3,1280,3,80]{1,3,2,0:T(8,128)(2,1)S(1)}, u32[]{:S(2)}, u32[]{:S(2)}) collective-permute-start(bf16[3,1280,3,80]{1,3,2,0:T(8,128)(2,1)} %bitcast.170), channel_id=1, source_target_pairs={{0,16},{8,24},{16,0},{24,8},{1,17},{9,25},{17,1},{25,9},{2,18},{10... | collective-permute-start | bytes 5529608 | tf_op jit(solution)/shard_map/ppermute | solution.py:40
  9.5 55.0 %collective-permute-start.3 = (bf16[3,1280,3,80]{1,3,2,0:T(8,128)(2,1)}, bf16[3,1280,3,80]{1,3,2,0:T(8,128)(2,1)}, u32[]{:S(2)}, u32[]{:S(2)}) collective-permute-start(bf16[3,1280,3,80]{1,3,2,0:T(8,128)(2,1)} %bitcast.171), channel_id=1, source_target_pairs={{0,8},{8,0},{16,24},{24,16},{1,9},{9,1},{17,25},{25,17},{2,10},{10... | collective-permute-start | bytes 5529608 | tf_op jit(solution)/shard_map/ppermute | solution.py:41
  49.9 14.6 %collective-permute-start.5 = (bf16[3,1280,3,80]{1,3,2,0:T(8,128)(2,1)S(1)}, bf16[3,1280,3,80]{1,3,2,0:T(8,128)(2,1)}, u32[]{:S(2)}, u32[]{:S(2)}) collective-permute-start(bf16[3,1280,3,80]{1,3,2,0:T(8,128)(2,1)S(1)} %collective-permute-done.4), channel_id=1, source_target_pairs={{0,8},{8,0},{16,24},{24,16},{1,9},{9,1},{17,25},{25,17},{2,10},{10... | collective-permute-start | bytes 5529608 | tf_op jit(solution)/shard_map/ppermute | solution.py:42
  49.9 151.0 %all-gather.6.cloned.1.call-start = ((), (), s32[]{:S(2)}) async-start(), calls=%async_computation.1 | async-start | bytes 3932160 | tf_op jit(solution)/shard_map/all_gather | solution.py:207
  51.7 4.3 %collective-permute-start = (f32[2,32]{1,0:T(2,128)S(1)}, f32[2,32]{1,0:T(2,128)S(1)}, u32[]{:S(2)}, u32[]{:S(2)}) collective-permute-start(f32[2,32]{1,0:T(2,128)S(1)} %pad_maximum_fusion.2), channel_id=1, source_target_pairs={{0,2},{2,0},{4,6},{6,4},{1,3},{3,1},{5,7},{7,5},{8,10},{10,8},{12,... | collective-permute-start | bytes 776 | tf_op jit(solution)/shard_map/ppermute | solution.py:30
  56.0 4.5 %collective-permute-start.1 = (f32[2,32]{1,0:T(2,128)S(1)}, f32[2,32]{1,0:T(2,128)S(1)}, u32[]{:S(2)}, u32[]{:S(2)}) collective-permute-start(f32[2,32]{1,0:T(2,128)S(1)} %fusion.63), channel_id=1, source_target_pairs={{0,4},{2,6},{4,0},{6,2},{1,5},{3,7},{5,1},{7,3},{8,12},{10,14},{12... | collective-permute-start | bytes 776 | tf_op jit(solution)/shard_map/ppermute | solution.py:30
  60.5 3.6 %collective-permute-start.2 = (f32[2,32]{1,0:T(2,128)S(1)}, f32[2,32]{1,0:T(2,128)S(1)}, u32[]{:S(2)}, u32[]{:S(2)}) collective-permute-start(f32[2,32]{1,0:T(2,128)S(1)} %fusion.84), channel_id=1, source_target_pairs={{0,1},{1,0},{2,3},{3,2},{4,5},{5,4},{6,7},{7,6},{8,9},{9,8},{10,11... | collective-permute-start | bytes 776 | tf_op jit(solution)/shard_map/ppermute | solution.py:30
  73.1 33.4 %copy-start.7 = (f32[1280]{0:T(1024)S(1)}, f32[1280]{0:T(1024)}, u32[]{:S(2)}) copy-start(f32[1280]{0:T(1024)} %param.13) | copy-start | bytes 15364
  73.1 33.4 %copy-start.8 = (f32[1280]{0:T(1024)S(1)}, f32[1280]{0:T(1024)}, u32[]{:S(2)}) copy-start(f32[1280]{0:T(1024)} %param.12) | copy-start | bytes 15364
  106.5 3.7 %copy-start.4 = (bf16[1,1280,3,320]{1,3,2,0:T(8,128)(2,1)S(1)}, bf16[1,1280,3,320]{1,3,2,0:T(8,128)(2,1)}, u32[]{:S(2)}) copy-start(bf16[1,1280,3,320]{1,3,2,0:T(8,128)(2,1)} %get-tuple-element.18) | copy-start | bytes 7372804
  110.2 10.1 %copy-start.3 = (bf16[1,1280,3,320]{1,3,2,0:T(8,128)(2,1)S(1)}, bf16[1,1280,3,320]{1,3,2,0:T(8,128)(2,1)}, u32[]{:S(2)}) copy-start(bf16[1,1280,3,320]{1,3,2,0:T(8,128)(2,1)} %get-tuple-element.17) | copy-start | bytes 7372804
  114.2 11.2 %collective-permute-start.7 = (bf16[1,4,1,32,1280]{4,3,2,0,1:T(8,128)(2,1)S(1)}, bf16[1,4,1,32,1280]{4,3,2,0,1:T(8,128)(2,1)S(1)}, u32[]{:S(2)}, u32[]{:S(2)}) collective-permute-start(bf16[1,4,1,32,1280]{4,3,2,0,1:T(8,128)(2,1)S(1)} %get-tuple-element.10), channel_id=1, source_target_pairs={{1,0},{3,2},{5,4},{7,6},{9,8},{11,10},{13,12},{15,14},{17,16},{19,... | collective-permute-start | bytes 983048 | tf_op jit(solution)/shard_map/ppermute | solution.py:156
  115.5 11.1 %collective-permute-start.6 = (bf16[1,4,1,32,1280]{4,3,2,0,1:T(8,128)(2,1)S(1)}, bf16[1,4,1,32,1280]{4,3,2,0,1:T(8,128)(2,1)S(1)}, u32[]{:S(2)}, u32[]{:S(2)}) collective-permute-start(bf16[1,4,1,32,1280]{4,3,2,0,1:T(8,128)(2,1)S(1)} %get-tuple-element.9), channel_id=1, source_target_pairs={{0,1},{2,3},{4,5},{6,7},{8,9},{10,11},{12,13},{14,15},{16,17},{18,... | collective-permute-start | bytes 983048 | tf_op jit(solution)/shard_map/ppermute | solution.py:155
  131.5 6.3 %copy-start.6 = (bf16[3,1280,80]{1,2,0:T(8,128)(2,1)S(1)}, bf16[3,1280,80]{1,2,0:T(8,128)(2,1)}, u32[]{:S(2)}) copy-start(bf16[3,1280,80]{1,2,0:T(8,128)(2,1)} %param.11) | copy-start | bytes 1843204
  132.0 4.1 %collective-permute-start.8 = (f32[2,8]{1,0:T(2,128)S(1)}, f32[2,8]{1,0:T(2,128)S(1)}, u32[]{:S(2)}, u32[]{:S(2)}) collective-permute-start(f32[2,8]{1,0:T(2,128)S(1)} %pad_maximum_fusion.3), channel_id=1, source_target_pairs={{0,1},{1,0},{2,3},{3,2},{4,5},{5,4},{6,7},{7,6},{8,9},{9,8},{10,11... | collective-permute-start | bytes 200 | tf_op jit(solution)/shard_map/ppermute | solution.py:18
  137.9 13.6 %collective-permute-start.10 = (bf16[3,1280,80]{1,2,0:T(8,128)(2,1)S(1)}, bf16[3,1280,80]{1,2,0:T(8,128)(2,1)}, u32[]{:S(2)}, u32[]{:S(2)}) collective-permute-start(bf16[3,1280,80]{1,2,0:T(8,128)(2,1)S(1)} %copy-done.6), channel_id=1, source_target_pairs={{0,16},{8,24},{16,0},{24,8},{1,17},{9,25},{17,1},{25,9},{2,18},{10... | collective-permute-start | bytes 1843208 | tf_op jit(solution)/shard_map/ppermute | solution.py:40
  139.4 14.3 %collective-permute-start.9 = (bf16[3,1280,80]{1,2,0:T(8,128)(2,1)S(1)}, bf16[3,1280,80]{1,2,0:T(8,128)(2,1)}, u32[]{:S(2)}, u32[]{:S(2)}) collective-permute-start(bf16[3,1280,80]{1,2,0:T(8,128)(2,1)S(1)} %copy-done.6), channel_id=1, source_target_pairs={{0,8},{8,0},{16,24},{24,16},{1,9},{9,1},{17,25},{25,17},{2,10},{10... | collective-permute-start | bytes 1843208 | tf_op jit(solution)/shard_map/ppermute | solution.py:41
  151.5 3.8 %collective-permute-start.11 = (bf16[3,1280,80]{1,2,0:T(8,128)(2,1)}, bf16[3,1280,80]{1,2,0:T(8,128)(2,1)}, u32[]{:S(2)}, u32[]{:S(2)}) collective-permute-start(bf16[3,1280,80]{1,2,0:T(8,128)(2,1)} %collective-permute-done.10), channel_id=1, source_target_pairs={{0,8},{8,0},{16,24},{24,16},{1,9},{9,1},{17,25},{25,17},{2,10},{10... | collective-permute-start | bytes 1843208 | tf_op jit(solution)/shard_map/ppermute | solution.py:42
  166.3 6.9 %copy-start.1 = (bf16[4,8,32,320]{3,2,1,0:T(8,128)(2,1)S(1)}, bf16[4,8,32,320]{3,2,1,0:T(8,128)(2,1)}, u32[]{:S(2)}) copy-start(bf16[4,8,32,320]{3,2,1,0:T(8,128)(2,1)} %multiply_convert_fusion.1) | copy-start | bytes 1966084
  201.0 2.5 %copy-start.5 = (bf16[16,8,32,320]{3,2,1,0:T(8,128)(2,1)S(1)}, bf16[16,8,32,320]{3,2,1,0:T(8,128)(2,1)}, u32[]{:S(2)}) copy-start(bf16[16,8,32,320]{3,2,1,0:T(8,128)(2,1)} %all-gather.6.cloned.1.call-done) | copy-start | bytes 7864324
  203.5 2.2 copy-start
  208.0 9.7 %collective-permute-start.12 = (bf16[1,8,32,320]{3,2,1,0:T(8,128)(2,1)S(1)}, bf16[1,8,32,320]{3,2,1,0:T(8,128)(2,1)S(1)}, u32[]{:S(2)}, u32[]{:S(2)}) collective-permute-start(bf16[1,8,32,320]{3,2,1,0:T(8,128)(2,1)S(1)} %get-tuple-element.39), channel_id=1, source_target_pairs={{0,2},{2,4},{4,6},{6,0},{1,3},{3,5},{5,7},{7,1},{8,10},{10,12},{12... | collective-permute-start | bytes 491528 | tf_op jit(solution)/shard_map/ppermute | solution.py:233
  208.1 16.8 %collective-permute-start.13 = (bf16[1,8,32,320]{3,2,1,0:T(8,128)(2,1)S(1)}, bf16[1,8,32,320]{3,2,1,0:T(8,128)(2,1)S(1)}, u32[]{:S(2)}, u32[]{:S(2)}) collective-permute-start(bf16[1,8,32,320]{3,2,1,0:T(8,128)(2,1)S(1)} %get-tuple-element.38), channel_id=1, source_target_pairs={{0,4},{2,6},{4,0},{6,2},{1,5},{3,7},{5,1},{7,3},{8,12},{10,14},{12... | collective-permute-start | bytes 491528 | tf_op jit(solution)/shard_map/ppermute | solution.py:233
  209.3 15.5 %collective-permute-start.14 = (bf16[1,8,32,320]{3,2,1,0:T(8,128)(2,1)S(1)}, bf16[1,8,32,320]{3,2,1,0:T(8,128)(2,1)S(1)}, u32[]{:S(2)}, u32[]{:S(2)}) collective-permute-start(bf16[1,8,32,320]{3,2,1,0:T(8,128)(2,1)S(1)} %get-tuple-element.37), channel_id=1, source_target_pairs={{0,6},{2,0},{4,2},{6,4},{1,7},{3,1},{5,3},{7,5},{8,14},{10,8},{12,... | collective-permute-start | bytes 491528 | tf_op jit(solution)/shard_map/ppermute | solution.py:233
  227.5 1.4 copy-start.2
  227.5 1.4 copy-start.9
Sparse Core Ops, SparseCore 0:
  50.0 56.3 all-gather.3
  138.0 62.9 all-gather.5

commit v14 on v12

--- a/solution.py
+++ b/solution.py
@@ -159,10 +159,8 @@
         )
 
     product = tap(first_mid, 1)
-    product = product + jnp.pad(tap(first_mid[:, :-1], 0), ((0, 0), (1, 0), (0, 0), (0, 0)))
-    product = product + jnp.pad(tap(first_mid[:, 1:], 2), ((0, 0), (0, 1), (0, 0), (0, 0)))
-    product = product + jnp.pad(tap(first_above, 0), ((0, 0), (0, rows - 1), (0, 0), (0, 0)))
-    product = product + jnp.pad(tap(first_below, 2), ((0, 0), (rows - 1, 0), (0, 0), (0, 0)))
+    product = product + tap(jnp.concatenate([first_above, first_mid[:, :-1]], axis=1), 0)
+    product = product + tap(jnp.concatenate([first_mid[:, 1:], first_below], axis=1), 2)
     left = jnp.pad(product[:, :, :-1, :local], ((0, 0), (0, 0), (1, 0), (0, 0)))
     right = jnp.pad(product[:, :, 1:, 2 * local :], ((0, 0), (0, 0), (0, 1), (0, 0)))
     spatial = (left + product[..., local : 2 * local] + right)[None]

time: 234 us -> 237 us (1.013)
  waiting for transfers between devices: 126 us -> 131 us
    ppermute x1, waiting for transfers between devices: 0.01 us -> 4.13 us  [shards(): below = lax.ppermute(raw[:, :, :1], 'row', up)]
    pad x1 -> x0, matrix products: 2.9 us -> none  [shards(): jnp.pad(tap(first_mid[:, :-1], 0), ((0, 0), (1, 0), (0, 0), (0, 0)))]
    dot_general x4 -> x3, matrix products: 7.32 us -> 8.73 us  [tap(): jnp.einsum('frxc,cn->frxn', field, wide[row_tap], preferred_element_type=...]
  transfers between devices with their start and end apart: 17 -> 17, of which waited for: 9 -> 12; matrix products, arithmetic and copies ran while one was open for 22% -> 19% of each run, Pallas kernels for 0% -> 0%
where the time goes in v14:
time: 237 us; the launch traced here: 236 us
  waiting for transfers between devices  131 us (55%)
  local copies, waits for them, and re-layouts  30.6 us (13%)
  other arithmetic  22.9 us (10%)
  starting transfers between devices  20.2 us (9%)
  matrix products  17 us (7%)
  between operations  14.1 us (6%)
    ppermute x2, waiting for transfers between devices, gather_rep(): across = lax.ppermute(w, 'rep', [(k, k ^ 2) for k in range(size)])  52.2 us
    all_gather x1, waiting for transfers between devices, shards(): raw = lax.all_gather(activations, 'frame', axis=1, tiled=True)  31.3 us
    all_gather x1, waiting for transfers between devices, shards(): second_all = lax.all_gather(second[0], 'frame', axis=0, tiled=False)  23.1 us
    ppermute x3, waiting for transfers between devices, shards(): lax.ppermute(piece, 'frame', [(k, (k + shift) % frame_size) for k in rang...  12.9 us
    dot_general x3, matrix products, tap(): jnp.einsum('frxc,cn->frxn', field, wide[row_tap], preferred_element_type=...  8.73 us
    concatenate x2, other arithmetic, gather_rep(): return jnp.concatenate(blocks, axis=-1)  8.49 us
    dot_general x4, matrix products, product(): jnp.einsum('frxc,cn->frxn', source, weights, preferred_element_type=jnp.f...  8.31 us
    reshape x1, local copies, waits for them, and re-layouts, shards(): taps.transpose(2, 1, 3, 0, 4)  6.94 us
  transfers between devices with their start and end apart: 17, of which 12 were waited for; matrix products, arithmetic and copies ran while one was open for 19% of the time, Pallas kernels for 0%

profile of v14, /device:TPU:0, one launch (start us, length us, event | category | flops | bytes accessed | tf_op | source)
XLA Modules:
  0.0 235.9 jit_solution(17304722456794516458)
XLA Ops:
  6.5 3.0 %collective-permute-start.4 = (bf16[3,1280,3,80]{1,3,2,0:T(8,128)(2,1)}, bf16[3,1280,3,80]{1,3,2,0:T(8,128)(2,1)S(1)}, u32[]{:S(2)}, u32[]{:S(2)}) collective-permute-start(bf16[3,1280,3,80]{1,3,2,0:T(8,128)(2,1)} %bitcast.155), channel_id=1, source_target_pairs={{0,16},{8,24},{16,0},{24,8},{1,17},{9,25},{17,1},{25,9},{2,18},{10... | collective-permute-start | bytes 5529608 | tf_op jit(solution)/shard_map/ppermute | solution.py:40
  9.5 40.4 %collective-permute-done.4 = bf16[3,1280,3,80]{1,3,2,0:T(8,128)(2,1)S(1)} collective-permute-done((bf16[3,1280,3,80]{1,3,2,0:T(8,128)(2,1)}, bf16[3,1280,3,80]{1,3,2,0:T(8,128)(2,1)S(1)}, u32[]{:S(2)}, u32[]{:S(2)}) %collective-permute-start.4) | collective-permute-done | bytes 1843232 | tf_op jit(solution)/shard_map/ppermute | solution.py:40
  51.7 1.9 collective-permute-start
  55.3 2.9 %collective-permute-start.1 = (f32[2,32]{1,0:T(2,128)S(1)}, f32[2,32]{1,0:T(2,128)S(1)}, u32[]{:S(2)}, u32[]{:S(2)}) collective-permute-start(f32[2,32]{1,0:T(2,128)S(1)} %fusion.48), channel_id=1, source_target_pairs={{0,4},{2,6},{4,0},{6,2},{1,5},{3,7},{5,1},{7,3},{8,12},{10,14},{12... | collective-permute-start | bytes 776 | tf_op jit(solution)/shard_map/ppermute | solution.py:30
  59.9 1.8 collective-permute-start.2
  63.9 3.1 %select_select_fusion.3 = (bf16[3,1280,3,80]{1,3,2,0:T(8,128)(2,1)S(1)}, bf16[3,1280,3,80]{1,3,2,0:T(8,128)(2,1)S(1)}, bf16[3,1280,3,80]{1,3,2,0:T(8,128)(2,1)S(1)}, bf16[3,1280,3,80]{1,3,2,0:T(8,128)(2,1)S(1)}) fusion(bf16[3,1280,3,80]{1,3,2,0:T(8,128)(2,1)} %bitcast.157, bf16[3,1280,3,80]{1,3,2,0:T(8,128)(2,1)} %collective-permute-done.3, ...), kind=kLoop, calls=%fused_computation.20 | loop fusion | flops 11059200 | bytes 14745612 | tf_op jit(solution)/shard_map/jit(_where)/select_n | solution.py:49
  66.9 5.5 %pad_maximum_fusion = bf16[3,1280,3,320]{1,3,2,0:T(8,128)(2,1)S(1)} fusion(bf16[3,1280,3,80]{1,3,2,0:T(8,128)(2,1)S(1)} %get-tuple-element.14, bf16[3,1280,3,80]{1,3,2,0:T(8,128)(2,1)S(1)} %get-tuple-element.15, bf16[3,1280,3,80]{1,3,2,0:T(8,128)(2,1)S(1)} %get-tuple-element.16, bf16[3,1280,3,80]{1,3,2,0:T(8,128)(2,1)S(1)} %get-tuple-element.13), kind=kLoop, calls=%fused_computation | loop fusion | flops 29491200 | bytes 14745600 | tf_op jit(solution)/shard_map/concatenate | solution.py:51
  72.5 2.7 %fusion.51 = (bf16[1,1280,3,320]{1,3,2,0:T(8,128)(2,1)S(1)}, bf16[1,1280,3,320]{1,3,2,0:T(8,128)(2,1)}, bf16[1,1280,3,320]{1,3,2,0:T(8,128)(2,1)}) fusion(bf16[3,1280,3,320]{1,3,2,0:T(8,128)(2,1)S(1)} %pad_maximum_fusion), kind=kLoop, calls=%fused_computation.105 | loop fusion | bytes 14745600 | tf_op jit(solution)/shard_map/slice | solution.py:158
  75.2 31.3 %all-gather.4.cloned.1.call-done = bf16[1,4,8,32,1280]{4,3,1,2,0:T(8,128)(2,1)} async-done(((bf16[1,1,8,32,1280]{4,3,1,2,0:T(8,128)(2,1)}), bf16[1,4,8,32,1280]{4,3,1,2,0:T(8,128)(2,1)}) %all-gather.4.cloned.1.call-update) | async-done | bytes 2621456 | tf_op jit(solution)/shard_map/all_gather | solution.py:119
  107.6 3.4 %collective-permute-start.6 = (bf16[1,4,1,32,1280]{4,3,1,2,0:T(8,128)(2,1)S(1)}, bf16[1,4,1,32,1280]{4,3,1,2,0:T(8,128)(2,1)S(1)}, u32[]{:S(2)}, u32[]{:S(2)}) collective-permute-start(bf16[1,4,1,32,1280]{4,3,1,2,0:T(8,128)(2,1)S(1)} %get-tuple-element.25), channel_id=1, source_target_pairs={{0,1},{2,3},{4,5},{6,7},{8,9},{10,11},{12,13},{14,15},{16,17},{18,... | collective-permute-start | bytes 983048 | tf_op jit(solution)/shard_map/ppermute | solution.py:125
  112.5 3.2 %copy_bitcast_fusion = bf16[4,8,32,1280]{3,2,1,0:T(8,128)(2,1)S(1)} fusion(bf16[1,4,8,32,1280]{4,3,1,2,0:T(8,128)(2,1)} %all-gather.4.cloned.1.call-done, f32[1280]{0:T(1024)S(1)} %copy-done.7, f32[1280]{0:T(1024)S(1)} %copy-done.8, f32[1280]{0:T(1024)S(1)} %mul.103, f32[1280]{0:T(1024)S(1)} %sub.50), kind=kLoop, calls=%fused_computation.13 | loop fusion | flops 13107200 | bytes 5263360 | tf_op jit(solution)/shard_map/squeeze | solution.py:148
  116.3 1.5 collective-permute-done.6
  117.8 4.1 %collective-permute-done.7 = bf16[1,4,1,32,1280]{4,3,1,2,0:T(8,128)(2,1)S(1)} collective-permute-done((bf16[1,4,1,32,1280]{4,3,1,2,0:T(8,128)(2,1)S(1)}, bf16[1,4,1,32,1280]{4,3,1,2,0:T(8,128)(2,1)S(1)}, u32[]{:S(2)}, u32[]{:S(2)}) %collective-permute-start.7) | collective-permute-done | bytes 327712 | tf_op jit(solution)/shard_map/ppermute | solution.py:126
  122.4 2.9 %fusion = f32[4,8,32,960]{3,2,1,0:T(8,128)S(1)} fusion(bf16[1280,960,1,1]{0,1,3,2:T(8,128)(2,1)S(1)} %bitcast.154, bf16[4,7,32,1280]{3,2,1,0:T(8,128)(2,1)S(1)} %get-tuple-element.27, bf16[4,1,32,1280]{3,2,1,0:T(8,128)(2,1)S(1)} %get-tuple-element.52), kind=kOutput, calls=%fused_computation.5 | convolution fusion | flops 2517893120 | bytes 9011200 | tf_op jit(solution)/shard_map/frxc,cn->frxn/dot_general | solution.py:157
  125.3 2.9 %fusion.4 = f32[4,8,32,960]{3,2,1,0:T(8,128)S(1)} fusion(bf16[1280,960,1,1]{0,1,3,2:T(8,128)(2,1)S(1)} %bitcast.153, bf16[4,1,32,1280]{3,2,1,0:T(8,128)(2,1)S(1)} %get-tuple-element.53, bf16[4,7,32,1280]{3,2,1,0:T(8,128)(2,1)S(1)} %get-tuple-element.28), kind=kOutput, calls=%fused_computation.9 | convolution fusion | flops 2517893120 | bytes 9011200 | tf_op jit(solution)/shard_map/frxc,cn->frxn/dot_general | solution.py:157
  128.3 2.9 %add_add_fusion.1 = f32[4,8,32,960]{3,2,1,0:T(8,128)S(1)} fusion(f32[4,8,32,960]{3,2,1,0:T(8,128)S(1)} %fusion.4, f32[4,8,32,960]{3,2,1,0:T(8,128)S(1)} %fusion, bf16[4,8,32,1280]{3,2,1,0:T(8,128)(2,1)S(1)} %copy_bitcast_fusion, bf16[1280,960,1,1]{0,1,3,2:T(8,128)(2,1)S(1)} %bitcast.152), kind=kOutput, calls=%fused_computation.3 | convolution fusion | flops 2518548480 | bytes 16875520 | tf_op jit(solution)/shard_map/frxc,cn->frxn/dot_general | solution.py:157
  132.9 3.5 %collective-permute-done.8 = f32[2,8]{1,0:T(2,128)S(1)} collective-permute-done((f32[2,8]{1,0:T(2,128)S(1)}, f32[2,8]{1,0:T(2,128)S(1)}, u32[]{:S(2)}, u32[]{:S(2)}) %collective-permute-start.8) | collective-permute-done | bytes 96 | tf_op jit(solution)/shard_map/ppermute | solution.py:18
  138.2 1.5 collective-permute-start.10
  139.8 11.8 %collective-permute-done.10 = bf16[3,1280,80]{1,2,0:T(8,128)(2,1)} collective-permute-done((bf16[3,1280,80]{1,2,0:T(8,128)(2,1)S(1)}, bf16[3,1280,80]{1,2,0:T(8,128)(2,1)}, u32[]{:S(2)}, u32[]{:S(2)}) %collective-permute-start.10) | collective-permute-done | bytes 614432 | tf_op jit(solution)/shard_map/ppermute | solution.py:40
  152.2 1.5 copy.95
  153.8 1.5 copy.97
  155.3 2.2 copy.96
  157.5 1.7 select_select_fusion.7
  159.2 3.0 %pad_maximum_fusion.1 = bf16[3,1280,320]{2,1,0:T(8,128)(2,1)S(1)} fusion(bf16[3,1280,80]{2,1,0:T(8,128)(2,1)S(1)} %get-tuple-element.22, bf16[3,1280,80]{2,1,0:T(8,128)(2,1)S(1)} %get-tuple-element.23, bf16[3,1280,80]{2,1,0:T(8,128)(2,1)S(1)} %get-tuple-element.24, bf16[3,1280,80]{2,1,0:T(8,128)(2,1)S(1)} %get-tuple-element.21), kind=kLoop, calls=%fused_computation.4 | loop fusion | flops 9830400 | bytes 4915200 | tf_op jit(solution)/shard_map/concatenate | solution.py:51
  162.2 4.4 %copy.111 = bf16[4,4,80,3,320]{4,3,2,1,0:T(4,128)(2,1)} copy(bf16[4,4,80,3,320]{4,2,0,1,3:T(8,128)(2,1)S(1)} %bitcast.150) | data formatting | bytes 4915200 | tf_op jit(solution)/shard_map/transpose | solution.py:205
  166.6 6.9 %reshape.328 = bf16[4,320,960]{2,1,0:T(8,128)(2,1)S(1)} reshape(bf16[4,4,80,3,320]{4,3,2,1,0:T(4,128)(2,1)} %copy.111) | data formatting | bytes 4915200 | tf_op jit(solution)/shard_map/reshape | solution.py:205
  173.5 3.2 %fusion.25 = f32[4,8,32,960]{3,2,1,0:T(8,128)} fusion(bf16[4,8,32,320]{3,2,1,0:T(8,128)(2,1)S(1)} %copy-done.1, bf16[4,320,960]{2,1,0:T(8,128)(2,1)S(1)} %reshape.328, s32[]{:T(128)S(6)} %select_n.448), kind=kOutput, calls=%fused_computation.46 | convolution fusion | flops 629145600 | bytes 5373956 | tf_op jit(solution)/shard_map/frxc,cn->frxn/dot_general | solution.py:209
  176.8 23.1 %all-gather.6.cloned.1.call-done = bf16[16,8,32,320]{3,2,1,0:T(8,128)(2,1)} async-done(((bf16[4,8,32,320]{3,2,1,0:T(8,128)(2,1)}), bf16[16,8,32,320]{3,2,1,0:T(8,128)(2,1)}) %all-gather.6.cloned.1.call-update) | async-done | bytes 2621456 | tf_op jit(solution)/shard_map/all_gather | solution.py:203
  199.9 2.5 %fusion.17 = f32[4,8,32,960]{3,2,1,0:T(8,128)S(1)} fusion(bf16[4,4,8,32,320]{4,3,2,1,0:T(8,128)(2,1)} %bitcast.158, s32[]{:T(128)S(6)} %select_n.474, bf16[4,320,960]{2,1,0:T(8,128)(2,1)S(1)} %reshape.328), kind=kOutput, calls=%fused_computation.38 | convolution fusion | flops 629145600 | bytes 5374976 | tf_op jit(solution)/shard_map/frxc,cn->frxn/dot_general | solution.py:209
  208.3 2.7 %collective-permute-start.14 = (bf16[1,8,32,320]{3,2,1,0:T(8,128)(2,1)S(1)}, bf16[1,8,32,320]{3,2,1,0:T(8,128)(2,1)S(1)}, u32[]{:S(2)}, u32[]{:S(2)}) collective-permute-start(bf16[1,8,32,320]{3,2,1,0:T(8,128)(2,1)S(1)} %get-tuple-element.33), channel_id=1, source_target_pairs={{0,6},{2,0},{4,2},{6,4},{1,7},{3,1},{5,3},{7,5},{8,14},{10,8},{12,... | collective-permute-start | bytes 491528 | tf_op jit(solution)/shard_map/ppermute | solution.py:229
  211.0 5.7 %collective-permute-done.12 = bf16[1,8,32,320]{3,2,1,0:T(8,128)(2,1)S(1)} collective-permute-done((bf16[1,8,32,320]{3,2,1,0:T(8,128)(2,1)S(1)}, bf16[1,8,32,320]{3,2,1,0:T(8,128)(2,1)S(1)}, u32[]{:S(2)}, u32[]{:S(2)}) %collective-permute-start.12) | collective-permute-done | bytes 163872 | tf_op jit(solution)/shard_map/ppermute | solution.py:229
  216.6 7.2 %collective-permute-done.13 = bf16[1,8,32,320]{3,2,1,0:T(8,128)(2,1)S(1)} collective-permute-done((bf16[1,8,32,320]{3,2,1,0:T(8,128)(2,1)S(1)}, bf16[1,8,32,320]{3,2,1,0:T(8,128)(2,1)S(1)}, u32[]{:S(2)}, u32[]{:S(2)}) %collective-permute-start.13) | collective-permute-done | bytes 163872 | tf_op jit(solution)/shard_map/ppermute | solution.py:229
  (113 shorter events, 25.9 us)
Async XLA Ops:
  6.5 99.9 %all-gather.4.cloned.1.call-start = ((), (), s32[]{:S(2)}) async-start(), calls=%async_computation | async-start | bytes 3276800 | tf_op jit(solution)/shard_map/all_gather | solution.py:119
  6.5 43.4 %collective-permute-start.4 = (bf16[3,1280,3,80]{1,3,2,0:T(8,128)(2,1)}, bf16[3,1280,3,80]{1,3,2,0:T(8,128)(2,1)S(1)}, u32[]{:S(2)}, u32[]{:S(2)}) collective-permute-start(bf16[3,1280,3,80]{1,3,2,0:T(8,128)(2,1)} %bitcast.155), channel_id=1, source_target_pairs={{0,16},{8,24},{16,0},{24,8},{1,17},{9,25},{17,1},{25,9},{2,18},{10... | collective-permute-start | bytes 5529608 | tf_op jit(solution)/shard_map/ppermute | solution.py:40
  9.5 54.4 %collective-permute-start.3 = (bf16[3,1280,3,80]{1,3,2,0:T(8,128)(2,1)}, bf16[3,1280,3,80]{1,3,2,0:T(8,128)(2,1)}, u32[]{:S(2)}, u32[]{:S(2)}) collective-permute-start(bf16[3,1280,3,80]{1,3,2,0:T(8,128)(2,1)} %bitcast.156), channel_id=1, source_target_pairs={{0,8},{8,0},{16,24},{24,16},{1,9},{9,1},{17,25},{25,17},{2,10},{10... | collective-permute-start | bytes 5529608 | tf_op jit(solution)/shard_map/ppermute | solution.py:41
  49.9 14.0 %collective-permute-start.5 = (bf16[3,1280,3,80]{1,3,2,0:T(8,128)(2,1)S(1)}, bf16[3,1280,3,80]{1,3,2,0:T(8,128)(2,1)}, u32[]{:S(2)}, u32[]{:S(2)}) collective-permute-start(bf16[3,1280,3,80]{1,3,2,0:T(8,128)(2,1)S(1)} %collective-permute-done.4), channel_id=1, source_target_pairs={{0,8},{8,0},{16,24},{24,16},{1,9},{9,1},{17,25},{25,17},{2,10},{10... | collective-permute-start | bytes 5529608 | tf_op jit(solution)/shard_map/ppermute | solution.py:42
  49.9 150.0 %all-gather.6.cloned.1.call-start = ((), (), s32[]{:S(2)}) async-start(), calls=%async_computation.1 | async-start | bytes 3932160 | tf_op jit(solution)/shard_map/all_gather | solution.py:203
  51.7 3.6 %collective-permute-start = (f32[2,32]{1,0:T(2,128)S(1)}, f32[2,32]{1,0:T(2,128)S(1)}, u32[]{:S(2)}, u32[]{:S(2)}) collective-permute-start(f32[2,32]{1,0:T(2,128)S(1)} %pad_maximum_fusion.2), channel_id=1, source_target_pairs={{0,2},{2,0},{4,6},{6,4},{1,3},{3,1},{5,7},{7,5},{8,10},{10,8},{12,... | collective-permute-start | bytes 776 | tf_op jit(solution)/shard_map/ppermute | solution.py:30
  55.3 4.5 %collective-permute-start.1 = (f32[2,32]{1,0:T(2,128)S(1)}, f32[2,32]{1,0:T(2,128)S(1)}, u32[]{:S(2)}, u32[]{:S(2)}) collective-permute-start(f32[2,32]{1,0:T(2,128)S(1)} %fusion.48), channel_id=1, source_target_pairs={{0,4},{2,6},{4,0},{6,2},{1,5},{3,7},{5,1},{7,3},{8,12},{10,14},{12... | collective-permute-start | bytes 776 | tf_op jit(solution)/shard_map/ppermute | solution.py:30
  59.9 3.6 %collective-permute-start.2 = (f32[2,32]{1,0:T(2,128)S(1)}, f32[2,32]{1,0:T(2,128)S(1)}, u32[]{:S(2)}, u32[]{:S(2)}) collective-permute-start(f32[2,32]{1,0:T(2,128)S(1)} %fusion.65), channel_id=1, source_target_pairs={{0,1},{1,0},{2,3},{3,2},{4,5},{5,4},{6,7},{7,6},{8,9},{9,8},{10,11... | collective-permute-start | bytes 776 | tf_op jit(solution)/shard_map/ppermute | solution.py:30
  72.4 40.0 %copy-start.7 = (f32[1280]{0:T(1024)S(1)}, f32[1280]{0:T(1024)}, u32[]{:S(2)}) copy-start(f32[1280]{0:T(1024)} %param.13) | copy-start | bytes 15364
  72.5 40.0 %copy-start.8 = (f32[1280]{0:T(1024)S(1)}, f32[1280]{0:T(1024)}, u32[]{:S(2)}) copy-start(f32[1280]{0:T(1024)} %param.12) | copy-start | bytes 15364
  107.6 10.2 %collective-permute-start.6 = (bf16[1,4,1,32,1280]{4,3,1,2,0:T(8,128)(2,1)S(1)}, bf16[1,4,1,32,1280]{4,3,1,2,0:T(8,128)(2,1)S(1)}, u32[]{:S(2)}, u32[]{:S(2)}) collective-permute-start(bf16[1,4,1,32,1280]{4,3,1,2,0:T(8,128)(2,1)S(1)} %get-tuple-element.25), channel_id=1, source_target_pairs={{0,1},{2,3},{4,5},{6,7},{8,9},{10,11},{12,13},{14,15},{16,17},{18,... | collective-permute-start | bytes 983048 | tf_op jit(solution)/shard_map/ppermute | solution.py:125
  111.0 10.9 %collective-permute-start.7 = (bf16[1,4,1,32,1280]{4,3,1,2,0:T(8,128)(2,1)S(1)}, bf16[1,4,1,32,1280]{4,3,1,2,0:T(8,128)(2,1)S(1)}, u32[]{:S(2)}, u32[]{:S(2)}) collective-permute-start(bf16[1,4,1,32,1280]{4,3,1,2,0:T(8,128)(2,1)S(1)} %get-tuple-element.26), channel_id=1, source_target_pairs={{1,0},{3,2},{5,4},{7,6},{9,8},{11,10},{13,12},{15,14},{17,16},{19,... | collective-permute-start | bytes 983048 | tf_op jit(solution)/shard_map/ppermute | solution.py:126
  115.7 6.7 %copy-start.4 = (bf16[1,1280,3,320]{1,3,2,0:T(8,128)(2,1)S(1)}, bf16[1,1280,3,320]{1,3,2,0:T(8,128)(2,1)}, u32[]{:S(2)}) copy-start(bf16[1,1280,3,320]{1,3,2,0:T(8,128)(2,1)} %get-tuple-element.12) | copy-start | bytes 7372804
  122.4 2.9 %copy-start.3 = (bf16[1,1280,3,320]{1,3,2,0:T(8,128)(2,1)S(1)}, bf16[1,1280,3,320]{1,3,2,0:T(8,128)(2,1)}, u32[]{:S(2)}) copy-start(bf16[1,1280,3,320]{1,3,2,0:T(8,128)(2,1)} %get-tuple-element.11) | copy-start | bytes 7372804
  132.3 5.9 %copy-start.6 = (bf16[3,1280,80]{1,2,0:T(8,128)(2,1)S(1)}, bf16[3,1280,80]{1,2,0:T(8,128)(2,1)}, u32[]{:S(2)}) copy-start(bf16[3,1280,80]{1,2,0:T(8,128)(2,1)} %param.11) | copy-start | bytes 1843204
  132.8 3.6 %collective-permute-start.8 = (f32[2,8]{1,0:T(2,128)S(1)}, f32[2,8]{1,0:T(2,128)S(1)}, u32[]{:S(2)}, u32[]{:S(2)}) collective-permute-start(f32[2,8]{1,0:T(2,128)S(1)} %pad_maximum_fusion.3), channel_id=1, source_target_pairs={{0,1},{1,0},{2,3},{3,2},{4,5},{5,4},{6,7},{7,6},{8,9},{9,8},{10,11... | collective-permute-start | bytes 200 | tf_op jit(solution)/shard_map/ppermute | solution.py:18
  138.2 13.3 %collective-permute-start.10 = (bf16[3,1280,80]{1,2,0:T(8,128)(2,1)S(1)}, bf16[3,1280,80]{1,2,0:T(8,128)(2,1)}, u32[]{:S(2)}, u32[]{:S(2)}) collective-permute-start(bf16[3,1280,80]{1,2,0:T(8,128)(2,1)S(1)} %copy-done.6), channel_id=1, source_target_pairs={{0,16},{8,24},{16,0},{24,8},{1,17},{9,25},{17,1},{25,9},{2,18},{10... | collective-permute-start | bytes 1843208 | tf_op jit(solution)/shard_map/ppermute | solution.py:40
  139.7 14.0 %collective-permute-start.9 = (bf16[3,1280,80]{1,2,0:T(8,128)(2,1)S(1)}, bf16[3,1280,80]{1,2,0:T(8,128)(2,1)}, u32[]{:S(2)}, u32[]{:S(2)}) collective-permute-start(bf16[3,1280,80]{1,2,0:T(8,128)(2,1)S(1)} %copy-done.6), channel_id=1, source_target_pairs={{0,8},{8,0},{16,24},{24,16},{1,9},{9,1},{17,25},{25,17},{2,10},{10... | collective-permute-start | bytes 1843208 | tf_op jit(solution)/shard_map/ppermute | solution.py:41
  151.5 3.8 %collective-permute-start.11 = (bf16[3,1280,80]{1,2,0:T(8,128)(2,1)}, bf16[3,1280,80]{1,2,0:T(8,128)(2,1)}, u32[]{:S(2)}, u32[]{:S(2)}) collective-permute-start(bf16[3,1280,80]{1,2,0:T(8,128)(2,1)} %collective-permute-done.10), channel_id=1, source_target_pairs={{0,8},{8,0},{16,24},{24,16},{1,9},{9,1},{17,25},{25,17},{2,10},{10... | collective-permute-start | bytes 1843208 | tf_op jit(solution)/shard_map/ppermute | solution.py:42
  166.6 6.9 %copy-start.1 = (bf16[4,8,32,320]{3,2,1,0:T(8,128)(2,1)S(1)}, bf16[4,8,32,320]{3,2,1,0:T(8,128)(2,1)}, u32[]{:S(2)}) copy-start(bf16[4,8,32,320]{3,2,1,0:T(8,128)(2,1)} %multiply_convert_fusion.1) | copy-start | bytes 1966084
  199.9 2.5 %copy-start.5 = (bf16[16,8,32,320]{3,2,1,0:T(8,128)(2,1)S(1)}, bf16[16,8,32,320]{3,2,1,0:T(8,128)(2,1)}, u32[]{:S(2)}) copy-start(bf16[16,8,32,320]{3,2,1,0:T(8,128)(2,1)} %all-gather.6.cloned.1.call-done) | copy-start | bytes 7864324
  202.4 2.2 copy-start
  206.9 9.7 %collective-permute-start.12 = (bf16[1,8,32,320]{3,2,1,0:T(8,128)(2,1)S(1)}, bf16[1,8,32,320]{3,2,1,0:T(8,128)(2,1)S(1)}, u32[]{:S(2)}, u32[]{:S(2)}) collective-permute-start(bf16[1,8,32,320]{3,2,1,0:T(8,128)(2,1)S(1)} %get-tuple-element.35), channel_id=1, source_target_pairs={{0,2},{2,4},{4,6},{6,0},{1,3},{3,5},{5,7},{7,1},{8,10},{10,12},{12... | collective-permute-start | bytes 491528 | tf_op jit(solution)/shard_map/ppermute | solution.py:229
  207.0 16.8 %collective-permute-start.13 = (bf16[1,8,32,320]{3,2,1,0:T(8,128)(2,1)S(1)}, bf16[1,8,32,320]{3,2,1,0:T(8,128)(2,1)S(1)}, u32[]{:S(2)}, u32[]{:S(2)}) collective-permute-start(bf16[1,8,32,320]{3,2,1,0:T(8,128)(2,1)S(1)} %get-tuple-element.34), channel_id=1, source_target_pairs={{0,4},{2,6},{4,0},{6,2},{1,5},{3,7},{5,1},{7,3},{8,12},{10,14},{12... | collective-permute-start | bytes 491528 | tf_op jit(solution)/shard_map/ppermute | solution.py:229
  208.3 15.5 %collective-permute-start.14 = (bf16[1,8,32,320]{3,2,1,0:T(8,128)(2,1)S(1)}, bf16[1,8,32,320]{3,2,1,0:T(8,128)(2,1)S(1)}, u32[]{:S(2)}, u32[]{:S(2)}) collective-permute-start(bf16[1,8,32,320]{3,2,1,0:T(8,128)(2,1)S(1)} %get-tuple-element.33), channel_id=1, source_target_pairs={{0,6},{2,0},{4,2},{6,4},{1,7},{3,1},{5,3},{7,5},{8,14},{10,8},{12,... | collective-permute-start | bytes 491528 | tf_op jit(solution)/shard_map/ppermute | solution.py:229
  226.4 1.4 copy-start.2
  226.4 1.4 copy-start.9
Sparse Core Ops, SparseCore 0:
  50.0 56.3 all-gather.3
  138.3 61.5 all-gather.5

commit v15 on v12

--- a/solution.py
+++ b/solution.py
@@ -104,7 +104,6 @@
     frame_size = lax.axis_size("frame")
     row_size = lax.axis_size("row")
     frame_index = lax.axis_index("frame")
-    row_index = lax.axis_index("row")
     channels = activations.shape[-1]
     rows = activations.shape[2]
     cols = activations.shape[3]
@@ -119,14 +118,6 @@
     raw = lax.all_gather(activations, "frame", axis=1, tiled=True)
     frames = raw.shape[1]
 
-    if row_size > 1:
-        down = [(i, i + 1) for i in range(row_size - 1)]
-        up = [(i + 1, i) for i in range(row_size - 1)]
-        above = lax.ppermute(raw[:, :, rows - 1 :], "row", down)
-        below = lax.ppermute(raw[:, :, :1], "row", up)
-    else:
-        above = jnp.zeros_like(raw[:, :, :1])
-        below = jnp.zeros_like(raw[:, :, :1])
 
     grouped = activations.astype(jnp.float32).reshape(1, -1, GROUPS, width)
     stats = jnp.concatenate(
@@ -146,10 +137,14 @@
         return silu_bf16(normed)
 
     first_mid = lax.optimization_barrier(first_norm(raw)[0])
-    first_above = jnp.where(row_index > 0, first_norm(above), jnp.zeros((), jnp.bfloat16))[0]
-    first_below = jnp.where(
-        row_index < row_size - 1, first_norm(below), jnp.zeros((), jnp.bfloat16)
-    )[0]
+    if row_size > 1:
+        down = [(i, i + 1) for i in range(row_size - 1)]
+        up = [(i + 1, i) for i in range(row_size - 1)]
+        first_above = lax.ppermute(first_mid[:, rows - 1 :], "row", down)
+        first_below = lax.ppermute(first_mid[:, :1], "row", up)
+    else:
+        first_above = jnp.zeros_like(first_mid[:, :1])
+        first_below = jnp.zeros_like(first_mid[:, :1])
 
     wide = spatial_w.reshape(3, channels, 3 * local)
 

time: 234 us -> 234 us (level)
    ppermute x1, starting transfers between devices: 0.07 us -> 2.43 us  [pair_sum(): lax.ppermute(v, axis, [(0, 1), (1, 0)])]
  transfers between devices with their start and end apart: 17 -> 17, of which waited for: 9 -> 9; matrix products, arithmetic and copies ran while one was open for 22% -> 20% of each run, Pallas kernels for 0% -> 0%
where the time goes in v15:
time: 234 us; the launch traced here: 233 us
  waiting for transfers between devices  126 us (54%)
  local copies, waits for them, and re-layouts  29 us (12%)
  starting transfers between devices  23.2 us (10%)
  other arithmetic  22.7 us (10%)
  matrix products  18.5 us (8%)
  between operations  14.1 us (6%)
    ppermute x2, waiting for transfers between devices, gather_rep(): across = lax.ppermute(w, 'rep', [(k, k ^ 2) for k in range(size)])  52.4 us
    all_gather x1, waiting for transfers between devices, shards(): raw = lax.all_gather(activations, 'frame', axis=1, tiled=True)  30.6 us
    all_gather x1, waiting for transfers between devices, shards(): second_all = lax.all_gather(second[0], 'frame', axis=0, tiled=False)  24.6 us
    ppermute x3, waiting for transfers between devices, shards(): lax.ppermute(piece, 'frame', [(k, (k + shift) % frame_size) for k in rang...  12.9 us
    dot_general x4, matrix products, product(): jnp.einsum('frxc,cn->frxn', source, weights, preferred_element_type=jnp.f...  8.29 us
    concatenate x2, other arithmetic, gather_rep(): return jnp.concatenate(blocks, axis=-1)  8.27 us
    dot_general x4, matrix products, tap(): jnp.einsum('frxc,cn->frxn', field, wide[row_tap], preferred_element_type=...  7.26 us
    reshape x1, local copies, waits for them, and re-layouts, shards(): taps.transpose(2, 1, 3, 0, 4)  6.93 us
  transfers between devices with their start and end apart: 17, of which 9 were waited for; matrix products, arithmetic and copies ran while one was open for 20% of the time, Pallas kernels for 0%

profile of v15, /device:TPU:0, one launch (start us, length us, event | category | flops | bytes accessed | tf_op | source)
XLA Modules:
  0.0 233.1 jit_solution(7015124097229803724)
XLA Ops:
  6.5 3.0 %collective-permute-start.4 = (bf16[3,1280,3,80]{1,3,2,0:T(8,128)(2,1)}, bf16[3,1280,3,80]{1,3,2,0:T(8,128)(2,1)S(1)}, u32[]{:S(2)}, u32[]{:S(2)}) collective-permute-start(bf16[3,1280,3,80]{1,3,2,0:T(8,128)(2,1)} %bitcast.170), channel_id=1, source_target_pairs={{0,16},{8,24},{16,0},{24,8},{1,17},{9,25},{17,1},{25,9},{2,18},{10... | collective-permute-start | bytes 5529608 | tf_op jit(solution)/shard_map/ppermute | solution.py:40
  9.5 40.4 %collective-permute-done.4 = bf16[3,1280,3,80]{1,3,2,0:T(8,128)(2,1)S(1)} collective-permute-done((bf16[3,1280,3,80]{1,3,2,0:T(8,128)(2,1)}, bf16[3,1280,3,80]{1,3,2,0:T(8,128)(2,1)S(1)}, u32[]{:S(2)}, u32[]{:S(2)}) %collective-permute-start.4) | collective-permute-done | bytes 1843232 | tf_op jit(solution)/shard_map/ppermute | solution.py:40
  51.7 1.9 collective-permute-start
  56.0 2.7 %collective-permute-start.1 = (f32[2,32]{1,0:T(2,128)S(1)}, f32[2,32]{1,0:T(2,128)S(1)}, u32[]{:S(2)}, u32[]{:S(2)}) collective-permute-start(f32[2,32]{1,0:T(2,128)S(1)} %fusion.39), channel_id=1, source_target_pairs={{0,4},{2,6},{4,0},{6,2},{1,5},{3,7},{5,1},{7,3},{8,12},{10,14},{12... | collective-permute-start | bytes 776 | tf_op jit(solution)/shard_map/ppermute | solution.py:30
  58.7 1.9 collective-permute-done.1
  60.5 1.6 collective-permute-start.2
  62.3 1.9 collective-permute-done.2
  64.5 3.1 %select_select_fusion.3 = (bf16[3,1280,3,80]{1,3,2,0:T(8,128)(2,1)S(1)}, bf16[3,1280,3,80]{1,3,2,0:T(8,128)(2,1)S(1)}, bf16[3,1280,3,80]{1,3,2,0:T(8,128)(2,1)S(1)}, bf16[3,1280,3,80]{1,3,2,0:T(8,128)(2,1)S(1)}) fusion(bf16[3,1280,3,80]{1,3,2,0:T(8,128)(2,1)} %bitcast.172, bf16[3,1280,3,80]{1,3,2,0:T(8,128)(2,1)} %collective-permute-done.3, ...), kind=kLoop, calls=%fused_computation.14 | loop fusion | flops 11059200 | bytes 14745612 | tf_op jit(solution)/shard_map/jit(_where)/select_n | solution.py:49
  67.6 5.5 %pad_maximum_fusion = bf16[3,1280,3,320]{1,3,2,0:T(8,128)(2,1)S(1)} fusion(bf16[3,1280,3,80]{1,3,2,0:T(8,128)(2,1)S(1)} %get-tuple-element.14, bf16[3,1280,3,80]{1,3,2,0:T(8,128)(2,1)S(1)} %get-tuple-element.15, bf16[3,1280,3,80]{1,3,2,0:T(8,128)(2,1)S(1)} %get-tuple-element.16, bf16[3,1280,3,80]{1,3,2,0:T(8,128)(2,1)S(1)} %get-tuple-element.13), kind=kLoop, calls=%fused_computation | loop fusion | flops 29491200 | bytes 14745600 | tf_op jit(solution)/shard_map/concatenate | solution.py:51
  73.1 2.7 %fusion.42 = (bf16[1,1280,3,320]{1,3,2,0:T(8,128)(2,1)}, bf16[1,1280,3,320]{1,3,2,0:T(8,128)(2,1)}, bf16[1,1280,3,320]{1,3,2,0:T(8,128)(2,1)S(1)}) fusion(bf16[3,1280,3,320]{1,3,2,0:T(8,128)(2,1)S(1)} %pad_maximum_fusion), kind=kLoop, calls=%fused_computation.95 | loop fusion | bytes 14745600 | tf_op jit(solution)/shard_map/slice | solution.py:153
  75.9 30.6 %all-gather.4.cloned.1.call-done = bf16[1,4,8,32,1280]{4,3,2,0,1:T(8,128)(2,1)} async-done(((bf16[1,1,8,32,1280]{4,3,2,0,1:T(8,128)(2,1)}), bf16[1,4,8,32,1280]{4,3,2,0,1:T(8,128)(2,1)}) %all-gather.4.cloned.1.call-update) | async-done | bytes 2621456 | tf_op jit(solution)/shard_map/all_gather | solution.py:118
  106.5 3.7 %fusion = bf16[4,8,32,1280]{3,2,1,0:T(8,128)(2,1)S(1)} fusion(bf16[1,4,8,32,1280]{4,3,2,0,1:T(8,128)(2,1)} %all-gather.4.cloned.1.call-done, f32[1280]{0:T(1024)S(1)} %copy-done.7, f32[1280]{0:T(1024)S(1)} %copy-done.8, f32[1280]{0:T(1024)S(1)} %broadcast_in_dim.24, f32[1280]{0:T(1024)S(1)} %broadcast_in_dim.22), kind=kLoop, calls=%fused_computation.5 | loop fusion | flops 13107200 | bytes 5263360 | tf_op jit(solution)/shard_map/squeeze | solution.py:139
  111.5 4.8 %collective-permute-start.6 = (bf16[4,1,32,1280]{3,2,1,0:T(8,128)(2,1)S(1)}, bf16[4,1,32,1280]{3,2,1,0:T(8,128)(2,1)S(1)}, u32[]{:S(2)}, u32[]{:S(2)}) collective-permute-start(bf16[4,1,32,1280]{3,2,1,0:T(8,128)(2,1)S(1)} %get-tuple-element.25), channel_id=1, source_target_pairs={{0,1},{2,3},{4,5},{6,7},{8,9},{10,11},{12,13},{14,15},{16,17},{18,... | collective-permute-start | bytes 983048 | tf_op jit(solution)/shard_map/ppermute | solution.py:143
  116.3 2.6 %fusion.50 = f32[4,7,32,960]{3,2,1,0:T(8,128)S(1)} fusion(bf16[4,8,32,1280]{3,2,1,0:T(8,128)(2,1)S(1)} %fusion, bf16[1280,960,1,1]{0,1,3,2:T(8,128)(2,1)S(1)} %bitcast.166), kind=kOutput, calls=%fused_computation.103 | convolution fusion | flops 2202009600 | bytes 8519680 | tf_op jit(solution)/shard_map/frxc,cn->frxn/dot_general | solution.py:152
  118.9 2.9 %fusion.1 = f32[4,8,32,960]{3,2,1,0:T(8,128)S(1)} fusion(bf16[1280,960,1,1]{0,1,3,2:T(8,128)(2,1)S(1)} %bitcast.164, bf16[4,8,32,1280]{3,2,1,0:T(8,128)(2,1)S(1)} %fusion), kind=kOutput, calls=%fused_computation.6 | convolution fusion | flops 2202009600 | bytes 8683520 | tf_op jit(solution)/shard_map/jit(_pad)/pad | solution.py:157
  123.6 2.9 %pad_add_fusion = f32[4,8,32,960]{3,2,1,0:T(8,128)S(1)} fusion(f32[4,1,32,960]{3,2,1,0:T(8,128)S(1)} %convolution_bitcast_fusion, f32[4,1,32,960]{3,2,1,0:T(8,128)S(1)} %convolution_bitcast_fusion.1, f32[4,7,32,960]{3,2,1,0:T(8,128)S(1)} %fusion.50, f32[4,8,32,960]{3,2,1,0:T(8,128)S(1)} %fusion.1, bf16[4,8,32,1280]{3,2,1,0:T(8,128)(2,1)S(1)} %fusion, ...), kind=kOutput, calls=%fused_computation.3 | convolution fusion | flops 2520514560 | bytes 17367040 | tf_op jit(solution)/shard_map/frxc,cn->frxn/dot_general | solution.py:152
  128.1 2.4 %collective-permute-start.8 = (f32[2,8]{1,0:T(2,128)S(1)}, f32[2,8]{1,0:T(2,128)S(1)}, u32[]{:S(2)}, u32[]{:S(2)}) collective-permute-start(f32[2,8]{1,0:T(2,128)S(1)} %pad_maximum_fusion.3), channel_id=1, source_target_pairs={{0,1},{1,0},{2,3},{3,2},{4,5},{5,4},{6,7},{7,6},{8,9},{9,8},{10,11... | collective-permute-start | bytes 200 | tf_op jit(solution)/shard_map/ppermute | solution.py:18
  133.9 1.5 collective-permute-start.10
  135.5 12.1 %collective-permute-done.10 = bf16[3,1280,80]{1,2,0:T(8,128)(2,1)} collective-permute-done((bf16[3,1280,80]{1,2,0:T(8,128)(2,1)S(1)}, bf16[3,1280,80]{1,2,0:T(8,128)(2,1)}, u32[]{:S(2)}, u32[]{:S(2)}) %collective-permute-start.10) | collective-permute-done | bytes 614432 | tf_op jit(solution)/shard_map/ppermute | solution.py:40
  148.2 1.5 copy.87
  149.8 1.5 copy.89
  151.3 2.2 copy.88
  153.5 1.7 select_select_fusion.7
  155.2 2.8 %pad_maximum_fusion.1 = bf16[3,1280,320]{2,1,0:T(8,128)(2,1)S(1)} fusion(bf16[3,1280,80]{2,1,0:T(8,128)(2,1)S(1)} %get-tuple-element.22, bf16[3,1280,80]{2,1,0:T(8,128)(2,1)S(1)} %get-tuple-element.23, bf16[3,1280,80]{2,1,0:T(8,128)(2,1)S(1)} %get-tuple-element.24, bf16[3,1280,80]{2,1,0:T(8,128)(2,1)S(1)} %get-tuple-element.21), kind=kLoop, calls=%fused_computation.4 | loop fusion | flops 9830400 | bytes 4915200 | tf_op jit(solution)/shard_map/concatenate | solution.py:51
  157.9 4.4 %copy.103 = bf16[4,4,80,3,320]{4,3,2,1,0:T(4,128)(2,1)} copy(bf16[4,4,80,3,320]{4,2,0,1,3:T(8,128)(2,1)S(1)} %bitcast.163) | data formatting | bytes 4915200 | tf_op jit(solution)/shard_map/transpose | solution.py:202
  162.3 6.9 %reshape.328 = bf16[4,320,960]{2,1,0:T(8,128)(2,1)S(1)} reshape(bf16[4,4,80,3,320]{4,3,2,1,0:T(4,128)(2,1)} %copy.103) | data formatting | bytes 4915200 | tf_op jit(solution)/shard_map/reshape | solution.py:202
  169.3 3.2 %fusion.20 = f32[4,8,32,960]{3,2,1,0:T(8,128)} fusion(bf16[4,8,32,320]{3,2,1,0:T(8,128)(2,1)S(1)} %copy-done.2, bf16[4,320,960]{2,1,0:T(8,128)(2,1)S(1)} %reshape.328, s32[]{:T(128)S(6)} %select_n.430), kind=kOutput, calls=%fused_computation.42 | convolution fusion | flops 629145600 | bytes 5373956 | tf_op jit(solution)/shard_map/frxc,cn->frxn/dot_general | solution.py:206
  172.5 24.6 %all-gather.6.cloned.1.call-done = bf16[16,8,32,320]{3,2,1,0:T(8,128)(2,1)} async-done(((bf16[4,8,32,320]{3,2,1,0:T(8,128)(2,1)}), bf16[16,8,32,320]{3,2,1,0:T(8,128)(2,1)}) %all-gather.6.cloned.1.call-update) | async-done | bytes 2621456 | tf_op jit(solution)/shard_map/all_gather | solution.py:200
  197.0 2.5 %fusion.10 = f32[4,8,32,960]{3,2,1,0:T(8,128)S(1)} fusion(bf16[4,4,8,32,320]{4,3,2,1,0:T(8,128)(2,1)} %bitcast.173, s32[]{:T(128)S(6)} %select_n.458, bf16[4,320,960]{2,1,0:T(8,128)(2,1)S(1)} %reshape.328), kind=kOutput, calls=%fused_computation.32 | convolution fusion | flops 629145600 | bytes 5374976 | tf_op jit(solution)/shard_map/frxc,cn->frxn/dot_general | solution.py:206
  205.4 2.7 %collective-permute-start.14 = (bf16[1,8,32,320]{3,2,1,0:T(8,128)(2,1)S(1)}, bf16[1,8,32,320]{3,2,1,0:T(8,128)(2,1)S(1)}, u32[]{:S(2)}, u32[]{:S(2)}) collective-permute-start(bf16[1,8,32,320]{3,2,1,0:T(8,128)(2,1)S(1)} %get-tuple-element.31), channel_id=1, source_target_pairs={{0,6},{2,0},{4,2},{6,4},{1,7},{3,1},{5,3},{7,5},{8,14},{10,8},{12,... | collective-permute-start | bytes 491528 | tf_op jit(solution)/shard_map/ppermute | solution.py:226
  208.1 5.7 %collective-permute-done.12 = bf16[1,8,32,320]{3,2,1,0:T(8,128)(2,1)S(1)} collective-permute-done((bf16[1,8,32,320]{3,2,1,0:T(8,128)(2,1)S(1)}, bf16[1,8,32,320]{3,2,1,0:T(8,128)(2,1)S(1)}, u32[]{:S(2)}, u32[]{:S(2)}) %collective-permute-start.12) | collective-permute-done | bytes 163872 | tf_op jit(solution)/shard_map/ppermute | solution.py:226
  213.8 7.2 %collective-permute-done.13 = bf16[1,8,32,320]{3,2,1,0:T(8,128)(2,1)S(1)} collective-permute-done((bf16[1,8,32,320]{3,2,1,0:T(8,128)(2,1)S(1)}, bf16[1,8,32,320]{3,2,1,0:T(8,128)(2,1)S(1)}, u32[]{:S(2)}, u32[]{:S(2)}) %collective-permute-start.13) | collective-permute-done | bytes 163872 | tf_op jit(solution)/shard_map/ppermute | solution.py:226
  (113 shorter events, 24.2 us)
Async XLA Ops:
  6.5 99.9 %all-gather.4.cloned.1.call-start = ((), (), s32[]{:S(2)}) async-start(), calls=%async_computation | async-start | bytes 3276800 | tf_op jit(solution)/shard_map/all_gather | solution.py:118
  6.5 43.4 %collective-permute-start.4 = (bf16[3,1280,3,80]{1,3,2,0:T(8,128)(2,1)}, bf16[3,1280,3,80]{1,3,2,0:T(8,128)(2,1)S(1)}, u32[]{:S(2)}, u32[]{:S(2)}) collective-permute-start(bf16[3,1280,3,80]{1,3,2,0:T(8,128)(2,1)} %bitcast.170), channel_id=1, source_target_pairs={{0,16},{8,24},{16,0},{24,8},{1,17},{9,25},{17,1},{25,9},{2,18},{10... | collective-permute-start | bytes 5529608 | tf_op jit(solution)/shard_map/ppermute | solution.py:40
  9.5 55.0 %collective-permute-start.3 = (bf16[3,1280,3,80]{1,3,2,0:T(8,128)(2,1)}, bf16[3,1280,3,80]{1,3,2,0:T(8,128)(2,1)}, u32[]{:S(2)}, u32[]{:S(2)}) collective-permute-start(bf16[3,1280,3,80]{1,3,2,0:T(8,128)(2,1)} %bitcast.171), channel_id=1, source_target_pairs={{0,8},{8,0},{16,24},{24,16},{1,9},{9,1},{17,25},{25,17},{2,10},{10... | collective-permute-start | bytes 5529608 | tf_op jit(solution)/shard_map/ppermute | solution.py:41
  49.9 14.6 %collective-permute-start.5 = (bf16[3,1280,3,80]{1,3,2,0:T(8,128)(2,1)S(1)}, bf16[3,1280,3,80]{1,3,2,0:T(8,128)(2,1)}, u32[]{:S(2)}, u32[]{:S(2)}) collective-permute-start(bf16[3,1280,3,80]{1,3,2,0:T(8,128)(2,1)S(1)} %collective-permute-done.4), channel_id=1, source_target_pairs={{0,8},{8,0},{16,24},{24,16},{1,9},{9,1},{17,25},{25,17},{2,10},{10... | collective-permute-start | bytes 5529608 | tf_op jit(solution)/shard_map/ppermute | solution.py:42
  49.9 147.1 %all-gather.6.cloned.1.call-start = ((), (), s32[]{:S(2)}) async-start(), calls=%async_computation.1 | async-start | bytes 3932160 | tf_op jit(solution)/shard_map/all_gather | solution.py:200
  51.7 4.3 %collective-permute-start = (f32[2,32]{1,0:T(2,128)S(1)}, f32[2,32]{1,0:T(2,128)S(1)}, u32[]{:S(2)}, u32[]{:S(2)}) collective-permute-start(f32[2,32]{1,0:T(2,128)S(1)} %pad_maximum_fusion.2), channel_id=1, source_target_pairs={{0,2},{2,0},{4,6},{6,4},{1,3},{3,1},{5,7},{7,5},{8,10},{10,8},{12,... | collective-permute-start | bytes 776 | tf_op jit(solution)/shard_map/ppermute | solution.py:30
  56.0 4.5 %collective-permute-start.1 = (f32[2,32]{1,0:T(2,128)S(1)}, f32[2,32]{1,0:T(2,128)S(1)}, u32[]{:S(2)}, u32[]{:S(2)}) collective-permute-start(f32[2,32]{1,0:T(2,128)S(1)} %fusion.39), channel_id=1, source_target_pairs={{0,4},{2,6},{4,0},{6,2},{1,5},{3,7},{5,1},{7,3},{8,12},{10,14},{12... | collective-permute-start | bytes 776 | tf_op jit(solution)/shard_map/ppermute | solution.py:30
  60.5 3.6 %collective-permute-start.2 = (f32[2,32]{1,0:T(2,128)S(1)}, f32[2,32]{1,0:T(2,128)S(1)}, u32[]{:S(2)}, u32[]{:S(2)}) collective-permute-start(f32[2,32]{1,0:T(2,128)S(1)} %fusion.59), channel_id=1, source_target_pairs={{0,1},{1,0},{2,3},{3,2},{4,5},{5,4},{6,7},{7,6},{8,9},{9,8},{10,11... | collective-permute-start | bytes 776 | tf_op jit(solution)/shard_map/ppermute | solution.py:30
  73.1 33.4 %copy-start.7 = (f32[1280]{0:T(1024)S(1)}, f32[1280]{0:T(1024)}, u32[]{:S(2)}) copy-start(f32[1280]{0:T(1024)} %param.13) | copy-start | bytes 15364
  73.1 33.4 %copy-start.8 = (f32[1280]{0:T(1024)S(1)}, f32[1280]{0:T(1024)}, u32[]{:S(2)}) copy-start(f32[1280]{0:T(1024)} %param.12) | copy-start | bytes 15364
  106.5 9.8 %copy-start.1 = (bf16[1,1280,3,320]{1,3,2,0:T(8,128)(2,1)S(1)}, bf16[1,1280,3,320]{1,3,2,0:T(8,128)(2,1)}, u32[]{:S(2)}) copy-start(bf16[1,1280,3,320]{1,3,2,0:T(8,128)(2,1)} %get-tuple-element.11) | copy-start | bytes 7372804
  110.2 11.6 %collective-permute-start.7 = (bf16[4,1,32,1280]{3,2,1,0:T(8,128)(2,1)S(1)}, bf16[4,1,32,1280]{3,2,1,0:T(8,128)(2,1)S(1)}, u32[]{:S(2)}, u32[]{:S(2)}) collective-permute-start(bf16[4,1,32,1280]{3,2,1,0:T(8,128)(2,1)S(1)} %get-tuple-element.26), channel_id=1, source_target_pairs={{1,0},{3,2},{5,4},{7,6},{9,8},{11,10},{13,12},{15,14},{17,16},{19,... | collective-permute-start | bytes 983048 | tf_op jit(solution)/shard_map/ppermute | solution.py:144
  111.5 11.2 %collective-permute-start.6 = (bf16[4,1,32,1280]{3,2,1,0:T(8,128)(2,1)S(1)}, bf16[4,1,32,1280]{3,2,1,0:T(8,128)(2,1)S(1)}, u32[]{:S(2)}, u32[]{:S(2)}) collective-permute-start(bf16[4,1,32,1280]{3,2,1,0:T(8,128)(2,1)S(1)} %get-tuple-element.25), channel_id=1, source_target_pairs={{0,1},{2,3},{4,5},{6,7},{8,9},{10,11},{12,13},{14,15},{16,17},{18,... | collective-permute-start | bytes 983048 | tf_op jit(solution)/shard_map/ppermute | solution.py:143
  121.8 1.8 copy-start.4
  127.7 6.2 %copy-start.6 = (bf16[3,1280,80]{1,2,0:T(8,128)(2,1)S(1)}, bf16[3,1280,80]{1,2,0:T(8,128)(2,1)}, u32[]{:S(2)}) copy-start(bf16[3,1280,80]{1,2,0:T(8,128)(2,1)} %param.11) | copy-start | bytes 1843204
  128.1 4.0 %collective-permute-start.8 = (f32[2,8]{1,0:T(2,128)S(1)}, f32[2,8]{1,0:T(2,128)S(1)}, u32[]{:S(2)}, u32[]{:S(2)}) collective-permute-start(f32[2,8]{1,0:T(2,128)S(1)} %pad_maximum_fusion.3), channel_id=1, source_target_pairs={{0,1},{1,0},{2,3},{3,2},{4,5},{5,4},{6,7},{7,6},{8,9},{9,8},{10,11... | collective-permute-start | bytes 200 | tf_op jit(solution)/shard_map/ppermute | solution.py:18
  133.9 13.6 %collective-permute-start.10 = (bf16[3,1280,80]{1,2,0:T(8,128)(2,1)S(1)}, bf16[3,1280,80]{1,2,0:T(8,128)(2,1)}, u32[]{:S(2)}, u32[]{:S(2)}) collective-permute-start(bf16[3,1280,80]{1,2,0:T(8,128)(2,1)S(1)} %copy-done.6), channel_id=1, source_target_pairs={{0,16},{8,24},{16,0},{24,8},{1,17},{9,25},{17,1},{25,9},{2,18},{10... | collective-permute-start | bytes 1843208 | tf_op jit(solution)/shard_map/ppermute | solution.py:40
  135.5 14.3 %collective-permute-start.9 = (bf16[3,1280,80]{1,2,0:T(8,128)(2,1)S(1)}, bf16[3,1280,80]{1,2,0:T(8,128)(2,1)}, u32[]{:S(2)}, u32[]{:S(2)}) collective-permute-start(bf16[3,1280,80]{1,2,0:T(8,128)(2,1)S(1)} %copy-done.6), channel_id=1, source_target_pairs={{0,8},{8,0},{16,24},{24,16},{1,9},{9,1},{17,25},{25,17},{2,10},{10... | collective-permute-start | bytes 1843208 | tf_op jit(solution)/shard_map/ppermute | solution.py:41
  147.5 3.8 %collective-permute-start.11 = (bf16[3,1280,80]{1,2,0:T(8,128)(2,1)}, bf16[3,1280,80]{1,2,0:T(8,128)(2,1)}, u32[]{:S(2)}, u32[]{:S(2)}) collective-permute-start(bf16[3,1280,80]{1,2,0:T(8,128)(2,1)} %collective-permute-done.10), channel_id=1, source_target_pairs={{0,8},{8,0},{16,24},{24,16},{1,9},{9,1},{17,25},{25,17},{2,10},{10... | collective-permute-start | bytes 1843208 | tf_op jit(solution)/shard_map/ppermute | solution.py:42
  162.3 6.9 %copy-start.2 = (bf16[4,8,32,320]{3,2,1,0:T(8,128)(2,1)S(1)}, bf16[4,8,32,320]{3,2,1,0:T(8,128)(2,1)}, u32[]{:S(2)}) copy-start(bf16[4,8,32,320]{3,2,1,0:T(8,128)(2,1)} %multiply_convert_fusion.1) | copy-start | bytes 1966084
  197.0 2.5 %copy-start.5 = (bf16[16,8,32,320]{3,2,1,0:T(8,128)(2,1)S(1)}, bf16[16,8,32,320]{3,2,1,0:T(8,128)(2,1)}, u32[]{:S(2)}) copy-start(bf16[16,8,32,320]{3,2,1,0:T(8,128)(2,1)} %all-gather.6.cloned.1.call-done) | copy-start | bytes 7864324
  199.6 2.2 copy-start
  204.0 9.7 %collective-permute-start.12 = (bf16[1,8,32,320]{3,2,1,0:T(8,128)(2,1)S(1)}, bf16[1,8,32,320]{3,2,1,0:T(8,128)(2,1)S(1)}, u32[]{:S(2)}, u32[]{:S(2)}) collective-permute-start(bf16[1,8,32,320]{3,2,1,0:T(8,128)(2,1)S(1)} %get-tuple-element.33), channel_id=1, source_target_pairs={{0,2},{2,4},{4,6},{6,0},{1,3},{3,5},{5,7},{7,1},{8,10},{10,12},{12... | collective-permute-start | bytes 491528 | tf_op jit(solution)/shard_map/ppermute | solution.py:226
  204.1 16.8 %collective-permute-start.13 = (bf16[1,8,32,320]{3,2,1,0:T(8,128)(2,1)S(1)}, bf16[1,8,32,320]{3,2,1,0:T(8,128)(2,1)S(1)}, u32[]{:S(2)}, u32[]{:S(2)}) collective-permute-start(bf16[1,8,32,320]{3,2,1,0:T(8,128)(2,1)S(1)} %get-tuple-element.32), channel_id=1, source_target_pairs={{0,4},{2,6},{4,0},{6,2},{1,5},{3,7},{5,1},{7,3},{8,12},{10,14},{12... | collective-permute-start | bytes 491528 | tf_op jit(solution)/shard_map/ppermute | solution.py:226
  205.4 15.5 %collective-permute-start.14 = (bf16[1,8,32,320]{3,2,1,0:T(8,128)(2,1)S(1)}, bf16[1,8,32,320]{3,2,1,0:T(8,128)(2,1)S(1)}, u32[]{:S(2)}, u32[]{:S(2)}) collective-permute-start(bf16[1,8,32,320]{3,2,1,0:T(8,128)(2,1)S(1)} %get-tuple-element.31), channel_id=1, source_target_pairs={{0,6},{2,0},{4,2},{6,4},{1,7},{3,1},{5,3},{7,5},{8,14},{10,8},{12,... | collective-permute-start | bytes 491528 | tf_op jit(solution)/shard_map/ppermute | solution.py:226
  223.6 1.4 copy-start.3
  223.6 1.4 copy-start.9
Sparse Core Ops, SparseCore 0:
  50.0 56.3 all-gather.3
  134.0 62.9 all-gather.5
